TPU v7x, 128 devices: a whole 4x4x4 slice. The times are simulated.
128 devices in a mesh: ind: 32 (over z_hi, x, y), win: 4 (over z_lo, core).
Axes of the slice: x: 4, y: 4, z: 4 (z_hi: 2, z_lo: 2; z = z_hi * 2 + z_lo), core: 2. Of those that a mesh axis runs over, the one named last changes fastest.
Arguments:
- dosage: bfloat16 [65536, 4096], P('ind', 'win'), may hold values from 0 to 2
- tail: bfloat16 [65536, 512], P('ind'), may hold values from 0 to 2
- missing: int32 [4608], replicated, may hold values from 0 to 32767
- start: float32 [8, 1024, 8], P('win'), may hold values from -6 to 6
Outputs:
- loadings: float32 [8, 1024, 8], P('win')
- variances: float32 [8, 8], P('win')
- scores: float32 [65536, 8], P('ind', 'win')
All inputs are finite; a program needn't handle non-finite values.
Results may differ from a plain program's by a relative error of at most 0.0024.
Values may be sent and summed in bfloat16 or wider, within the bound.
No kernel may reach another device: no remote copies, remote signals or barrier semaphores. Data moves between devices by JAX's collectives and lax.ppermute only.
A program may use at most 128 MiB of HBM per device.

v0:
```python
import jax
import jax.numpy as jnp
from jax import lax
from jax.sharding import PartitionSpec as P

ITERS = 6
HIGHEST = lax.Precision.HIGHEST


def passed_along(array, axis, by):
    size = lax.axis_size(axis)
    pairs = [(i, i + by) for i in range(size) if 0 <= i + by < size]
    return lax.ppermute(array, axis, pairs)


def swapped(value, axis, mask):
    size = lax.axis_size(axis)
    return lax.ppermute(value, axis, [(i, i ^ mask) for i in range(size)])


def summed(value, axis):
    size = lax.axis_size(axis)
    if size & (size - 1):
        return lax.psum(value, axis)
    bit = 1
    while bit < size:
        if bit * 4 <= size:
            near = swapped(value, axis, bit)
            mid = swapped(value, axis, 2 * bit)
            far = swapped(value, axis, 3 * bit)
            value = (value + near) + (mid + far)
            bit *= 4
        else:
            value = value + swapped(value, axis, bit)
            bit *= 2
    return value


def orthonormal(image):
    gram = jnp.einsum("swk,swl->skl", image, image, precision=HIGHEST)
    factor = jnp.linalg.cholesky(gram)
    solved = jax.vmap(lambda fac, rhs: jax.scipy.linalg.solve_triangular(fac, rhs, lower=True))(
        factor, jnp.swapaxes(image, 1, 2)
    )
    return jnp.swapaxes(solved, 1, 2)


def pieces(value):
    high = lax.reduce_precision(value, exponent_bits=8, mantissa_bits=7)
    rest = value - high
    mid = lax.reduce_precision(rest, exponent_bits=8, mantissa_bits=7)
    low = rest - mid
    return high.astype(jnp.bfloat16), mid.astype(jnp.bfloat16), low.astype(jnp.bfloat16)


def thirds(value):
    width = value.shape[1] // 3
    return (value[:, :width] + value[:, width : 2 * width]) + value[:, 2 * width :]


def product(left, right):
    l1, l2, l3 = pieces(left)
    r1, r2, r3 = pieces(right)
    lhs = jnp.concatenate([l1, l1, l2, l1, l2, l3], 1)
    rhs = jnp.concatenate([r1, r2, r1, r3, r2, r1], 1)
    return lax.dot_general(lhs, rhs, (((1,), (1,)), ((), ())), preferred_element_type=jnp.float32)


def widened(basis, half_cols):
    pad = jnp.zeros((half_cols, basis.shape[2]), basis.dtype)
    first = jnp.concatenate([basis[0], pad], axis=0)
    second = jnp.concatenate([pad, basis[1]], axis=0)
    return jnp.concatenate([first, second], axis=1)


def shards(dosage, tail, missing, start):
    win_count = lax.axis_size("win")
    position = lax.axis_index("win")
    columns = dosage.shape[1]
    half_cols = columns // 2
    comps = start.shape[2]
    total = dosage.shape[0] * lax.axis_size("ind")
    received = passed_along(dosage[:, :half_cols], "win", -1)
    following = jnp.where(position == win_count - 1, tail, received)
    region = jnp.concatenate([dosage, following], axis=1)
    regionf = region.astype(jnp.float32)
    stats = summed(jnp.stack([jnp.sum(regionf, axis=0), jnp.sum(regionf * regionf, axis=0)]), "ind")
    mean = stats[0] / total
    var = stats[1] / total - mean * mean
    miss_here = lax.dynamic_slice_in_dim(missing, position * columns, columns + half_cols)
    weight = jnp.sqrt((total - miss_here.astype(jnp.float32)) / total)
    stand = ((regionf - mean) / jnp.sqrt(var + 1e-05) * weight).astype(jnp.bfloat16)
    standf = stand.astype(jnp.float32)

    def project(basis):
        wide = widened(basis, half_cols)
        return thirds(jnp.dot(stand, jnp.concatenate(pieces(wide), 1), preferred_element_type=jnp.float32))

    def image_of(basis):
        proj = project(basis)
        split = jnp.concatenate(pieces(proj), 1)
        back = thirds(lax.dot_general(stand, split, (((0,), (0,)), ((), ())), preferred_element_type=jnp.float32))
        parts = jnp.stack([back[:columns, :comps], back[half_cols:, comps:]], 0)
        return summed(parts, "ind") / total

    basis = lax.fori_loop(0, ITERS, lambda step, basis: orthonormal(image_of(basis)), start)
    proj = project(basis)
    variances = summed(jnp.sum(proj * proj, axis=0), "ind").reshape(2, comps) / total
    first = standf[:, :columns] - product(proj[:, :comps], basis[0])
    second = standf[:, half_cols:] - product(proj[:, comps:], basis[1])
    scores = jnp.stack([jnp.sum(first * first, axis=1), jnp.sum(second * second, axis=1)], 1) / columns
    return (basis, variances, scores)


def solution(mesh):
    in_specs = (P("ind", "win"), P("ind", None), P(), P("win", None, None))
    out_specs = (P("win", None, None), P("win", None), P("ind", "win"))
    return jax.shard_map(shards, mesh=mesh, in_specs=in_specs, out_specs=out_specs, check_vma=False)
```

profile of v0, /device:TPU:32, one launch (start us, length us, event | category | flops | bytes accessed | tf_op | source)
XLA Modules:
  0.0 296.6 jit_solution(14299437457779430909)
XLA Ops:
  0.6 6.6 %copy.19 = bf16[2048,1024]{0,1:T(8,128)(2,1)} copy(bf16[2048,1024]{1,0:T(8,128)(2,1)} %param.6) | data formatting | bytes 8388608 | tf_op args[0]
  7.3 3.1 %slice.100 = bf16[2048,512]{0,1:T(8,128)(2,1)} slice(bf16[2048,1024]{0,1:T(8,128)(2,1)} %copy.19), slice={[0:2048], [0:512]} | slice | bytes 4194304 | tf_op jit(solution)/shard_map/slice | solution.py:83
  12.3 2.5 copy.18
  14.8 21.3 %collective-permute-done.7 = bf16[2048,512]{0,1:T(8,128)(2,1)} collective-permute-done((bf16[2048,512]{0,1:T(8,128)(2,1)}, bf16[2048,512]{0,1:T(8,128)(2,1)}, u32[]{:S(2)}, u32[]{:S(2)}) %collective-permute-start.7) | collective-permute-done | bytes 2097184 | tf_op jit(solution)/shard_map/ppermute | solution.py:13
  38.0 3.7 %convert_reduce_fusion = (f32[1536]{0:T(1024)S(1)}, f32[1536]{0:T(1024)S(1)}) fusion(bf16[2048,512]{0,1:T(8,128)(2,1)S(1)} %broadcast_select_fusion, bf16[2048,1024]{0,1:T(8,128)(2,1)S(1)} %copy-done.2), kind=kLoop, calls=%fused_computation.53 | loop fusion | flops 22017024 | bytes 6303744 | tf_op jit(solution)/shard_map/reduce_sum | solution.py:87
  41.7 3.1 %collective-permute-start.10 = (f32[2,1536]{1,0:T(2,128)S(1)}, f32[2,1536]{1,0:T(2,128)S(1)}, u32[]{:S(2)}, u32[]{:S(2)}) collective-permute-start(f32[2,1536]{1,0:T(2,128)S(1)} %pad_maximum_fusion.2), channel_id=1, source_target_pairs={{0,12},{4,8},{8,4},{12,0},{16,28},{20,24},{24,20},{28,16},{32,44},... | collective-permute-start | bytes 36872 | tf_op jit(solution)/shard_map/ppermute | solution.py:18
  51.8 2.7 collective-permute-start.12
  57.0 2.4 collective-permute-done.13
  59.4 3.2 %collective-permute-start.14 = (f32[2,1536]{1,0:T(2,128)S(1)}, f32[2,1536]{1,0:T(2,128)S(1)}, u32[]{:S(2)}, u32[]{:S(2)}) collective-permute-start(f32[2,1536]{1,0:T(2,128)S(1)} %add_add_fusion.2), channel_id=1, source_target_pairs={{0,64},{4,68},{8,72},{12,76},{16,80},{20,84},{24,88},{28,92},{32,9... | collective-permute-start | bytes 36872 | tf_op jit(solution)/shard_map/ppermute | solution.py:18
  64.8 9.6 %fusion.42 = (f32[2048,1536]{0,1:T(8,128)}, bf16[2048,1536]{0,1:T(8,128)(2,1)}) fusion(f32[1536]{0:T(1024)S(1)} %multiply_sqrt_fusion, f32[1536]{0:T(1024)S(1)} %get-tuple-element.30, f32[1536]{0:T(1024)S(1)} %get-tuple-element.29, bf16[2048,512]{0,1:T(8,128)(2,1)S(1)} %broadcast_select_fusion, bf16[2048,1024]{0,1:T(8,128)(2,1)} %copy.19), kind=kLoop, calls=%fused_computation.143 | loop fusion | flops 28311552 | bytes 25184256 | tf_op jit(solution)/shard_map/convert_element_type | solution.py:93
  74.3 8.8 %copy.20 = bf16[2048,1536]{1,0:T(8,128)(2,1)} copy(bf16[2048,1536]{0,1:T(8,128)(2,1)} %get-tuple-element.40) | data formatting | bytes 12582912 | tf_op jit(solution)/shard_map/while | solution.py:106
  83.1 184.7 %while.10 = (s32[]{:T(128)}, f32[2,1024,8]{1,2,0:T(8,128)S(1)}, bf16[2048,1536]{1,0:T(8,128)(2,1)}, s32[]{:T(128)}) while((s32[]{:T(128)}, f32[2,1024,8]{1,2,0:T(8,128)S(1)}, bf16[2048,1536]{1,0:T(8,128)(2,1)}, s32[]{:T(128)}) %tuple.57), condition=%wide.region_5.6_spmd, body=%wide.region_2.5_spmd.sunk | while | flops 609027072 | bytes 43456232 | solution.py:106
  83.1 4.9 %convolution_bitcast_fusion.4 = f32[2048,48]{0,1:T(8,128)S(1)} fusion(bf16[2048,1536]{1,0:T(8,128)(2,1)} %get-tuple-element.122, bf16[1536,16]{0,1:T(8,128)(2,1)S(1)} %get-tuple-element.103, bf16[1536,16]{0,1:T(8,128)(2,1)S(1)} %get-tuple-element.104, bf16[1536,16]{0,1:T(8,128)(2,1)S(1)} %get-tuple-element.105), kind=kOutput, calls=%fused_computation.1.clone.1 | convolution fusion | flops 302432256 | bytes 6832128 | tf_op jit(solution)/shard_map/while/body/eval_jaxpr/dot_general | solution.py:97
  90.9 3.0 %collective-permute-start.1 = (f32[2,1024,8]{1,2,0:T(8,128)S(1)}, f32[2,1024,8]{1,2,0:T(8,128)S(1)}, u32[]{:S(2)}, u32[]{:S(2)}) collective-permute-start(f32[2,1024,8]{1,2,0:T(8,128)S(1)} %pad_maximum_fusion.4), channel_id=1, source_target_pairs={{0,12},{4,8},{8,4},{12,0},{16,28},{20,24},{24,20},{28,16},{32,44},... | collective-permute-start | bytes 196616 | tf_op jit(solution)/shard_map/while/body/eval_jaxpr/ppermute | solution.py:18
  101.8 2.8 collective-permute-done.3
  105.9 3.1 %collective-permute-start.6 = (f32[2,1024,8]{1,2,0:T(8,128)S(1)}, f32[2,1024,8]{1,2,0:T(8,128)S(1)}, u32[]{:S(2)}, u32[]{:S(2)}) collective-permute-start(f32[2,1024,8]{1,2,0:T(8,128)S(1)} %add_add_fusion.9), channel_id=1, source_target_pairs={{0,64},{4,68},{8,72},{12,76},{16,80},{20,84},{24,88},{28,92},{32,9... | collective-permute-start | bytes 196616 | tf_op jit(solution)/shard_map/while/body/eval_jaxpr/ppermute | solution.py:18
  109.0 2.8 collective-permute-done.6
  115.4 4.9 %convolution_bitcast_fusion.4 = f32[2048,48]{0,1:T(8,128)S(1)} fusion(bf16[2048,1536]{1,0:T(8,128)(2,1)} %get-tuple-element.122, bf16[1536,16]{0,1:T(8,128)(2,1)S(1)} %get-tuple-element.103, bf16[1536,16]{0,1:T(8,128)(2,1)S(1)} %get-tuple-element.104, bf16[1536,16]{0,1:T(8,128)(2,1)S(1)} %get-tuple-element.105), kind=kOutput, calls=%fused_computation.1.clone.1 | convolution fusion | flops 302432256 | bytes 6832128 | tf_op jit(solution)/shard_map/while/body/eval_jaxpr/dot_general | solution.py:97
  121.8 2.7 collective-permute-start.1
  125.1 2.5 collective-permute-done
  132.4 2.3 collective-permute-done.3
  136.3 3.1 %collective-permute-start.6 = (f32[2,1024,8]{1,2,0:T(8,128)S(1)}, f32[2,1024,8]{1,2,0:T(8,128)S(1)}, u32[]{:S(2)}, u32[]{:S(2)}) collective-permute-start(f32[2,1024,8]{1,2,0:T(8,128)S(1)} %add_add_fusion.9), channel_id=1, source_target_pairs={{0,64},{4,68},{8,72},{12,76},{16,80},{20,84},{24,88},{28,92},{32,9... | collective-permute-start | bytes 196616 | tf_op jit(solution)/shard_map/while/body/eval_jaxpr/ppermute | solution.py:18
  139.4 2.8 collective-permute-done.6
  145.8 4.9 %convolution_bitcast_fusion.4 = f32[2048,48]{0,1:T(8,128)S(1)} fusion(bf16[2048,1536]{1,0:T(8,128)(2,1)} %get-tuple-element.122, bf16[1536,16]{0,1:T(8,128)(2,1)S(1)} %get-tuple-element.103, bf16[1536,16]{0,1:T(8,128)(2,1)S(1)} %get-tuple-element.104, bf16[1536,16]{0,1:T(8,128)(2,1)S(1)} %get-tuple-element.105), kind=kOutput, calls=%fused_computation.1.clone.1 | convolution fusion | flops 302432256 | bytes 6832128 | tf_op jit(solution)/shard_map/while/body/eval_jaxpr/dot_general | solution.py:97
  155.5 2.3 collective-permute-done
  160.2 2.4 collective-permute-start.4
  163.0 2.3 collective-permute-done.3
  166.9 3.1 %collective-permute-start.6 = (f32[2,1024,8]{1,2,0:T(8,128)S(1)}, f32[2,1024,8]{1,2,0:T(8,128)S(1)}, u32[]{:S(2)}, u32[]{:S(2)}) collective-permute-start(f32[2,1024,8]{1,2,0:T(8,128)S(1)} %add_add_fusion.9), channel_id=1, source_target_pairs={{0,64},{4,68},{8,72},{12,76},{16,80},{20,84},{24,88},{28,92},{32,9... | collective-permute-start | bytes 196616 | tf_op jit(solution)/shard_map/while/body/eval_jaxpr/ppermute | solution.py:18
  170.0 2.8 collective-permute-done.6
  176.4 4.9 %convolution_bitcast_fusion.4 = f32[2048,48]{0,1:T(8,128)S(1)} fusion(bf16[2048,1536]{1,0:T(8,128)(2,1)} %get-tuple-element.122, bf16[1536,16]{0,1:T(8,128)(2,1)S(1)} %get-tuple-element.103, bf16[1536,16]{0,1:T(8,128)(2,1)S(1)} %get-tuple-element.104, bf16[1536,16]{0,1:T(8,128)(2,1)S(1)} %get-tuple-element.105), kind=kOutput, calls=%fused_computation.1.clone.1 | convolution fusion | flops 302432256 | bytes 6832128 | tf_op jit(solution)/shard_map/while/body/eval_jaxpr/dot_general | solution.py:97
  186.1 2.3 collective-permute-done
  193.5 2.3 collective-permute-done.3
  197.4 3.1 %collective-permute-start.6 = (f32[2,1024,8]{1,2,0:T(8,128)S(1)}, f32[2,1024,8]{1,2,0:T(8,128)S(1)}, u32[]{:S(2)}, u32[]{:S(2)}) collective-permute-start(f32[2,1024,8]{1,2,0:T(8,128)S(1)} %add_add_fusion.9), channel_id=1, source_target_pairs={{0,64},{4,68},{8,72},{12,76},{16,80},{20,84},{24,88},{28,92},{32,9... | collective-permute-start | bytes 196616 | tf_op jit(solution)/shard_map/while/body/eval_jaxpr/ppermute | solution.py:18
  200.5 2.8 collective-permute-done.6
  206.9 4.9 %convolution_bitcast_fusion.4 = f32[2048,48]{0,1:T(8,128)S(1)} fusion(bf16[2048,1536]{1,0:T(8,128)(2,1)} %get-tuple-element.122, bf16[1536,16]{0,1:T(8,128)(2,1)S(1)} %get-tuple-element.103, bf16[1536,16]{0,1:T(8,128)(2,1)S(1)} %get-tuple-element.104, bf16[1536,16]{0,1:T(8,128)(2,1)S(1)} %get-tuple-element.105), kind=kOutput, calls=%fused_computation.1.clone.1 | convolution fusion | flops 302432256 | bytes 6832128 | tf_op jit(solution)/shard_map/while/body/eval_jaxpr/dot_general | solution.py:97
  216.6 2.3 collective-permute-done
  224.0 2.3 collective-permute-done.3
  228.0 3.1 %collective-permute-start.6 = (f32[2,1024,8]{1,2,0:T(8,128)S(1)}, f32[2,1024,8]{1,2,0:T(8,128)S(1)}, u32[]{:S(2)}, u32[]{:S(2)}) collective-permute-start(f32[2,1024,8]{1,2,0:T(8,128)S(1)} %add_add_fusion.9), channel_id=1, source_target_pairs={{0,64},{4,68},{8,72},{12,76},{16,80},{20,84},{24,88},{28,92},{32,9... | collective-permute-start | bytes 196616 | tf_op jit(solution)/shard_map/while/body/eval_jaxpr/ppermute | solution.py:18
  231.1 2.8 collective-permute-done.6
  237.5 4.9 %convolution_bitcast_fusion.4 = f32[2048,48]{0,1:T(8,128)S(1)} fusion(bf16[2048,1536]{1,0:T(8,128)(2,1)} %get-tuple-element.122, bf16[1536,16]{0,1:T(8,128)(2,1)S(1)} %get-tuple-element.103, bf16[1536,16]{0,1:T(8,128)(2,1)S(1)} %get-tuple-element.104, bf16[1536,16]{0,1:T(8,128)(2,1)S(1)} %get-tuple-element.105), kind=kOutput, calls=%fused_computation.1.clone.1 | convolution fusion | flops 302432256 | bytes 6832128 | tf_op jit(solution)/shard_map/while/body/eval_jaxpr/dot_general | solution.py:97
  247.2 2.3 collective-permute-done
  258.4 3.1 %collective-permute-start.6 = (f32[2,1024,8]{1,2,0:T(8,128)S(1)}, f32[2,1024,8]{1,2,0:T(8,128)S(1)}, u32[]{:S(2)}, u32[]{:S(2)}) collective-permute-start(f32[2,1024,8]{1,2,0:T(8,128)S(1)} %add_add_fusion.9), channel_id=1, source_target_pairs={{0,64},{4,68},{8,72},{12,76},{16,80},{20,84},{24,88},{28,92},{32,9... | collective-permute-start | bytes 196616 | tf_op jit(solution)/shard_map/while/body/eval_jaxpr/ppermute | solution.py:18
  261.5 2.8 collective-permute-done.6
  267.9 4.2 %fusion.28 = f32[2048,48]{0,1:T(8,128)S(1)} fusion(bf16[2048,1536]{0,1:T(8,128)(2,1)} %get-tuple-element.40, bf16[1536,16]{0,1:T(8,128)(2,1)S(1)} %get-tuple-element.68, bf16[1536,16]{0,1:T(8,128)(2,1)S(1)} %get-tuple-element.67, bf16[1536,16]{0,1:T(8,128)(2,1)S(1)} %get-tuple-element.66), kind=kOutput, calls=%fused_computation.66 | convolution fusion | flops 302432256 | bytes 6832128 | tf_op jit(solution)/shard_map/dot_general | solution.py:97
  272.7 2.7 collective-permute-start.16
  277.3 4.7 %fusion.27 = f32[2048]{0:T(1024)S(1)} fusion(f32[2048,1536]{0,1:T(8,128)} %get-tuple-element.39, bf16[2048,48]{0,1:T(8,128)(2,1)S(1)} %get-tuple-element.52, bf16[1024,48]{0,1:T(8,128)(2,1)S(1)} %get-tuple-element.56), kind=kOutput, calls=%fused_computation.63 | convolution fusion | flops 207616000 | bytes 8691712 | tf_op jit(solution)/shard_map/dot_general | solution.py:66
  283.8 2.3 collective-permute-start.19
  290.9 3.0 %collective-permute-start.21 = (f32[16]{0:T(128)S(1)}, f32[16]{0:T(128)S(1)}, u32[]{:S(2)}, u32[]{:S(2)}) collective-permute-start(f32[16]{0:T(128)S(1)} %add_add_fusion.4), channel_id=1, source_target_pairs={{0,64},{4,68},{8,72},{12,76},{16,80},{20,84},{24,88},{28,92},{32,9... | collective-permute-start | bytes 200 | tf_op jit(solution)/shard_map/ppermute | solution.py:18
  (264 shorter events, 115.1 us)
Async XLA Ops:
  10.4 25.8 %collective-permute-start.7 = (bf16[2048,512]{0,1:T(8,128)(2,1)}, bf16[2048,512]{0,1:T(8,128)(2,1)}, u32[]{:S(2)}, u32[]{:S(2)}) collective-permute-start(bf16[2048,512]{0,1:T(8,128)(2,1)} %slice.100), channel_id=1, source_target_pairs={{1,0},{2,1},{3,2},{5,4},{6,5},{7,6},{9,8},{10,9},{11,10},{13,12},{... | collective-permute-start | bytes 6291464 | tf_op jit(solution)/shard_map/ppermute | solution.py:13
  41.7 5.0 %collective-permute-start.10 = (f32[2,1536]{1,0:T(2,128)S(1)}, f32[2,1536]{1,0:T(2,128)S(1)}, u32[]{:S(2)}, u32[]{:S(2)}) collective-permute-start(f32[2,1536]{1,0:T(2,128)S(1)} %pad_maximum_fusion.2), channel_id=1, source_target_pairs={{0,12},{4,8},{8,4},{12,0},{16,28},{20,24},{24,20},{28,16},{32,44},... | collective-permute-start | bytes 36872 | tf_op jit(solution)/shard_map/ppermute | solution.py:18
  45.0 5.2 %collective-permute-start.9 = (f32[2,1536]{1,0:T(2,128)S(1)}, f32[2,1536]{1,0:T(2,128)S(1)}, u32[]{:S(2)}, u32[]{:S(2)}) collective-permute-start(f32[2,1536]{1,0:T(2,128)S(1)} %pad_maximum_fusion.2), channel_id=1, source_target_pairs={{0,8},{4,12},{8,0},{12,4},{16,24},{20,28},{24,16},{28,20},{32,40},... | collective-permute-start | bytes 36872 | tf_op jit(solution)/shard_map/ppermute | solution.py:18
  50.2 4.8 %collective-permute-start.11 = (f32[2,1536]{1,0:T(2,128)S(1)}, f32[2,1536]{1,0:T(2,128)S(1)}, u32[]{:S(2)}, u32[]{:S(2)}) collective-permute-start(f32[2,1536]{1,0:T(2,128)S(1)} %add_add_fusion.3), channel_id=1, source_target_pairs={{0,16},{4,20},{8,24},{12,28},{16,0},{20,4},{24,8},{28,12},{32,48},... | collective-permute-start | bytes 36872 | tf_op jit(solution)/shard_map/ppermute | solution.py:18
  51.8 5.2 %collective-permute-start.12 = (f32[2,1536]{1,0:T(2,128)S(1)}, f32[2,1536]{1,0:T(2,128)S(1)}, u32[]{:S(2)}, u32[]{:S(2)}) collective-permute-start(f32[2,1536]{1,0:T(2,128)S(1)} %add_add_fusion.3), channel_id=1, source_target_pairs={{0,32},{4,36},{8,40},{12,44},{16,48},{20,52},{24,56},{28,60},{32,0... | collective-permute-start | bytes 36872 | tf_op jit(solution)/shard_map/ppermute | solution.py:18
  54.5 4.9 %collective-permute-start.13 = (f32[2,1536]{1,0:T(2,128)S(1)}, f32[2,1536]{1,0:T(2,128)S(1)}, u32[]{:S(2)}, u32[]{:S(2)}) collective-permute-start(f32[2,1536]{1,0:T(2,128)S(1)} %add_add_fusion.3), channel_id=1, source_target_pairs={{0,48},{4,52},{8,56},{12,60},{16,32},{20,36},{24,40},{28,44},{32,1... | collective-permute-start | bytes 36872 | tf_op jit(solution)/shard_map/ppermute | solution.py:18
  59.4 5.3 %collective-permute-start.14 = (f32[2,1536]{1,0:T(2,128)S(1)}, f32[2,1536]{1,0:T(2,128)S(1)}, u32[]{:S(2)}, u32[]{:S(2)}) collective-permute-start(f32[2,1536]{1,0:T(2,128)S(1)} %add_add_fusion.2), channel_id=1, source_target_pairs={{0,64},{4,68},{8,72},{12,76},{16,80},{20,84},{24,88},{28,92},{32,9... | collective-permute-start | bytes 36872 | tf_op jit(solution)/shard_map/ppermute | solution.py:18
  89.3 5.8 %collective-permute-start = (f32[2,1024,8]{1,2,0:T(8,128)S(1)}, f32[2,1024,8]{1,2,0:T(8,128)S(1)}, u32[]{:S(2)}, u32[]{:S(2)}) collective-permute-start(f32[2,1024,8]{1,2,0:T(8,128)S(1)} %pad_maximum_fusion.4), channel_id=1, source_target_pairs={{0,8},{4,12},{8,0},{12,4},{16,24},{20,28},{24,16},{28,20},{32,40},... | collective-permute-start | bytes 196616 | tf_op jit(solution)/shard_map/while/body/eval_jaxpr/ppermute | solution.py:18
  90.9 5.6 %collective-permute-start.1 = (f32[2,1024,8]{1,2,0:T(8,128)S(1)}, f32[2,1024,8]{1,2,0:T(8,128)S(1)}, u32[]{:S(2)}, u32[]{:S(2)}) collective-permute-start(f32[2,1024,8]{1,2,0:T(8,128)S(1)} %pad_maximum_fusion.4), channel_id=1, source_target_pairs={{0,12},{4,8},{8,4},{12,0},{16,28},{20,24},{24,20},{28,16},{32,44},... | collective-permute-start | bytes 196616 | tf_op jit(solution)/shard_map/while/body/eval_jaxpr/ppermute | solution.py:18
  93.9 4.3 %collective-permute-start.2 = (f32[2,1024,8]{1,2,0:T(8,128)S(1)}, f32[2,1024,8]{1,2,0:T(8,128)S(1)}, u32[]{:S(2)}, u32[]{:S(2)}) collective-permute-start(f32[2,1024,8]{1,2,0:T(8,128)S(1)} %pad_maximum_fusion.4), channel_id=1, source_target_pairs={{0,4},{4,0},{8,12},{12,8},{16,20},{20,16},{24,28},{28,24},{32,36},... | collective-permute-start | bytes 196616 | tf_op jit(solution)/shard_map/while/body/eval_jaxpr/ppermute | solution.py:18
  98.2 6.4 %collective-permute-start.3 = (f32[2,1024,8]{1,2,0:T(8,128)S(1)}, f32[2,1024,8]{1,2,0:T(8,128)S(1)}, u32[]{:S(2)}, u32[]{:S(2)}) collective-permute-start(f32[2,1024,8]{1,2,0:T(8,128)S(1)} %add_add_fusion.8), channel_id=1, source_target_pairs={{0,32},{4,36},{8,40},{12,44},{16,48},{20,52},{24,56},{28,60},{32,0... | collective-permute-start | bytes 196616 | tf_op jit(solution)/shard_map/while/body/eval_jaxpr/ppermute | solution.py:18
  98.8 7.1 %collective-permute-start.4 = (f32[2,1024,8]{1,2,0:T(8,128)S(1)}, f32[2,1024,8]{1,2,0:T(8,128)S(1)}, u32[]{:S(2)}, u32[]{:S(2)}) collective-permute-start(f32[2,1024,8]{1,2,0:T(8,128)S(1)} %add_add_fusion.8), channel_id=1, source_target_pairs={{0,48},{4,52},{8,56},{12,60},{16,32},{20,36},{24,40},{28,44},{32,1... | collective-permute-start | bytes 196616 | tf_op jit(solution)/shard_map/while/body/eval_jaxpr/ppermute | solution.py:18
  100.2 5.7 %collective-permute-start.5 = (f32[2,1024,8]{1,2,0:T(8,128)S(1)}, f32[2,1024,8]{1,2,0:T(8,128)S(1)}, u32[]{:S(2)}, u32[]{:S(2)}) collective-permute-start(f32[2,1024,8]{1,2,0:T(8,128)S(1)} %add_add_fusion.8), channel_id=1, source_target_pairs={{0,16},{4,20},{8,24},{12,28},{16,0},{20,4},{24,8},{28,12},{32,48},... | collective-permute-start | bytes 196616 | tf_op jit(solution)/shard_map/while/body/eval_jaxpr/ppermute | solution.py:18
  105.9 5.8 %collective-permute-start.6 = (f32[2,1024,8]{1,2,0:T(8,128)S(1)}, f32[2,1024,8]{1,2,0:T(8,128)S(1)}, u32[]{:S(2)}, u32[]{:S(2)}) collective-permute-start(f32[2,1024,8]{1,2,0:T(8,128)S(1)} %add_add_fusion.9), channel_id=1, source_target_pairs={{0,64},{4,68},{8,72},{12,76},{16,80},{20,84},{24,88},{28,92},{32,9... | collective-permute-start | bytes 196616 | tf_op jit(solution)/shard_map/while/body/eval_jaxpr/ppermute | solution.py:18
  121.5 6.1 %collective-permute-start = (f32[2,1024,8]{1,2,0:T(8,128)S(1)}, f32[2,1024,8]{1,2,0:T(8,128)S(1)}, u32[]{:S(2)}, u32[]{:S(2)}) collective-permute-start(f32[2,1024,8]{1,2,0:T(8,128)S(1)} %pad_maximum_fusion.4), channel_id=1, source_target_pairs={{0,8},{4,12},{8,0},{12,4},{16,24},{20,28},{24,16},{28,20},{32,40},... | collective-permute-start | bytes 196616 | tf_op jit(solution)/shard_map/while/body/eval_jaxpr/ppermute | solution.py:18
  121.8 6.2 %collective-permute-start.1 = (f32[2,1024,8]{1,2,0:T(8,128)S(1)}, f32[2,1024,8]{1,2,0:T(8,128)S(1)}, u32[]{:S(2)}, u32[]{:S(2)}) collective-permute-start(f32[2,1024,8]{1,2,0:T(8,128)S(1)} %pad_maximum_fusion.4), channel_id=1, source_target_pairs={{0,12},{4,8},{8,4},{12,0},{16,28},{20,24},{24,20},{28,16},{32,44},... | collective-permute-start | bytes 196616 | tf_op jit(solution)/shard_map/while/body/eval_jaxpr/ppermute | solution.py:18
  128.9 5.9 %collective-permute-start.3 = (f32[2,1024,8]{1,2,0:T(8,128)S(1)}, f32[2,1024,8]{1,2,0:T(8,128)S(1)}, u32[]{:S(2)}, u32[]{:S(2)}) collective-permute-start(f32[2,1024,8]{1,2,0:T(8,128)S(1)} %add_add_fusion.8), channel_id=1, source_target_pairs={{0,32},{4,36},{8,40},{12,44},{16,48},{20,52},{24,56},{28,60},{32,0... | collective-permute-start | bytes 196616 | tf_op jit(solution)/shard_map/while/body/eval_jaxpr/ppermute | solution.py:18
  129.8 5.6 %collective-permute-start.4 = (f32[2,1024,8]{1,2,0:T(8,128)S(1)}, f32[2,1024,8]{1,2,0:T(8,128)S(1)}, u32[]{:S(2)}, u32[]{:S(2)}) collective-permute-start(f32[2,1024,8]{1,2,0:T(8,128)S(1)} %add_add_fusion.8), channel_id=1, source_target_pairs={{0,48},{4,52},{8,56},{12,60},{16,32},{20,36},{24,40},{28,44},{32,1... | collective-permute-start | bytes 196616 | tf_op jit(solution)/shard_map/while/body/eval_jaxpr/ppermute | solution.py:18
  136.3 5.8 %collective-permute-start.6 = (f32[2,1024,8]{1,2,0:T(8,128)S(1)}, f32[2,1024,8]{1,2,0:T(8,128)S(1)}, u32[]{:S(2)}, u32[]{:S(2)}) collective-permute-start(f32[2,1024,8]{1,2,0:T(8,128)S(1)} %add_add_fusion.9), channel_id=1, source_target_pairs={{0,64},{4,68},{8,72},{12,76},{16,80},{20,84},{24,88},{28,92},{32,9... | collective-permute-start | bytes 196616 | tf_op jit(solution)/shard_map/while/body/eval_jaxpr/ppermute | solution.py:18
  152.0 5.8 %collective-permute-start = (f32[2,1024,8]{1,2,0:T(8,128)S(1)}, f32[2,1024,8]{1,2,0:T(8,128)S(1)}, u32[]{:S(2)}, u32[]{:S(2)}) collective-permute-start(f32[2,1024,8]{1,2,0:T(8,128)S(1)} %pad_maximum_fusion.4), channel_id=1, source_target_pairs={{0,8},{4,12},{8,0},{12,4},{16,24},{20,28},{24,16},{28,20},{32,40},... | collective-permute-start | bytes 196616 | tf_op jit(solution)/shard_map/while/body/eval_jaxpr/ppermute | solution.py:18
  153.9 5.5 %collective-permute-start.1 = (f32[2,1024,8]{1,2,0:T(8,128)S(1)}, f32[2,1024,8]{1,2,0:T(8,128)S(1)}, u32[]{:S(2)}, u32[]{:S(2)}) collective-permute-start(f32[2,1024,8]{1,2,0:T(8,128)S(1)} %pad_maximum_fusion.4), channel_id=1, source_target_pairs={{0,12},{4,8},{8,4},{12,0},{16,28},{20,24},{24,20},{28,16},{32,44},... | collective-permute-start | bytes 196616 | tf_op jit(solution)/shard_map/while/body/eval_jaxpr/ppermute | solution.py:18
  155.0 4.4 %collective-permute-start.2 = (f32[2,1024,8]{1,2,0:T(8,128)S(1)}, f32[2,1024,8]{1,2,0:T(8,128)S(1)}, u32[]{:S(2)}, u32[]{:S(2)}) collective-permute-start(f32[2,1024,8]{1,2,0:T(8,128)S(1)} %pad_maximum_fusion.4), channel_id=1, source_target_pairs={{0,4},{4,0},{8,12},{12,8},{16,20},{20,16},{24,28},{28,24},{32,36},... | collective-permute-start | bytes 196616 | tf_op jit(solution)/shard_map/while/body/eval_jaxpr/ppermute | solution.py:18
  159.4 5.9 %collective-permute-start.3 = (f32[2,1024,8]{1,2,0:T(8,128)S(1)}, f32[2,1024,8]{1,2,0:T(8,128)S(1)}, u32[]{:S(2)}, u32[]{:S(2)}) collective-permute-start(f32[2,1024,8]{1,2,0:T(8,128)S(1)} %add_add_fusion.8), channel_id=1, source_target_pairs={{0,32},{4,36},{8,40},{12,44},{16,48},{20,52},{24,56},{28,60},{32,0... | collective-permute-start | bytes 196616 | tf_op jit(solution)/shard_map/while/body/eval_jaxpr/ppermute | solution.py:18
  160.2 5.7 %collective-permute-start.4 = (f32[2,1024,8]{1,2,0:T(8,128)S(1)}, f32[2,1024,8]{1,2,0:T(8,128)S(1)}, u32[]{:S(2)}, u32[]{:S(2)}) collective-permute-start(f32[2,1024,8]{1,2,0:T(8,128)S(1)} %add_add_fusion.8), channel_id=1, source_target_pairs={{0,48},{4,52},{8,56},{12,60},{16,32},{20,36},{24,40},{28,44},{32,1... | collective-permute-start | bytes 196616 | tf_op jit(solution)/shard_map/while/body/eval_jaxpr/ppermute | solution.py:18
  166.9 5.8 %collective-permute-start.6 = (f32[2,1024,8]{1,2,0:T(8,128)S(1)}, f32[2,1024,8]{1,2,0:T(8,128)S(1)}, u32[]{:S(2)}, u32[]{:S(2)}) collective-permute-start(f32[2,1024,8]{1,2,0:T(8,128)S(1)} %add_add_fusion.9), channel_id=1, source_target_pairs={{0,64},{4,68},{8,72},{12,76},{16,80},{20,84},{24,88},{28,92},{32,9... | collective-permute-start | bytes 196616 | tf_op jit(solution)/shard_map/while/body/eval_jaxpr/ppermute | solution.py:18
  182.6 5.8 %collective-permute-start = (f32[2,1024,8]{1,2,0:T(8,128)S(1)}, f32[2,1024,8]{1,2,0:T(8,128)S(1)}, u32[]{:S(2)}, u32[]{:S(2)}) collective-permute-start(f32[2,1024,8]{1,2,0:T(8,128)S(1)} %pad_maximum_fusion.4), channel_id=1, source_target_pairs={{0,8},{4,12},{8,0},{12,4},{16,24},{20,28},{24,16},{28,20},{32,40},... | collective-permute-start | bytes 196616 | tf_op jit(solution)/shard_map/while/body/eval_jaxpr/ppermute | solution.py:18
  183.9 5.5 %collective-permute-start.1 = (f32[2,1024,8]{1,2,0:T(8,128)S(1)}, f32[2,1024,8]{1,2,0:T(8,128)S(1)}, u32[]{:S(2)}, u32[]{:S(2)}) collective-permute-start(f32[2,1024,8]{1,2,0:T(8,128)S(1)} %pad_maximum_fusion.4), channel_id=1, source_target_pairs={{0,12},{4,8},{8,4},{12,0},{16,28},{20,24},{24,20},{28,16},{32,44},... | collective-permute-start | bytes 196616 | tf_op jit(solution)/shard_map/while/body/eval_jaxpr/ppermute | solution.py:18
  189.9 5.8 %collective-permute-start.3 = (f32[2,1024,8]{1,2,0:T(8,128)S(1)}, f32[2,1024,8]{1,2,0:T(8,128)S(1)}, u32[]{:S(2)}, u32[]{:S(2)}) collective-permute-start(f32[2,1024,8]{1,2,0:T(8,128)S(1)} %add_add_fusion.8), channel_id=1, source_target_pairs={{0,32},{4,36},{8,40},{12,44},{16,48},{20,52},{24,56},{28,60},{32,0... | collective-permute-start | bytes 196616 | tf_op jit(solution)/shard_map/while/body/eval_jaxpr/ppermute | solution.py:18
  191.1 5.5 %collective-permute-start.4 = (f32[2,1024,8]{1,2,0:T(8,128)S(1)}, f32[2,1024,8]{1,2,0:T(8,128)S(1)}, u32[]{:S(2)}, u32[]{:S(2)}) collective-permute-start(f32[2,1024,8]{1,2,0:T(8,128)S(1)} %add_add_fusion.8), channel_id=1, source_target_pairs={{0,48},{4,52},{8,56},{12,60},{16,32},{20,36},{24,40},{28,44},{32,1... | collective-permute-start | bytes 196616 | tf_op jit(solution)/shard_map/while/body/eval_jaxpr/ppermute | solution.py:18
  193.1 4.3 %collective-permute-start.5 = (f32[2,1024,8]{1,2,0:T(8,128)S(1)}, f32[2,1024,8]{1,2,0:T(8,128)S(1)}, u32[]{:S(2)}, u32[]{:S(2)}) collective-permute-start(f32[2,1024,8]{1,2,0:T(8,128)S(1)} %add_add_fusion.8), channel_id=1, source_target_pairs={{0,16},{4,20},{8,24},{12,28},{16,0},{20,4},{24,8},{28,12},{32,48},... | collective-permute-start | bytes 196616 | tf_op jit(solution)/shard_map/while/body/eval_jaxpr/ppermute | solution.py:18
  197.4 5.8 %collective-permute-start.6 = (f32[2,1024,8]{1,2,0:T(8,128)S(1)}, f32[2,1024,8]{1,2,0:T(8,128)S(1)}, u32[]{:S(2)}, u32[]{:S(2)}) collective-permute-start(f32[2,1024,8]{1,2,0:T(8,128)S(1)} %add_add_fusion.9), channel_id=1, source_target_pairs={{0,64},{4,68},{8,72},{12,76},{16,80},{20,84},{24,88},{28,92},{32,9... | collective-permute-start | bytes 196616 | tf_op jit(solution)/shard_map/while/body/eval_jaxpr/ppermute | solution.py:18
  213.0 5.8 %collective-permute-start = (f32[2,1024,8]{1,2,0:T(8,128)S(1)}, f32[2,1024,8]{1,2,0:T(8,128)S(1)}, u32[]{:S(2)}, u32[]{:S(2)}) collective-permute-start(f32[2,1024,8]{1,2,0:T(8,128)S(1)} %pad_maximum_fusion.4), channel_id=1, source_target_pairs={{0,8},{4,12},{8,0},{12,4},{16,24},{20,28},{24,16},{28,20},{32,40},... | collective-permute-start | bytes 196616 | tf_op jit(solution)/shard_map/while/body/eval_jaxpr/ppermute | solution.py:18
  215.0 5.5 %collective-permute-start.1 = (f32[2,1024,8]{1,2,0:T(8,128)S(1)}, f32[2,1024,8]{1,2,0:T(8,128)S(1)}, u32[]{:S(2)}, u32[]{:S(2)}) collective-permute-start(f32[2,1024,8]{1,2,0:T(8,128)S(1)} %pad_maximum_fusion.4), channel_id=1, source_target_pairs={{0,12},{4,8},{8,4},{12,0},{16,28},{20,24},{24,20},{28,16},{32,44},... | collective-permute-start | bytes 196616 | tf_op jit(solution)/shard_map/while/body/eval_jaxpr/ppermute | solution.py:18
  220.5 5.8 %collective-permute-start.3 = (f32[2,1024,8]{1,2,0:T(8,128)S(1)}, f32[2,1024,8]{1,2,0:T(8,128)S(1)}, u32[]{:S(2)}, u32[]{:S(2)}) collective-permute-start(f32[2,1024,8]{1,2,0:T(8,128)S(1)} %add_add_fusion.8), channel_id=1, source_target_pairs={{0,32},{4,36},{8,40},{12,44},{16,48},{20,52},{24,56},{28,60},{32,0... | collective-permute-start | bytes 196616 | tf_op jit(solution)/shard_map/while/body/eval_jaxpr/ppermute | solution.py:18
  221.7 5.5 %collective-permute-start.4 = (f32[2,1024,8]{1,2,0:T(8,128)S(1)}, f32[2,1024,8]{1,2,0:T(8,128)S(1)}, u32[]{:S(2)}, u32[]{:S(2)}) collective-permute-start(f32[2,1024,8]{1,2,0:T(8,128)S(1)} %add_add_fusion.8), channel_id=1, source_target_pairs={{0,48},{4,52},{8,56},{12,60},{16,32},{20,36},{24,40},{28,44},{32,1... | collective-permute-start | bytes 196616 | tf_op jit(solution)/shard_map/while/body/eval_jaxpr/ppermute | solution.py:18
  228.0 5.8 %collective-permute-start.6 = (f32[2,1024,8]{1,2,0:T(8,128)S(1)}, f32[2,1024,8]{1,2,0:T(8,128)S(1)}, u32[]{:S(2)}, u32[]{:S(2)}) collective-permute-start(f32[2,1024,8]{1,2,0:T(8,128)S(1)} %add_add_fusion.9), channel_id=1, source_target_pairs={{0,64},{4,68},{8,72},{12,76},{16,80},{20,84},{24,88},{28,92},{32,9... | collective-permute-start | bytes 196616 | tf_op jit(solution)/shard_map/while/body/eval_jaxpr/ppermute | solution.py:18
  243.6 5.8 %collective-permute-start = (f32[2,1024,8]{1,2,0:T(8,128)S(1)}, f32[2,1024,8]{1,2,0:T(8,128)S(1)}, u32[]{:S(2)}, u32[]{:S(2)}) collective-permute-start(f32[2,1024,8]{1,2,0:T(8,128)S(1)} %pad_maximum_fusion.4), channel_id=1, source_target_pairs={{0,8},{4,12},{8,0},{12,4},{16,24},{20,28},{24,16},{28,20},{32,40},... | collective-permute-start | bytes 196616 | tf_op jit(solution)/shard_map/while/body/eval_jaxpr/ppermute | solution.py:18
  244.9 5.5 %collective-permute-start.1 = (f32[2,1024,8]{1,2,0:T(8,128)S(1)}, f32[2,1024,8]{1,2,0:T(8,128)S(1)}, u32[]{:S(2)}, u32[]{:S(2)}) collective-permute-start(f32[2,1024,8]{1,2,0:T(8,128)S(1)} %pad_maximum_fusion.4), channel_id=1, source_target_pairs={{0,12},{4,8},{8,4},{12,0},{16,28},{20,24},{24,20},{28,16},{32,44},... | collective-permute-start | bytes 196616 | tf_op jit(solution)/shard_map/while/body/eval_jaxpr/ppermute | solution.py:18
  250.9 5.8 %collective-permute-start.3 = (f32[2,1024,8]{1,2,0:T(8,128)S(1)}, f32[2,1024,8]{1,2,0:T(8,128)S(1)}, u32[]{:S(2)}, u32[]{:S(2)}) collective-permute-start(f32[2,1024,8]{1,2,0:T(8,128)S(1)} %add_add_fusion.8), channel_id=1, source_target_pairs={{0,32},{4,36},{8,40},{12,44},{16,48},{20,52},{24,56},{28,60},{32,0... | collective-permute-start | bytes 196616 | tf_op jit(solution)/shard_map/while/body/eval_jaxpr/ppermute | solution.py:18
  252.1 5.5 %collective-permute-start.4 = (f32[2,1024,8]{1,2,0:T(8,128)S(1)}, f32[2,1024,8]{1,2,0:T(8,128)S(1)}, u32[]{:S(2)}, u32[]{:S(2)}) collective-permute-start(f32[2,1024,8]{1,2,0:T(8,128)S(1)} %add_add_fusion.8), channel_id=1, source_target_pairs={{0,48},{4,52},{8,56},{12,60},{16,32},{20,36},{24,40},{28,44},{32,1... | collective-permute-start | bytes 196616 | tf_op jit(solution)/shard_map/while/body/eval_jaxpr/ppermute | solution.py:18
  258.4 5.8 %collective-permute-start.6 = (f32[2,1024,8]{1,2,0:T(8,128)S(1)}, f32[2,1024,8]{1,2,0:T(8,128)S(1)}, u32[]{:S(2)}, u32[]{:S(2)}) collective-permute-start(f32[2,1024,8]{1,2,0:T(8,128)S(1)} %add_add_fusion.9), channel_id=1, source_target_pairs={{0,64},{4,68},{8,72},{12,76},{16,80},{20,84},{24,88},{28,92},{32,9... | collective-permute-start | bytes 196616 | tf_op jit(solution)/shard_map/while/body/eval_jaxpr/ppermute | solution.py:18
  272.2 11.1 %collective-permute-start.15 = (f32[16]{0:T(128)S(1)}, f32[16]{0:T(128)S(1)}, u32[]{:S(2)}, u32[]{:S(2)}) collective-permute-start(f32[16]{0:T(128)S(1)} %get-tuple-element.41), channel_id=1, source_target_pairs={{0,4},{4,0},{8,12},{12,8},{16,20},{20,16},{24,28},{28,24},{32,36},... | collective-permute-start | bytes 200 | tf_op jit(solution)/shard_map/ppermute | solution.py:18
  272.7 10.6 %collective-permute-start.16 = (f32[16]{0:T(128)S(1)}, f32[16]{0:T(128)S(1)}, u32[]{:S(2)}, u32[]{:S(2)}) collective-permute-start(f32[16]{0:T(128)S(1)} %get-tuple-element.41), channel_id=1, source_target_pairs={{0,8},{4,12},{8,0},{12,4},{16,24},{20,28},{24,16},{28,20},{32,40},... | collective-permute-start | bytes 200 | tf_op jit(solution)/shard_map/ppermute | solution.py:18
  275.4 7.9 %collective-permute-start.17 = (f32[16]{0:T(128)S(1)}, f32[16]{0:T(128)S(1)}, u32[]{:S(2)}, u32[]{:S(2)}) collective-permute-start(f32[16]{0:T(128)S(1)} %get-tuple-element.41), channel_id=1, source_target_pairs={{0,12},{4,8},{8,4},{12,0},{16,28},{20,24},{24,20},{28,16},{32,44},... | collective-permute-start | bytes 200 | tf_op jit(solution)/shard_map/ppermute | solution.py:18
  283.4 4.8 %collective-permute-start.18 = (f32[16]{0:T(128)S(1)}, f32[16]{0:T(128)S(1)}, u32[]{:S(2)}, u32[]{:S(2)}) collective-permute-start(f32[16]{0:T(128)S(1)} %add_add_fusion.5), channel_id=1, source_target_pairs={{0,16},{4,20},{8,24},{12,28},{16,0},{20,4},{24,8},{28,12},{32,48},... | collective-permute-start | bytes 200 | tf_op jit(solution)/shard_map/ppermute | solution.py:18
  283.8 5.1 %collective-permute-start.19 = (f32[16]{0:T(128)S(1)}, f32[16]{0:T(128)S(1)}, u32[]{:S(2)}, u32[]{:S(2)}) collective-permute-start(f32[16]{0:T(128)S(1)} %add_add_fusion.5), channel_id=1, source_target_pairs={{0,32},{4,36},{8,40},{12,44},{16,48},{20,52},{24,56},{28,60},{32,0... | collective-permute-start | bytes 200 | tf_op jit(solution)/shard_map/ppermute | solution.py:18
  286.1 4.8 %collective-permute-start.20 = (f32[16]{0:T(128)S(1)}, f32[16]{0:T(128)S(1)}, u32[]{:S(2)}, u32[]{:S(2)}) collective-permute-start(f32[16]{0:T(128)S(1)} %add_add_fusion.5), channel_id=1, source_target_pairs={{0,48},{4,52},{8,56},{12,60},{16,32},{20,36},{24,40},{28,44},{32,1... | collective-permute-start | bytes 200 | tf_op jit(solution)/shard_map/ppermute | solution.py:18
  290.9 5.1 %collective-permute-start.21 = (f32[16]{0:T(128)S(1)}, f32[16]{0:T(128)S(1)}, u32[]{:S(2)}, u32[]{:S(2)}) collective-permute-start(f32[16]{0:T(128)S(1)} %add_add_fusion.4), channel_id=1, source_target_pairs={{0,64},{4,68},{8,72},{12,76},{16,80},{20,84},{24,88},{28,92},{32,9... | collective-permute-start | bytes 200 | tf_op jit(solution)/shard_map/ppermute | solution.py:18
  (20 other events, 139.6 us)
where the time goes:
time: 297 us
  waiting for transfers between devices  98.4 us (33%)
  starting transfers between devices  89.4 us (30%)
  matrix products  49.2 us (17%)
  other arithmetic  35.6 us (12%)
  local copies, waits for them, and re-layouts  22.2 us (7%)
    ppermute x56, starting transfers between devices, swapped(): return lax.ppermute(value, axis, [(i, i ^ mask) for i in range(size)])  87.5 us
    ppermute x56, waiting for transfers between devices, swapped(): return lax.ppermute(value, axis, [(i, i ^ mask) for i in range(size)])  77.1 us
    dot_general x7, matrix products, project(): jnp.dot(stand, jnp.concatenate(pieces(wide), 1), preferred_element_type=j...  33.4 us
    ppermute x1, waiting for transfers between devices, passed_along(): return lax.ppermute(array, axis, pairs)  21.3 us
    another operation x24, other arithmetic, orthonormal(): factor = jnp.linalg.cholesky(gram)  9.76 us
    convert_element_type x1, other arithmetic, shards(): standf = stand.astype(jnp.float32)  9.58 us
    unnamed x12, local copies, waits for them, and re-layouts  9.12 us
    while x1, local copies, waits for them, and re-layouts, shards(): lax.fori_loop(0, ITERS, lambda step, basis: orthonormal(image_of(basis)),...  8.75 us
  transfers between devices with their start and end apart: 57, of which 49 were waited for; matrix products, arithmetic and copies ran while one was open for 3% of the time, Pallas kernels for 0%

commit v1 on v0

--- a/solution.py
+++ b/solution.py
@@ -90,7 +90,6 @@
     miss_here = lax.dynamic_slice_in_dim(missing, position * columns, columns + half_cols)
     weight = jnp.sqrt((total - miss_here.astype(jnp.float32)) / total)
     stand = ((regionf - mean) / jnp.sqrt(var + 1e-05) * weight).astype(jnp.bfloat16)
-    standf = stand.astype(jnp.float32)
 
     def project(basis):
         wide = widened(basis, half_cols)
@@ -106,8 +105,8 @@
     basis = lax.fori_loop(0, ITERS, lambda step, basis: orthonormal(image_of(basis)), start)
     proj = project(basis)
     variances = summed(jnp.sum(proj * proj, axis=0), "ind").reshape(2, comps) / total
-    first = standf[:, :columns] - product(proj[:, :comps], basis[0])
-    second = standf[:, half_cols:] - product(proj[:, comps:], basis[1])
+    first = stand[:, :columns].astype(jnp.float32) - product(proj[:, :comps], basis[0])
+    second = stand[:, half_cols:].astype(jnp.float32) - product(proj[:, comps:], basis[1])
     scores = jnp.stack([jnp.sum(first * first, axis=1), jnp.sum(second * second, axis=1)], 1) / columns
     return (basis, variances, scores)
 

time: 297 us -> 294 us (0.990)
    unnamed x12 -> x14, local copies, waits for them, and re-layouts: 9.12 us -> 10.6 us
where the time goes in v1:
time: 294 us
  waiting for transfers between devices  98.5 us (34%)
  starting transfers between devices  89.4 us (30%)
  matrix products  47.5 us (16%)
  other arithmetic  32.9 us (11%)
  local copies, waits for them, and re-layouts  23.6 us (8%)
    ppermute x56, starting transfers between devices, swapped(): return lax.ppermute(value, axis, [(i, i ^ mask) for i in range(size)])  87.4 us
    ppermute x56, waiting for transfers between devices, swapped(): return lax.ppermute(value, axis, [(i, i ^ mask) for i in range(size)])  77.2 us
    dot_general x7, matrix products, project(): jnp.dot(stand, jnp.concatenate(pieces(wide), 1), preferred_element_type=j...  33.2 us
    ppermute x1, waiting for transfers between devices, passed_along(): return lax.ppermute(array, axis, pairs)  21.3 us
    unnamed x14, local copies, waits for them, and re-layouts  10.6 us
    another operation x24, other arithmetic, orthonormal(): factor = jnp.linalg.cholesky(gram)  9.76 us
    while x1, local copies, waits for them, and re-layouts, shards(): lax.fori_loop(0, ITERS, lambda step, basis: orthonormal(image_of(basis)),...  8.67 us
    another operation x18, other arithmetic, orthonormal(): jax.scipy.linalg.solve_triangular(fac, rhs, lower=True)  8.03 us
  transfers between devices with their start and end apart: 57, of which 49 were waited for; matrix products, arithmetic and copies ran while one was open for 3% of the time, Pallas kernels for 0%

profile of v1, /device:TPU:32, one launch (start us, length us, event | category | flops | bytes accessed | tf_op | source)
XLA Modules:
  0.0 293.6 jit_solution(4662051010605552885)
XLA Ops:
  0.6 6.7 %copy.19 = bf16[2048,1024]{0,1:T(8,128)(2,1)} copy(bf16[2048,1024]{1,0:T(8,128)(2,1)} %param.6) | data formatting | bytes 8388608 | tf_op args[0]
  7.3 3.1 %slice.100 = bf16[2048,512]{0,1:T(8,128)(2,1)} slice(bf16[2048,1024]{0,1:T(8,128)(2,1)} %copy.19), slice={[0:2048], [0:512]} | slice | bytes 4194304 | tf_op jit(solution)/shard_map/slice | solution.py:83
  12.4 2.5 copy.18
  14.9 21.3 %collective-permute-done.7 = bf16[2048,512]{0,1:T(8,128)(2,1)} collective-permute-done((bf16[2048,512]{0,1:T(8,128)(2,1)}, bf16[2048,512]{0,1:T(8,128)(2,1)}, u32[]{:S(2)}, u32[]{:S(2)}) %collective-permute-start.7) | collective-permute-done | bytes 2097184 | tf_op jit(solution)/shard_map/ppermute | solution.py:13
  38.0 3.7 %convert_reduce_fusion = (f32[1536]{0:T(1024)S(1)}, f32[1536]{0:T(1024)S(1)}) fusion(bf16[2048,512]{0,1:T(8,128)(2,1)S(1)} %broadcast_select_fusion, bf16[2048,1024]{0,1:T(8,128)(2,1)S(1)} %copy-done.1), kind=kLoop, calls=%fused_computation.53 | loop fusion | flops 22017024 | bytes 6303744 | tf_op jit(solution)/shard_map/reduce_sum | solution.py:87
  41.8 3.1 %collective-permute-start.10 = (f32[2,1536]{1,0:T(2,128)S(1)}, f32[2,1536]{1,0:T(2,128)S(1)}, u32[]{:S(2)}, u32[]{:S(2)}) collective-permute-start(f32[2,1536]{1,0:T(2,128)S(1)} %pad_maximum_fusion.2), channel_id=1, source_target_pairs={{0,12},{4,8},{8,4},{12,0},{16,28},{20,24},{24,20},{28,16},{32,44},... | collective-permute-start | bytes 36872 | tf_op jit(solution)/shard_map/ppermute | solution.py:18
  51.8 2.7 collective-permute-start.12
  57.0 2.4 collective-permute-done.13
  59.5 3.2 %collective-permute-start.14 = (f32[2,1536]{1,0:T(2,128)S(1)}, f32[2,1536]{1,0:T(2,128)S(1)}, u32[]{:S(2)}, u32[]{:S(2)}) collective-permute-start(f32[2,1536]{1,0:T(2,128)S(1)} %add_add_fusion.2), channel_id=1, source_target_pairs={{0,64},{4,68},{8,72},{12,76},{16,80},{20,84},{24,88},{28,92},{32,9... | collective-permute-start | bytes 36872 | tf_op jit(solution)/shard_map/ppermute | solution.py:18
  64.8 6.9 %fusion.23 = bf16[2048,1536]{0,1:T(8,128)(2,1)} fusion(f32[1536]{0:T(1024)S(1)} %multiply_sqrt_fusion, f32[1536]{0:T(1024)S(1)} %get-tuple-element.32, f32[1536]{0:T(1024)S(1)} %get-tuple-element.31, bf16[2048,512]{0,1:T(8,128)(2,1)S(1)} %broadcast_select_fusion, bf16[2048,1024]{0,1:T(8,128)(2,1)} %copy.19), kind=kLoop, calls=%fused_computation.57 | loop fusion | flops 25165824 | bytes 12601344 | tf_op jit(solution)/shard_map/convert_element_type | solution.py:92
  71.7 8.7 %copy.20 = bf16[2048,1536]{1,0:T(8,128)(2,1)} copy(bf16[2048,1536]{0,1:T(8,128)(2,1)} %fusion.23) | data formatting | bytes 12582912 | tf_op jit(solution)/shard_map/while | solution.py:105
  80.3 184.7 %while.10 = (s32[]{:T(128)}, f32[2,1024,8]{1,2,0:T(8,128)S(1)}, bf16[2048,1536]{1,0:T(8,128)(2,1)}, s32[]{:T(128)}) while((s32[]{:T(128)}, f32[2,1024,8]{1,2,0:T(8,128)S(1)}, bf16[2048,1536]{1,0:T(8,128)(2,1)}, s32[]{:T(128)}) %tuple.56), condition=%wide.region_5.6_spmd, body=%wide.region_2.5_spmd.sunk | while | flops 609027072 | bytes 43456232 | solution.py:105
  80.4 4.9 %convolution_bitcast_fusion.4 = f32[2048,48]{0,1:T(8,128)S(1)} fusion(bf16[2048,1536]{1,0:T(8,128)(2,1)} %get-tuple-element.120, bf16[1536,16]{0,1:T(8,128)(2,1)S(1)} %get-tuple-element.101, bf16[1536,16]{0,1:T(8,128)(2,1)S(1)} %get-tuple-element.102, bf16[1536,16]{0,1:T(8,128)(2,1)S(1)} %get-tuple-element.103), kind=kOutput, calls=%fused_computation.1.clone.1 | convolution fusion | flops 302432256 | bytes 6832128 | tf_op jit(solution)/shard_map/while/body/eval_jaxpr/dot_general | solution.py:96
  88.2 3.0 %collective-permute-start.1 = (f32[2,1024,8]{1,2,0:T(8,128)S(1)}, f32[2,1024,8]{1,2,0:T(8,128)S(1)}, u32[]{:S(2)}, u32[]{:S(2)}) collective-permute-start(f32[2,1024,8]{1,2,0:T(8,128)S(1)} %pad_maximum_fusion.4), channel_id=1, source_target_pairs={{0,12},{4,8},{8,4},{12,0},{16,28},{20,24},{24,20},{28,16},{32,44},... | collective-permute-start | bytes 196616 | tf_op jit(solution)/shard_map/while/body/eval_jaxpr/ppermute | solution.py:18
  99.0 2.8 collective-permute-done.3
  103.1 3.0 %collective-permute-start.6 = (f32[2,1024,8]{1,2,0:T(8,128)S(1)}, f32[2,1024,8]{1,2,0:T(8,128)S(1)}, u32[]{:S(2)}, u32[]{:S(2)}) collective-permute-start(f32[2,1024,8]{1,2,0:T(8,128)S(1)} %add_add_fusion.9), channel_id=1, source_target_pairs={{0,64},{4,68},{8,72},{12,76},{16,80},{20,84},{24,88},{28,92},{32,9... | collective-permute-start | bytes 196616 | tf_op jit(solution)/shard_map/while/body/eval_jaxpr/ppermute | solution.py:18
  106.2 2.8 collective-permute-done.6
  112.6 4.9 %convolution_bitcast_fusion.4 = f32[2048,48]{0,1:T(8,128)S(1)} fusion(bf16[2048,1536]{1,0:T(8,128)(2,1)} %get-tuple-element.120, bf16[1536,16]{0,1:T(8,128)(2,1)S(1)} %get-tuple-element.101, bf16[1536,16]{0,1:T(8,128)(2,1)S(1)} %get-tuple-element.102, bf16[1536,16]{0,1:T(8,128)(2,1)S(1)} %get-tuple-element.103), kind=kOutput, calls=%fused_computation.1.clone.1 | convolution fusion | flops 302432256 | bytes 6832128 | tf_op jit(solution)/shard_map/while/body/eval_jaxpr/dot_general | solution.py:96
  119.1 2.7 collective-permute-start.1
  122.3 2.5 collective-permute-done
  129.7 2.3 collective-permute-done.3
  133.6 3.0 %collective-permute-start.6 = (f32[2,1024,8]{1,2,0:T(8,128)S(1)}, f32[2,1024,8]{1,2,0:T(8,128)S(1)}, u32[]{:S(2)}, u32[]{:S(2)}) collective-permute-start(f32[2,1024,8]{1,2,0:T(8,128)S(1)} %add_add_fusion.9), channel_id=1, source_target_pairs={{0,64},{4,68},{8,72},{12,76},{16,80},{20,84},{24,88},{28,92},{32,9... | collective-permute-start | bytes 196616 | tf_op jit(solution)/shard_map/while/body/eval_jaxpr/ppermute | solution.py:18
  136.6 2.8 collective-permute-done.6
  143.1 4.9 %convolution_bitcast_fusion.4 = f32[2048,48]{0,1:T(8,128)S(1)} fusion(bf16[2048,1536]{1,0:T(8,128)(2,1)} %get-tuple-element.120, bf16[1536,16]{0,1:T(8,128)(2,1)S(1)} %get-tuple-element.101, bf16[1536,16]{0,1:T(8,128)(2,1)S(1)} %get-tuple-element.102, bf16[1536,16]{0,1:T(8,128)(2,1)S(1)} %get-tuple-element.103), kind=kOutput, calls=%fused_computation.1.clone.1 | convolution fusion | flops 302432256 | bytes 6832128 | tf_op jit(solution)/shard_map/while/body/eval_jaxpr/dot_general | solution.py:96
  152.8 2.3 collective-permute-done
  157.5 2.4 collective-permute-start.4
  160.2 2.3 collective-permute-done.3
  164.2 3.0 %collective-permute-start.6 = (f32[2,1024,8]{1,2,0:T(8,128)S(1)}, f32[2,1024,8]{1,2,0:T(8,128)S(1)}, u32[]{:S(2)}, u32[]{:S(2)}) collective-permute-start(f32[2,1024,8]{1,2,0:T(8,128)S(1)} %add_add_fusion.9), channel_id=1, source_target_pairs={{0,64},{4,68},{8,72},{12,76},{16,80},{20,84},{24,88},{28,92},{32,9... | collective-permute-start | bytes 196616 | tf_op jit(solution)/shard_map/while/body/eval_jaxpr/ppermute | solution.py:18
  167.2 2.8 collective-permute-done.6
  173.7 4.9 %convolution_bitcast_fusion.4 = f32[2048,48]{0,1:T(8,128)S(1)} fusion(bf16[2048,1536]{1,0:T(8,128)(2,1)} %get-tuple-element.120, bf16[1536,16]{0,1:T(8,128)(2,1)S(1)} %get-tuple-element.101, bf16[1536,16]{0,1:T(8,128)(2,1)S(1)} %get-tuple-element.102, bf16[1536,16]{0,1:T(8,128)(2,1)S(1)} %get-tuple-element.103), kind=kOutput, calls=%fused_computation.1.clone.1 | convolution fusion | flops 302432256 | bytes 6832128 | tf_op jit(solution)/shard_map/while/body/eval_jaxpr/dot_general | solution.py:96
  183.4 2.3 collective-permute-done
  190.7 2.3 collective-permute-done.3
  194.6 3.0 %collective-permute-start.6 = (f32[2,1024,8]{1,2,0:T(8,128)S(1)}, f32[2,1024,8]{1,2,0:T(8,128)S(1)}, u32[]{:S(2)}, u32[]{:S(2)}) collective-permute-start(f32[2,1024,8]{1,2,0:T(8,128)S(1)} %add_add_fusion.9), channel_id=1, source_target_pairs={{0,64},{4,68},{8,72},{12,76},{16,80},{20,84},{24,88},{28,92},{32,9... | collective-permute-start | bytes 196616 | tf_op jit(solution)/shard_map/while/body/eval_jaxpr/ppermute | solution.py:18
  197.7 2.8 collective-permute-done.6
  204.1 4.9 %convolution_bitcast_fusion.4 = f32[2048,48]{0,1:T(8,128)S(1)} fusion(bf16[2048,1536]{1,0:T(8,128)(2,1)} %get-tuple-element.120, bf16[1536,16]{0,1:T(8,128)(2,1)S(1)} %get-tuple-element.101, bf16[1536,16]{0,1:T(8,128)(2,1)S(1)} %get-tuple-element.102, bf16[1536,16]{0,1:T(8,128)(2,1)S(1)} %get-tuple-element.103), kind=kOutput, calls=%fused_computation.1.clone.1 | convolution fusion | flops 302432256 | bytes 6832128 | tf_op jit(solution)/shard_map/while/body/eval_jaxpr/dot_general | solution.py:96
  213.8 2.3 collective-permute-done
  221.3 2.3 collective-permute-done.3
  225.2 3.0 %collective-permute-start.6 = (f32[2,1024,8]{1,2,0:T(8,128)S(1)}, f32[2,1024,8]{1,2,0:T(8,128)S(1)}, u32[]{:S(2)}, u32[]{:S(2)}) collective-permute-start(f32[2,1024,8]{1,2,0:T(8,128)S(1)} %add_add_fusion.9), channel_id=1, source_target_pairs={{0,64},{4,68},{8,72},{12,76},{16,80},{20,84},{24,88},{28,92},{32,9... | collective-permute-start | bytes 196616 | tf_op jit(solution)/shard_map/while/body/eval_jaxpr/ppermute | solution.py:18
  228.3 2.8 collective-permute-done.6
  234.7 4.9 %convolution_bitcast_fusion.4 = f32[2048,48]{0,1:T(8,128)S(1)} fusion(bf16[2048,1536]{1,0:T(8,128)(2,1)} %get-tuple-element.120, bf16[1536,16]{0,1:T(8,128)(2,1)S(1)} %get-tuple-element.101, bf16[1536,16]{0,1:T(8,128)(2,1)S(1)} %get-tuple-element.102, bf16[1536,16]{0,1:T(8,128)(2,1)S(1)} %get-tuple-element.103), kind=kOutput, calls=%fused_computation.1.clone.1 | convolution fusion | flops 302432256 | bytes 6832128 | tf_op jit(solution)/shard_map/while/body/eval_jaxpr/dot_general | solution.py:96
  244.4 2.3 collective-permute-done
  255.7 3.0 %collective-permute-start.6 = (f32[2,1024,8]{1,2,0:T(8,128)S(1)}, f32[2,1024,8]{1,2,0:T(8,128)S(1)}, u32[]{:S(2)}, u32[]{:S(2)}) collective-permute-start(f32[2,1024,8]{1,2,0:T(8,128)S(1)} %add_add_fusion.9), channel_id=1, source_target_pairs={{0,64},{4,68},{8,72},{12,76},{16,80},{20,84},{24,88},{28,92},{32,9... | collective-permute-start | bytes 196616 | tf_op jit(solution)/shard_map/while/body/eval_jaxpr/ppermute | solution.py:18
  258.7 2.8 collective-permute-done.6
  265.2 4.0 %fusion.24 = f32[2048,48]{0,1:T(8,128)S(1)} fusion(bf16[2048,1536]{0,1:T(8,128)(2,1)} %fusion.23, bf16[1536,16]{0,1:T(8,128)(2,1)S(1)} %get-tuple-element.66, bf16[1536,16]{0,1:T(8,128)(2,1)S(1)} %get-tuple-element.65, bf16[1536,16]{0,1:T(8,128)(2,1)S(1)} %get-tuple-element.64), kind=kOutput, calls=%fused_computation.62 | convolution fusion | flops 302432256 | bytes 6832128 | tf_op jit(solution)/shard_map/dot_general | solution.py:96
  269.8 2.7 collective-permute-start.16
  277.1 3.2 %multiply_reduce_fusion.1 = (f32[2048]{0:T(1024)S(1)}, f32[2048]{0:T(1024)S(1)}) fusion(bf16[2048,1536]{0,1:T(8,128)(2,1)S(1)} %bitcast.80, f32[2048,1024]{0,1:T(8,128)S(1)} %fusion.38, bf16[2048,48]{0,1:T(8,128)(2,1)S(1)} %constant_dynamic-update-slice_fusion, bf16[1024,48]{0,1:T(8,128)(2,1)S(1)} %get-tuple-element.55), kind=kOutput, calls=%fused_computation.59 | convolution fusion | flops 218099712 | bytes 17088512 | tf_op jit(solution)/shard_map/dot_general | solution.py:66
  280.8 2.3 collective-permute-start.19
  287.8 3.0 %collective-permute-start.21 = (f32[16]{0:T(128)S(1)}, f32[16]{0:T(128)S(1)}, u32[]{:S(2)}, u32[]{:S(2)}) collective-permute-start(f32[16]{0:T(128)S(1)} %add_add_fusion.4), channel_id=1, source_target_pairs={{0,64},{4,68},{8,72},{12,76},{16,80},{20,84},{24,88},{28,92},{32,9... | collective-permute-start | bytes 200 | tf_op jit(solution)/shard_map/ppermute | solution.py:18
  (268 shorter events, 116.4 us)
Async XLA Ops:
  10.5 25.8 %collective-permute-start.7 = (bf16[2048,512]{0,1:T(8,128)(2,1)}, bf16[2048,512]{0,1:T(8,128)(2,1)}, u32[]{:S(2)}, u32[]{:S(2)}) collective-permute-start(bf16[2048,512]{0,1:T(8,128)(2,1)} %slice.100), channel_id=1, source_target_pairs={{1,0},{2,1},{3,2},{5,4},{6,5},{7,6},{9,8},{10,9},{11,10},{13,12},{... | collective-permute-start | bytes 6291464 | tf_op jit(solution)/shard_map/ppermute | solution.py:13
  41.8 5.0 %collective-permute-start.10 = (f32[2,1536]{1,0:T(2,128)S(1)}, f32[2,1536]{1,0:T(2,128)S(1)}, u32[]{:S(2)}, u32[]{:S(2)}) collective-permute-start(f32[2,1536]{1,0:T(2,128)S(1)} %pad_maximum_fusion.2), channel_id=1, source_target_pairs={{0,12},{4,8},{8,4},{12,0},{16,28},{20,24},{24,20},{28,16},{32,44},... | collective-permute-start | bytes 36872 | tf_op jit(solution)/shard_map/ppermute | solution.py:18
  45.0 5.2 %collective-permute-start.9 = (f32[2,1536]{1,0:T(2,128)S(1)}, f32[2,1536]{1,0:T(2,128)S(1)}, u32[]{:S(2)}, u32[]{:S(2)}) collective-permute-start(f32[2,1536]{1,0:T(2,128)S(1)} %pad_maximum_fusion.2), channel_id=1, source_target_pairs={{0,8},{4,12},{8,0},{12,4},{16,24},{20,28},{24,16},{28,20},{32,40},... | collective-permute-start | bytes 36872 | tf_op jit(solution)/shard_map/ppermute | solution.py:18
  50.2 4.8 %collective-permute-start.11 = (f32[2,1536]{1,0:T(2,128)S(1)}, f32[2,1536]{1,0:T(2,128)S(1)}, u32[]{:S(2)}, u32[]{:S(2)}) collective-permute-start(f32[2,1536]{1,0:T(2,128)S(1)} %add_add_fusion.3), channel_id=1, source_target_pairs={{0,16},{4,20},{8,24},{12,28},{16,0},{20,4},{24,8},{28,12},{32,48},... | collective-permute-start | bytes 36872 | tf_op jit(solution)/shard_map/ppermute | solution.py:18
  51.8 5.2 %collective-permute-start.12 = (f32[2,1536]{1,0:T(2,128)S(1)}, f32[2,1536]{1,0:T(2,128)S(1)}, u32[]{:S(2)}, u32[]{:S(2)}) collective-permute-start(f32[2,1536]{1,0:T(2,128)S(1)} %add_add_fusion.3), channel_id=1, source_target_pairs={{0,32},{4,36},{8,40},{12,44},{16,48},{20,52},{24,56},{28,60},{32,0... | collective-permute-start | bytes 36872 | tf_op jit(solution)/shard_map/ppermute | solution.py:18
  54.5 4.9 %collective-permute-start.13 = (f32[2,1536]{1,0:T(2,128)S(1)}, f32[2,1536]{1,0:T(2,128)S(1)}, u32[]{:S(2)}, u32[]{:S(2)}) collective-permute-start(f32[2,1536]{1,0:T(2,128)S(1)} %add_add_fusion.3), channel_id=1, source_target_pairs={{0,48},{4,52},{8,56},{12,60},{16,32},{20,36},{24,40},{28,44},{32,1... | collective-permute-start | bytes 36872 | tf_op jit(solution)/shard_map/ppermute | solution.py:18
  59.5 5.3 %collective-permute-start.14 = (f32[2,1536]{1,0:T(2,128)S(1)}, f32[2,1536]{1,0:T(2,128)S(1)}, u32[]{:S(2)}, u32[]{:S(2)}) collective-permute-start(f32[2,1536]{1,0:T(2,128)S(1)} %add_add_fusion.2), channel_id=1, source_target_pairs={{0,64},{4,68},{8,72},{12,76},{16,80},{20,84},{24,88},{28,92},{32,9... | collective-permute-start | bytes 36872 | tf_op jit(solution)/shard_map/ppermute | solution.py:18
  86.5 5.8 %collective-permute-start = (f32[2,1024,8]{1,2,0:T(8,128)S(1)}, f32[2,1024,8]{1,2,0:T(8,128)S(1)}, u32[]{:S(2)}, u32[]{:S(2)}) collective-permute-start(f32[2,1024,8]{1,2,0:T(8,128)S(1)} %pad_maximum_fusion.4), channel_id=1, source_target_pairs={{0,8},{4,12},{8,0},{12,4},{16,24},{20,28},{24,16},{28,20},{32,40},... | collective-permute-start | bytes 196616 | tf_op jit(solution)/shard_map/while/body/eval_jaxpr/ppermute | solution.py:18
  88.2 5.6 %collective-permute-start.1 = (f32[2,1024,8]{1,2,0:T(8,128)S(1)}, f32[2,1024,8]{1,2,0:T(8,128)S(1)}, u32[]{:S(2)}, u32[]{:S(2)}) collective-permute-start(f32[2,1024,8]{1,2,0:T(8,128)S(1)} %pad_maximum_fusion.4), channel_id=1, source_target_pairs={{0,12},{4,8},{8,4},{12,0},{16,28},{20,24},{24,20},{28,16},{32,44},... | collective-permute-start | bytes 196616 | tf_op jit(solution)/shard_map/while/body/eval_jaxpr/ppermute | solution.py:18
  95.5 6.4 %collective-permute-start.3 = (f32[2,1024,8]{1,2,0:T(8,128)S(1)}, f32[2,1024,8]{1,2,0:T(8,128)S(1)}, u32[]{:S(2)}, u32[]{:S(2)}) collective-permute-start(f32[2,1024,8]{1,2,0:T(8,128)S(1)} %add_add_fusion.8), channel_id=1, source_target_pairs={{0,32},{4,36},{8,40},{12,44},{16,48},{20,52},{24,56},{28,60},{32,0... | collective-permute-start | bytes 196616 | tf_op jit(solution)/shard_map/while/body/eval_jaxpr/ppermute | solution.py:18
  96.1 7.1 %collective-permute-start.4 = (f32[2,1024,8]{1,2,0:T(8,128)S(1)}, f32[2,1024,8]{1,2,0:T(8,128)S(1)}, u32[]{:S(2)}, u32[]{:S(2)}) collective-permute-start(f32[2,1024,8]{1,2,0:T(8,128)S(1)} %add_add_fusion.8), channel_id=1, source_target_pairs={{0,48},{4,52},{8,56},{12,60},{16,32},{20,36},{24,40},{28,44},{32,1... | collective-permute-start | bytes 196616 | tf_op jit(solution)/shard_map/while/body/eval_jaxpr/ppermute | solution.py:18
  97.4 5.7 %collective-permute-start.5 = (f32[2,1024,8]{1,2,0:T(8,128)S(1)}, f32[2,1024,8]{1,2,0:T(8,128)S(1)}, u32[]{:S(2)}, u32[]{:S(2)}) collective-permute-start(f32[2,1024,8]{1,2,0:T(8,128)S(1)} %add_add_fusion.8), channel_id=1, source_target_pairs={{0,16},{4,20},{8,24},{12,28},{16,0},{20,4},{24,8},{28,12},{32,48},... | collective-permute-start | bytes 196616 | tf_op jit(solution)/shard_map/while/body/eval_jaxpr/ppermute | solution.py:18
  103.1 5.8 %collective-permute-start.6 = (f32[2,1024,8]{1,2,0:T(8,128)S(1)}, f32[2,1024,8]{1,2,0:T(8,128)S(1)}, u32[]{:S(2)}, u32[]{:S(2)}) collective-permute-start(f32[2,1024,8]{1,2,0:T(8,128)S(1)} %add_add_fusion.9), channel_id=1, source_target_pairs={{0,64},{4,68},{8,72},{12,76},{16,80},{20,84},{24,88},{28,92},{32,9... | collective-permute-start | bytes 196616 | tf_op jit(solution)/shard_map/while/body/eval_jaxpr/ppermute | solution.py:18
  118.8 6.1 %collective-permute-start = (f32[2,1024,8]{1,2,0:T(8,128)S(1)}, f32[2,1024,8]{1,2,0:T(8,128)S(1)}, u32[]{:S(2)}, u32[]{:S(2)}) collective-permute-start(f32[2,1024,8]{1,2,0:T(8,128)S(1)} %pad_maximum_fusion.4), channel_id=1, source_target_pairs={{0,8},{4,12},{8,0},{12,4},{16,24},{20,28},{24,16},{28,20},{32,40},... | collective-permute-start | bytes 196616 | tf_op jit(solution)/shard_map/while/body/eval_jaxpr/ppermute | solution.py:18
  119.1 6.2 %collective-permute-start.1 = (f32[2,1024,8]{1,2,0:T(8,128)S(1)}, f32[2,1024,8]{1,2,0:T(8,128)S(1)}, u32[]{:S(2)}, u32[]{:S(2)}) collective-permute-start(f32[2,1024,8]{1,2,0:T(8,128)S(1)} %pad_maximum_fusion.4), channel_id=1, source_target_pairs={{0,12},{4,8},{8,4},{12,0},{16,28},{20,24},{24,20},{28,16},{32,44},... | collective-permute-start | bytes 196616 | tf_op jit(solution)/shard_map/while/body/eval_jaxpr/ppermute | solution.py:18
  121.8 4.3 %collective-permute-start.2 = (f32[2,1024,8]{1,2,0:T(8,128)S(1)}, f32[2,1024,8]{1,2,0:T(8,128)S(1)}, u32[]{:S(2)}, u32[]{:S(2)}) collective-permute-start(f32[2,1024,8]{1,2,0:T(8,128)S(1)} %pad_maximum_fusion.4), channel_id=1, source_target_pairs={{0,4},{4,0},{8,12},{12,8},{16,20},{20,16},{24,28},{28,24},{32,36},... | collective-permute-start | bytes 196616 | tf_op jit(solution)/shard_map/while/body/eval_jaxpr/ppermute | solution.py:18
  126.1 5.9 %collective-permute-start.3 = (f32[2,1024,8]{1,2,0:T(8,128)S(1)}, f32[2,1024,8]{1,2,0:T(8,128)S(1)}, u32[]{:S(2)}, u32[]{:S(2)}) collective-permute-start(f32[2,1024,8]{1,2,0:T(8,128)S(1)} %add_add_fusion.8), channel_id=1, source_target_pairs={{0,32},{4,36},{8,40},{12,44},{16,48},{20,52},{24,56},{28,60},{32,0... | collective-permute-start | bytes 196616 | tf_op jit(solution)/shard_map/while/body/eval_jaxpr/ppermute | solution.py:18
  127.1 5.6 %collective-permute-start.4 = (f32[2,1024,8]{1,2,0:T(8,128)S(1)}, f32[2,1024,8]{1,2,0:T(8,128)S(1)}, u32[]{:S(2)}, u32[]{:S(2)}) collective-permute-start(f32[2,1024,8]{1,2,0:T(8,128)S(1)} %add_add_fusion.8), channel_id=1, source_target_pairs={{0,48},{4,52},{8,56},{12,60},{16,32},{20,36},{24,40},{28,44},{32,1... | collective-permute-start | bytes 196616 | tf_op jit(solution)/shard_map/while/body/eval_jaxpr/ppermute | solution.py:18
  133.6 5.8 %collective-permute-start.6 = (f32[2,1024,8]{1,2,0:T(8,128)S(1)}, f32[2,1024,8]{1,2,0:T(8,128)S(1)}, u32[]{:S(2)}, u32[]{:S(2)}) collective-permute-start(f32[2,1024,8]{1,2,0:T(8,128)S(1)} %add_add_fusion.9), channel_id=1, source_target_pairs={{0,64},{4,68},{8,72},{12,76},{16,80},{20,84},{24,88},{28,92},{32,9... | collective-permute-start | bytes 196616 | tf_op jit(solution)/shard_map/while/body/eval_jaxpr/ppermute | solution.py:18
  149.2 5.8 %collective-permute-start = (f32[2,1024,8]{1,2,0:T(8,128)S(1)}, f32[2,1024,8]{1,2,0:T(8,128)S(1)}, u32[]{:S(2)}, u32[]{:S(2)}) collective-permute-start(f32[2,1024,8]{1,2,0:T(8,128)S(1)} %pad_maximum_fusion.4), channel_id=1, source_target_pairs={{0,8},{4,12},{8,0},{12,4},{16,24},{20,28},{24,16},{28,20},{32,40},... | collective-permute-start | bytes 196616 | tf_op jit(solution)/shard_map/while/body/eval_jaxpr/ppermute | solution.py:18
  151.2 5.5 %collective-permute-start.1 = (f32[2,1024,8]{1,2,0:T(8,128)S(1)}, f32[2,1024,8]{1,2,0:T(8,128)S(1)}, u32[]{:S(2)}, u32[]{:S(2)}) collective-permute-start(f32[2,1024,8]{1,2,0:T(8,128)S(1)} %pad_maximum_fusion.4), channel_id=1, source_target_pairs={{0,12},{4,8},{8,4},{12,0},{16,28},{20,24},{24,20},{28,16},{32,44},... | collective-permute-start | bytes 196616 | tf_op jit(solution)/shard_map/while/body/eval_jaxpr/ppermute | solution.py:18
  152.3 4.4 %collective-permute-start.2 = (f32[2,1024,8]{1,2,0:T(8,128)S(1)}, f32[2,1024,8]{1,2,0:T(8,128)S(1)}, u32[]{:S(2)}, u32[]{:S(2)}) collective-permute-start(f32[2,1024,8]{1,2,0:T(8,128)S(1)} %pad_maximum_fusion.4), channel_id=1, source_target_pairs={{0,4},{4,0},{8,12},{12,8},{16,20},{20,16},{24,28},{28,24},{32,36},... | collective-permute-start | bytes 196616 | tf_op jit(solution)/shard_map/while/body/eval_jaxpr/ppermute | solution.py:18
  156.7 5.9 %collective-permute-start.3 = (f32[2,1024,8]{1,2,0:T(8,128)S(1)}, f32[2,1024,8]{1,2,0:T(8,128)S(1)}, u32[]{:S(2)}, u32[]{:S(2)}) collective-permute-start(f32[2,1024,8]{1,2,0:T(8,128)S(1)} %add_add_fusion.8), channel_id=1, source_target_pairs={{0,32},{4,36},{8,40},{12,44},{16,48},{20,52},{24,56},{28,60},{32,0... | collective-permute-start | bytes 196616 | tf_op jit(solution)/shard_map/while/body/eval_jaxpr/ppermute | solution.py:18
  157.5 5.7 %collective-permute-start.4 = (f32[2,1024,8]{1,2,0:T(8,128)S(1)}, f32[2,1024,8]{1,2,0:T(8,128)S(1)}, u32[]{:S(2)}, u32[]{:S(2)}) collective-permute-start(f32[2,1024,8]{1,2,0:T(8,128)S(1)} %add_add_fusion.8), channel_id=1, source_target_pairs={{0,48},{4,52},{8,56},{12,60},{16,32},{20,36},{24,40},{28,44},{32,1... | collective-permute-start | bytes 196616 | tf_op jit(solution)/shard_map/while/body/eval_jaxpr/ppermute | solution.py:18
  159.9 4.3 %collective-permute-start.5 = (f32[2,1024,8]{1,2,0:T(8,128)S(1)}, f32[2,1024,8]{1,2,0:T(8,128)S(1)}, u32[]{:S(2)}, u32[]{:S(2)}) collective-permute-start(f32[2,1024,8]{1,2,0:T(8,128)S(1)} %add_add_fusion.8), channel_id=1, source_target_pairs={{0,16},{4,20},{8,24},{12,28},{16,0},{20,4},{24,8},{28,12},{32,48},... | collective-permute-start | bytes 196616 | tf_op jit(solution)/shard_map/while/body/eval_jaxpr/ppermute | solution.py:18
  164.2 5.8 %collective-permute-start.6 = (f32[2,1024,8]{1,2,0:T(8,128)S(1)}, f32[2,1024,8]{1,2,0:T(8,128)S(1)}, u32[]{:S(2)}, u32[]{:S(2)}) collective-permute-start(f32[2,1024,8]{1,2,0:T(8,128)S(1)} %add_add_fusion.9), channel_id=1, source_target_pairs={{0,64},{4,68},{8,72},{12,76},{16,80},{20,84},{24,88},{28,92},{32,9... | collective-permute-start | bytes 196616 | tf_op jit(solution)/shard_map/while/body/eval_jaxpr/ppermute | solution.py:18
  179.8 5.8 %collective-permute-start = (f32[2,1024,8]{1,2,0:T(8,128)S(1)}, f32[2,1024,8]{1,2,0:T(8,128)S(1)}, u32[]{:S(2)}, u32[]{:S(2)}) collective-permute-start(f32[2,1024,8]{1,2,0:T(8,128)S(1)} %pad_maximum_fusion.4), channel_id=1, source_target_pairs={{0,8},{4,12},{8,0},{12,4},{16,24},{20,28},{24,16},{28,20},{32,40},... | collective-permute-start | bytes 196616 | tf_op jit(solution)/shard_map/while/body/eval_jaxpr/ppermute | solution.py:18
  181.1 5.5 %collective-permute-start.1 = (f32[2,1024,8]{1,2,0:T(8,128)S(1)}, f32[2,1024,8]{1,2,0:T(8,128)S(1)}, u32[]{:S(2)}, u32[]{:S(2)}) collective-permute-start(f32[2,1024,8]{1,2,0:T(8,128)S(1)} %pad_maximum_fusion.4), channel_id=1, source_target_pairs={{0,12},{4,8},{8,4},{12,0},{16,28},{20,24},{24,20},{28,16},{32,44},... | collective-permute-start | bytes 196616 | tf_op jit(solution)/shard_map/while/body/eval_jaxpr/ppermute | solution.py:18
  187.1 5.8 %collective-permute-start.3 = (f32[2,1024,8]{1,2,0:T(8,128)S(1)}, f32[2,1024,8]{1,2,0:T(8,128)S(1)}, u32[]{:S(2)}, u32[]{:S(2)}) collective-permute-start(f32[2,1024,8]{1,2,0:T(8,128)S(1)} %add_add_fusion.8), channel_id=1, source_target_pairs={{0,32},{4,36},{8,40},{12,44},{16,48},{20,52},{24,56},{28,60},{32,0... | collective-permute-start | bytes 196616 | tf_op jit(solution)/shard_map/while/body/eval_jaxpr/ppermute | solution.py:18
  188.3 5.5 %collective-permute-start.4 = (f32[2,1024,8]{1,2,0:T(8,128)S(1)}, f32[2,1024,8]{1,2,0:T(8,128)S(1)}, u32[]{:S(2)}, u32[]{:S(2)}) collective-permute-start(f32[2,1024,8]{1,2,0:T(8,128)S(1)} %add_add_fusion.8), channel_id=1, source_target_pairs={{0,48},{4,52},{8,56},{12,60},{16,32},{20,36},{24,40},{28,44},{32,1... | collective-permute-start | bytes 196616 | tf_op jit(solution)/shard_map/while/body/eval_jaxpr/ppermute | solution.py:18
  194.6 5.8 %collective-permute-start.6 = (f32[2,1024,8]{1,2,0:T(8,128)S(1)}, f32[2,1024,8]{1,2,0:T(8,128)S(1)}, u32[]{:S(2)}, u32[]{:S(2)}) collective-permute-start(f32[2,1024,8]{1,2,0:T(8,128)S(1)} %add_add_fusion.9), channel_id=1, source_target_pairs={{0,64},{4,68},{8,72},{12,76},{16,80},{20,84},{24,88},{28,92},{32,9... | collective-permute-start | bytes 196616 | tf_op jit(solution)/shard_map/while/body/eval_jaxpr/ppermute | solution.py:18
  210.3 5.8 %collective-permute-start = (f32[2,1024,8]{1,2,0:T(8,128)S(1)}, f32[2,1024,8]{1,2,0:T(8,128)S(1)}, u32[]{:S(2)}, u32[]{:S(2)}) collective-permute-start(f32[2,1024,8]{1,2,0:T(8,128)S(1)} %pad_maximum_fusion.4), channel_id=1, source_target_pairs={{0,8},{4,12},{8,0},{12,4},{16,24},{20,28},{24,16},{28,20},{32,40},... | collective-permute-start | bytes 196616 | tf_op jit(solution)/shard_map/while/body/eval_jaxpr/ppermute | solution.py:18
  212.2 5.5 %collective-permute-start.1 = (f32[2,1024,8]{1,2,0:T(8,128)S(1)}, f32[2,1024,8]{1,2,0:T(8,128)S(1)}, u32[]{:S(2)}, u32[]{:S(2)}) collective-permute-start(f32[2,1024,8]{1,2,0:T(8,128)S(1)} %pad_maximum_fusion.4), channel_id=1, source_target_pairs={{0,12},{4,8},{8,4},{12,0},{16,28},{20,24},{24,20},{28,16},{32,44},... | collective-permute-start | bytes 196616 | tf_op jit(solution)/shard_map/while/body/eval_jaxpr/ppermute | solution.py:18
  217.7 5.8 %collective-permute-start.3 = (f32[2,1024,8]{1,2,0:T(8,128)S(1)}, f32[2,1024,8]{1,2,0:T(8,128)S(1)}, u32[]{:S(2)}, u32[]{:S(2)}) collective-permute-start(f32[2,1024,8]{1,2,0:T(8,128)S(1)} %add_add_fusion.8), channel_id=1, source_target_pairs={{0,32},{4,36},{8,40},{12,44},{16,48},{20,52},{24,56},{28,60},{32,0... | collective-permute-start | bytes 196616 | tf_op jit(solution)/shard_map/while/body/eval_jaxpr/ppermute | solution.py:18
  218.9 5.5 %collective-permute-start.4 = (f32[2,1024,8]{1,2,0:T(8,128)S(1)}, f32[2,1024,8]{1,2,0:T(8,128)S(1)}, u32[]{:S(2)}, u32[]{:S(2)}) collective-permute-start(f32[2,1024,8]{1,2,0:T(8,128)S(1)} %add_add_fusion.8), channel_id=1, source_target_pairs={{0,48},{4,52},{8,56},{12,60},{16,32},{20,36},{24,40},{28,44},{32,1... | collective-permute-start | bytes 196616 | tf_op jit(solution)/shard_map/while/body/eval_jaxpr/ppermute | solution.py:18
  225.2 5.8 %collective-permute-start.6 = (f32[2,1024,8]{1,2,0:T(8,128)S(1)}, f32[2,1024,8]{1,2,0:T(8,128)S(1)}, u32[]{:S(2)}, u32[]{:S(2)}) collective-permute-start(f32[2,1024,8]{1,2,0:T(8,128)S(1)} %add_add_fusion.9), channel_id=1, source_target_pairs={{0,64},{4,68},{8,72},{12,76},{16,80},{20,84},{24,88},{28,92},{32,9... | collective-permute-start | bytes 196616 | tf_op jit(solution)/shard_map/while/body/eval_jaxpr/ppermute | solution.py:18
  240.9 5.8 %collective-permute-start = (f32[2,1024,8]{1,2,0:T(8,128)S(1)}, f32[2,1024,8]{1,2,0:T(8,128)S(1)}, u32[]{:S(2)}, u32[]{:S(2)}) collective-permute-start(f32[2,1024,8]{1,2,0:T(8,128)S(1)} %pad_maximum_fusion.4), channel_id=1, source_target_pairs={{0,8},{4,12},{8,0},{12,4},{16,24},{20,28},{24,16},{28,20},{32,40},... | collective-permute-start | bytes 196616 | tf_op jit(solution)/shard_map/while/body/eval_jaxpr/ppermute | solution.py:18
  242.1 5.5 %collective-permute-start.1 = (f32[2,1024,8]{1,2,0:T(8,128)S(1)}, f32[2,1024,8]{1,2,0:T(8,128)S(1)}, u32[]{:S(2)}, u32[]{:S(2)}) collective-permute-start(f32[2,1024,8]{1,2,0:T(8,128)S(1)} %pad_maximum_fusion.4), channel_id=1, source_target_pairs={{0,12},{4,8},{8,4},{12,0},{16,28},{20,24},{24,20},{28,16},{32,44},... | collective-permute-start | bytes 196616 | tf_op jit(solution)/shard_map/while/body/eval_jaxpr/ppermute | solution.py:18
  248.2 5.8 %collective-permute-start.3 = (f32[2,1024,8]{1,2,0:T(8,128)S(1)}, f32[2,1024,8]{1,2,0:T(8,128)S(1)}, u32[]{:S(2)}, u32[]{:S(2)}) collective-permute-start(f32[2,1024,8]{1,2,0:T(8,128)S(1)} %add_add_fusion.8), channel_id=1, source_target_pairs={{0,32},{4,36},{8,40},{12,44},{16,48},{20,52},{24,56},{28,60},{32,0... | collective-permute-start | bytes 196616 | tf_op jit(solution)/shard_map/while/body/eval_jaxpr/ppermute | solution.py:18
  249.4 5.5 %collective-permute-start.4 = (f32[2,1024,8]{1,2,0:T(8,128)S(1)}, f32[2,1024,8]{1,2,0:T(8,128)S(1)}, u32[]{:S(2)}, u32[]{:S(2)}) collective-permute-start(f32[2,1024,8]{1,2,0:T(8,128)S(1)} %add_add_fusion.8), channel_id=1, source_target_pairs={{0,48},{4,52},{8,56},{12,60},{16,32},{20,36},{24,40},{28,44},{32,1... | collective-permute-start | bytes 196616 | tf_op jit(solution)/shard_map/while/body/eval_jaxpr/ppermute | solution.py:18
  255.7 5.8 %collective-permute-start.6 = (f32[2,1024,8]{1,2,0:T(8,128)S(1)}, f32[2,1024,8]{1,2,0:T(8,128)S(1)}, u32[]{:S(2)}, u32[]{:S(2)}) collective-permute-start(f32[2,1024,8]{1,2,0:T(8,128)S(1)} %add_add_fusion.9), channel_id=1, source_target_pairs={{0,64},{4,68},{8,72},{12,76},{16,80},{20,84},{24,88},{28,92},{32,9... | collective-permute-start | bytes 196616 | tf_op jit(solution)/shard_map/while/body/eval_jaxpr/ppermute | solution.py:18
  269.3 11.0 %collective-permute-start.15 = (f32[16]{0:T(128)S(1)}, f32[16]{0:T(128)S(1)}, u32[]{:S(2)}, u32[]{:S(2)}) collective-permute-start(f32[16]{0:T(128)S(1)} %get-tuple-element.41), channel_id=1, source_target_pairs={{0,4},{4,0},{8,12},{12,8},{16,20},{20,16},{24,28},{28,24},{32,36},... | collective-permute-start | bytes 200 | tf_op jit(solution)/shard_map/ppermute | solution.py:18
  269.8 10.5 %collective-permute-start.16 = (f32[16]{0:T(128)S(1)}, f32[16]{0:T(128)S(1)}, u32[]{:S(2)}, u32[]{:S(2)}) collective-permute-start(f32[16]{0:T(128)S(1)} %get-tuple-element.41), channel_id=1, source_target_pairs={{0,8},{4,12},{8,0},{12,4},{16,24},{20,28},{24,16},{28,20},{32,40},... | collective-permute-start | bytes 200 | tf_op jit(solution)/shard_map/ppermute | solution.py:18
  272.5 7.8 %collective-permute-start.17 = (f32[16]{0:T(128)S(1)}, f32[16]{0:T(128)S(1)}, u32[]{:S(2)}, u32[]{:S(2)}) collective-permute-start(f32[16]{0:T(128)S(1)} %get-tuple-element.41), channel_id=1, source_target_pairs={{0,12},{4,8},{8,4},{12,0},{16,28},{20,24},{24,20},{28,16},{32,44},... | collective-permute-start | bytes 200 | tf_op jit(solution)/shard_map/ppermute | solution.py:18
  280.3 4.8 %collective-permute-start.18 = (f32[16]{0:T(128)S(1)}, f32[16]{0:T(128)S(1)}, u32[]{:S(2)}, u32[]{:S(2)}) collective-permute-start(f32[16]{0:T(128)S(1)} %add_add_fusion.5), channel_id=1, source_target_pairs={{0,16},{4,20},{8,24},{12,28},{16,0},{20,4},{24,8},{28,12},{32,48},... | collective-permute-start | bytes 200 | tf_op jit(solution)/shard_map/ppermute | solution.py:18
  280.8 5.1 %collective-permute-start.19 = (f32[16]{0:T(128)S(1)}, f32[16]{0:T(128)S(1)}, u32[]{:S(2)}, u32[]{:S(2)}) collective-permute-start(f32[16]{0:T(128)S(1)} %add_add_fusion.5), channel_id=1, source_target_pairs={{0,32},{4,36},{8,40},{12,44},{16,48},{20,52},{24,56},{28,60},{32,0... | collective-permute-start | bytes 200 | tf_op jit(solution)/shard_map/ppermute | solution.py:18
  283.1 4.8 %collective-permute-start.20 = (f32[16]{0:T(128)S(1)}, f32[16]{0:T(128)S(1)}, u32[]{:S(2)}, u32[]{:S(2)}) collective-permute-start(f32[16]{0:T(128)S(1)} %add_add_fusion.5), channel_id=1, source_target_pairs={{0,48},{4,52},{8,56},{12,60},{16,32},{20,36},{24,40},{28,44},{32,1... | collective-permute-start | bytes 200 | tf_op jit(solution)/shard_map/ppermute | solution.py:18
  287.8 5.1 %collective-permute-start.21 = (f32[16]{0:T(128)S(1)}, f32[16]{0:T(128)S(1)}, u32[]{:S(2)}, u32[]{:S(2)}) collective-permute-start(f32[16]{0:T(128)S(1)} %add_add_fusion.4), channel_id=1, source_target_pairs={{0,64},{4,68},{8,72},{12,76},{16,80},{20,84},{24,88},{28,92},{32,9... | collective-permute-start | bytes 200 | tf_op jit(solution)/shard_map/ppermute | solution.py:18
  (21 other events, 126.9 us)

commit v2 on v1

--- a/solution.py
+++ b/solution.py
@@ -24,15 +24,12 @@
         return lax.psum(value, axis)
     bit = 1
     while bit < size:
-        if bit * 4 <= size:
-            near = swapped(value, axis, bit)
-            mid = swapped(value, axis, 2 * bit)
-            far = swapped(value, axis, 3 * bit)
-            value = (value + near) + (mid + far)
-            bit *= 4
-        else:
-            value = value + swapped(value, axis, bit)
-            bit *= 2
+        group = 8 if bit * 8 <= size and bit > 1 else min(4, size // bit)
+        got = [value] + [swapped(value, axis, bit * offset) for offset in range(1, group)]
+        while len(got) > 1:
+            got = [got[i] + got[i + 1] for i in range(0, len(got), 2)]
+        value = got[0]
+        bit *= group
     return value
 
 

time: 294 us -> 330 us (1.12)
  starting transfers between devices: 89.4 us -> 142 us
  waiting for transfers between devices: 98.5 us -> 81.9 us
    ppermute x56 -> x80, starting transfers between devices: 87.4 us -> 140 us  [swapped(): return lax.ppermute(value, axis, [(i, i ^ mask) for i in range(size)])]
    ppermute x56 -> x80, waiting for transfers between devices: 77.2 us -> 60.6 us  [swapped(): return lax.ppermute(value, axis, [(i, i ^ mask) for i in range(size)])]
  transfers between devices with their start and end apart: 57 -> 81, of which waited for: 49 -> 37; matrix products, arithmetic and copies ran while one was open for 3% -> 3% of each run, Pallas kernels for 0% -> 0%
where the time goes in v2:
time: 330 us
  starting transfers between devices  142 us (43%)
  waiting for transfers between devices  81.9 us (25%)
  matrix products  47.4 us (14%)
  other arithmetic  33 us (10%)
  local copies, waits for them, and re-layouts  23.5 us (7%)
    ppermute x80, starting transfers between devices, swapped(): return lax.ppermute(value, axis, [(i, i ^ mask) for i in range(size)])  140 us
    ppermute x80, waiting for transfers between devices, swapped(): return lax.ppermute(value, axis, [(i, i ^ mask) for i in range(size)])  60.6 us
    dot_general x7, matrix products, project(): jnp.dot(stand, jnp.concatenate(pieces(wide), 1), preferred_element_type=j...  33.2 us
    ppermute x1, waiting for transfers between devices, passed_along(): return lax.ppermute(array, axis, pairs)  21.3 us
    unnamed x14, local copies, waits for them, and re-layouts  10.5 us
    another operation x24, other arithmetic, orthonormal(): factor = jnp.linalg.cholesky(gram)  9.75 us
    while x1, local copies, waits for them, and re-layouts, shards(): lax.fori_loop(0, ITERS, lambda step, basis: orthonormal(image_of(basis)),...  8.68 us
    another operation x18, other arithmetic, orthonormal(): jax.scipy.linalg.solve_triangular(fac, rhs, lower=True)  8.03 us
  transfers between devices with their start and end apart: 81, of which 37 were waited for; matrix products, arithmetic and copies ran while one was open for 3% of the time, Pallas kernels for 0%

profile of v2, /device:TPU:32, one launch (start us, length us, event | category | flops | bytes accessed | tf_op | source)
XLA Modules:
  0.0 329.5 jit_solution(5233478214136818113)
XLA Ops:
  0.6 6.6 %copy.19 = bf16[2048,1024]{0,1:T(8,128)(2,1)} copy(bf16[2048,1024]{1,0:T(8,128)(2,1)} %param.6) | data formatting | bytes 8388608 | tf_op args[0]
  7.3 3.2 slice.100
  12.3 2.5 copy.18
  14.8 21.3 %collective-permute-done.10 = bf16[2048,512]{0,1:T(8,128)(2,1)} collective-permute-done((bf16[2048,512]{0,1:T(8,128)(2,1)}, bf16[2048,512]{0,1:T(8,128)(2,1)}, u32[]{:S(2)}, u32[]{:S(2)}) %collective-permute-start.10) | collective-permute-done | bytes 2097184 | tf_op jit(solution)/shard_map/ppermute | solution.py:13
  38.0 3.7 %convert_reduce_fusion = (f32[1536]{0:T(1024)S(1)}, f32[1536]{0:T(1024)S(1)}) fusion(bf16[2048,512]{0,1:T(8,128)(2,1)S(1)} %broadcast_select_fusion, bf16[2048,1024]{0,1:T(8,128)(2,1)S(1)} %copy-done.1), kind=kLoop, calls=%fused_computation.49 | loop fusion | flops 22017024 | bytes 6303744 | tf_op jit(solution)/shard_map/reduce_sum | solution.py:84
  43.5 2.9 collective-permute-start.12
  48.7 2.6 collective-permute-done.13
  53.1 2.6 collective-permute-start.15
  56.1 3.0 collective-permute-start.17
  59.5 6.2 %collective-permute-start.19 = (f32[2,1536]{1,0:T(2,128)S(1)}, f32[2,1536]{1,0:T(2,128)S(1)}, u32[]{:S(2)}, u32[]{:S(2)}) collective-permute-start(f32[2,1536]{1,0:T(2,128)S(1)} %add_add_fusion.2), channel_id=1, source_target_pairs={{0,96},{4,100},{8,104},{12,108},{16,112},{20,116},{24,120},{28,124... | collective-permute-start | bytes 36872 | tf_op jit(solution)/shard_map/ppermute | solution.py:18
  67.5 5.5 %collective-permute-done.20 = f32[2,1536]{1,0:T(2,128)S(1)} collective-permute-done((f32[2,1536]{1,0:T(2,128)S(1)}, f32[2,1536]{1,0:T(2,128)S(1)}, u32[]{:S(2)}, u32[]{:S(2)}) %collective-permute-start.20) | collective-permute-done | bytes 12320 | tf_op jit(solution)/shard_map/ppermute | solution.py:18
  73.1 6.9 %fusion.20 = bf16[2048,1536]{0,1:T(8,128)(2,1)} fusion(f32[1536]{0:T(1024)S(1)} %multiply_sqrt_fusion, f32[1536]{0:T(1024)S(1)} %get-tuple-element.32, f32[1536]{0:T(1024)S(1)} %get-tuple-element.31, bf16[2048,512]{0,1:T(8,128)(2,1)S(1)} %broadcast_select_fusion, bf16[2048,1024]{0,1:T(8,128)(2,1)} %copy.19), kind=kLoop, calls=%fused_computation.53 | loop fusion | flops 25165824 | bytes 12601344 | tf_op jit(solution)/shard_map/convert_element_type | solution.py:89
  80.0 8.7 %copy.20 = bf16[2048,1536]{1,0:T(8,128)(2,1)} copy(bf16[2048,1536]{0,1:T(8,128)(2,1)} %fusion.20) | data formatting | bytes 12582912 | tf_op jit(solution)/shard_map/while | solution.py:102
  88.7 206.4 %while.10 = (s32[]{:T(128)}, f32[2,1024,8]{1,2,0:T(8,128)S(1)}, bf16[2048,1536]{1,0:T(8,128)(2,1)}, s32[]{:T(128)}) while((s32[]{:T(128)}, f32[2,1024,8]{1,2,0:T(8,128)S(1)}, bf16[2048,1536]{1,0:T(8,128)(2,1)}, s32[]{:T(128)}) %tuple.56), condition=%wide.region_5.6_spmd, body=%wide.region_2.5_spmd.sunk | while | flops 609043456 | bytes 44373856 | solution.py:102
  88.8 4.9 %convolution_bitcast_fusion.4 = f32[2048,48]{0,1:T(8,128)S(1)} fusion(bf16[2048,1536]{1,0:T(8,128)(2,1)} %get-tuple-element.120, bf16[1536,16]{0,1:T(8,128)(2,1)S(1)} %get-tuple-element.101, bf16[1536,16]{0,1:T(8,128)(2,1)S(1)} %get-tuple-element.102, bf16[1536,16]{0,1:T(8,128)(2,1)S(1)} %get-tuple-element.103), kind=kOutput, calls=%fused_computation.1.clone.1 | convolution fusion | flops 302432256 | bytes 6832128 | tf_op jit(solution)/shard_map/while/body/eval_jaxpr/dot_general | solution.py:93
  101.9 2.7 collective-permute-start.4
  105.4 5.0 %collective-permute-start.6 = (f32[2,1024,8]{1,2,0:T(8,128)S(1)}, f32[2,1024,8]{1,2,0:T(8,128)S(1)}, u32[]{:S(2)}, u32[]{:S(2)}) collective-permute-start(f32[2,1024,8]{1,2,0:T(8,128)S(1)} %add_add_fusion.5), channel_id=1, source_target_pairs={{0,80},{4,84},{8,88},{12,92},{16,64},{20,68},{24,72},{28,76},{32,1... | collective-permute-start | bytes 196616 | tf_op jit(solution)/shard_map/while/body/eval_jaxpr/ppermute | solution.py:18
  113.9 2.4 collective-permute-done.7
  120.3 4.9 %convolution_bitcast_fusion.4 = f32[2048,48]{0,1:T(8,128)S(1)} fusion(bf16[2048,1536]{1,0:T(8,128)(2,1)} %get-tuple-element.120, bf16[1536,16]{0,1:T(8,128)(2,1)S(1)} %get-tuple-element.101, bf16[1536,16]{0,1:T(8,128)(2,1)S(1)} %get-tuple-element.102, bf16[1536,16]{0,1:T(8,128)(2,1)S(1)} %get-tuple-element.103), kind=kOutput, calls=%fused_computation.1.clone.1 | convolution fusion | flops 302432256 | bytes 6832128 | tf_op jit(solution)/shard_map/while/body/eval_jaxpr/dot_general | solution.py:93
  127.8 3.2 collective-permute-start.1
  137.3 4.7 %collective-permute-start.4 = (f32[2,1024,8]{1,2,0:T(8,128)S(1)}, f32[2,1024,8]{1,2,0:T(8,128)S(1)}, u32[]{:S(2)}, u32[]{:S(2)}) collective-permute-start(f32[2,1024,8]{1,2,0:T(8,128)S(1)} %add_add_fusion.5), channel_id=1, source_target_pairs={{0,112},{4,116},{8,120},{12,124},{16,96},{20,100},{24,104},{28,108... | collective-permute-start | bytes 196616 | tf_op jit(solution)/shard_map/while/body/eval_jaxpr/ppermute | solution.py:18
  142.1 2.5 collective-permute-start.6
  146.6 3.2 collective-permute-start.8
  157.7 4.9 %convolution_bitcast_fusion.4 = f32[2048,48]{0,1:T(8,128)S(1)} fusion(bf16[2048,1536]{1,0:T(8,128)(2,1)} %get-tuple-element.120, bf16[1536,16]{0,1:T(8,128)(2,1)S(1)} %get-tuple-element.101, bf16[1536,16]{0,1:T(8,128)(2,1)S(1)} %get-tuple-element.102, bf16[1536,16]{0,1:T(8,128)(2,1)S(1)} %get-tuple-element.103), kind=kOutput, calls=%fused_computation.1.clone.1 | convolution fusion | flops 302432256 | bytes 6832128 | tf_op jit(solution)/shard_map/while/body/eval_jaxpr/dot_general | solution.py:93
  167.4 2.4 collective-permute-done
  171.3 4.4 %collective-permute-start.4 = (f32[2,1024,8]{1,2,0:T(8,128)S(1)}, f32[2,1024,8]{1,2,0:T(8,128)S(1)}, u32[]{:S(2)}, u32[]{:S(2)}) collective-permute-start(f32[2,1024,8]{1,2,0:T(8,128)S(1)} %add_add_fusion.5), channel_id=1, source_target_pairs={{0,112},{4,116},{8,120},{12,124},{16,96},{20,100},{24,104},{28,108... | collective-permute-start | bytes 196616 | tf_op jit(solution)/shard_map/while/body/eval_jaxpr/ppermute | solution.py:18
  176.1 3.4 %collective-permute-start.6 = (f32[2,1024,8]{1,2,0:T(8,128)S(1)}, f32[2,1024,8]{1,2,0:T(8,128)S(1)}, u32[]{:S(2)}, u32[]{:S(2)}) collective-permute-start(f32[2,1024,8]{1,2,0:T(8,128)S(1)} %add_add_fusion.5), channel_id=1, source_target_pairs={{0,80},{4,84},{8,88},{12,92},{16,64},{20,68},{24,72},{28,76},{32,1... | collective-permute-start | bytes 196616 | tf_op jit(solution)/shard_map/while/body/eval_jaxpr/ppermute | solution.py:18
  191.3 4.9 %convolution_bitcast_fusion.4 = f32[2048,48]{0,1:T(8,128)S(1)} fusion(bf16[2048,1536]{1,0:T(8,128)(2,1)} %get-tuple-element.120, bf16[1536,16]{0,1:T(8,128)(2,1)S(1)} %get-tuple-element.101, bf16[1536,16]{0,1:T(8,128)(2,1)S(1)} %get-tuple-element.102, bf16[1536,16]{0,1:T(8,128)(2,1)S(1)} %get-tuple-element.103), kind=kOutput, calls=%fused_computation.1.clone.1 | convolution fusion | flops 302432256 | bytes 6832128 | tf_op jit(solution)/shard_map/while/body/eval_jaxpr/dot_general | solution.py:93
  197.5 2.8 collective-permute-start
  203.3 2.4 collective-permute-done.1
  206.8 4.1 %collective-permute-start.4 = (f32[2,1024,8]{1,2,0:T(8,128)S(1)}, f32[2,1024,8]{1,2,0:T(8,128)S(1)}, u32[]{:S(2)}, u32[]{:S(2)}) collective-permute-start(f32[2,1024,8]{1,2,0:T(8,128)S(1)} %add_add_fusion.5), channel_id=1, source_target_pairs={{0,112},{4,116},{8,120},{12,124},{16,96},{20,100},{24,104},{28,108... | collective-permute-start | bytes 196616 | tf_op jit(solution)/shard_map/while/body/eval_jaxpr/ppermute | solution.py:18
  211.0 3.7 %collective-permute-start.6 = (f32[2,1024,8]{1,2,0:T(8,128)S(1)}, f32[2,1024,8]{1,2,0:T(8,128)S(1)}, u32[]{:S(2)}, u32[]{:S(2)}) collective-permute-start(f32[2,1024,8]{1,2,0:T(8,128)S(1)} %add_add_fusion.5), channel_id=1, source_target_pairs={{0,80},{4,84},{8,88},{12,92},{16,64},{20,68},{24,72},{28,76},{32,1... | collective-permute-start | bytes 196616 | tf_op jit(solution)/shard_map/while/body/eval_jaxpr/ppermute | solution.py:18
  216.1 2.4 collective-permute-start.8
  226.5 4.9 %convolution_bitcast_fusion.4 = f32[2048,48]{0,1:T(8,128)S(1)} fusion(bf16[2048,1536]{1,0:T(8,128)(2,1)} %get-tuple-element.120, bf16[1536,16]{0,1:T(8,128)(2,1)S(1)} %get-tuple-element.101, bf16[1536,16]{0,1:T(8,128)(2,1)S(1)} %get-tuple-element.102, bf16[1536,16]{0,1:T(8,128)(2,1)S(1)} %get-tuple-element.103), kind=kOutput, calls=%fused_computation.1.clone.1 | convolution fusion | flops 302432256 | bytes 6832128 | tf_op jit(solution)/shard_map/while/body/eval_jaxpr/dot_general | solution.py:93
  240.7 4.1 %collective-permute-start.4 = (f32[2,1024,8]{1,2,0:T(8,128)S(1)}, f32[2,1024,8]{1,2,0:T(8,128)S(1)}, u32[]{:S(2)}, u32[]{:S(2)}) collective-permute-start(f32[2,1024,8]{1,2,0:T(8,128)S(1)} %add_add_fusion.5), channel_id=1, source_target_pairs={{0,112},{4,116},{8,120},{12,124},{16,96},{20,100},{24,104},{28,108... | collective-permute-start | bytes 196616 | tf_op jit(solution)/shard_map/while/body/eval_jaxpr/ppermute | solution.py:18
  244.9 3.7 %collective-permute-start.6 = (f32[2,1024,8]{1,2,0:T(8,128)S(1)}, f32[2,1024,8]{1,2,0:T(8,128)S(1)}, u32[]{:S(2)}, u32[]{:S(2)}) collective-permute-start(f32[2,1024,8]{1,2,0:T(8,128)S(1)} %add_add_fusion.5), channel_id=1, source_target_pairs={{0,80},{4,84},{8,88},{12,92},{16,64},{20,68},{24,72},{28,76},{32,1... | collective-permute-start | bytes 196616 | tf_op jit(solution)/shard_map/while/body/eval_jaxpr/ppermute | solution.py:18
  250.1 2.4 collective-permute-start.8
  260.4 4.9 %convolution_bitcast_fusion.4 = f32[2048,48]{0,1:T(8,128)S(1)} fusion(bf16[2048,1536]{1,0:T(8,128)(2,1)} %get-tuple-element.120, bf16[1536,16]{0,1:T(8,128)(2,1)S(1)} %get-tuple-element.101, bf16[1536,16]{0,1:T(8,128)(2,1)S(1)} %get-tuple-element.102, bf16[1536,16]{0,1:T(8,128)(2,1)S(1)} %get-tuple-element.103), kind=kOutput, calls=%fused_computation.1.clone.1 | convolution fusion | flops 302432256 | bytes 6832128 | tf_op jit(solution)/shard_map/while/body/eval_jaxpr/dot_general | solution.py:93
  275.5 4.1 %collective-permute-start.4 = (f32[2,1024,8]{1,2,0:T(8,128)S(1)}, f32[2,1024,8]{1,2,0:T(8,128)S(1)}, u32[]{:S(2)}, u32[]{:S(2)}) collective-permute-start(f32[2,1024,8]{1,2,0:T(8,128)S(1)} %add_add_fusion.5), channel_id=1, source_target_pairs={{0,112},{4,116},{8,120},{12,124},{16,96},{20,100},{24,104},{28,108... | collective-permute-start | bytes 196616 | tf_op jit(solution)/shard_map/while/body/eval_jaxpr/ppermute | solution.py:18
  279.7 3.7 %collective-permute-start.6 = (f32[2,1024,8]{1,2,0:T(8,128)S(1)}, f32[2,1024,8]{1,2,0:T(8,128)S(1)}, u32[]{:S(2)}, u32[]{:S(2)}) collective-permute-start(f32[2,1024,8]{1,2,0:T(8,128)S(1)} %add_add_fusion.5), channel_id=1, source_target_pairs={{0,80},{4,84},{8,88},{12,92},{16,64},{20,68},{24,72},{28,76},{32,1... | collective-permute-start | bytes 196616 | tf_op jit(solution)/shard_map/while/body/eval_jaxpr/ppermute | solution.py:18
  284.8 2.4 collective-permute-start.8
  295.2 4.0 %fusion.21 = f32[2048,48]{0,1:T(8,128)S(1)} fusion(bf16[2048,1536]{0,1:T(8,128)(2,1)} %fusion.20, bf16[1536,16]{0,1:T(8,128)(2,1)S(1)} %get-tuple-element.66, bf16[1536,16]{0,1:T(8,128)(2,1)S(1)} %get-tuple-element.65, bf16[1536,16]{0,1:T(8,128)(2,1)S(1)} %get-tuple-element.64), kind=kOutput, calls=%fused_computation.58 | convolution fusion | flops 302432256 | bytes 6832128 | tf_op jit(solution)/shard_map/dot_general | solution.py:93
  299.4 3.5 %collective-permute-start.22 = (f32[16]{0:T(128)S(1)}, f32[16]{0:T(128)S(1)}, u32[]{:S(2)}, u32[]{:S(2)}) collective-permute-start(f32[16]{0:T(128)S(1)} %get-tuple-element.41), channel_id=1, source_target_pairs={{0,8},{4,12},{8,0},{12,4},{16,24},{20,28},{24,16},{28,20},{32,40},... | collective-permute-start | bytes 200 | tf_op jit(solution)/shard_map/ppermute | solution.py:18
  307.1 3.2 multiply_reduce_fusion.1
  311.0 2.7 collective-permute-start.25
  317.6 4.1 %collective-permute-start.29 = (f32[16]{0:T(128)S(1)}, f32[16]{0:T(128)S(1)}, u32[]{:S(2)}, u32[]{:S(2)}) collective-permute-start(f32[16]{0:T(128)S(1)} %add_add_fusion.3), channel_id=1, source_target_pairs={{0,96},{4,100},{8,104},{12,108},{16,112},{20,116},{24,120},{28,124... | collective-permute-start | bytes 200 | tf_op jit(solution)/shard_map/ppermute | solution.py:18
  321.7 4.1 %collective-permute-start.30 = (f32[16]{0:T(128)S(1)}, f32[16]{0:T(128)S(1)}, u32[]{:S(2)}, u32[]{:S(2)}) collective-permute-start(f32[16]{0:T(128)S(1)} %add_add_fusion.3), channel_id=1, source_target_pairs={{0,112},{4,116},{8,120},{12,124},{16,96},{20,100},{24,104},{28,108... | collective-permute-start | bytes 200 | tf_op jit(solution)/shard_map/ppermute | solution.py:18
  325.8 3.0 collective-permute-done.30
  (314 shorter events, 128.4 us)
Async XLA Ops:
  10.4 25.8 %collective-permute-start.10 = (bf16[2048,512]{0,1:T(8,128)(2,1)}, bf16[2048,512]{0,1:T(8,128)(2,1)}, u32[]{:S(2)}, u32[]{:S(2)}) collective-permute-start(bf16[2048,512]{0,1:T(8,128)(2,1)} %slice.100), channel_id=1, source_target_pairs={{1,0},{2,1},{3,2},{5,4},{6,5},{7,6},{9,8},{10,9},{11,10},{13,12},{... | collective-permute-start | bytes 6291464 | tf_op jit(solution)/shard_map/ppermute | solution.py:13
  51.4 8.2 %collective-permute-start.14 = (f32[2,1536]{1,0:T(2,128)S(1)}, f32[2,1536]{1,0:T(2,128)S(1)}, u32[]{:S(2)}, u32[]{:S(2)}) collective-permute-start(f32[2,1536]{1,0:T(2,128)S(1)} %add_add_fusion.2), channel_id=1, source_target_pairs={{0,16},{4,20},{8,24},{12,28},{16,0},{20,4},{24,8},{28,12},{32,48},... | collective-permute-start | bytes 36872 | tf_op jit(solution)/shard_map/ppermute | solution.py:18
  53.1 12.7 %collective-permute-start.15 = (f32[2,1536]{1,0:T(2,128)S(1)}, f32[2,1536]{1,0:T(2,128)S(1)}, u32[]{:S(2)}, u32[]{:S(2)}) collective-permute-start(f32[2,1536]{1,0:T(2,128)S(1)} %add_add_fusion.2), channel_id=1, source_target_pairs={{0,32},{4,36},{8,40},{12,44},{16,48},{20,52},{24,56},{28,60},{32,0... | collective-permute-start | bytes 36872 | tf_op jit(solution)/shard_map/ppermute | solution.py:18
  55.7 11.3 %collective-permute-start.16 = (f32[2,1536]{1,0:T(2,128)S(1)}, f32[2,1536]{1,0:T(2,128)S(1)}, u32[]{:S(2)}, u32[]{:S(2)}) collective-permute-start(f32[2,1536]{1,0:T(2,128)S(1)} %add_add_fusion.2), channel_id=1, source_target_pairs={{0,48},{4,52},{8,56},{12,60},{16,32},{20,36},{24,40},{28,44},{32,1... | collective-permute-start | bytes 36872 | tf_op jit(solution)/shard_map/ppermute | solution.py:18
  56.1 10.9 %collective-permute-start.17 = (f32[2,1536]{1,0:T(2,128)S(1)}, f32[2,1536]{1,0:T(2,128)S(1)}, u32[]{:S(2)}, u32[]{:S(2)}) collective-permute-start(f32[2,1536]{1,0:T(2,128)S(1)} %add_add_fusion.2), channel_id=1, source_target_pairs={{0,64},{4,68},{8,72},{12,76},{16,80},{20,84},{24,88},{28,92},{32,9... | collective-permute-start | bytes 36872 | tf_op jit(solution)/shard_map/ppermute | solution.py:18
  59.1 7.9 %collective-permute-start.18 = (f32[2,1536]{1,0:T(2,128)S(1)}, f32[2,1536]{1,0:T(2,128)S(1)}, u32[]{:S(2)}, u32[]{:S(2)}) collective-permute-start(f32[2,1536]{1,0:T(2,128)S(1)} %add_add_fusion.2), channel_id=1, source_target_pairs={{0,80},{4,84},{8,88},{12,92},{16,64},{20,68},{24,72},{28,76},{32,1... | collective-permute-start | bytes 36872 | tf_op jit(solution)/shard_map/ppermute | solution.py:18
  59.5 8.0 %collective-permute-start.19 = (f32[2,1536]{1,0:T(2,128)S(1)}, f32[2,1536]{1,0:T(2,128)S(1)}, u32[]{:S(2)}, u32[]{:S(2)}) collective-permute-start(f32[2,1536]{1,0:T(2,128)S(1)} %add_add_fusion.2), channel_id=1, source_target_pairs={{0,96},{4,100},{8,104},{12,108},{16,112},{20,116},{24,120},{28,124... | collective-permute-start | bytes 36872 | tf_op jit(solution)/shard_map/ppermute | solution.py:18
  65.7 7.3 %collective-permute-start.20 = (f32[2,1536]{1,0:T(2,128)S(1)}, f32[2,1536]{1,0:T(2,128)S(1)}, u32[]{:S(2)}, u32[]{:S(2)}) collective-permute-start(f32[2,1536]{1,0:T(2,128)S(1)} %add_add_fusion.2), channel_id=1, source_target_pairs={{0,112},{4,116},{8,120},{12,124},{16,96},{20,100},{24,104},{28,108... | collective-permute-start | bytes 36872 | tf_op jit(solution)/shard_map/ppermute | solution.py:18
  94.9 5.9 %collective-permute-start = (f32[2,1024,8]{1,2,0:T(8,128)S(1)}, f32[2,1024,8]{1,2,0:T(8,128)S(1)}, u32[]{:S(2)}, u32[]{:S(2)}) collective-permute-start(f32[2,1024,8]{1,2,0:T(8,128)S(1)} %pad_maximum_fusion.4), channel_id=1, source_target_pairs={{0,8},{4,12},{8,0},{12,4},{16,24},{20,28},{24,16},{28,20},{32,40},... | collective-permute-start | bytes 196616 | tf_op jit(solution)/shard_map/while/body/eval_jaxpr/ppermute | solution.py:18
  95.3 6.2 %collective-permute-start.1 = (f32[2,1024,8]{1,2,0:T(8,128)S(1)}, f32[2,1024,8]{1,2,0:T(8,128)S(1)}, u32[]{:S(2)}, u32[]{:S(2)}) collective-permute-start(f32[2,1024,8]{1,2,0:T(8,128)S(1)} %pad_maximum_fusion.4), channel_id=1, source_target_pairs={{0,12},{4,8},{8,4},{12,0},{16,28},{20,24},{24,20},{28,16},{32,44},... | collective-permute-start | bytes 196616 | tf_op jit(solution)/shard_map/while/body/eval_jaxpr/ppermute | solution.py:18
  101.5 9.0 %collective-permute-start.3 = (f32[2,1024,8]{1,2,0:T(8,128)S(1)}, f32[2,1024,8]{1,2,0:T(8,128)S(1)}, u32[]{:S(2)}, u32[]{:S(2)}) collective-permute-start(f32[2,1024,8]{1,2,0:T(8,128)S(1)} %add_add_fusion.5), channel_id=1, source_target_pairs={{0,96},{4,100},{8,104},{12,108},{16,112},{20,116},{24,120},{28,124... | collective-permute-start | bytes 196616 | tf_op jit(solution)/shard_map/while/body/eval_jaxpr/ppermute | solution.py:18
  101.9 10.4 %collective-permute-start.4 = (f32[2,1024,8]{1,2,0:T(8,128)S(1)}, f32[2,1024,8]{1,2,0:T(8,128)S(1)}, u32[]{:S(2)}, u32[]{:S(2)}) collective-permute-start(f32[2,1024,8]{1,2,0:T(8,128)S(1)} %add_add_fusion.5), channel_id=1, source_target_pairs={{0,112},{4,116},{8,120},{12,124},{16,96},{20,100},{24,104},{28,108... | collective-permute-start | bytes 196616 | tf_op jit(solution)/shard_map/while/body/eval_jaxpr/ppermute | solution.py:18
  104.6 9.4 %collective-permute-start.5 = (f32[2,1024,8]{1,2,0:T(8,128)S(1)}, f32[2,1024,8]{1,2,0:T(8,128)S(1)}, u32[]{:S(2)}, u32[]{:S(2)}) collective-permute-start(f32[2,1024,8]{1,2,0:T(8,128)S(1)} %add_add_fusion.5), channel_id=1, source_target_pairs={{0,64},{4,68},{8,72},{12,76},{16,80},{20,84},{24,88},{28,92},{32,9... | collective-permute-start | bytes 196616 | tf_op jit(solution)/shard_map/while/body/eval_jaxpr/ppermute | solution.py:18
  105.4 8.5 %collective-permute-start.6 = (f32[2,1024,8]{1,2,0:T(8,128)S(1)}, f32[2,1024,8]{1,2,0:T(8,128)S(1)}, u32[]{:S(2)}, u32[]{:S(2)}) collective-permute-start(f32[2,1024,8]{1,2,0:T(8,128)S(1)} %add_add_fusion.5), channel_id=1, source_target_pairs={{0,80},{4,84},{8,88},{12,92},{16,64},{20,68},{24,72},{28,76},{32,1... | collective-permute-start | bytes 196616 | tf_op jit(solution)/shard_map/while/body/eval_jaxpr/ppermute | solution.py:18
  110.4 5.9 %collective-permute-start.7 = (f32[2,1024,8]{1,2,0:T(8,128)S(1)}, f32[2,1024,8]{1,2,0:T(8,128)S(1)}, u32[]{:S(2)}, u32[]{:S(2)}) collective-permute-start(f32[2,1024,8]{1,2,0:T(8,128)S(1)} %add_add_fusion.5), channel_id=1, source_target_pairs={{0,32},{4,36},{8,40},{12,44},{16,48},{20,52},{24,56},{28,60},{32,0... | collective-permute-start | bytes 196616 | tf_op jit(solution)/shard_map/while/body/eval_jaxpr/ppermute | solution.py:18
  110.4 6.2 %collective-permute-start.8 = (f32[2,1024,8]{1,2,0:T(8,128)S(1)}, f32[2,1024,8]{1,2,0:T(8,128)S(1)}, u32[]{:S(2)}, u32[]{:S(2)}) collective-permute-start(f32[2,1024,8]{1,2,0:T(8,128)S(1)} %add_add_fusion.5), channel_id=1, source_target_pairs={{0,48},{4,52},{8,56},{12,60},{16,32},{20,36},{24,40},{28,44},{32,1... | collective-permute-start | bytes 196616 | tf_op jit(solution)/shard_map/while/body/eval_jaxpr/ppermute | solution.py:18
  135.6 11.0 %collective-permute-start.3 = (f32[2,1024,8]{1,2,0:T(8,128)S(1)}, f32[2,1024,8]{1,2,0:T(8,128)S(1)}, u32[]{:S(2)}, u32[]{:S(2)}) collective-permute-start(f32[2,1024,8]{1,2,0:T(8,128)S(1)} %add_add_fusion.5), channel_id=1, source_target_pairs={{0,96},{4,100},{8,104},{12,108},{16,112},{20,116},{24,120},{28,124... | collective-permute-start | bytes 196616 | tf_op jit(solution)/shard_map/while/body/eval_jaxpr/ppermute | solution.py:18
  137.3 12.4 %collective-permute-start.4 = (f32[2,1024,8]{1,2,0:T(8,128)S(1)}, f32[2,1024,8]{1,2,0:T(8,128)S(1)}, u32[]{:S(2)}, u32[]{:S(2)}) collective-permute-start(f32[2,1024,8]{1,2,0:T(8,128)S(1)} %add_add_fusion.5), channel_id=1, source_target_pairs={{0,112},{4,116},{8,120},{12,124},{16,96},{20,100},{24,104},{28,108... | collective-permute-start | bytes 196616 | tf_op jit(solution)/shard_map/while/body/eval_jaxpr/ppermute | solution.py:18
  142.1 7.7 %collective-permute-start.5 = (f32[2,1024,8]{1,2,0:T(8,128)S(1)}, f32[2,1024,8]{1,2,0:T(8,128)S(1)}, u32[]{:S(2)}, u32[]{:S(2)}) collective-permute-start(f32[2,1024,8]{1,2,0:T(8,128)S(1)} %add_add_fusion.5), channel_id=1, source_target_pairs={{0,64},{4,68},{8,72},{12,76},{16,80},{20,84},{24,88},{28,92},{32,9... | collective-permute-start | bytes 196616 | tf_op jit(solution)/shard_map/while/body/eval_jaxpr/ppermute | solution.py:18
  142.1 7.7 %collective-permute-start.6 = (f32[2,1024,8]{1,2,0:T(8,128)S(1)}, f32[2,1024,8]{1,2,0:T(8,128)S(1)}, u32[]{:S(2)}, u32[]{:S(2)}) collective-permute-start(f32[2,1024,8]{1,2,0:T(8,128)S(1)} %add_add_fusion.5), channel_id=1, source_target_pairs={{0,80},{4,84},{8,88},{12,92},{16,64},{20,68},{24,72},{28,76},{32,1... | collective-permute-start | bytes 196616 | tf_op jit(solution)/shard_map/while/body/eval_jaxpr/ppermute | solution.py:18
  163.8 6.0 %collective-permute-start = (f32[2,1024,8]{1,2,0:T(8,128)S(1)}, f32[2,1024,8]{1,2,0:T(8,128)S(1)}, u32[]{:S(2)}, u32[]{:S(2)}) collective-permute-start(f32[2,1024,8]{1,2,0:T(8,128)S(1)} %pad_maximum_fusion.4), channel_id=1, source_target_pairs={{0,8},{4,12},{8,0},{12,4},{16,24},{20,28},{24,16},{28,20},{32,40},... | collective-permute-start | bytes 196616 | tf_op jit(solution)/shard_map/while/body/eval_jaxpr/ppermute | solution.py:18
  164.2 6.2 %collective-permute-start.1 = (f32[2,1024,8]{1,2,0:T(8,128)S(1)}, f32[2,1024,8]{1,2,0:T(8,128)S(1)}, u32[]{:S(2)}, u32[]{:S(2)}) collective-permute-start(f32[2,1024,8]{1,2,0:T(8,128)S(1)} %pad_maximum_fusion.4), channel_id=1, source_target_pairs={{0,12},{4,8},{8,4},{12,0},{16,28},{20,24},{24,20},{28,16},{32,44},... | collective-permute-start | bytes 196616 | tf_op jit(solution)/shard_map/while/body/eval_jaxpr/ppermute | solution.py:18
  170.6 10.6 %collective-permute-start.3 = (f32[2,1024,8]{1,2,0:T(8,128)S(1)}, f32[2,1024,8]{1,2,0:T(8,128)S(1)}, u32[]{:S(2)}, u32[]{:S(2)}) collective-permute-start(f32[2,1024,8]{1,2,0:T(8,128)S(1)} %add_add_fusion.5), channel_id=1, source_target_pairs={{0,96},{4,100},{8,104},{12,108},{16,112},{20,116},{24,120},{28,124... | collective-permute-start | bytes 196616 | tf_op jit(solution)/shard_map/while/body/eval_jaxpr/ppermute | solution.py:18
  171.3 12.1 %collective-permute-start.4 = (f32[2,1024,8]{1,2,0:T(8,128)S(1)}, f32[2,1024,8]{1,2,0:T(8,128)S(1)}, u32[]{:S(2)}, u32[]{:S(2)}) collective-permute-start(f32[2,1024,8]{1,2,0:T(8,128)S(1)} %add_add_fusion.5), channel_id=1, source_target_pairs={{0,112},{4,116},{8,120},{12,124},{16,96},{20,100},{24,104},{28,108... | collective-permute-start | bytes 196616 | tf_op jit(solution)/shard_map/while/body/eval_jaxpr/ppermute | solution.py:18
  175.7 7.7 %collective-permute-start.5 = (f32[2,1024,8]{1,2,0:T(8,128)S(1)}, f32[2,1024,8]{1,2,0:T(8,128)S(1)}, u32[]{:S(2)}, u32[]{:S(2)}) collective-permute-start(f32[2,1024,8]{1,2,0:T(8,128)S(1)} %add_add_fusion.5), channel_id=1, source_target_pairs={{0,64},{4,68},{8,72},{12,76},{16,80},{20,84},{24,88},{28,92},{32,9... | collective-permute-start | bytes 196616 | tf_op jit(solution)/shard_map/while/body/eval_jaxpr/ppermute | solution.py:18
  176.1 7.4 %collective-permute-start.6 = (f32[2,1024,8]{1,2,0:T(8,128)S(1)}, f32[2,1024,8]{1,2,0:T(8,128)S(1)}, u32[]{:S(2)}, u32[]{:S(2)}) collective-permute-start(f32[2,1024,8]{1,2,0:T(8,128)S(1)} %add_add_fusion.5), channel_id=1, source_target_pairs={{0,80},{4,84},{8,88},{12,92},{16,64},{20,68},{24,72},{28,76},{32,1... | collective-permute-start | bytes 196616 | tf_op jit(solution)/shard_map/while/body/eval_jaxpr/ppermute | solution.py:18
  205.7 10.4 %collective-permute-start.3 = (f32[2,1024,8]{1,2,0:T(8,128)S(1)}, f32[2,1024,8]{1,2,0:T(8,128)S(1)}, u32[]{:S(2)}, u32[]{:S(2)}) collective-permute-start(f32[2,1024,8]{1,2,0:T(8,128)S(1)} %add_add_fusion.5), channel_id=1, source_target_pairs={{0,96},{4,100},{8,104},{12,108},{16,112},{20,116},{24,120},{28,124... | collective-permute-start | bytes 196616 | tf_op jit(solution)/shard_map/while/body/eval_jaxpr/ppermute | solution.py:18
  206.8 11.8 %collective-permute-start.4 = (f32[2,1024,8]{1,2,0:T(8,128)S(1)}, f32[2,1024,8]{1,2,0:T(8,128)S(1)}, u32[]{:S(2)}, u32[]{:S(2)}) collective-permute-start(f32[2,1024,8]{1,2,0:T(8,128)S(1)} %add_add_fusion.5), channel_id=1, source_target_pairs={{0,112},{4,116},{8,120},{12,124},{16,96},{20,100},{24,104},{28,108... | collective-permute-start | bytes 196616 | tf_op jit(solution)/shard_map/while/body/eval_jaxpr/ppermute | solution.py:18
  210.9 7.7 %collective-permute-start.5 = (f32[2,1024,8]{1,2,0:T(8,128)S(1)}, f32[2,1024,8]{1,2,0:T(8,128)S(1)}, u32[]{:S(2)}, u32[]{:S(2)}) collective-permute-start(f32[2,1024,8]{1,2,0:T(8,128)S(1)} %add_add_fusion.5), channel_id=1, source_target_pairs={{0,64},{4,68},{8,72},{12,76},{16,80},{20,84},{24,88},{28,92},{32,9... | collective-permute-start | bytes 196616 | tf_op jit(solution)/shard_map/while/body/eval_jaxpr/ppermute | solution.py:18
  211.0 7.6 %collective-permute-start.6 = (f32[2,1024,8]{1,2,0:T(8,128)S(1)}, f32[2,1024,8]{1,2,0:T(8,128)S(1)}, u32[]{:S(2)}, u32[]{:S(2)}) collective-permute-start(f32[2,1024,8]{1,2,0:T(8,128)S(1)} %add_add_fusion.5), channel_id=1, source_target_pairs={{0,80},{4,84},{8,88},{12,92},{16,64},{20,68},{24,72},{28,76},{32,1... | collective-permute-start | bytes 196616 | tf_op jit(solution)/shard_map/while/body/eval_jaxpr/ppermute | solution.py:18
  239.7 10.4 %collective-permute-start.3 = (f32[2,1024,8]{1,2,0:T(8,128)S(1)}, f32[2,1024,8]{1,2,0:T(8,128)S(1)}, u32[]{:S(2)}, u32[]{:S(2)}) collective-permute-start(f32[2,1024,8]{1,2,0:T(8,128)S(1)} %add_add_fusion.5), channel_id=1, source_target_pairs={{0,96},{4,100},{8,104},{12,108},{16,112},{20,116},{24,120},{28,124... | collective-permute-start | bytes 196616 | tf_op jit(solution)/shard_map/while/body/eval_jaxpr/ppermute | solution.py:18
  240.7 11.8 %collective-permute-start.4 = (f32[2,1024,8]{1,2,0:T(8,128)S(1)}, f32[2,1024,8]{1,2,0:T(8,128)S(1)}, u32[]{:S(2)}, u32[]{:S(2)}) collective-permute-start(f32[2,1024,8]{1,2,0:T(8,128)S(1)} %add_add_fusion.5), channel_id=1, source_target_pairs={{0,112},{4,116},{8,120},{12,124},{16,96},{20,100},{24,104},{28,108... | collective-permute-start | bytes 196616 | tf_op jit(solution)/shard_map/while/body/eval_jaxpr/ppermute | solution.py:18
  244.8 7.7 %collective-permute-start.5 = (f32[2,1024,8]{1,2,0:T(8,128)S(1)}, f32[2,1024,8]{1,2,0:T(8,128)S(1)}, u32[]{:S(2)}, u32[]{:S(2)}) collective-permute-start(f32[2,1024,8]{1,2,0:T(8,128)S(1)} %add_add_fusion.5), channel_id=1, source_target_pairs={{0,64},{4,68},{8,72},{12,76},{16,80},{20,84},{24,88},{28,92},{32,9... | collective-permute-start | bytes 196616 | tf_op jit(solution)/shard_map/while/body/eval_jaxpr/ppermute | solution.py:18
  244.9 7.6 %collective-permute-start.6 = (f32[2,1024,8]{1,2,0:T(8,128)S(1)}, f32[2,1024,8]{1,2,0:T(8,128)S(1)}, u32[]{:S(2)}, u32[]{:S(2)}) collective-permute-start(f32[2,1024,8]{1,2,0:T(8,128)S(1)} %add_add_fusion.5), channel_id=1, source_target_pairs={{0,80},{4,84},{8,88},{12,92},{16,64},{20,68},{24,72},{28,76},{32,1... | collective-permute-start | bytes 196616 | tf_op jit(solution)/shard_map/while/body/eval_jaxpr/ppermute | solution.py:18
  274.4 10.4 %collective-permute-start.3 = (f32[2,1024,8]{1,2,0:T(8,128)S(1)}, f32[2,1024,8]{1,2,0:T(8,128)S(1)}, u32[]{:S(2)}, u32[]{:S(2)}) collective-permute-start(f32[2,1024,8]{1,2,0:T(8,128)S(1)} %add_add_fusion.5), channel_id=1, source_target_pairs={{0,96},{4,100},{8,104},{12,108},{16,112},{20,116},{24,120},{28,124... | collective-permute-start | bytes 196616 | tf_op jit(solution)/shard_map/while/body/eval_jaxpr/ppermute | solution.py:18
  275.5 11.8 %collective-permute-start.4 = (f32[2,1024,8]{1,2,0:T(8,128)S(1)}, f32[2,1024,8]{1,2,0:T(8,128)S(1)}, u32[]{:S(2)}, u32[]{:S(2)}) collective-permute-start(f32[2,1024,8]{1,2,0:T(8,128)S(1)} %add_add_fusion.5), channel_id=1, source_target_pairs={{0,112},{4,116},{8,120},{12,124},{16,96},{20,100},{24,104},{28,108... | collective-permute-start | bytes 196616 | tf_op jit(solution)/shard_map/while/body/eval_jaxpr/ppermute | solution.py:18
  279.6 7.7 %collective-permute-start.5 = (f32[2,1024,8]{1,2,0:T(8,128)S(1)}, f32[2,1024,8]{1,2,0:T(8,128)S(1)}, u32[]{:S(2)}, u32[]{:S(2)}) collective-permute-start(f32[2,1024,8]{1,2,0:T(8,128)S(1)} %add_add_fusion.5), channel_id=1, source_target_pairs={{0,64},{4,68},{8,72},{12,76},{16,80},{20,84},{24,88},{28,92},{32,9... | collective-permute-start | bytes 196616 | tf_op jit(solution)/shard_map/while/body/eval_jaxpr/ppermute | solution.py:18
  279.7 7.6 %collective-permute-start.6 = (f32[2,1024,8]{1,2,0:T(8,128)S(1)}, f32[2,1024,8]{1,2,0:T(8,128)S(1)}, u32[]{:S(2)}, u32[]{:S(2)}) collective-permute-start(f32[2,1024,8]{1,2,0:T(8,128)S(1)} %add_add_fusion.5), channel_id=1, source_target_pairs={{0,80},{4,84},{8,88},{12,92},{16,64},{20,68},{24,72},{28,76},{32,1... | collective-permute-start | bytes 196616 | tf_op jit(solution)/shard_map/while/body/eval_jaxpr/ppermute | solution.py:18
  299.4 11.6 %collective-permute-start.21 = (f32[16]{0:T(128)S(1)}, f32[16]{0:T(128)S(1)}, u32[]{:S(2)}, u32[]{:S(2)}) collective-permute-start(f32[16]{0:T(128)S(1)} %get-tuple-element.41), channel_id=1, source_target_pairs={{0,4},{4,0},{8,12},{12,8},{16,20},{20,16},{24,28},{28,24},{32,36},... | collective-permute-start | bytes 200 | tf_op jit(solution)/shard_map/ppermute | solution.py:18
  299.4 11.5 %collective-permute-start.22 = (f32[16]{0:T(128)S(1)}, f32[16]{0:T(128)S(1)}, u32[]{:S(2)}, u32[]{:S(2)}) collective-permute-start(f32[16]{0:T(128)S(1)} %get-tuple-element.41), channel_id=1, source_target_pairs={{0,8},{4,12},{8,0},{12,4},{16,24},{20,28},{24,16},{28,20},{32,40},... | collective-permute-start | bytes 200 | tf_op jit(solution)/shard_map/ppermute | solution.py:18
  302.9 8.0 %collective-permute-start.23 = (f32[16]{0:T(128)S(1)}, f32[16]{0:T(128)S(1)}, u32[]{:S(2)}, u32[]{:S(2)}) collective-permute-start(f32[16]{0:T(128)S(1)} %get-tuple-element.41), channel_id=1, source_target_pairs={{0,12},{4,8},{8,4},{12,0},{16,28},{20,24},{24,20},{28,16},{32,44},... | collective-permute-start | bytes 200 | tf_op jit(solution)/shard_map/ppermute | solution.py:18
  311.0 6.6 %collective-permute-start.24 = (f32[16]{0:T(128)S(1)}, f32[16]{0:T(128)S(1)}, u32[]{:S(2)}, u32[]{:S(2)}) collective-permute-start(f32[16]{0:T(128)S(1)} %add_add_fusion.3), channel_id=1, source_target_pairs={{0,16},{4,20},{8,24},{12,28},{16,0},{20,4},{24,8},{28,12},{32,48},... | collective-permute-start | bytes 200 | tf_op jit(solution)/shard_map/ppermute | solution.py:18
  311.0 10.7 %collective-permute-start.25 = (f32[16]{0:T(128)S(1)}, f32[16]{0:T(128)S(1)}, u32[]{:S(2)}, u32[]{:S(2)}) collective-permute-start(f32[16]{0:T(128)S(1)} %add_add_fusion.3), channel_id=1, source_target_pairs={{0,32},{4,36},{8,40},{12,44},{16,48},{20,52},{24,56},{28,60},{32,0... | collective-permute-start | bytes 200 | tf_op jit(solution)/shard_map/ppermute | solution.py:18
  313.7 12.1 %collective-permute-start.26 = (f32[16]{0:T(128)S(1)}, f32[16]{0:T(128)S(1)}, u32[]{:S(2)}, u32[]{:S(2)}) collective-permute-start(f32[16]{0:T(128)S(1)} %add_add_fusion.3), channel_id=1, source_target_pairs={{0,48},{4,52},{8,56},{12,60},{16,32},{20,36},{24,40},{28,44},{32,1... | collective-permute-start | bytes 200 | tf_op jit(solution)/shard_map/ppermute | solution.py:18
  315.7 10.1 %collective-permute-start.27 = (f32[16]{0:T(128)S(1)}, f32[16]{0:T(128)S(1)}, u32[]{:S(2)}, u32[]{:S(2)}) collective-permute-start(f32[16]{0:T(128)S(1)} %add_add_fusion.3), channel_id=1, source_target_pairs={{0,64},{4,68},{8,72},{12,76},{16,80},{20,84},{24,88},{28,92},{32,9... | collective-permute-start | bytes 200 | tf_op jit(solution)/shard_map/ppermute | solution.py:18
  315.8 10.0 %collective-permute-start.28 = (f32[16]{0:T(128)S(1)}, f32[16]{0:T(128)S(1)}, u32[]{:S(2)}, u32[]{:S(2)}) collective-permute-start(f32[16]{0:T(128)S(1)} %add_add_fusion.3), channel_id=1, source_target_pairs={{0,80},{4,84},{8,88},{12,92},{16,64},{20,68},{24,72},{28,76},{32,1... | collective-permute-start | bytes 200 | tf_op jit(solution)/shard_map/ppermute | solution.py:18
  317.6 8.2 %collective-permute-start.29 = (f32[16]{0:T(128)S(1)}, f32[16]{0:T(128)S(1)}, u32[]{:S(2)}, u32[]{:S(2)}) collective-permute-start(f32[16]{0:T(128)S(1)} %add_add_fusion.3), channel_id=1, source_target_pairs={{0,96},{4,100},{8,104},{12,108},{16,112},{20,116},{24,120},{28,124... | collective-permute-start | bytes 200 | tf_op jit(solution)/shard_map/ppermute | solution.py:18
  321.7 7.2 %collective-permute-start.30 = (f32[16]{0:T(128)S(1)}, f32[16]{0:T(128)S(1)}, u32[]{:S(2)}, u32[]{:S(2)}) collective-permute-start(f32[16]{0:T(128)S(1)} %add_add_fusion.3), channel_id=1, source_target_pairs={{0,112},{4,116},{8,120},{12,124},{16,96},{20,100},{24,104},{28,108... | collective-permute-start | bytes 200 | tf_op jit(solution)/shard_map/ppermute | solution.py:18
  (45 other events, 257.9 us)

commit v3 on v1

--- a/solution.py
+++ b/solution.py
@@ -1,6 +1,7 @@
 import jax
 import jax.numpy as jnp
 from jax import lax
+from jax.experimental.layout import Layout, with_layout_constraint
 from jax.sharding import PartitionSpec as P
 
 ITERS = 6
@@ -90,6 +91,7 @@
     miss_here = lax.dynamic_slice_in_dim(missing, position * columns, columns + half_cols)
     weight = jnp.sqrt((total - miss_here.astype(jnp.float32)) / total)
     stand = ((regionf - mean) / jnp.sqrt(var + 1e-05) * weight).astype(jnp.bfloat16)
+    stand = with_layout_constraint(stand, Layout(major_to_minor=(0, 1)))
 
     def project(basis):
         wide = widened(basis, half_cols)

time: 294 us -> 275 us (0.935)
  local copies, waits for them, and re-layouts: 23.6 us -> 4.48 us
    unnamed x14 -> x10, local copies, waits for them, and re-layouts: 10.6 us -> 1.54 us
    while x13 -> x12, local copies, waits for them, and re-layouts: 8.7 us -> 0.02 us  [the longest x1 8.67 us: shards(): lax.fori_loop(0, ITERS, lambda step, basis: orthonormal(image_of(basis)),...]
  transfers between devices with their start and end apart: 57 -> 57, of which waited for: 49 -> 51; matrix products, arithmetic and copies ran while one was open for 3% -> 2% of each run, Pallas kernels for 0% -> 0%
where the time goes in v3:
time: 275 us
  waiting for transfers between devices  100 us (36%)
  starting transfers between devices  89.6 us (33%)
  matrix products  48 us (17%)
  other arithmetic  30.7 us (11%)
  local copies, waits for them, and re-layouts  4.48 us (2%)
    ppermute x56, starting transfers between devices, swapped(): return lax.ppermute(value, axis, [(i, i ^ mask) for i in range(size)])  87.6 us
    ppermute x56, waiting for transfers between devices, swapped(): return lax.ppermute(value, axis, [(i, i ^ mask) for i in range(size)])  76.8 us
    dot_general x7, matrix products, project(): jnp.dot(stand, jnp.concatenate(pieces(wide), 1), preferred_element_type=j...  33.9 us
    ppermute x1, waiting for transfers between devices, passed_along(): return lax.ppermute(array, axis, pairs)  23.5 us
    another operation x24, other arithmetic, orthonormal(): factor = jnp.linalg.cholesky(gram)  9.76 us
    another operation x18, other arithmetic, orthonormal(): jax.scipy.linalg.solve_triangular(fac, rhs, lower=True)  8.03 us
    dot_general x6, matrix products, image_of(): lax.dot_general(stand, split, (((0,), (0,)), ((), ())), preferred_element...  6.76 us
    convert_element_type x1, other arithmetic, shards(): ((regionf - mean) / jnp.sqrt(var + 1e-05) * weight).astype(jnp.bfloat16)  6.38 us
  transfers between devices with their start and end apart: 57, of which 51 were waited for; matrix products, arithmetic and copies ran while one was open for 2% of the time, Pallas kernels for 0%

profile of v3, /device:TPU:32, one launch (start us, length us, event | category | flops | bytes accessed | tf_op | source)
XLA Modules:
  0.0 274.7 jit_solution(9762166792470346260)
XLA Ops:
  4.3 23.5 %collective-permute-done.7 = bf16[2048,512]{1,0:T(8,128)(2,1)} collective-permute-done((bf16[2048,512]{1,0:T(8,128)(2,1)S(1)}, bf16[2048,512]{1,0:T(8,128)(2,1)}, u32[]{:S(2)}, u32[]{:S(2)}) %collective-permute-start.7) | collective-permute-done | bytes 2097184 | tf_op jit(solution)/shard_map/ppermute | solution.py:14
  31.6 3.1 %collective-permute-start.10 = (f32[2,1536]{1,0:T(2,128)S(1)}, f32[2,1536]{1,0:T(2,128)S(1)}, u32[]{:S(2)}, u32[]{:S(2)}) collective-permute-start(f32[2,1536]{1,0:T(2,128)S(1)} %pad_maximum_fusion.2), channel_id=1, source_target_pairs={{0,12},{4,8},{8,4},{12,0},{16,28},{20,24},{24,20},{28,16},{32,44},... | collective-permute-start | bytes 36872 | tf_op jit(solution)/shard_map/ppermute | solution.py:19
  41.8 2.7 collective-permute-start.12
  44.8 2.1 collective-permute-done.12
  47.0 2.4 collective-permute-done.13
  49.4 3.1 %collective-permute-start.14 = (f32[2,1536]{1,0:T(2,128)S(1)}, f32[2,1536]{1,0:T(2,128)S(1)}, u32[]{:S(2)}, u32[]{:S(2)}) collective-permute-start(f32[2,1536]{1,0:T(2,128)S(1)} %add_add_fusion.2), channel_id=1, source_target_pairs={{0,64},{4,68},{8,72},{12,76},{16,80},{20,84},{24,88},{28,92},{32,9... | collective-permute-start | bytes 36872 | tf_op jit(solution)/shard_map/ppermute | solution.py:19
  54.8 6.4 %fusion.23 = bf16[2048,1536]{1,0:T(8,128)(2,1)} fusion(f32[1536]{0:T(1024)S(1)} %multiply_sqrt_fusion, f32[1536]{0:T(1024)S(1)} %get-tuple-element.26, f32[1536]{0:T(1024)S(1)} %get-tuple-element.25, bf16[2048,512]{1,0:T(8,128)(2,1)S(1)} %broadcast_select_fusion, bf16[2048,1024]{1,0:T(8,128)(2,1)} %param.6), kind=kLoop, calls=%fused_computation.57 | loop fusion | flops 25165824 | bytes 12601344 | tf_op jit(solution)/shard_map/convert_element_type | solution.py:93
  61.2 184.5 %while.10 = (s32[]{:T(128)}, f32[2,1024,8]{1,2,0:T(8,128)S(1)}, bf16[2048,1536]{1,0:T(8,128)(2,1)}, s32[]{:T(128)}) while((s32[]{:T(128)}, f32[2,1024,8]{1,2,0:T(8,128)S(1)}, bf16[2048,1536]{1,0:T(8,128)(2,1)}, s32[]{:T(128)}) %tuple.54), condition=%wide.region_5.6_spmd, body=%wide.region_2.5_spmd.sunk | while | flops 609027072 | bytes 43456232 | solution.py:107
  61.2 4.9 %convolution_bitcast_fusion.4 = f32[2048,48]{0,1:T(8,128)S(1)} fusion(bf16[2048,1536]{1,0:T(8,128)(2,1)} %get-tuple-element.114, bf16[1536,16]{0,1:T(8,128)(2,1)S(1)} %get-tuple-element.95, bf16[1536,16]{0,1:T(8,128)(2,1)S(1)} %get-tuple-element.96, bf16[1536,16]{0,1:T(8,128)(2,1)S(1)} %get-tuple-element.97), kind=kOutput, calls=%fused_computation.1.clone.1 | convolution fusion | flops 302432256 | bytes 6832128 | tf_op jit(solution)/shard_map/while/body/eval_jaxpr/dot_general | solution.py:98
  68.8 3.1 %collective-permute-start.1 = (f32[2,1024,8]{1,2,0:T(8,128)S(1)}, f32[2,1024,8]{1,2,0:T(8,128)S(1)}, u32[]{:S(2)}, u32[]{:S(2)}) collective-permute-start(f32[2,1024,8]{1,2,0:T(8,128)S(1)} %pad_maximum_fusion.4), channel_id=1, source_target_pairs={{0,12},{4,8},{8,4},{12,0},{16,28},{20,24},{24,20},{28,16},{32,44},... | collective-permute-start | bytes 196616 | tf_op jit(solution)/shard_map/while/body/eval_jaxpr/ppermute | solution.py:19
  74.3 2.2 collective-permute-done.2
  80.1 2.3 collective-permute-done.3
  83.8 3.1 %collective-permute-start.6 = (f32[2,1024,8]{1,2,0:T(8,128)S(1)}, f32[2,1024,8]{1,2,0:T(8,128)S(1)}, u32[]{:S(2)}, u32[]{:S(2)}) collective-permute-start(f32[2,1024,8]{1,2,0:T(8,128)S(1)} %add_add_fusion.9), channel_id=1, source_target_pairs={{0,64},{4,68},{8,72},{12,76},{16,80},{20,84},{24,88},{28,92},{32,9... | collective-permute-start | bytes 196616 | tf_op jit(solution)/shard_map/while/body/eval_jaxpr/ppermute | solution.py:19
  86.9 2.8 %collective-permute-done.6 = f32[2,1024,8]{1,2,0:T(8,128)S(1)} collective-permute-done((f32[2,1024,8]{1,2,0:T(8,128)S(1)}, f32[2,1024,8]{1,2,0:T(8,128)S(1)}, u32[]{:S(2)}, u32[]{:S(2)}) %collective-permute-start.6) | collective-permute-done | bytes 65568 | tf_op jit(solution)/shard_map/while/body/eval_jaxpr/ppermute | solution.py:19
  93.3 4.9 %convolution_bitcast_fusion.4 = f32[2048,48]{0,1:T(8,128)S(1)} fusion(bf16[2048,1536]{1,0:T(8,128)(2,1)} %get-tuple-element.114, bf16[1536,16]{0,1:T(8,128)(2,1)S(1)} %get-tuple-element.95, bf16[1536,16]{0,1:T(8,128)(2,1)S(1)} %get-tuple-element.96, bf16[1536,16]{0,1:T(8,128)(2,1)S(1)} %get-tuple-element.97), kind=kOutput, calls=%fused_computation.1.clone.1 | convolution fusion | flops 302432256 | bytes 6832128 | tf_op jit(solution)/shard_map/while/body/eval_jaxpr/dot_general | solution.py:98
  100.1 2.1 collective-permute-start.1
  103.0 2.3 collective-permute-done
  107.3 2.3 collective-permute-start.4
  110.1 2.3 collective-permute-done.3
  113.8 3.1 %collective-permute-start.6 = (f32[2,1024,8]{1,2,0:T(8,128)S(1)}, f32[2,1024,8]{1,2,0:T(8,128)S(1)}, u32[]{:S(2)}, u32[]{:S(2)}) collective-permute-start(f32[2,1024,8]{1,2,0:T(8,128)S(1)} %add_add_fusion.9), channel_id=1, source_target_pairs={{0,64},{4,68},{8,72},{12,76},{16,80},{20,84},{24,88},{28,92},{32,9... | collective-permute-start | bytes 196616 | tf_op jit(solution)/shard_map/while/body/eval_jaxpr/ppermute | solution.py:19
  116.9 2.8 %collective-permute-done.6 = f32[2,1024,8]{1,2,0:T(8,128)S(1)} collective-permute-done((f32[2,1024,8]{1,2,0:T(8,128)S(1)}, f32[2,1024,8]{1,2,0:T(8,128)S(1)}, u32[]{:S(2)}, u32[]{:S(2)}) %collective-permute-start.6) | collective-permute-done | bytes 65568 | tf_op jit(solution)/shard_map/while/body/eval_jaxpr/ppermute | solution.py:19
  123.3 4.9 %convolution_bitcast_fusion.4 = f32[2048,48]{0,1:T(8,128)S(1)} fusion(bf16[2048,1536]{1,0:T(8,128)(2,1)} %get-tuple-element.114, bf16[1536,16]{0,1:T(8,128)(2,1)S(1)} %get-tuple-element.95, bf16[1536,16]{0,1:T(8,128)(2,1)S(1)} %get-tuple-element.96, bf16[1536,16]{0,1:T(8,128)(2,1)S(1)} %get-tuple-element.97), kind=kOutput, calls=%fused_computation.1.clone.1 | convolution fusion | flops 302432256 | bytes 6832128 | tf_op jit(solution)/shard_map/while/body/eval_jaxpr/dot_general | solution.py:98
  129.5 2.1 collective-permute-start
  138.1 2.5 collective-permute-start.4
  141.2 2.3 collective-permute-done.3
  144.8 3.1 %collective-permute-start.6 = (f32[2,1024,8]{1,2,0:T(8,128)S(1)}, f32[2,1024,8]{1,2,0:T(8,128)S(1)}, u32[]{:S(2)}, u32[]{:S(2)}) collective-permute-start(f32[2,1024,8]{1,2,0:T(8,128)S(1)} %add_add_fusion.9), channel_id=1, source_target_pairs={{0,64},{4,68},{8,72},{12,76},{16,80},{20,84},{24,88},{28,92},{32,9... | collective-permute-start | bytes 196616 | tf_op jit(solution)/shard_map/while/body/eval_jaxpr/ppermute | solution.py:19
  147.9 2.8 %collective-permute-done.6 = f32[2,1024,8]{1,2,0:T(8,128)S(1)} collective-permute-done((f32[2,1024,8]{1,2,0:T(8,128)S(1)}, f32[2,1024,8]{1,2,0:T(8,128)S(1)}, u32[]{:S(2)}, u32[]{:S(2)}) %collective-permute-start.6) | collective-permute-done | bytes 65568 | tf_op jit(solution)/shard_map/while/body/eval_jaxpr/ppermute | solution.py:19
  154.3 4.9 %convolution_bitcast_fusion.4 = f32[2048,48]{0,1:T(8,128)S(1)} fusion(bf16[2048,1536]{1,0:T(8,128)(2,1)} %get-tuple-element.114, bf16[1536,16]{0,1:T(8,128)(2,1)S(1)} %get-tuple-element.95, bf16[1536,16]{0,1:T(8,128)(2,1)S(1)} %get-tuple-element.96, bf16[1536,16]{0,1:T(8,128)(2,1)S(1)} %get-tuple-element.97), kind=kOutput, calls=%fused_computation.1.clone.1 | convolution fusion | flops 302432256 | bytes 6832128 | tf_op jit(solution)/shard_map/while/body/eval_jaxpr/dot_general | solution.py:98
  164.0 2.3 collective-permute-done
  171.1 2.3 collective-permute-done.3
  175.2 3.0 %collective-permute-start.6 = (f32[2,1024,8]{1,2,0:T(8,128)S(1)}, f32[2,1024,8]{1,2,0:T(8,128)S(1)}, u32[]{:S(2)}, u32[]{:S(2)}) collective-permute-start(f32[2,1024,8]{1,2,0:T(8,128)S(1)} %add_add_fusion.9), channel_id=1, source_target_pairs={{0,64},{4,68},{8,72},{12,76},{16,80},{20,84},{24,88},{28,92},{32,9... | collective-permute-start | bytes 196616 | tf_op jit(solution)/shard_map/while/body/eval_jaxpr/ppermute | solution.py:19
  178.2 2.8 %collective-permute-done.6 = f32[2,1024,8]{1,2,0:T(8,128)S(1)} collective-permute-done((f32[2,1024,8]{1,2,0:T(8,128)S(1)}, f32[2,1024,8]{1,2,0:T(8,128)S(1)}, u32[]{:S(2)}, u32[]{:S(2)}) %collective-permute-start.6) | collective-permute-done | bytes 65568 | tf_op jit(solution)/shard_map/while/body/eval_jaxpr/ppermute | solution.py:19
  184.6 4.9 %convolution_bitcast_fusion.4 = f32[2048,48]{0,1:T(8,128)S(1)} fusion(bf16[2048,1536]{1,0:T(8,128)(2,1)} %get-tuple-element.114, bf16[1536,16]{0,1:T(8,128)(2,1)S(1)} %get-tuple-element.95, bf16[1536,16]{0,1:T(8,128)(2,1)S(1)} %get-tuple-element.96, bf16[1536,16]{0,1:T(8,128)(2,1)S(1)} %get-tuple-element.97), kind=kOutput, calls=%fused_computation.1.clone.1 | convolution fusion | flops 302432256 | bytes 6832128 | tf_op jit(solution)/shard_map/while/body/eval_jaxpr/dot_general | solution.py:98
  194.4 2.3 collective-permute-done
  202.2 2.3 collective-permute-done.3
  205.9 3.1 %collective-permute-start.6 = (f32[2,1024,8]{1,2,0:T(8,128)S(1)}, f32[2,1024,8]{1,2,0:T(8,128)S(1)}, u32[]{:S(2)}, u32[]{:S(2)}) collective-permute-start(f32[2,1024,8]{1,2,0:T(8,128)S(1)} %add_add_fusion.9), channel_id=1, source_target_pairs={{0,64},{4,68},{8,72},{12,76},{16,80},{20,84},{24,88},{28,92},{32,9... | collective-permute-start | bytes 196616 | tf_op jit(solution)/shard_map/while/body/eval_jaxpr/ppermute | solution.py:19
  209.0 2.8 %collective-permute-done.6 = f32[2,1024,8]{1,2,0:T(8,128)S(1)} collective-permute-done((f32[2,1024,8]{1,2,0:T(8,128)S(1)}, f32[2,1024,8]{1,2,0:T(8,128)S(1)}, u32[]{:S(2)}, u32[]{:S(2)}) %collective-permute-start.6) | collective-permute-done | bytes 65568 | tf_op jit(solution)/shard_map/while/body/eval_jaxpr/ppermute | solution.py:19
  215.4 4.9 %convolution_bitcast_fusion.4 = f32[2048,48]{0,1:T(8,128)S(1)} fusion(bf16[2048,1536]{1,0:T(8,128)(2,1)} %get-tuple-element.114, bf16[1536,16]{0,1:T(8,128)(2,1)S(1)} %get-tuple-element.95, bf16[1536,16]{0,1:T(8,128)(2,1)S(1)} %get-tuple-element.96, bf16[1536,16]{0,1:T(8,128)(2,1)S(1)} %get-tuple-element.97), kind=kOutput, calls=%fused_computation.1.clone.1 | convolution fusion | flops 302432256 | bytes 6832128 | tf_op jit(solution)/shard_map/while/body/eval_jaxpr/dot_general | solution.py:98
  225.1 2.3 collective-permute-done
  232.1 2.3 collective-permute-done.3
  236.2 3.0 %collective-permute-start.6 = (f32[2,1024,8]{1,2,0:T(8,128)S(1)}, f32[2,1024,8]{1,2,0:T(8,128)S(1)}, u32[]{:S(2)}, u32[]{:S(2)}) collective-permute-start(f32[2,1024,8]{1,2,0:T(8,128)S(1)} %add_add_fusion.9), channel_id=1, source_target_pairs={{0,64},{4,68},{8,72},{12,76},{16,80},{20,84},{24,88},{28,92},{32,9... | collective-permute-start | bytes 196616 | tf_op jit(solution)/shard_map/while/body/eval_jaxpr/ppermute | solution.py:19
  239.3 2.8 %collective-permute-done.6 = f32[2,1024,8]{1,2,0:T(8,128)S(1)} collective-permute-done((f32[2,1024,8]{1,2,0:T(8,128)S(1)}, f32[2,1024,8]{1,2,0:T(8,128)S(1)}, u32[]{:S(2)}, u32[]{:S(2)}) %collective-permute-start.6) | collective-permute-done | bytes 65568 | tf_op jit(solution)/shard_map/while/body/eval_jaxpr/ppermute | solution.py:19
  245.7 4.7 %fusion.24 = f32[2048,48]{0,1:T(8,128)S(1)} fusion(bf16[2048,1536]{1,0:T(8,128)(2,1)} %get-tuple-element.116, bf16[1536,16]{0,1:T(8,128)(2,1)S(1)} %get-tuple-element.60, bf16[1536,16]{0,1:T(8,128)(2,1)S(1)} %get-tuple-element.59, bf16[1536,16]{0,1:T(8,128)(2,1)S(1)} %get-tuple-element.58), kind=kOutput, calls=%fused_computation.62 | convolution fusion | flops 302432256 | bytes 6832128 | tf_op jit(solution)/shard_map/dot_general | solution.py:98
  251.4 2.1 collective-permute-start.16
  258.4 3.0 %multiply_reduce_fusion.1 = (f32[2048]{0:T(1024)S(1)}, f32[2048]{0:T(1024)S(1)}) fusion(bf16[2048,1536]{1,0:T(8,128)(2,1)S(1)} %bitcast.80, f32[2048,1024]{1,0:T(8,128)S(1)} %fusion.38, bf16[2048,48]{0,1:T(8,128)(2,1)S(1)} %constant_dynamic-update-slice_fusion, bf16[1024,48]{0,1:T(8,128)(2,1)S(1)} %get-tuple-element.49), kind=kOutput, calls=%fused_computation.59 | convolution fusion | flops 218099712 | bytes 17088512 | tf_op jit(solution)/shard_map/dot_general | solution.py:67
  261.8 2.5 collective-permute-start.19
  266.8 2.2 collective-permute-done.20
  269.0 3.0 %collective-permute-start.21 = (f32[16]{0:T(128)S(1)}, f32[16]{0:T(128)S(1)}, u32[]{:S(2)}, u32[]{:S(2)}) collective-permute-start(f32[16]{0:T(128)S(1)} %add_add_fusion.4), channel_id=1, source_target_pairs={{0,64},{4,68},{8,72},{12,76},{16,80},{20,84},{24,88},{28,92},{32,9... | collective-permute-start | bytes 200 | tf_op jit(solution)/shard_map/ppermute | solution.py:19
  (263 shorter events, 110.7 us)
Async XLA Ops:
  2.4 25.5 %collective-permute-start.7 = (bf16[2048,512]{1,0:T(8,128)(2,1)S(1)}, bf16[2048,512]{1,0:T(8,128)(2,1)}, u32[]{:S(2)}, u32[]{:S(2)}) collective-permute-start(bf16[2048,512]{1,0:T(8,128)(2,1)S(1)} %slice.80), channel_id=1, source_target_pairs={{1,0},{2,1},{3,2},{5,4},{6,5},{7,6},{9,8},{10,9},{11,10},{13,12},{... | collective-permute-start | bytes 6291464 | tf_op jit(solution)/shard_map/ppermute | solution.py:14
  31.6 5.0 %collective-permute-start.10 = (f32[2,1536]{1,0:T(2,128)S(1)}, f32[2,1536]{1,0:T(2,128)S(1)}, u32[]{:S(2)}, u32[]{:S(2)}) collective-permute-start(f32[2,1536]{1,0:T(2,128)S(1)} %pad_maximum_fusion.2), channel_id=1, source_target_pairs={{0,12},{4,8},{8,4},{12,0},{16,28},{20,24},{24,20},{28,16},{32,44},... | collective-permute-start | bytes 36872 | tf_op jit(solution)/shard_map/ppermute | solution.py:19
  34.8 5.2 %collective-permute-start.9 = (f32[2,1536]{1,0:T(2,128)S(1)}, f32[2,1536]{1,0:T(2,128)S(1)}, u32[]{:S(2)}, u32[]{:S(2)}) collective-permute-start(f32[2,1536]{1,0:T(2,128)S(1)} %pad_maximum_fusion.2), channel_id=1, source_target_pairs={{0,8},{4,12},{8,0},{12,4},{16,24},{20,28},{24,16},{28,20},{32,40},... | collective-permute-start | bytes 36872 | tf_op jit(solution)/shard_map/ppermute | solution.py:19
  40.1 4.8 %collective-permute-start.11 = (f32[2,1536]{1,0:T(2,128)S(1)}, f32[2,1536]{1,0:T(2,128)S(1)}, u32[]{:S(2)}, u32[]{:S(2)}) collective-permute-start(f32[2,1536]{1,0:T(2,128)S(1)} %add_add_fusion.3), channel_id=1, source_target_pairs={{0,16},{4,20},{8,24},{12,28},{16,0},{20,4},{24,8},{28,12},{32,48},... | collective-permute-start | bytes 36872 | tf_op jit(solution)/shard_map/ppermute | solution.py:19
  41.8 5.2 %collective-permute-start.12 = (f32[2,1536]{1,0:T(2,128)S(1)}, f32[2,1536]{1,0:T(2,128)S(1)}, u32[]{:S(2)}, u32[]{:S(2)}) collective-permute-start(f32[2,1536]{1,0:T(2,128)S(1)} %add_add_fusion.3), channel_id=1, source_target_pairs={{0,32},{4,36},{8,40},{12,44},{16,48},{20,52},{24,56},{28,60},{32,0... | collective-permute-start | bytes 36872 | tf_op jit(solution)/shard_map/ppermute | solution.py:19
  44.5 4.9 %collective-permute-start.13 = (f32[2,1536]{1,0:T(2,128)S(1)}, f32[2,1536]{1,0:T(2,128)S(1)}, u32[]{:S(2)}, u32[]{:S(2)}) collective-permute-start(f32[2,1536]{1,0:T(2,128)S(1)} %add_add_fusion.3), channel_id=1, source_target_pairs={{0,48},{4,52},{8,56},{12,60},{16,32},{20,36},{24,40},{28,44},{32,1... | collective-permute-start | bytes 36872 | tf_op jit(solution)/shard_map/ppermute | solution.py:19
  49.4 5.3 %collective-permute-start.14 = (f32[2,1536]{1,0:T(2,128)S(1)}, f32[2,1536]{1,0:T(2,128)S(1)}, u32[]{:S(2)}, u32[]{:S(2)}) collective-permute-start(f32[2,1536]{1,0:T(2,128)S(1)} %add_add_fusion.2), channel_id=1, source_target_pairs={{0,64},{4,68},{8,72},{12,76},{16,80},{20,84},{24,88},{28,92},{32,9... | collective-permute-start | bytes 36872 | tf_op jit(solution)/shard_map/ppermute | solution.py:19
  67.3 5.8 %collective-permute-start = (f32[2,1024,8]{1,2,0:T(8,128)S(1)}, f32[2,1024,8]{1,2,0:T(8,128)S(1)}, u32[]{:S(2)}, u32[]{:S(2)}) collective-permute-start(f32[2,1024,8]{1,2,0:T(8,128)S(1)} %pad_maximum_fusion.4), channel_id=1, source_target_pairs={{0,8},{4,12},{8,0},{12,4},{16,24},{20,28},{24,16},{28,20},{32,40},... | collective-permute-start | bytes 196616 | tf_op jit(solution)/shard_map/while/body/eval_jaxpr/ppermute | solution.py:19
  68.8 5.5 %collective-permute-start.1 = (f32[2,1024,8]{1,2,0:T(8,128)S(1)}, f32[2,1024,8]{1,2,0:T(8,128)S(1)}, u32[]{:S(2)}, u32[]{:S(2)}) collective-permute-start(f32[2,1024,8]{1,2,0:T(8,128)S(1)} %pad_maximum_fusion.4), channel_id=1, source_target_pairs={{0,12},{4,8},{8,4},{12,0},{16,28},{20,24},{24,20},{28,16},{32,44},... | collective-permute-start | bytes 196616 | tf_op jit(solution)/shard_map/while/body/eval_jaxpr/ppermute | solution.py:19
  72.0 4.5 %collective-permute-start.2 = (f32[2,1024,8]{1,2,0:T(8,128)S(1)}, f32[2,1024,8]{1,2,0:T(8,128)S(1)}, u32[]{:S(2)}, u32[]{:S(2)}) collective-permute-start(f32[2,1024,8]{1,2,0:T(8,128)S(1)} %pad_maximum_fusion.4), channel_id=1, source_target_pairs={{0,4},{4,0},{8,12},{12,8},{16,20},{20,16},{24,28},{28,24},{32,36},... | collective-permute-start | bytes 196616 | tf_op jit(solution)/shard_map/while/body/eval_jaxpr/ppermute | solution.py:19
  76.6 5.9 %collective-permute-start.3 = (f32[2,1024,8]{1,2,0:T(8,128)S(1)}, f32[2,1024,8]{1,2,0:T(8,128)S(1)}, u32[]{:S(2)}, u32[]{:S(2)}) collective-permute-start(f32[2,1024,8]{1,2,0:T(8,128)S(1)} %add_add_fusion.8), channel_id=1, source_target_pairs={{0,32},{4,36},{8,40},{12,44},{16,48},{20,52},{24,56},{28,60},{32,0... | collective-permute-start | bytes 196616 | tf_op jit(solution)/shard_map/while/body/eval_jaxpr/ppermute | solution.py:19
  76.7 7.1 %collective-permute-start.4 = (f32[2,1024,8]{1,2,0:T(8,128)S(1)}, f32[2,1024,8]{1,2,0:T(8,128)S(1)}, u32[]{:S(2)}, u32[]{:S(2)}) collective-permute-start(f32[2,1024,8]{1,2,0:T(8,128)S(1)} %add_add_fusion.8), channel_id=1, source_target_pairs={{0,48},{4,52},{8,56},{12,60},{16,32},{20,36},{24,40},{28,44},{32,1... | collective-permute-start | bytes 196616 | tf_op jit(solution)/shard_map/while/body/eval_jaxpr/ppermute | solution.py:19
  78.6 5.2 %collective-permute-start.5 = (f32[2,1024,8]{1,2,0:T(8,128)S(1)}, f32[2,1024,8]{1,2,0:T(8,128)S(1)}, u32[]{:S(2)}, u32[]{:S(2)}) collective-permute-start(f32[2,1024,8]{1,2,0:T(8,128)S(1)} %add_add_fusion.8), channel_id=1, source_target_pairs={{0,16},{4,20},{8,24},{12,28},{16,0},{20,4},{24,8},{28,12},{32,48},... | collective-permute-start | bytes 196616 | tf_op jit(solution)/shard_map/while/body/eval_jaxpr/ppermute | solution.py:19
  83.8 5.8 %collective-permute-start.6 = (f32[2,1024,8]{1,2,0:T(8,128)S(1)}, f32[2,1024,8]{1,2,0:T(8,128)S(1)}, u32[]{:S(2)}, u32[]{:S(2)}) collective-permute-start(f32[2,1024,8]{1,2,0:T(8,128)S(1)} %add_add_fusion.9), channel_id=1, source_target_pairs={{0,64},{4,68},{8,72},{12,76},{16,80},{20,84},{24,88},{28,92},{32,9... | collective-permute-start | bytes 196616 | tf_op jit(solution)/shard_map/while/body/eval_jaxpr/ppermute | solution.py:19
  99.4 5.9 %collective-permute-start = (f32[2,1024,8]{1,2,0:T(8,128)S(1)}, f32[2,1024,8]{1,2,0:T(8,128)S(1)}, u32[]{:S(2)}, u32[]{:S(2)}) collective-permute-start(f32[2,1024,8]{1,2,0:T(8,128)S(1)} %pad_maximum_fusion.4), channel_id=1, source_target_pairs={{0,8},{4,12},{8,0},{12,4},{16,24},{20,28},{24,16},{28,20},{32,40},... | collective-permute-start | bytes 196616 | tf_op jit(solution)/shard_map/while/body/eval_jaxpr/ppermute | solution.py:19
  100.1 5.9 %collective-permute-start.1 = (f32[2,1024,8]{1,2,0:T(8,128)S(1)}, f32[2,1024,8]{1,2,0:T(8,128)S(1)}, u32[]{:S(2)}, u32[]{:S(2)}) collective-permute-start(f32[2,1024,8]{1,2,0:T(8,128)S(1)} %pad_maximum_fusion.4), channel_id=1, source_target_pairs={{0,12},{4,8},{8,4},{12,0},{16,28},{20,24},{24,20},{28,16},{32,44},... | collective-permute-start | bytes 196616 | tf_op jit(solution)/shard_map/while/body/eval_jaxpr/ppermute | solution.py:19
  102.2 4.3 %collective-permute-start.2 = (f32[2,1024,8]{1,2,0:T(8,128)S(1)}, f32[2,1024,8]{1,2,0:T(8,128)S(1)}, u32[]{:S(2)}, u32[]{:S(2)}) collective-permute-start(f32[2,1024,8]{1,2,0:T(8,128)S(1)} %pad_maximum_fusion.4), channel_id=1, source_target_pairs={{0,4},{4,0},{8,12},{12,8},{16,20},{20,16},{24,28},{28,24},{32,36},... | collective-permute-start | bytes 196616 | tf_op jit(solution)/shard_map/while/body/eval_jaxpr/ppermute | solution.py:19
  106.5 5.9 %collective-permute-start.3 = (f32[2,1024,8]{1,2,0:T(8,128)S(1)}, f32[2,1024,8]{1,2,0:T(8,128)S(1)}, u32[]{:S(2)}, u32[]{:S(2)}) collective-permute-start(f32[2,1024,8]{1,2,0:T(8,128)S(1)} %add_add_fusion.8), channel_id=1, source_target_pairs={{0,32},{4,36},{8,40},{12,44},{16,48},{20,52},{24,56},{28,60},{32,0... | collective-permute-start | bytes 196616 | tf_op jit(solution)/shard_map/while/body/eval_jaxpr/ppermute | solution.py:19
  107.3 5.7 %collective-permute-start.4 = (f32[2,1024,8]{1,2,0:T(8,128)S(1)}, f32[2,1024,8]{1,2,0:T(8,128)S(1)}, u32[]{:S(2)}, u32[]{:S(2)}) collective-permute-start(f32[2,1024,8]{1,2,0:T(8,128)S(1)} %add_add_fusion.8), channel_id=1, source_target_pairs={{0,48},{4,52},{8,56},{12,60},{16,32},{20,36},{24,40},{28,44},{32,1... | collective-permute-start | bytes 196616 | tf_op jit(solution)/shard_map/while/body/eval_jaxpr/ppermute | solution.py:19
  113.8 5.8 %collective-permute-start.6 = (f32[2,1024,8]{1,2,0:T(8,128)S(1)}, f32[2,1024,8]{1,2,0:T(8,128)S(1)}, u32[]{:S(2)}, u32[]{:S(2)}) collective-permute-start(f32[2,1024,8]{1,2,0:T(8,128)S(1)} %add_add_fusion.9), channel_id=1, source_target_pairs={{0,64},{4,68},{8,72},{12,76},{16,80},{20,84},{24,88},{28,92},{32,9... | collective-permute-start | bytes 196616 | tf_op jit(solution)/shard_map/while/body/eval_jaxpr/ppermute | solution.py:19
  129.5 5.8 %collective-permute-start = (f32[2,1024,8]{1,2,0:T(8,128)S(1)}, f32[2,1024,8]{1,2,0:T(8,128)S(1)}, u32[]{:S(2)}, u32[]{:S(2)}) collective-permute-start(f32[2,1024,8]{1,2,0:T(8,128)S(1)} %pad_maximum_fusion.4), channel_id=1, source_target_pairs={{0,8},{4,12},{8,0},{12,4},{16,24},{20,28},{24,16},{28,20},{32,40},... | collective-permute-start | bytes 196616 | tf_op jit(solution)/shard_map/while/body/eval_jaxpr/ppermute | solution.py:19
  131.6 5.5 %collective-permute-start.1 = (f32[2,1024,8]{1,2,0:T(8,128)S(1)}, f32[2,1024,8]{1,2,0:T(8,128)S(1)}, u32[]{:S(2)}, u32[]{:S(2)}) collective-permute-start(f32[2,1024,8]{1,2,0:T(8,128)S(1)} %pad_maximum_fusion.4), channel_id=1, source_target_pairs={{0,12},{4,8},{8,4},{12,0},{16,28},{20,24},{24,20},{28,16},{32,44},... | collective-permute-start | bytes 196616 | tf_op jit(solution)/shard_map/while/body/eval_jaxpr/ppermute | solution.py:19
  137.6 5.9 %collective-permute-start.3 = (f32[2,1024,8]{1,2,0:T(8,128)S(1)}, f32[2,1024,8]{1,2,0:T(8,128)S(1)}, u32[]{:S(2)}, u32[]{:S(2)}) collective-permute-start(f32[2,1024,8]{1,2,0:T(8,128)S(1)} %add_add_fusion.8), channel_id=1, source_target_pairs={{0,32},{4,36},{8,40},{12,44},{16,48},{20,52},{24,56},{28,60},{32,0... | collective-permute-start | bytes 196616 | tf_op jit(solution)/shard_map/while/body/eval_jaxpr/ppermute | solution.py:19
  138.1 6.1 %collective-permute-start.4 = (f32[2,1024,8]{1,2,0:T(8,128)S(1)}, f32[2,1024,8]{1,2,0:T(8,128)S(1)}, u32[]{:S(2)}, u32[]{:S(2)}) collective-permute-start(f32[2,1024,8]{1,2,0:T(8,128)S(1)} %add_add_fusion.8), channel_id=1, source_target_pairs={{0,48},{4,52},{8,56},{12,60},{16,32},{20,36},{24,40},{28,44},{32,1... | collective-permute-start | bytes 196616 | tf_op jit(solution)/shard_map/while/body/eval_jaxpr/ppermute | solution.py:19
  144.8 5.8 %collective-permute-start.6 = (f32[2,1024,8]{1,2,0:T(8,128)S(1)}, f32[2,1024,8]{1,2,0:T(8,128)S(1)}, u32[]{:S(2)}, u32[]{:S(2)}) collective-permute-start(f32[2,1024,8]{1,2,0:T(8,128)S(1)} %add_add_fusion.9), channel_id=1, source_target_pairs={{0,64},{4,68},{8,72},{12,76},{16,80},{20,84},{24,88},{28,92},{32,9... | collective-permute-start | bytes 196616 | tf_op jit(solution)/shard_map/while/body/eval_jaxpr/ppermute | solution.py:19
  160.5 5.9 %collective-permute-start = (f32[2,1024,8]{1,2,0:T(8,128)S(1)}, f32[2,1024,8]{1,2,0:T(8,128)S(1)}, u32[]{:S(2)}, u32[]{:S(2)}) collective-permute-start(f32[2,1024,8]{1,2,0:T(8,128)S(1)} %pad_maximum_fusion.4), channel_id=1, source_target_pairs={{0,8},{4,12},{8,0},{12,4},{16,24},{20,28},{24,16},{28,20},{32,40},... | collective-permute-start | bytes 196616 | tf_op jit(solution)/shard_map/while/body/eval_jaxpr/ppermute | solution.py:19
  161.5 5.5 %collective-permute-start.1 = (f32[2,1024,8]{1,2,0:T(8,128)S(1)}, f32[2,1024,8]{1,2,0:T(8,128)S(1)}, u32[]{:S(2)}, u32[]{:S(2)}) collective-permute-start(f32[2,1024,8]{1,2,0:T(8,128)S(1)} %pad_maximum_fusion.4), channel_id=1, source_target_pairs={{0,12},{4,8},{8,4},{12,0},{16,28},{20,24},{24,20},{28,16},{32,44},... | collective-permute-start | bytes 196616 | tf_op jit(solution)/shard_map/while/body/eval_jaxpr/ppermute | solution.py:19
  167.5 5.8 %collective-permute-start.3 = (f32[2,1024,8]{1,2,0:T(8,128)S(1)}, f32[2,1024,8]{1,2,0:T(8,128)S(1)}, u32[]{:S(2)}, u32[]{:S(2)}) collective-permute-start(f32[2,1024,8]{1,2,0:T(8,128)S(1)} %add_add_fusion.8), channel_id=1, source_target_pairs={{0,32},{4,36},{8,40},{12,44},{16,48},{20,52},{24,56},{28,60},{32,0... | collective-permute-start | bytes 196616 | tf_op jit(solution)/shard_map/while/body/eval_jaxpr/ppermute | solution.py:19
  168.8 5.5 %collective-permute-start.4 = (f32[2,1024,8]{1,2,0:T(8,128)S(1)}, f32[2,1024,8]{1,2,0:T(8,128)S(1)}, u32[]{:S(2)}, u32[]{:S(2)}) collective-permute-start(f32[2,1024,8]{1,2,0:T(8,128)S(1)} %add_add_fusion.8), channel_id=1, source_target_pairs={{0,48},{4,52},{8,56},{12,60},{16,32},{20,36},{24,40},{28,44},{32,1... | collective-permute-start | bytes 196616 | tf_op jit(solution)/shard_map/while/body/eval_jaxpr/ppermute | solution.py:19
  170.9 4.3 %collective-permute-start.5 = (f32[2,1024,8]{1,2,0:T(8,128)S(1)}, f32[2,1024,8]{1,2,0:T(8,128)S(1)}, u32[]{:S(2)}, u32[]{:S(2)}) collective-permute-start(f32[2,1024,8]{1,2,0:T(8,128)S(1)} %add_add_fusion.8), channel_id=1, source_target_pairs={{0,16},{4,20},{8,24},{12,28},{16,0},{20,4},{24,8},{28,12},{32,48},... | collective-permute-start | bytes 196616 | tf_op jit(solution)/shard_map/while/body/eval_jaxpr/ppermute | solution.py:19
  175.2 5.8 %collective-permute-start.6 = (f32[2,1024,8]{1,2,0:T(8,128)S(1)}, f32[2,1024,8]{1,2,0:T(8,128)S(1)}, u32[]{:S(2)}, u32[]{:S(2)}) collective-permute-start(f32[2,1024,8]{1,2,0:T(8,128)S(1)} %add_add_fusion.9), channel_id=1, source_target_pairs={{0,64},{4,68},{8,72},{12,76},{16,80},{20,84},{24,88},{28,92},{32,9... | collective-permute-start | bytes 196616 | tf_op jit(solution)/shard_map/while/body/eval_jaxpr/ppermute | solution.py:19
  190.8 5.8 %collective-permute-start = (f32[2,1024,8]{1,2,0:T(8,128)S(1)}, f32[2,1024,8]{1,2,0:T(8,128)S(1)}, u32[]{:S(2)}, u32[]{:S(2)}) collective-permute-start(f32[2,1024,8]{1,2,0:T(8,128)S(1)} %pad_maximum_fusion.4), channel_id=1, source_target_pairs={{0,8},{4,12},{8,0},{12,4},{16,24},{20,28},{24,16},{28,20},{32,40},... | collective-permute-start | bytes 196616 | tf_op jit(solution)/shard_map/while/body/eval_jaxpr/ppermute | solution.py:19
  192.6 5.5 %collective-permute-start.1 = (f32[2,1024,8]{1,2,0:T(8,128)S(1)}, f32[2,1024,8]{1,2,0:T(8,128)S(1)}, u32[]{:S(2)}, u32[]{:S(2)}) collective-permute-start(f32[2,1024,8]{1,2,0:T(8,128)S(1)} %pad_maximum_fusion.4), channel_id=1, source_target_pairs={{0,12},{4,8},{8,4},{12,0},{16,28},{20,24},{24,20},{28,16},{32,44},... | collective-permute-start | bytes 196616 | tf_op jit(solution)/shard_map/while/body/eval_jaxpr/ppermute | solution.py:19
  198.6 5.9 %collective-permute-start.3 = (f32[2,1024,8]{1,2,0:T(8,128)S(1)}, f32[2,1024,8]{1,2,0:T(8,128)S(1)}, u32[]{:S(2)}, u32[]{:S(2)}) collective-permute-start(f32[2,1024,8]{1,2,0:T(8,128)S(1)} %add_add_fusion.8), channel_id=1, source_target_pairs={{0,32},{4,36},{8,40},{12,44},{16,48},{20,52},{24,56},{28,60},{32,0... | collective-permute-start | bytes 196616 | tf_op jit(solution)/shard_map/while/body/eval_jaxpr/ppermute | solution.py:19
  199.6 5.6 %collective-permute-start.4 = (f32[2,1024,8]{1,2,0:T(8,128)S(1)}, f32[2,1024,8]{1,2,0:T(8,128)S(1)}, u32[]{:S(2)}, u32[]{:S(2)}) collective-permute-start(f32[2,1024,8]{1,2,0:T(8,128)S(1)} %add_add_fusion.8), channel_id=1, source_target_pairs={{0,48},{4,52},{8,56},{12,60},{16,32},{20,36},{24,40},{28,44},{32,1... | collective-permute-start | bytes 196616 | tf_op jit(solution)/shard_map/while/body/eval_jaxpr/ppermute | solution.py:19
  205.9 5.8 %collective-permute-start.6 = (f32[2,1024,8]{1,2,0:T(8,128)S(1)}, f32[2,1024,8]{1,2,0:T(8,128)S(1)}, u32[]{:S(2)}, u32[]{:S(2)}) collective-permute-start(f32[2,1024,8]{1,2,0:T(8,128)S(1)} %add_add_fusion.9), channel_id=1, source_target_pairs={{0,64},{4,68},{8,72},{12,76},{16,80},{20,84},{24,88},{28,92},{32,9... | collective-permute-start | bytes 196616 | tf_op jit(solution)/shard_map/while/body/eval_jaxpr/ppermute | solution.py:19
  221.5 5.9 %collective-permute-start = (f32[2,1024,8]{1,2,0:T(8,128)S(1)}, f32[2,1024,8]{1,2,0:T(8,128)S(1)}, u32[]{:S(2)}, u32[]{:S(2)}) collective-permute-start(f32[2,1024,8]{1,2,0:T(8,128)S(1)} %pad_maximum_fusion.4), channel_id=1, source_target_pairs={{0,8},{4,12},{8,0},{12,4},{16,24},{20,28},{24,16},{28,20},{32,40},... | collective-permute-start | bytes 196616 | tf_op jit(solution)/shard_map/while/body/eval_jaxpr/ppermute | solution.py:19
  222.5 5.5 %collective-permute-start.1 = (f32[2,1024,8]{1,2,0:T(8,128)S(1)}, f32[2,1024,8]{1,2,0:T(8,128)S(1)}, u32[]{:S(2)}, u32[]{:S(2)}) collective-permute-start(f32[2,1024,8]{1,2,0:T(8,128)S(1)} %pad_maximum_fusion.4), channel_id=1, source_target_pairs={{0,12},{4,8},{8,4},{12,0},{16,28},{20,24},{24,20},{28,16},{32,44},... | collective-permute-start | bytes 196616 | tf_op jit(solution)/shard_map/while/body/eval_jaxpr/ppermute | solution.py:19
  228.6 5.8 %collective-permute-start.3 = (f32[2,1024,8]{1,2,0:T(8,128)S(1)}, f32[2,1024,8]{1,2,0:T(8,128)S(1)}, u32[]{:S(2)}, u32[]{:S(2)}) collective-permute-start(f32[2,1024,8]{1,2,0:T(8,128)S(1)} %add_add_fusion.8), channel_id=1, source_target_pairs={{0,32},{4,36},{8,40},{12,44},{16,48},{20,52},{24,56},{28,60},{32,0... | collective-permute-start | bytes 196616 | tf_op jit(solution)/shard_map/while/body/eval_jaxpr/ppermute | solution.py:19
  229.9 5.5 %collective-permute-start.4 = (f32[2,1024,8]{1,2,0:T(8,128)S(1)}, f32[2,1024,8]{1,2,0:T(8,128)S(1)}, u32[]{:S(2)}, u32[]{:S(2)}) collective-permute-start(f32[2,1024,8]{1,2,0:T(8,128)S(1)} %add_add_fusion.8), channel_id=1, source_target_pairs={{0,48},{4,52},{8,56},{12,60},{16,32},{20,36},{24,40},{28,44},{32,1... | collective-permute-start | bytes 196616 | tf_op jit(solution)/shard_map/while/body/eval_jaxpr/ppermute | solution.py:19
  236.2 5.8 %collective-permute-start.6 = (f32[2,1024,8]{1,2,0:T(8,128)S(1)}, f32[2,1024,8]{1,2,0:T(8,128)S(1)}, u32[]{:S(2)}, u32[]{:S(2)}) collective-permute-start(f32[2,1024,8]{1,2,0:T(8,128)S(1)} %add_add_fusion.9), channel_id=1, source_target_pairs={{0,64},{4,68},{8,72},{12,76},{16,80},{20,84},{24,88},{28,92},{32,9... | collective-permute-start | bytes 196616 | tf_op jit(solution)/shard_map/while/body/eval_jaxpr/ppermute | solution.py:19
  250.6 10.9 %collective-permute-start.15 = (f32[16]{0:T(128)S(1)}, f32[16]{0:T(128)S(1)}, u32[]{:S(2)}, u32[]{:S(2)}) collective-permute-start(f32[16]{0:T(128)S(1)} %get-tuple-element.35), channel_id=1, source_target_pairs={{0,4},{4,0},{8,12},{12,8},{16,20},{20,16},{24,28},{28,24},{32,36},... | collective-permute-start | bytes 200 | tf_op jit(solution)/shard_map/ppermute | solution.py:19
  251.4 10.0 %collective-permute-start.16 = (f32[16]{0:T(128)S(1)}, f32[16]{0:T(128)S(1)}, u32[]{:S(2)}, u32[]{:S(2)}) collective-permute-start(f32[16]{0:T(128)S(1)} %get-tuple-element.35), channel_id=1, source_target_pairs={{0,8},{4,12},{8,0},{12,4},{16,24},{20,28},{24,16},{28,20},{32,40},... | collective-permute-start | bytes 200 | tf_op jit(solution)/shard_map/ppermute | solution.py:19
  253.6 7.9 %collective-permute-start.17 = (f32[16]{0:T(128)S(1)}, f32[16]{0:T(128)S(1)}, u32[]{:S(2)}, u32[]{:S(2)}) collective-permute-start(f32[16]{0:T(128)S(1)} %get-tuple-element.35), channel_id=1, source_target_pairs={{0,12},{4,8},{8,4},{12,0},{16,28},{20,24},{24,20},{28,16},{32,44},... | collective-permute-start | bytes 200 | tf_op jit(solution)/shard_map/ppermute | solution.py:19
  261.5 4.8 %collective-permute-start.18 = (f32[16]{0:T(128)S(1)}, f32[16]{0:T(128)S(1)}, u32[]{:S(2)}, u32[]{:S(2)}) collective-permute-start(f32[16]{0:T(128)S(1)} %add_add_fusion.5), channel_id=1, source_target_pairs={{0,16},{4,20},{8,24},{12,28},{16,0},{20,4},{24,8},{28,12},{32,48},... | collective-permute-start | bytes 200 | tf_op jit(solution)/shard_map/ppermute | solution.py:19
  261.8 5.1 %collective-permute-start.19 = (f32[16]{0:T(128)S(1)}, f32[16]{0:T(128)S(1)}, u32[]{:S(2)}, u32[]{:S(2)}) collective-permute-start(f32[16]{0:T(128)S(1)} %add_add_fusion.5), channel_id=1, source_target_pairs={{0,32},{4,36},{8,40},{12,44},{16,48},{20,52},{24,56},{28,60},{32,0... | collective-permute-start | bytes 200 | tf_op jit(solution)/shard_map/ppermute | solution.py:19
  264.2 4.8 %collective-permute-start.20 = (f32[16]{0:T(128)S(1)}, f32[16]{0:T(128)S(1)}, u32[]{:S(2)}, u32[]{:S(2)}) collective-permute-start(f32[16]{0:T(128)S(1)} %add_add_fusion.5), channel_id=1, source_target_pairs={{0,48},{4,52},{8,56},{12,60},{16,32},{20,36},{24,40},{28,44},{32,1... | collective-permute-start | bytes 200 | tf_op jit(solution)/shard_map/ppermute | solution.py:19
  269.0 5.1 %collective-permute-start.21 = (f32[16]{0:T(128)S(1)}, f32[16]{0:T(128)S(1)}, u32[]{:S(2)}, u32[]{:S(2)}) collective-permute-start(f32[16]{0:T(128)S(1)} %add_add_fusion.4), channel_id=1, source_target_pairs={{0,64},{4,68},{8,72},{12,76},{16,80},{20,84},{24,88},{28,92},{32,9... | collective-permute-start | bytes 200 | tf_op jit(solution)/shard_map/ppermute | solution.py:19
  (20 other events, 115.8 us)

commit v4 on v3

--- a/solution.py
+++ b/solution.py
@@ -1,6 +1,7 @@
 import jax
 import jax.numpy as jnp
 from jax import lax
+from jax.experimental import pallas as pl
 from jax.experimental.layout import Layout, with_layout_constraint
 from jax.sharding import PartitionSpec as P
 
@@ -67,6 +68,22 @@
     return lax.dot_general(lhs, rhs, (((1,), (1,)), ((), ())), preferred_element_type=jnp.float32)
 
 
+def _times_kernel(rows_ref, right_ref, out_ref):
+    out_ref[...] = jnp.dot(rows_ref[...], right_ref[...], preferred_element_type=jnp.float32)
+
+
+def times(rows, right, block=512):
+    count, inner = rows.shape
+    width = right.shape[1]
+    return pl.pallas_call(
+        _times_kernel,
+        grid=(count // block,),
+        in_specs=[pl.BlockSpec((block, inner), lambda i: (i, 0)), pl.BlockSpec((inner, width), lambda i: (0, 0))],
+        out_specs=pl.BlockSpec((block, width), lambda i: (i, 0)),
+        out_shape=jax.ShapeDtypeStruct((count, width), jnp.float32),
+    )(rows, right)
+
+
 def widened(basis, half_cols):
     pad = jnp.zeros((half_cols, basis.shape[2]), basis.dtype)
     first = jnp.concatenate([basis[0], pad], axis=0)
@@ -95,7 +112,7 @@
 
     def project(basis):
         wide = widened(basis, half_cols)
-        return thirds(jnp.dot(stand, jnp.concatenate(pieces(wide), 1), preferred_element_type=jnp.float32))
+        return thirds(times(stand, jnp.concatenate(pieces(wide), 1)))
 
     def image_of(basis):
         proj = project(basis)

time: 275 us -> 335 us (1.22)
  Pallas kernels: 0 us -> 38.8 us
  other arithmetic: 30.7 us -> 54.9 us
  matrix products: 48 us -> 31.8 us
  local copies, waits for them, and re-layouts: 4.48 us -> 16.7 us
    pallas_call x0 -> x7, Pallas kernels: none -> 38.8 us  [times(): pl.pallas_call(_times_kernel, grid=(count // block,), in_specs=[pl.BlockS...]
    dot_general x7 -> x0, matrix products: 33.9 us -> none  [project(): jnp.dot(stand, jnp.concatenate(pieces(wide), 1), preferred_element_type=j...]
    dot_general x6, matrix products: 6.76 us -> 23.5 us  [image_of(): lax.dot_general(stand, split, (((0,), (0,)), ((), ())), preferred_element...]
    convert_element_type x13, other arithmetic: 0.29 us -> 16.7 us  [pieces(): high.astype(jnp.bfloat16)]
    concatenate x0 -> x9, local copies, waits for them, and re-layouts: none -> 7.02 us  [the longest x7 6.4 us: project(): return thirds(times(stand, jnp.concatenate(pieces(wide), 1)))]
    convert_element_type x0 -> x16, local copies, waits for them, and re-layouts: none -> 3.98 us  [the longest x8 2.52 us: pieces(): high.astype(jnp.bfloat16)]
  transfers between devices with their start and end apart: 57 -> 57, of which waited for: 51 -> 51; matrix products, arithmetic and copies ran while one was open for 2% -> 3% of each run, Pallas kernels for 0% -> 0%
where the time goes in v4:
time: 335 us; the launch traced here: 334 us
  waiting for transfers between devices  99.5 us (30%)
  starting transfers between devices  90.8 us (27%)
  other arithmetic  54.9 us (16%)
  Pallas kernels  38.8 us (12%)
  matrix products  31.8 us (9%)
  local copies, waits for them, and re-layouts  16.7 us (5%)
    ppermute x56, starting transfers between devices, swapped(): return lax.ppermute(value, axis, [(i, i ^ mask) for i in range(size)])  88.8 us
    ppermute x56, waiting for transfers between devices, swapped(): return lax.ppermute(value, axis, [(i, i ^ mask) for i in range(size)])  76 us
    pallas_call x7, Pallas kernels, times(): pl.pallas_call(_times_kernel, grid=(count // block,), in_specs=[pl.BlockS...  38.8 us
    ppermute x1, waiting for transfers between devices, passed_along(): return lax.ppermute(array, axis, pairs)  23.5 us
    dot_general x6, matrix products, image_of(): lax.dot_general(stand, split, (((0,), (0,)), ((), ())), preferred_element...  23.5 us
    convert_element_type x13, other arithmetic, pieces(): high.astype(jnp.bfloat16)  16.7 us
    another operation x24, other arithmetic, orthonormal(): factor = jnp.linalg.cholesky(gram)  9.76 us
    another operation x18, other arithmetic, orthonormal(): jax.scipy.linalg.solve_triangular(fac, rhs, lower=True)  8.03 us
  transfers between devices with their start and end apart: 57, of which 51 were waited for; matrix products, arithmetic and copies ran while one was open for 3% of the time, Pallas kernels for 0%

profile of v4, /device:TPU:32, one launch (start us, length us, event | category | flops | bytes accessed | tf_op | source)
XLA Modules:
  0.0 334.2 jit_solution(18304972933035888821)
XLA Ops:
  4.3 23.5 %collective-permute-done.7 = bf16[2048,512]{1,0:T(8,128)(2,1)} collective-permute-done((bf16[2048,512]{1,0:T(8,128)(2,1)S(1)}, bf16[2048,512]{1,0:T(8,128)(2,1)}, u32[]{:S(2)}, u32[]{:S(2)}) %collective-permute-start.7) | collective-permute-done | bytes 2097184 | tf_op jit(solution)/shard_map/ppermute | solution.py:15
  31.6 3.1 collective-permute-start.10
  41.8 2.7 collective-permute-start.12
  49.4 3.1 collective-permute-start.14
  54.8 6.4 %fusion.16.rows_ref = bf16[2048,1536]{1,0:T(8,128)(2,1)} fusion(f32[1536]{0:T(1024)S(1)} %multiply_sqrt_fusion, f32[1536]{0:T(1024)S(1)} %get-tuple-element.26, f32[1536]{0:T(1024)S(1)} %get-tuple-element.25, bf16[2048,512]{1,0:T(8,128)(2,1)S(1)} %broadcast_select_fusion, bf16[2048,1024]{1,0:T(8,128)(2,1)} %param.6), kind=kLoop, calls=%fused_computation.50 | loop fusion | flops 25165824 | bytes 12601344 | tf_op jit(solution)/shard_map/convert_element_type | solution.py:110
  61.1 232.6 %while.10 = (s32[]{:T(128)}, f32[2,1024,8]{1,2,0:T(8,128)S(1)}, bf16[2048,1536]{1,0:T(8,128)(2,1)}, s32[]{:T(128)}) while((s32[]{:T(128)}, f32[2,1024,8]{1,2,0:T(8,128)S(1)}, bf16[2048,1536]{1,0:T(8,128)(2,1)}, s32[]{:T(128)}) %tuple.54), condition=%wide.region_5.6_spmd, body=%wide.region_2.5_spmd.sunk | while | flops 307135520 | bytes 12572369 | solution.py:124
  62.1 5.5 %eval_jaxpr.1 = f32[2048,48]{1,0:T(8,128)} custom-call(bf16[2048,1536]{1,0:T(8,128)(2,1)} %get-tuple-element.112.rows_ref, bf16[1536,48]{1,0:T(8,128)(2,1)} %copy.89.right_ref), custom_call_target="tpu_custom_call" | custom-call | tf_op jit(solution)/shard_map/while/body/eval_jaxpr/pallas_call | solution.py:78
  67.6 2.8 reduce-precision_convert_fusion.18
  71.3 3.9 %convolution_bitcast_fusion.2 = f32[1536,48]{0,1:T(8,128)S(1)} fusion(bf16[2048,1536]{1,0:T(8,128)(2,1)} %get-tuple-element.112.rows_ref, bf16[2048,16]{0,1:T(8,128)(2,1)S(1)} %copy.90, bf16[2048,16]{0,1:T(8,128)(2,1)S(1)} %copy.91, bf16[2048,16]{0,1:T(8,128)(2,1)S(1)} %copy.92), kind=kOutput, calls=%fused_computation.clone.1 | convolution fusion | flops 302579712 | bytes 6782976 | tf_op jit(solution)/shard_map/while/body/eval_jaxpr/dot_general | solution.py:120
  76.8 3.1 collective-permute-start.1
  90.8 3.1 collective-permute-start.6
  93.9 2.8 collective-permute-done.6
  101.2 5.5 %eval_jaxpr.1 = f32[2048,48]{1,0:T(8,128)} custom-call(bf16[2048,1536]{1,0:T(8,128)(2,1)} %get-tuple-element.112.rows_ref, bf16[1536,48]{1,0:T(8,128)(2,1)} %copy.89.right_ref), custom_call_target="tpu_custom_call" | custom-call | tf_op jit(solution)/shard_map/while/body/eval_jaxpr/pallas_call | solution.py:78
  106.7 2.8 reduce-precision_convert_fusion.18
  110.4 3.9 %convolution_bitcast_fusion.2 = f32[1536,48]{0,1:T(8,128)S(1)} fusion(bf16[2048,1536]{1,0:T(8,128)(2,1)} %get-tuple-element.112.rows_ref, bf16[2048,16]{0,1:T(8,128)(2,1)S(1)} %copy.90, bf16[2048,16]{0,1:T(8,128)(2,1)S(1)} %copy.91, bf16[2048,16]{0,1:T(8,128)(2,1)S(1)} %copy.92), kind=kOutput, calls=%fused_computation.clone.1 | convolution fusion | flops 302579712 | bytes 6782976 | tf_op jit(solution)/shard_map/while/body/eval_jaxpr/dot_general | solution.py:120
  114.6 2.5 collective-permute-start.1
  122.8 2.6 collective-permute-start.4
  129.7 3.1 collective-permute-start.6
  132.8 2.8 collective-permute-done.6
  140.1 5.5 %eval_jaxpr.1 = f32[2048,48]{1,0:T(8,128)} custom-call(bf16[2048,1536]{1,0:T(8,128)(2,1)} %get-tuple-element.112.rows_ref, bf16[1536,48]{1,0:T(8,128)(2,1)} %copy.89.right_ref), custom_call_target="tpu_custom_call" | custom-call | tf_op jit(solution)/shard_map/while/body/eval_jaxpr/pallas_call | solution.py:78
  145.7 2.8 reduce-precision_convert_fusion.18
  149.3 3.9 %convolution_bitcast_fusion.2 = f32[1536,48]{0,1:T(8,128)S(1)} fusion(bf16[2048,1536]{1,0:T(8,128)(2,1)} %get-tuple-element.112.rows_ref, bf16[2048,16]{0,1:T(8,128)(2,1)S(1)} %copy.90, bf16[2048,16]{0,1:T(8,128)(2,1)S(1)} %copy.91, bf16[2048,16]{0,1:T(8,128)(2,1)S(1)} %copy.92), kind=kOutput, calls=%fused_computation.clone.1 | convolution fusion | flops 302579712 | bytes 6782976 | tf_op jit(solution)/shard_map/while/body/eval_jaxpr/dot_general | solution.py:120
  155.0 2.5 collective-permute-start.1
  161.9 2.5 collective-permute-start.4
  165.4 2.8 collective-permute-done.3
  168.7 3.0 collective-permute-start.6
  171.7 2.8 collective-permute-done.6
  179.1 5.5 %eval_jaxpr.1 = f32[2048,48]{1,0:T(8,128)} custom-call(bf16[2048,1536]{1,0:T(8,128)(2,1)} %get-tuple-element.112.rows_ref, bf16[1536,48]{1,0:T(8,128)(2,1)} %copy.89.right_ref), custom_call_target="tpu_custom_call" | custom-call | tf_op jit(solution)/shard_map/while/body/eval_jaxpr/pallas_call | solution.py:78
  184.6 2.8 reduce-precision_convert_fusion.18
  188.3 3.9 %convolution_bitcast_fusion.2 = f32[1536,48]{0,1:T(8,128)S(1)} fusion(bf16[2048,1536]{1,0:T(8,128)(2,1)} %get-tuple-element.112.rows_ref, bf16[2048,16]{0,1:T(8,128)(2,1)S(1)} %copy.90, bf16[2048,16]{0,1:T(8,128)(2,1)S(1)} %copy.91, bf16[2048,16]{0,1:T(8,128)(2,1)S(1)} %copy.92), kind=kOutput, calls=%fused_computation.clone.1 | convolution fusion | flops 302579712 | bytes 6782976 | tf_op jit(solution)/shard_map/while/body/eval_jaxpr/dot_general | solution.py:120
  195.8 2.6 collective-permute-done
  207.4 3.1 collective-permute-start.6
  210.5 2.7 collective-permute-done.6
  217.8 5.5 %eval_jaxpr.1 = f32[2048,48]{1,0:T(8,128)} custom-call(bf16[2048,1536]{1,0:T(8,128)(2,1)} %get-tuple-element.112.rows_ref, bf16[1536,48]{1,0:T(8,128)(2,1)} %copy.89.right_ref), custom_call_target="tpu_custom_call" | custom-call | tf_op jit(solution)/shard_map/while/body/eval_jaxpr/pallas_call | solution.py:78
  223.3 2.8 reduce-precision_convert_fusion.18
  227.0 3.9 %convolution_bitcast_fusion.2 = f32[1536,48]{0,1:T(8,128)S(1)} fusion(bf16[2048,1536]{1,0:T(8,128)(2,1)} %get-tuple-element.112.rows_ref, bf16[2048,16]{0,1:T(8,128)(2,1)S(1)} %copy.90, bf16[2048,16]{0,1:T(8,128)(2,1)S(1)} %copy.91, bf16[2048,16]{0,1:T(8,128)(2,1)S(1)} %copy.92), kind=kOutput, calls=%fused_computation.clone.1 | convolution fusion | flops 302579712 | bytes 6782976 | tf_op jit(solution)/shard_map/while/body/eval_jaxpr/dot_general | solution.py:120
  245.8 3.1 collective-permute-start.6
  249.0 2.7 collective-permute-done.6
  256.2 5.5 %eval_jaxpr.1 = f32[2048,48]{1,0:T(8,128)} custom-call(bf16[2048,1536]{1,0:T(8,128)(2,1)} %get-tuple-element.112.rows_ref, bf16[1536,48]{1,0:T(8,128)(2,1)} %copy.89.right_ref), custom_call_target="tpu_custom_call" | custom-call | tf_op jit(solution)/shard_map/while/body/eval_jaxpr/pallas_call | solution.py:78
  261.8 2.8 reduce-precision_convert_fusion.18
  265.4 3.9 %convolution_bitcast_fusion.2 = f32[1536,48]{0,1:T(8,128)S(1)} fusion(bf16[2048,1536]{1,0:T(8,128)(2,1)} %get-tuple-element.112.rows_ref, bf16[2048,16]{0,1:T(8,128)(2,1)S(1)} %copy.90, bf16[2048,16]{0,1:T(8,128)(2,1)S(1)} %copy.91, bf16[2048,16]{0,1:T(8,128)(2,1)S(1)} %copy.92), kind=kOutput, calls=%fused_computation.clone.1 | convolution fusion | flops 302579712 | bytes 6782976 | tf_op jit(solution)/shard_map/while/body/eval_jaxpr/dot_general | solution.py:120
  284.3 3.1 collective-permute-start.6
  287.5 2.7 collective-permute-done.6
  294.7 5.5 %shard_map.67 = f32[2048,48]{1,0:T(8,128)} custom-call(bf16[2048,1536]{1,0:T(8,128)(2,1)} %get-tuple-element.114, bf16[1536,48]{1,0:T(8,128)(2,1)} %copy.67.right_ref), custom_call_target="tpu_custom_call" | custom-call | tf_op jit(solution)/shard_map/pallas_call | solution.py:78
  300.3 2.8 multiply_reduce_fusion.2
  318.0 2.9 multiply_reduce_fusion.1
  321.3 2.5 collective-permute-start.19
  328.5 3.1 collective-permute-start.21
  (308 shorter events, 149.9 us)
Async XLA Ops:
  2.4 25.5 %collective-permute-start.7 = (bf16[2048,512]{1,0:T(8,128)(2,1)S(1)}, bf16[2048,512]{1,0:T(8,128)(2,1)}, u32[]{:S(2)}, u32[]{:S(2)}) collective-permute-start(bf16[2048,512]{1,0:T(8,128)(2,1)S(1)} %slice.80), channel_id=1, source_target_pairs={{1,0},{2,1},{3,2},{5,4},{6,5},{7,6},{9,8},{10,9},{11,10},{13,12},{... | collective-permute-start | bytes 6291464 | tf_op jit(solution)/shard_map/ppermute | solution.py:15
  31.6 5.0 %collective-permute-start.10 = (f32[2,1536]{1,0:T(2,128)S(1)}, f32[2,1536]{1,0:T(2,128)S(1)}, u32[]{:S(2)}, u32[]{:S(2)}) collective-permute-start(f32[2,1536]{1,0:T(2,128)S(1)} %pad_maximum_fusion.4), channel_id=1, source_target_pairs={{0,12},{4,8},{8,4},{12,0},{16,28},{20,24},{24,20},{28,16},{32,44},... | collective-permute-start | bytes 36872 | tf_op jit(solution)/shard_map/ppermute | solution.py:20
  34.8 5.2 %collective-permute-start.9 = (f32[2,1536]{1,0:T(2,128)S(1)}, f32[2,1536]{1,0:T(2,128)S(1)}, u32[]{:S(2)}, u32[]{:S(2)}) collective-permute-start(f32[2,1536]{1,0:T(2,128)S(1)} %pad_maximum_fusion.4), channel_id=1, source_target_pairs={{0,8},{4,12},{8,0},{12,4},{16,24},{20,28},{24,16},{28,20},{32,40},... | collective-permute-start | bytes 36872 | tf_op jit(solution)/shard_map/ppermute | solution.py:20
  40.1 4.8 %collective-permute-start.11 = (f32[2,1536]{1,0:T(2,128)S(1)}, f32[2,1536]{1,0:T(2,128)S(1)}, u32[]{:S(2)}, u32[]{:S(2)}) collective-permute-start(f32[2,1536]{1,0:T(2,128)S(1)} %add_add_fusion.3), channel_id=1, source_target_pairs={{0,16},{4,20},{8,24},{12,28},{16,0},{20,4},{24,8},{28,12},{32,48},... | collective-permute-start | bytes 36872 | tf_op jit(solution)/shard_map/ppermute | solution.py:20
  41.8 5.2 %collective-permute-start.12 = (f32[2,1536]{1,0:T(2,128)S(1)}, f32[2,1536]{1,0:T(2,128)S(1)}, u32[]{:S(2)}, u32[]{:S(2)}) collective-permute-start(f32[2,1536]{1,0:T(2,128)S(1)} %add_add_fusion.3), channel_id=1, source_target_pairs={{0,32},{4,36},{8,40},{12,44},{16,48},{20,52},{24,56},{28,60},{32,0... | collective-permute-start | bytes 36872 | tf_op jit(solution)/shard_map/ppermute | solution.py:20
  44.5 4.9 %collective-permute-start.13 = (f32[2,1536]{1,0:T(2,128)S(1)}, f32[2,1536]{1,0:T(2,128)S(1)}, u32[]{:S(2)}, u32[]{:S(2)}) collective-permute-start(f32[2,1536]{1,0:T(2,128)S(1)} %add_add_fusion.3), channel_id=1, source_target_pairs={{0,48},{4,52},{8,56},{12,60},{16,32},{20,36},{24,40},{28,44},{32,1... | collective-permute-start | bytes 36872 | tf_op jit(solution)/shard_map/ppermute | solution.py:20
  49.4 5.3 %collective-permute-start.14 = (f32[2,1536]{1,0:T(2,128)S(1)}, f32[2,1536]{1,0:T(2,128)S(1)}, u32[]{:S(2)}, u32[]{:S(2)}) collective-permute-start(f32[2,1536]{1,0:T(2,128)S(1)} %add_add_fusion.2), channel_id=1, source_target_pairs={{0,64},{4,68},{8,72},{12,76},{16,80},{20,84},{24,88},{28,92},{32,9... | collective-permute-start | bytes 36872 | tf_op jit(solution)/shard_map/ppermute | solution.py:20
  75.3 5.8 %collective-permute-start = (f32[2,1024,8]{1,2,0:T(8,128)S(1)}, f32[2,1024,8]{1,2,0:T(8,128)S(1)}, u32[]{:S(2)}, u32[]{:S(2)}) collective-permute-start(f32[2,1024,8]{1,2,0:T(8,128)S(1)} %pad_maximum_fusion.8), channel_id=1, source_target_pairs={{0,8},{4,12},{8,0},{12,4},{16,24},{20,28},{24,16},{28,20},{32,40},... | collective-permute-start | bytes 196616 | tf_op jit(solution)/shard_map/while/body/eval_jaxpr/ppermute | solution.py:20
  76.8 5.5 %collective-permute-start.1 = (f32[2,1024,8]{1,2,0:T(8,128)S(1)}, f32[2,1024,8]{1,2,0:T(8,128)S(1)}, u32[]{:S(2)}, u32[]{:S(2)}) collective-permute-start(f32[2,1024,8]{1,2,0:T(8,128)S(1)} %pad_maximum_fusion.8), channel_id=1, source_target_pairs={{0,12},{4,8},{8,4},{12,0},{16,28},{20,24},{24,20},{28,16},{32,44},... | collective-permute-start | bytes 196616 | tf_op jit(solution)/shard_map/while/body/eval_jaxpr/ppermute | solution.py:20
  84.2 5.9 %collective-permute-start.3 = (f32[2,1024,8]{1,2,0:T(8,128)S(1)}, f32[2,1024,8]{1,2,0:T(8,128)S(1)}, u32[]{:S(2)}, u32[]{:S(2)}) collective-permute-start(f32[2,1024,8]{1,2,0:T(8,128)S(1)} %add_add_fusion.8), channel_id=1, source_target_pairs={{0,32},{4,36},{8,40},{12,44},{16,48},{20,52},{24,56},{28,60},{32,0... | collective-permute-start | bytes 196616 | tf_op jit(solution)/shard_map/while/body/eval_jaxpr/ppermute | solution.py:20
  84.6 6.2 %collective-permute-start.4 = (f32[2,1024,8]{1,2,0:T(8,128)S(1)}, f32[2,1024,8]{1,2,0:T(8,128)S(1)}, u32[]{:S(2)}, u32[]{:S(2)}) collective-permute-start(f32[2,1024,8]{1,2,0:T(8,128)S(1)} %add_add_fusion.8), channel_id=1, source_target_pairs={{0,48},{4,52},{8,56},{12,60},{16,32},{20,36},{24,40},{28,44},{32,1... | collective-permute-start | bytes 196616 | tf_op jit(solution)/shard_map/while/body/eval_jaxpr/ppermute | solution.py:20
  86.0 4.8 %collective-permute-start.5 = (f32[2,1024,8]{1,2,0:T(8,128)S(1)}, f32[2,1024,8]{1,2,0:T(8,128)S(1)}, u32[]{:S(2)}, u32[]{:S(2)}) collective-permute-start(f32[2,1024,8]{1,2,0:T(8,128)S(1)} %add_add_fusion.8), channel_id=1, source_target_pairs={{0,16},{4,20},{8,24},{12,28},{16,0},{20,4},{24,8},{28,12},{32,48},... | collective-permute-start | bytes 196616 | tf_op jit(solution)/shard_map/while/body/eval_jaxpr/ppermute | solution.py:20
  90.8 5.8 %collective-permute-start.6 = (f32[2,1024,8]{1,2,0:T(8,128)S(1)}, f32[2,1024,8]{1,2,0:T(8,128)S(1)}, u32[]{:S(2)}, u32[]{:S(2)}) collective-permute-start(f32[2,1024,8]{1,2,0:T(8,128)S(1)} %add_add_fusion.9), channel_id=1, source_target_pairs={{0,64},{4,68},{8,72},{12,76},{16,80},{20,84},{24,88},{28,92},{32,9... | collective-permute-start | bytes 196616 | tf_op jit(solution)/shard_map/while/body/eval_jaxpr/ppermute | solution.py:20
  114.4 6.0 %collective-permute-start = (f32[2,1024,8]{1,2,0:T(8,128)S(1)}, f32[2,1024,8]{1,2,0:T(8,128)S(1)}, u32[]{:S(2)}, u32[]{:S(2)}) collective-permute-start(f32[2,1024,8]{1,2,0:T(8,128)S(1)} %pad_maximum_fusion.8), channel_id=1, source_target_pairs={{0,8},{4,12},{8,0},{12,4},{16,24},{20,28},{24,16},{28,20},{32,40},... | collective-permute-start | bytes 196616 | tf_op jit(solution)/shard_map/while/body/eval_jaxpr/ppermute | solution.py:20
  114.6 6.2 %collective-permute-start.1 = (f32[2,1024,8]{1,2,0:T(8,128)S(1)}, f32[2,1024,8]{1,2,0:T(8,128)S(1)}, u32[]{:S(2)}, u32[]{:S(2)}) collective-permute-start(f32[2,1024,8]{1,2,0:T(8,128)S(1)} %pad_maximum_fusion.8), channel_id=1, source_target_pairs={{0,12},{4,8},{8,4},{12,0},{16,28},{20,24},{24,20},{28,16},{32,44},... | collective-permute-start | bytes 196616 | tf_op jit(solution)/shard_map/while/body/eval_jaxpr/ppermute | solution.py:20
  121.4 5.8 %collective-permute-start.3 = (f32[2,1024,8]{1,2,0:T(8,128)S(1)}, f32[2,1024,8]{1,2,0:T(8,128)S(1)}, u32[]{:S(2)}, u32[]{:S(2)}) collective-permute-start(f32[2,1024,8]{1,2,0:T(8,128)S(1)} %add_add_fusion.8), channel_id=1, source_target_pairs={{0,32},{4,36},{8,40},{12,44},{16,48},{20,52},{24,56},{28,60},{32,0... | collective-permute-start | bytes 196616 | tf_op jit(solution)/shard_map/while/body/eval_jaxpr/ppermute | solution.py:20
  122.8 5.5 %collective-permute-start.4 = (f32[2,1024,8]{1,2,0:T(8,128)S(1)}, f32[2,1024,8]{1,2,0:T(8,128)S(1)}, u32[]{:S(2)}, u32[]{:S(2)}) collective-permute-start(f32[2,1024,8]{1,2,0:T(8,128)S(1)} %add_add_fusion.8), channel_id=1, source_target_pairs={{0,48},{4,52},{8,56},{12,60},{16,32},{20,36},{24,40},{28,44},{32,1... | collective-permute-start | bytes 196616 | tf_op jit(solution)/shard_map/while/body/eval_jaxpr/ppermute | solution.py:20
  129.7 5.8 %collective-permute-start.6 = (f32[2,1024,8]{1,2,0:T(8,128)S(1)}, f32[2,1024,8]{1,2,0:T(8,128)S(1)}, u32[]{:S(2)}, u32[]{:S(2)}) collective-permute-start(f32[2,1024,8]{1,2,0:T(8,128)S(1)} %add_add_fusion.9), channel_id=1, source_target_pairs={{0,64},{4,68},{8,72},{12,76},{16,80},{20,84},{24,88},{28,92},{32,9... | collective-permute-start | bytes 196616 | tf_op jit(solution)/shard_map/while/body/eval_jaxpr/ppermute | solution.py:20
  153.3 6.3 %collective-permute-start = (f32[2,1024,8]{1,2,0:T(8,128)S(1)}, f32[2,1024,8]{1,2,0:T(8,128)S(1)}, u32[]{:S(2)}, u32[]{:S(2)}) collective-permute-start(f32[2,1024,8]{1,2,0:T(8,128)S(1)} %pad_maximum_fusion.8), channel_id=1, source_target_pairs={{0,8},{4,12},{8,0},{12,4},{16,24},{20,28},{24,16},{28,20},{32,40},... | collective-permute-start | bytes 196616 | tf_op jit(solution)/shard_map/while/body/eval_jaxpr/ppermute | solution.py:20
  155.0 6.3 %collective-permute-start.1 = (f32[2,1024,8]{1,2,0:T(8,128)S(1)}, f32[2,1024,8]{1,2,0:T(8,128)S(1)}, u32[]{:S(2)}, u32[]{:S(2)}) collective-permute-start(f32[2,1024,8]{1,2,0:T(8,128)S(1)} %pad_maximum_fusion.8), channel_id=1, source_target_pairs={{0,12},{4,8},{8,4},{12,0},{16,28},{20,24},{24,20},{28,16},{32,44},... | collective-permute-start | bytes 196616 | tf_op jit(solution)/shard_map/while/body/eval_jaxpr/ppermute | solution.py:20
  161.8 6.3 %collective-permute-start.3 = (f32[2,1024,8]{1,2,0:T(8,128)S(1)}, f32[2,1024,8]{1,2,0:T(8,128)S(1)}, u32[]{:S(2)}, u32[]{:S(2)}) collective-permute-start(f32[2,1024,8]{1,2,0:T(8,128)S(1)} %add_add_fusion.8), channel_id=1, source_target_pairs={{0,32},{4,36},{8,40},{12,44},{16,48},{20,52},{24,56},{28,60},{32,0... | collective-permute-start | bytes 196616 | tf_op jit(solution)/shard_map/while/body/eval_jaxpr/ppermute | solution.py:20
  161.9 6.4 %collective-permute-start.4 = (f32[2,1024,8]{1,2,0:T(8,128)S(1)}, f32[2,1024,8]{1,2,0:T(8,128)S(1)}, u32[]{:S(2)}, u32[]{:S(2)}) collective-permute-start(f32[2,1024,8]{1,2,0:T(8,128)S(1)} %add_add_fusion.8), channel_id=1, source_target_pairs={{0,48},{4,52},{8,56},{12,60},{16,32},{20,36},{24,40},{28,44},{32,1... | collective-permute-start | bytes 196616 | tf_op jit(solution)/shard_map/while/body/eval_jaxpr/ppermute | solution.py:20
  164.4 4.3 %collective-permute-start.5 = (f32[2,1024,8]{1,2,0:T(8,128)S(1)}, f32[2,1024,8]{1,2,0:T(8,128)S(1)}, u32[]{:S(2)}, u32[]{:S(2)}) collective-permute-start(f32[2,1024,8]{1,2,0:T(8,128)S(1)} %add_add_fusion.8), channel_id=1, source_target_pairs={{0,16},{4,20},{8,24},{12,28},{16,0},{20,4},{24,8},{28,12},{32,48},... | collective-permute-start | bytes 196616 | tf_op jit(solution)/shard_map/while/body/eval_jaxpr/ppermute | solution.py:20
  168.7 5.8 %collective-permute-start.6 = (f32[2,1024,8]{1,2,0:T(8,128)S(1)}, f32[2,1024,8]{1,2,0:T(8,128)S(1)}, u32[]{:S(2)}, u32[]{:S(2)}) collective-permute-start(f32[2,1024,8]{1,2,0:T(8,128)S(1)} %add_add_fusion.9), channel_id=1, source_target_pairs={{0,64},{4,68},{8,72},{12,76},{16,80},{20,84},{24,88},{28,92},{32,9... | collective-permute-start | bytes 196616 | tf_op jit(solution)/shard_map/while/body/eval_jaxpr/ppermute | solution.py:20
  192.3 6.1 %collective-permute-start = (f32[2,1024,8]{1,2,0:T(8,128)S(1)}, f32[2,1024,8]{1,2,0:T(8,128)S(1)}, u32[]{:S(2)}, u32[]{:S(2)}) collective-permute-start(f32[2,1024,8]{1,2,0:T(8,128)S(1)} %pad_maximum_fusion.8), channel_id=1, source_target_pairs={{0,8},{4,12},{8,0},{12,4},{16,24},{20,28},{24,16},{28,20},{32,40},... | collective-permute-start | bytes 196616 | tf_op jit(solution)/shard_map/while/body/eval_jaxpr/ppermute | solution.py:20
  193.5 5.6 %collective-permute-start.1 = (f32[2,1024,8]{1,2,0:T(8,128)S(1)}, f32[2,1024,8]{1,2,0:T(8,128)S(1)}, u32[]{:S(2)}, u32[]{:S(2)}) collective-permute-start(f32[2,1024,8]{1,2,0:T(8,128)S(1)} %pad_maximum_fusion.8), channel_id=1, source_target_pairs={{0,12},{4,8},{8,4},{12,0},{16,28},{20,24},{24,20},{28,16},{32,44},... | collective-permute-start | bytes 196616 | tf_op jit(solution)/shard_map/while/body/eval_jaxpr/ppermute | solution.py:20
  199.7 5.8 %collective-permute-start.3 = (f32[2,1024,8]{1,2,0:T(8,128)S(1)}, f32[2,1024,8]{1,2,0:T(8,128)S(1)}, u32[]{:S(2)}, u32[]{:S(2)}) collective-permute-start(f32[2,1024,8]{1,2,0:T(8,128)S(1)} %add_add_fusion.8), channel_id=1, source_target_pairs={{0,32},{4,36},{8,40},{12,44},{16,48},{20,52},{24,56},{28,60},{32,0... | collective-permute-start | bytes 196616 | tf_op jit(solution)/shard_map/while/body/eval_jaxpr/ppermute | solution.py:20
  200.9 5.5 %collective-permute-start.4 = (f32[2,1024,8]{1,2,0:T(8,128)S(1)}, f32[2,1024,8]{1,2,0:T(8,128)S(1)}, u32[]{:S(2)}, u32[]{:S(2)}) collective-permute-start(f32[2,1024,8]{1,2,0:T(8,128)S(1)} %add_add_fusion.8), channel_id=1, source_target_pairs={{0,48},{4,52},{8,56},{12,60},{16,32},{20,36},{24,40},{28,44},{32,1... | collective-permute-start | bytes 196616 | tf_op jit(solution)/shard_map/while/body/eval_jaxpr/ppermute | solution.py:20
  203.1 4.3 %collective-permute-start.5 = (f32[2,1024,8]{1,2,0:T(8,128)S(1)}, f32[2,1024,8]{1,2,0:T(8,128)S(1)}, u32[]{:S(2)}, u32[]{:S(2)}) collective-permute-start(f32[2,1024,8]{1,2,0:T(8,128)S(1)} %add_add_fusion.8), channel_id=1, source_target_pairs={{0,16},{4,20},{8,24},{12,28},{16,0},{20,4},{24,8},{28,12},{32,48},... | collective-permute-start | bytes 196616 | tf_op jit(solution)/shard_map/while/body/eval_jaxpr/ppermute | solution.py:20
  207.4 5.8 %collective-permute-start.6 = (f32[2,1024,8]{1,2,0:T(8,128)S(1)}, f32[2,1024,8]{1,2,0:T(8,128)S(1)}, u32[]{:S(2)}, u32[]{:S(2)}) collective-permute-start(f32[2,1024,8]{1,2,0:T(8,128)S(1)} %add_add_fusion.9), channel_id=1, source_target_pairs={{0,64},{4,68},{8,72},{12,76},{16,80},{20,84},{24,88},{28,92},{32,9... | collective-permute-start | bytes 196616 | tf_op jit(solution)/shard_map/while/body/eval_jaxpr/ppermute | solution.py:20
  230.9 5.8 %collective-permute-start = (f32[2,1024,8]{1,2,0:T(8,128)S(1)}, f32[2,1024,8]{1,2,0:T(8,128)S(1)}, u32[]{:S(2)}, u32[]{:S(2)}) collective-permute-start(f32[2,1024,8]{1,2,0:T(8,128)S(1)} %pad_maximum_fusion.8), channel_id=1, source_target_pairs={{0,8},{4,12},{8,0},{12,4},{16,24},{20,28},{24,16},{28,20},{32,40},... | collective-permute-start | bytes 196616 | tf_op jit(solution)/shard_map/while/body/eval_jaxpr/ppermute | solution.py:20
  232.5 5.5 %collective-permute-start.1 = (f32[2,1024,8]{1,2,0:T(8,128)S(1)}, f32[2,1024,8]{1,2,0:T(8,128)S(1)}, u32[]{:S(2)}, u32[]{:S(2)}) collective-permute-start(f32[2,1024,8]{1,2,0:T(8,128)S(1)} %pad_maximum_fusion.8), channel_id=1, source_target_pairs={{0,12},{4,8},{8,4},{12,0},{16,28},{20,24},{24,20},{28,16},{32,44},... | collective-permute-start | bytes 196616 | tf_op jit(solution)/shard_map/while/body/eval_jaxpr/ppermute | solution.py:20
  238.8 5.9 %collective-permute-start.3 = (f32[2,1024,8]{1,2,0:T(8,128)S(1)}, f32[2,1024,8]{1,2,0:T(8,128)S(1)}, u32[]{:S(2)}, u32[]{:S(2)}) collective-permute-start(f32[2,1024,8]{1,2,0:T(8,128)S(1)} %add_add_fusion.8), channel_id=1, source_target_pairs={{0,32},{4,36},{8,40},{12,44},{16,48},{20,52},{24,56},{28,60},{32,0... | collective-permute-start | bytes 196616 | tf_op jit(solution)/shard_map/while/body/eval_jaxpr/ppermute | solution.py:20
  239.6 5.7 %collective-permute-start.4 = (f32[2,1024,8]{1,2,0:T(8,128)S(1)}, f32[2,1024,8]{1,2,0:T(8,128)S(1)}, u32[]{:S(2)}, u32[]{:S(2)}) collective-permute-start(f32[2,1024,8]{1,2,0:T(8,128)S(1)} %add_add_fusion.8), channel_id=1, source_target_pairs={{0,48},{4,52},{8,56},{12,60},{16,32},{20,36},{24,40},{28,44},{32,1... | collective-permute-start | bytes 196616 | tf_op jit(solution)/shard_map/while/body/eval_jaxpr/ppermute | solution.py:20
  241.5 4.3 %collective-permute-start.5 = (f32[2,1024,8]{1,2,0:T(8,128)S(1)}, f32[2,1024,8]{1,2,0:T(8,128)S(1)}, u32[]{:S(2)}, u32[]{:S(2)}) collective-permute-start(f32[2,1024,8]{1,2,0:T(8,128)S(1)} %add_add_fusion.8), channel_id=1, source_target_pairs={{0,16},{4,20},{8,24},{12,28},{16,0},{20,4},{24,8},{28,12},{32,48},... | collective-permute-start | bytes 196616 | tf_op jit(solution)/shard_map/while/body/eval_jaxpr/ppermute | solution.py:20
  245.8 5.8 %collective-permute-start.6 = (f32[2,1024,8]{1,2,0:T(8,128)S(1)}, f32[2,1024,8]{1,2,0:T(8,128)S(1)}, u32[]{:S(2)}, u32[]{:S(2)}) collective-permute-start(f32[2,1024,8]{1,2,0:T(8,128)S(1)} %add_add_fusion.9), channel_id=1, source_target_pairs={{0,64},{4,68},{8,72},{12,76},{16,80},{20,84},{24,88},{28,92},{32,9... | collective-permute-start | bytes 196616 | tf_op jit(solution)/shard_map/while/body/eval_jaxpr/ppermute | solution.py:20
  269.4 5.8 %collective-permute-start = (f32[2,1024,8]{1,2,0:T(8,128)S(1)}, f32[2,1024,8]{1,2,0:T(8,128)S(1)}, u32[]{:S(2)}, u32[]{:S(2)}) collective-permute-start(f32[2,1024,8]{1,2,0:T(8,128)S(1)} %pad_maximum_fusion.8), channel_id=1, source_target_pairs={{0,8},{4,12},{8,0},{12,4},{16,24},{20,28},{24,16},{28,20},{32,40},... | collective-permute-start | bytes 196616 | tf_op jit(solution)/shard_map/while/body/eval_jaxpr/ppermute | solution.py:20
  270.4 5.5 %collective-permute-start.1 = (f32[2,1024,8]{1,2,0:T(8,128)S(1)}, f32[2,1024,8]{1,2,0:T(8,128)S(1)}, u32[]{:S(2)}, u32[]{:S(2)}) collective-permute-start(f32[2,1024,8]{1,2,0:T(8,128)S(1)} %pad_maximum_fusion.8), channel_id=1, source_target_pairs={{0,12},{4,8},{8,4},{12,0},{16,28},{20,24},{24,20},{28,16},{32,44},... | collective-permute-start | bytes 196616 | tf_op jit(solution)/shard_map/while/body/eval_jaxpr/ppermute | solution.py:20
  276.7 5.8 %collective-permute-start.3 = (f32[2,1024,8]{1,2,0:T(8,128)S(1)}, f32[2,1024,8]{1,2,0:T(8,128)S(1)}, u32[]{:S(2)}, u32[]{:S(2)}) collective-permute-start(f32[2,1024,8]{1,2,0:T(8,128)S(1)} %add_add_fusion.8), channel_id=1, source_target_pairs={{0,32},{4,36},{8,40},{12,44},{16,48},{20,52},{24,56},{28,60},{32,0... | collective-permute-start | bytes 196616 | tf_op jit(solution)/shard_map/while/body/eval_jaxpr/ppermute | solution.py:20
  278.0 5.5 %collective-permute-start.4 = (f32[2,1024,8]{1,2,0:T(8,128)S(1)}, f32[2,1024,8]{1,2,0:T(8,128)S(1)}, u32[]{:S(2)}, u32[]{:S(2)}) collective-permute-start(f32[2,1024,8]{1,2,0:T(8,128)S(1)} %add_add_fusion.8), channel_id=1, source_target_pairs={{0,48},{4,52},{8,56},{12,60},{16,32},{20,36},{24,40},{28,44},{32,1... | collective-permute-start | bytes 196616 | tf_op jit(solution)/shard_map/while/body/eval_jaxpr/ppermute | solution.py:20
  284.3 5.8 %collective-permute-start.6 = (f32[2,1024,8]{1,2,0:T(8,128)S(1)}, f32[2,1024,8]{1,2,0:T(8,128)S(1)}, u32[]{:S(2)}, u32[]{:S(2)}) collective-permute-start(f32[2,1024,8]{1,2,0:T(8,128)S(1)} %add_add_fusion.9), channel_id=1, source_target_pairs={{0,64},{4,68},{8,72},{12,76},{16,80},{20,84},{24,88},{28,92},{32,9... | collective-permute-start | bytes 196616 | tf_op jit(solution)/shard_map/while/body/eval_jaxpr/ppermute | solution.py:20
  304.8 16.2 %collective-permute-start.15 = (f32[16]{0:T(128)S(1)}, f32[16]{0:T(128)S(1)}, u32[]{:S(2)}, u32[]{:S(2)}) collective-permute-start(f32[16]{0:T(128)S(1)} %get-tuple-element.35), channel_id=1, source_target_pairs={{0,4},{4,0},{8,12},{12,8},{16,20},{20,16},{24,28},{28,24},{32,36},... | collective-permute-start | bytes 200 | tf_op jit(solution)/shard_map/ppermute | solution.py:20
  305.7 15.3 %collective-permute-start.16 = (f32[16]{0:T(128)S(1)}, f32[16]{0:T(128)S(1)}, u32[]{:S(2)}, u32[]{:S(2)}) collective-permute-start(f32[16]{0:T(128)S(1)} %get-tuple-element.35), channel_id=1, source_target_pairs={{0,8},{4,12},{8,0},{12,4},{16,24},{20,28},{24,16},{28,20},{32,40},... | collective-permute-start | bytes 200 | tf_op jit(solution)/shard_map/ppermute | solution.py:20
  307.8 13.2 %collective-permute-start.17 = (f32[16]{0:T(128)S(1)}, f32[16]{0:T(128)S(1)}, u32[]{:S(2)}, u32[]{:S(2)}) collective-permute-start(f32[16]{0:T(128)S(1)} %get-tuple-element.35), channel_id=1, source_target_pairs={{0,12},{4,8},{8,4},{12,0},{16,28},{20,24},{24,20},{28,16},{32,44},... | collective-permute-start | bytes 200 | tf_op jit(solution)/shard_map/ppermute | solution.py:20
  321.0 4.8 %collective-permute-start.18 = (f32[16]{0:T(128)S(1)}, f32[16]{0:T(128)S(1)}, u32[]{:S(2)}, u32[]{:S(2)}) collective-permute-start(f32[16]{0:T(128)S(1)} %add_add_fusion.5), channel_id=1, source_target_pairs={{0,16},{4,20},{8,24},{12,28},{16,0},{20,4},{24,8},{28,12},{32,48},... | collective-permute-start | bytes 200 | tf_op jit(solution)/shard_map/ppermute | solution.py:20
  321.3 5.1 %collective-permute-start.19 = (f32[16]{0:T(128)S(1)}, f32[16]{0:T(128)S(1)}, u32[]{:S(2)}, u32[]{:S(2)}) collective-permute-start(f32[16]{0:T(128)S(1)} %add_add_fusion.5), channel_id=1, source_target_pairs={{0,32},{4,36},{8,40},{12,44},{16,48},{20,52},{24,56},{28,60},{32,0... | collective-permute-start | bytes 200 | tf_op jit(solution)/shard_map/ppermute | solution.py:20
  323.7 4.8 %collective-permute-start.20 = (f32[16]{0:T(128)S(1)}, f32[16]{0:T(128)S(1)}, u32[]{:S(2)}, u32[]{:S(2)}) collective-permute-start(f32[16]{0:T(128)S(1)} %add_add_fusion.5), channel_id=1, source_target_pairs={{0,48},{4,52},{8,56},{12,60},{16,32},{20,36},{24,40},{28,44},{32,1... | collective-permute-start | bytes 200 | tf_op jit(solution)/shard_map/ppermute | solution.py:20
  328.5 5.1 %collective-permute-start.21 = (f32[16]{0:T(128)S(1)}, f32[16]{0:T(128)S(1)}, u32[]{:S(2)}, u32[]{:S(2)}) collective-permute-start(f32[16]{0:T(128)S(1)} %add_add_fusion.4), channel_id=1, source_target_pairs={{0,64},{4,68},{8,72},{12,76},{16,80},{20,84},{24,88},{28,92},{32,9... | collective-permute-start | bytes 200 | tf_op jit(solution)/shard_map/ppermute | solution.py:20
  (19 other events, 133.9 us)

commit v5 on v2

--- a/solution.py
+++ b/solution.py
@@ -1,6 +1,7 @@
 import jax
 import jax.numpy as jnp
 from jax import lax
+from jax.experimental.layout import Layout, with_layout_constraint
 from jax.sharding import PartitionSpec as P
 
 ITERS = 6
@@ -22,14 +23,16 @@
     size = lax.axis_size(axis)
     if size & (size - 1):
         return lax.psum(value, axis)
+    levels = size.bit_length() - 1
     bit = 1
-    while bit < size:
-        group = 8 if bit * 8 <= size and bit > 1 else min(4, size // bit)
-        got = [value] + [swapped(value, axis, bit * offset) for offset in range(1, group)]
-        while len(got) > 1:
-            got = [got[i] + got[i + 1] for i in range(0, len(got), 2)]
-        value = got[0]
-        bit *= group
+    if levels % 2:
+        value = value + swapped(value, axis, size // 2)
+    while bit * 4 <= size:
+        near = swapped(value, axis, bit)
+        mid = swapped(value, axis, 2 * bit)
+        far = swapped(value, axis, 3 * bit)
+        value = (value + near) + (mid + far)
+        bit *= 4
     return value
 
 
@@ -87,6 +90,7 @@
     miss_here = lax.dynamic_slice_in_dim(missing, position * columns, columns + half_cols)
     weight = jnp.sqrt((total - miss_here.astype(jnp.float32)) / total)
     stand = ((regionf - mean) / jnp.sqrt(var + 1e-05) * weight).astype(jnp.bfloat16)
+    stand = with_layout_constraint(stand, Layout(major_to_minor=(0, 1)))
 
     def project(basis):
         wide = widened(basis, half_cols)

time: 330 us -> 276 us (0.84)
  starting transfers between devices: 142 us -> 87.7 us
  waiting for transfers between devices: 81.9 us -> 103 us
  local copies, waits for them, and re-layouts: 23.5 us -> 4.49 us
    ppermute x80 -> x56, starting transfers between devices: 140 us -> 85.8 us  [swapped(): return lax.ppermute(value, axis, [(i, i ^ mask) for i in range(size)])]
    ppermute x80 -> x56, waiting for transfers between devices: 60.6 us -> 79.2 us  [swapped(): return lax.ppermute(value, axis, [(i, i ^ mask) for i in range(size)])]
    unnamed x14 -> x10, local copies, waits for them, and re-layouts: 10.5 us -> 1.56 us
    while x13 -> x12, local copies, waits for them, and re-layouts: 8.7 us -> 0.02 us  [the longest x1 8.68 us: shards(): lax.fori_loop(0, ITERS, lambda step, basis: orthonormal(image_of(basis)),...]
  transfers between devices with their start and end apart: 81 -> 57, of which waited for: 37 -> 45; matrix products, arithmetic and copies ran while one was open for 3% -> 2% of each run, Pallas kernels for 0% -> 0%
where the time goes in v5:
time: 276 us; the launch traced here: 275 us
  waiting for transfers between devices  103 us (37%)
  starting transfers between devices  87.7 us (32%)
  matrix products  47.9 us (17%)
  other arithmetic  30.8 us (11%)
  local copies, waits for them, and re-layouts  4.49 us (2%)
    ppermute x56, starting transfers between devices, swapped(): return lax.ppermute(value, axis, [(i, i ^ mask) for i in range(size)])  85.8 us
    ppermute x56, waiting for transfers between devices, swapped(): return lax.ppermute(value, axis, [(i, i ^ mask) for i in range(size)])  79.2 us
    dot_general x7, matrix products, project(): jnp.dot(stand, jnp.concatenate(pieces(wide), 1), preferred_element_type=j...  33.9 us
    ppermute x1, waiting for transfers between devices, passed_along(): return lax.ppermute(array, axis, pairs)  23.6 us
    another operation x24, other arithmetic, orthonormal(): factor = jnp.linalg.cholesky(gram)  9.75 us
    another operation x18, other arithmetic, orthonormal(): jax.scipy.linalg.solve_triangular(fac, rhs, lower=True)  8.03 us
    dot_general x6, matrix products, image_of(): lax.dot_general(stand, split, (((0,), (0,)), ((), ())), preferred_element...  6.76 us
    convert_element_type x1, other arithmetic, shards(): ((regionf - mean) / jnp.sqrt(var + 1e-05) * weight).astype(jnp.bfloat16)  6.38 us
  transfers between devices with their start and end apart: 57, of which 45 were waited for; matrix products, arithmetic and copies ran while one was open for 2% of the time, Pallas kernels for 0%

profile of v5, /device:TPU:32, one launch (start us, length us, event | category | flops | bytes accessed | tf_op | source)
XLA Modules:
  0.0 275.3 jit_solution(3619215989020650298)
XLA Ops:
  4.3 23.6 %collective-permute-done.7 = bf16[2048,512]{1,0:T(8,128)(2,1)} collective-permute-done((bf16[2048,512]{1,0:T(8,128)(2,1)S(1)}, bf16[2048,512]{1,0:T(8,128)(2,1)}, u32[]{:S(2)}, u32[]{:S(2)}) %collective-permute-start.7) | collective-permute-done | bytes 2097184 | tf_op jit(solution)/shard_map/ppermute | solution.py:14
  31.7 3.1 %collective-permute-start.8 = (f32[2,1536]{1,0:T(2,128)S(1)}, f32[2,1536]{1,0:T(2,128)S(1)}, u32[]{:S(2)}, u32[]{:S(2)}) collective-permute-start(f32[2,1536]{1,0:T(2,128)S(1)} %pad_maximum_fusion.2), channel_id=1, source_target_pairs={{0,64},{4,68},{8,72},{12,76},{16,80},{20,84},{24,88},{28,92},{32,9... | collective-permute-start | bytes 36872 | tf_op jit(solution)/shard_map/ppermute | solution.py:19
  37.0 3.3 %collective-permute-start.10 = (f32[2,1536]{1,0:T(2,128)S(1)}, f32[2,1536]{1,0:T(2,128)S(1)}, u32[]{:S(2)}, u32[]{:S(2)}) collective-permute-start(f32[2,1536]{1,0:T(2,128)S(1)} %fusion.36), channel_id=1, source_target_pairs={{0,8},{4,12},{8,0},{12,4},{16,24},{20,28},{24,16},{28,20},{32,40},... | collective-permute-start | bytes 36872 | tf_op jit(solution)/shard_map/ppermute | solution.py:19
  42.3 2.9 %collective-permute-done.11 = f32[2,1536]{1,0:T(2,128)S(1)} collective-permute-done((f32[2,1536]{1,0:T(2,128)S(1)}, f32[2,1536]{1,0:T(2,128)S(1)}, u32[]{:S(2)}, u32[]{:S(2)}) %collective-permute-start.11) | collective-permute-done | bytes 12320 | tf_op jit(solution)/shard_map/ppermute | solution.py:19
  46.8 2.7 collective-permute-start.13
  52.0 2.4 collective-permute-done.14
  54.5 6.4 %fusion.21 = bf16[2048,1536]{1,0:T(8,128)(2,1)} fusion(f32[1536]{0:T(1024)S(1)} %multiply_sqrt_fusion, f32[1536]{0:T(1024)S(1)} %get-tuple-element.26, f32[1536]{0:T(1024)S(1)} %get-tuple-element.25, bf16[2048,512]{1,0:T(8,128)(2,1)S(1)} %broadcast_select_fusion, bf16[2048,1024]{1,0:T(8,128)(2,1)} %param.6), kind=kLoop, calls=%fused_computation.54 | loop fusion | flops 25165824 | bytes 12601344 | tf_op jit(solution)/shard_map/convert_element_type | solution.py:92
  60.9 183.3 %while.10 = (s32[]{:T(128)}, f32[2,1024,8]{1,2,0:T(8,128)S(1)}, bf16[2048,1536]{1,0:T(8,128)(2,1)}, s32[]{:T(128)}) while((s32[]{:T(128)}, f32[2,1024,8]{1,2,0:T(8,128)S(1)}, bf16[2048,1536]{1,0:T(8,128)(2,1)}, s32[]{:T(128)}) %tuple.54), condition=%wide.region_5.6_spmd, body=%wide.region_2.5_spmd.sunk | while | flops 609027072 | bytes 43587304 | solution.py:106
  61.0 4.9 %convolution_bitcast_fusion.4 = f32[2048,48]{0,1:T(8,128)S(1)} fusion(bf16[2048,1536]{1,0:T(8,128)(2,1)} %get-tuple-element.114, bf16[1536,16]{0,1:T(8,128)(2,1)S(1)} %get-tuple-element.95, bf16[1536,16]{0,1:T(8,128)(2,1)S(1)} %get-tuple-element.96, bf16[1536,16]{0,1:T(8,128)(2,1)S(1)} %get-tuple-element.97), kind=kOutput, calls=%fused_computation.1.clone.1 | convolution fusion | flops 302432256 | bytes 6832128 | tf_op jit(solution)/shard_map/while/body/eval_jaxpr/dot_general | solution.py:97
  67.1 3.1 %collective-permute-start = (f32[2,1024,8]{1,2,0:T(8,128)S(1)}, f32[2,1024,8]{1,2,0:T(8,128)S(1)}, u32[]{:S(2)}, u32[]{:S(2)}) collective-permute-start(f32[2,1024,8]{1,2,0:T(8,128)S(1)} %pad_maximum_fusion.4), channel_id=1, source_target_pairs={{0,64},{4,68},{8,72},{12,76},{16,80},{20,84},{24,88},{28,92},{32,9... | collective-permute-start | bytes 196616 | tf_op jit(solution)/shard_map/while/body/eval_jaxpr/ppermute | solution.py:19
  70.2 2.8 %collective-permute-done = f32[2,1024,8]{1,2,0:T(8,128)S(1)} collective-permute-done((f32[2,1024,8]{1,2,0:T(8,128)S(1)}, f32[2,1024,8]{1,2,0:T(8,128)S(1)}, u32[]{:S(2)}, u32[]{:S(2)}) %collective-permute-start) | collective-permute-done | bytes 65568 | tf_op jit(solution)/shard_map/while/body/eval_jaxpr/ppermute | solution.py:19
  76.6 3.0 %collective-permute-done.1 = f32[2,1024,8]{1,2,0:T(8,128)S(1)} collective-permute-done((f32[2,1024,8]{1,2,0:T(8,128)S(1)}, f32[2,1024,8]{1,2,0:T(8,128)S(1)}, u32[]{:S(2)}, u32[]{:S(2)}) %collective-permute-start.1) | collective-permute-done | bytes 65568 | tf_op jit(solution)/shard_map/while/body/eval_jaxpr/ppermute | solution.py:19
  84.5 2.8 %collective-permute-done.4 = f32[2,1024,8]{1,2,0:T(8,128)S(1)} collective-permute-done((f32[2,1024,8]{1,2,0:T(8,128)S(1)}, f32[2,1024,8]{1,2,0:T(8,128)S(1)}, u32[]{:S(2)}, u32[]{:S(2)}) %collective-permute-start.4) | collective-permute-done | bytes 65568 | tf_op jit(solution)/shard_map/while/body/eval_jaxpr/ppermute | solution.py:19
  91.5 4.9 %convolution_bitcast_fusion.4 = f32[2048,48]{0,1:T(8,128)S(1)} fusion(bf16[2048,1536]{1,0:T(8,128)(2,1)} %get-tuple-element.114, bf16[1536,16]{0,1:T(8,128)(2,1)S(1)} %get-tuple-element.95, bf16[1536,16]{0,1:T(8,128)(2,1)S(1)} %get-tuple-element.96, bf16[1536,16]{0,1:T(8,128)(2,1)S(1)} %get-tuple-element.97), kind=kOutput, calls=%fused_computation.1.clone.1 | convolution fusion | flops 302432256 | bytes 6832128 | tf_op jit(solution)/shard_map/while/body/eval_jaxpr/dot_general | solution.py:97
  97.6 3.1 %collective-permute-start = (f32[2,1024,8]{1,2,0:T(8,128)S(1)}, f32[2,1024,8]{1,2,0:T(8,128)S(1)}, u32[]{:S(2)}, u32[]{:S(2)}) collective-permute-start(f32[2,1024,8]{1,2,0:T(8,128)S(1)} %pad_maximum_fusion.4), channel_id=1, source_target_pairs={{0,64},{4,68},{8,72},{12,76},{16,80},{20,84},{24,88},{28,92},{32,9... | collective-permute-start | bytes 196616 | tf_op jit(solution)/shard_map/while/body/eval_jaxpr/ppermute | solution.py:19
  100.7 2.8 %collective-permute-done = f32[2,1024,8]{1,2,0:T(8,128)S(1)} collective-permute-done((f32[2,1024,8]{1,2,0:T(8,128)S(1)}, f32[2,1024,8]{1,2,0:T(8,128)S(1)}, u32[]{:S(2)}, u32[]{:S(2)}) %collective-permute-start) | collective-permute-done | bytes 65568 | tf_op jit(solution)/shard_map/while/body/eval_jaxpr/ppermute | solution.py:19
  107.0 2.8 %collective-permute-done.1 = f32[2,1024,8]{1,2,0:T(8,128)S(1)} collective-permute-done((f32[2,1024,8]{1,2,0:T(8,128)S(1)}, f32[2,1024,8]{1,2,0:T(8,128)S(1)}, u32[]{:S(2)}, u32[]{:S(2)}) %collective-permute-start.1) | collective-permute-done | bytes 65568 | tf_op jit(solution)/shard_map/while/body/eval_jaxpr/ppermute | solution.py:19
  112.0 2.3 collective-permute-start.5
  114.4 2.3 collective-permute-done.4
  122.2 4.9 %convolution_bitcast_fusion.4 = f32[2048,48]{0,1:T(8,128)S(1)} fusion(bf16[2048,1536]{1,0:T(8,128)(2,1)} %get-tuple-element.114, bf16[1536,16]{0,1:T(8,128)(2,1)S(1)} %get-tuple-element.95, bf16[1536,16]{0,1:T(8,128)(2,1)S(1)} %get-tuple-element.96, bf16[1536,16]{0,1:T(8,128)(2,1)S(1)} %get-tuple-element.97), kind=kOutput, calls=%fused_computation.1.clone.1 | convolution fusion | flops 302432256 | bytes 6832128 | tf_op jit(solution)/shard_map/while/body/eval_jaxpr/dot_general | solution.py:97
  128.4 3.1 %collective-permute-start = (f32[2,1024,8]{1,2,0:T(8,128)S(1)}, f32[2,1024,8]{1,2,0:T(8,128)S(1)}, u32[]{:S(2)}, u32[]{:S(2)}) collective-permute-start(f32[2,1024,8]{1,2,0:T(8,128)S(1)} %pad_maximum_fusion.4), channel_id=1, source_target_pairs={{0,64},{4,68},{8,72},{12,76},{16,80},{20,84},{24,88},{28,92},{32,9... | collective-permute-start | bytes 196616 | tf_op jit(solution)/shard_map/while/body/eval_jaxpr/ppermute | solution.py:19
  131.4 2.8 %collective-permute-done = f32[2,1024,8]{1,2,0:T(8,128)S(1)} collective-permute-done((f32[2,1024,8]{1,2,0:T(8,128)S(1)}, f32[2,1024,8]{1,2,0:T(8,128)S(1)}, u32[]{:S(2)}, u32[]{:S(2)}) %collective-permute-start) | collective-permute-done | bytes 65568 | tf_op jit(solution)/shard_map/while/body/eval_jaxpr/ppermute | solution.py:19
  134.2 2.2 collective-permute-start.1
  137.8 2.3 collective-permute-done.1
  142.3 2.4 collective-permute-start.5
  145.5 2.4 collective-permute-done.4
  152.6 4.9 %convolution_bitcast_fusion.4 = f32[2048,48]{0,1:T(8,128)S(1)} fusion(bf16[2048,1536]{1,0:T(8,128)(2,1)} %get-tuple-element.114, bf16[1536,16]{0,1:T(8,128)(2,1)S(1)} %get-tuple-element.95, bf16[1536,16]{0,1:T(8,128)(2,1)S(1)} %get-tuple-element.96, bf16[1536,16]{0,1:T(8,128)(2,1)S(1)} %get-tuple-element.97), kind=kOutput, calls=%fused_computation.1.clone.1 | convolution fusion | flops 302432256 | bytes 6832128 | tf_op jit(solution)/shard_map/while/body/eval_jaxpr/dot_general | solution.py:97
  158.8 3.1 %collective-permute-start = (f32[2,1024,8]{1,2,0:T(8,128)S(1)}, f32[2,1024,8]{1,2,0:T(8,128)S(1)}, u32[]{:S(2)}, u32[]{:S(2)}) collective-permute-start(f32[2,1024,8]{1,2,0:T(8,128)S(1)} %pad_maximum_fusion.4), channel_id=1, source_target_pairs={{0,64},{4,68},{8,72},{12,76},{16,80},{20,84},{24,88},{28,92},{32,9... | collective-permute-start | bytes 196616 | tf_op jit(solution)/shard_map/while/body/eval_jaxpr/ppermute | solution.py:19
  161.8 2.8 %collective-permute-done = f32[2,1024,8]{1,2,0:T(8,128)S(1)} collective-permute-done((f32[2,1024,8]{1,2,0:T(8,128)S(1)}, f32[2,1024,8]{1,2,0:T(8,128)S(1)}, u32[]{:S(2)}, u32[]{:S(2)}) %collective-permute-start) | collective-permute-done | bytes 65568 | tf_op jit(solution)/shard_map/while/body/eval_jaxpr/ppermute | solution.py:19
  168.2 2.3 collective-permute-done.1
  175.4 2.3 collective-permute-done.4
  183.3 4.9 %convolution_bitcast_fusion.4 = f32[2048,48]{0,1:T(8,128)S(1)} fusion(bf16[2048,1536]{1,0:T(8,128)(2,1)} %get-tuple-element.114, bf16[1536,16]{0,1:T(8,128)(2,1)S(1)} %get-tuple-element.95, bf16[1536,16]{0,1:T(8,128)(2,1)S(1)} %get-tuple-element.96, bf16[1536,16]{0,1:T(8,128)(2,1)S(1)} %get-tuple-element.97), kind=kOutput, calls=%fused_computation.1.clone.1 | convolution fusion | flops 302432256 | bytes 6832128 | tf_op jit(solution)/shard_map/while/body/eval_jaxpr/dot_general | solution.py:97
  189.4 3.1 %collective-permute-start = (f32[2,1024,8]{1,2,0:T(8,128)S(1)}, f32[2,1024,8]{1,2,0:T(8,128)S(1)}, u32[]{:S(2)}, u32[]{:S(2)}) collective-permute-start(f32[2,1024,8]{1,2,0:T(8,128)S(1)} %pad_maximum_fusion.4), channel_id=1, source_target_pairs={{0,64},{4,68},{8,72},{12,76},{16,80},{20,84},{24,88},{28,92},{32,9... | collective-permute-start | bytes 196616 | tf_op jit(solution)/shard_map/while/body/eval_jaxpr/ppermute | solution.py:19
  192.5 2.8 %collective-permute-done = f32[2,1024,8]{1,2,0:T(8,128)S(1)} collective-permute-done((f32[2,1024,8]{1,2,0:T(8,128)S(1)}, f32[2,1024,8]{1,2,0:T(8,128)S(1)}, u32[]{:S(2)}, u32[]{:S(2)}) %collective-permute-start) | collective-permute-done | bytes 65568 | tf_op jit(solution)/shard_map/while/body/eval_jaxpr/ppermute | solution.py:19
  198.8 2.3 collective-permute-done.1
  206.6 2.3 collective-permute-done.4
  213.7 4.9 %convolution_bitcast_fusion.4 = f32[2048,48]{0,1:T(8,128)S(1)} fusion(bf16[2048,1536]{1,0:T(8,128)(2,1)} %get-tuple-element.114, bf16[1536,16]{0,1:T(8,128)(2,1)S(1)} %get-tuple-element.95, bf16[1536,16]{0,1:T(8,128)(2,1)S(1)} %get-tuple-element.96, bf16[1536,16]{0,1:T(8,128)(2,1)S(1)} %get-tuple-element.97), kind=kOutput, calls=%fused_computation.1.clone.1 | convolution fusion | flops 302432256 | bytes 6832128 | tf_op jit(solution)/shard_map/while/body/eval_jaxpr/dot_general | solution.py:97
  219.8 3.1 %collective-permute-start = (f32[2,1024,8]{1,2,0:T(8,128)S(1)}, f32[2,1024,8]{1,2,0:T(8,128)S(1)}, u32[]{:S(2)}, u32[]{:S(2)}) collective-permute-start(f32[2,1024,8]{1,2,0:T(8,128)S(1)} %pad_maximum_fusion.4), channel_id=1, source_target_pairs={{0,64},{4,68},{8,72},{12,76},{16,80},{20,84},{24,88},{28,92},{32,9... | collective-permute-start | bytes 196616 | tf_op jit(solution)/shard_map/while/body/eval_jaxpr/ppermute | solution.py:19
  222.9 2.8 %collective-permute-done = f32[2,1024,8]{1,2,0:T(8,128)S(1)} collective-permute-done((f32[2,1024,8]{1,2,0:T(8,128)S(1)}, f32[2,1024,8]{1,2,0:T(8,128)S(1)}, u32[]{:S(2)}, u32[]{:S(2)}) %collective-permute-start) | collective-permute-done | bytes 65568 | tf_op jit(solution)/shard_map/while/body/eval_jaxpr/ppermute | solution.py:19
  229.3 2.3 collective-permute-done.1
  236.5 2.3 collective-permute-done.4
  244.3 4.7 %fusion.22 = f32[2048,48]{0,1:T(8,128)S(1)} fusion(bf16[2048,1536]{1,0:T(8,128)(2,1)} %get-tuple-element.116, bf16[1536,16]{0,1:T(8,128)(2,1)S(1)} %get-tuple-element.60, bf16[1536,16]{0,1:T(8,128)(2,1)S(1)} %get-tuple-element.59, bf16[1536,16]{0,1:T(8,128)(2,1)S(1)} %get-tuple-element.58), kind=kOutput, calls=%fused_computation.59 | convolution fusion | flops 302432256 | bytes 6832128 | tf_op jit(solution)/shard_map/dot_general | solution.py:97
  249.4 3.1 %collective-permute-start.15 = (f32[16]{0:T(128)S(1)}, f32[16]{0:T(128)S(1)}, u32[]{:S(2)}, u32[]{:S(2)}) collective-permute-start(f32[16]{0:T(128)S(1)} %get-tuple-element.35), channel_id=1, source_target_pairs={{0,64},{4,68},{8,72},{12,76},{16,80},{20,84},{24,88},{28,92},{32,9... | collective-permute-start | bytes 200 | tf_op jit(solution)/shard_map/ppermute | solution.py:19
  255.3 3.0 %multiply_reduce_fusion.1 = (f32[2048]{0:T(1024)S(1)}, f32[2048]{0:T(1024)S(1)}) fusion(bf16[2048,1536]{1,0:T(8,128)(2,1)S(1)} %bitcast.89, f32[2048,1024]{1,0:T(8,128)S(1)} %fusion.38, bf16[2048,48]{0,1:T(8,128)(2,1)S(1)} %constant_dynamic-update-slice_fusion, bf16[1024,48]{0,1:T(8,128)(2,1)S(1)} %get-tuple-element.49), kind=kOutput, calls=%fused_computation.56 | convolution fusion | flops 218099712 | bytes 17088512 | tf_op jit(solution)/shard_map/dot_general | solution.py:66
  259.7 2.8 %collective-permute-start.17 = (f32[16]{0:T(128)S(1)}, f32[16]{0:T(128)S(1)}, u32[]{:S(2)}, u32[]{:S(2)}) collective-permute-start(f32[16]{0:T(128)S(1)} %add.126), channel_id=1, source_target_pairs={{0,8},{4,12},{8,0},{12,4},{16,24},{20,28},{24,16},{28,20},{32,40},... | collective-permute-start | bytes 200 | tf_op jit(solution)/shard_map/ppermute | solution.py:19
  264.7 2.5 collective-permute-done.18
  267.3 2.6 collective-permute-start.20
  272.4 2.3 collective-permute-done.21
  (269 shorter events, 107.8 us)
Async XLA Ops:
  2.4 25.6 %collective-permute-start.7 = (bf16[2048,512]{1,0:T(8,128)(2,1)S(1)}, bf16[2048,512]{1,0:T(8,128)(2,1)}, u32[]{:S(2)}, u32[]{:S(2)}) collective-permute-start(bf16[2048,512]{1,0:T(8,128)(2,1)S(1)} %slice.80), channel_id=1, source_target_pairs={{1,0},{2,1},{3,2},{5,4},{6,5},{7,6},{9,8},{10,9},{11,10},{13,12},{... | collective-permute-start | bytes 6291464 | tf_op jit(solution)/shard_map/ppermute | solution.py:14
  31.7 5.3 %collective-permute-start.8 = (f32[2,1536]{1,0:T(2,128)S(1)}, f32[2,1536]{1,0:T(2,128)S(1)}, u32[]{:S(2)}, u32[]{:S(2)}) collective-permute-start(f32[2,1536]{1,0:T(2,128)S(1)} %pad_maximum_fusion.2), channel_id=1, source_target_pairs={{0,64},{4,68},{8,72},{12,76},{16,80},{20,84},{24,88},{28,92},{32,9... | collective-permute-start | bytes 36872 | tf_op jit(solution)/shard_map/ppermute | solution.py:19
  37.0 5.3 %collective-permute-start.10 = (f32[2,1536]{1,0:T(2,128)S(1)}, f32[2,1536]{1,0:T(2,128)S(1)}, u32[]{:S(2)}, u32[]{:S(2)}) collective-permute-start(f32[2,1536]{1,0:T(2,128)S(1)} %fusion.36), channel_id=1, source_target_pairs={{0,8},{4,12},{8,0},{12,4},{16,24},{20,28},{24,16},{28,20},{32,40},... | collective-permute-start | bytes 36872 | tf_op jit(solution)/shard_map/ppermute | solution.py:19
  40.3 4.9 %collective-permute-start.11 = (f32[2,1536]{1,0:T(2,128)S(1)}, f32[2,1536]{1,0:T(2,128)S(1)}, u32[]{:S(2)}, u32[]{:S(2)}) collective-permute-start(f32[2,1536]{1,0:T(2,128)S(1)} %fusion.36), channel_id=1, source_target_pairs={{0,12},{4,8},{8,4},{12,0},{16,28},{20,24},{24,20},{28,16},{32,44},... | collective-permute-start | bytes 36872 | tf_op jit(solution)/shard_map/ppermute | solution.py:19
  45.2 5.6 %collective-permute-start.12 = (f32[2,1536]{1,0:T(2,128)S(1)}, f32[2,1536]{1,0:T(2,128)S(1)}, u32[]{:S(2)}, u32[]{:S(2)}) collective-permute-start(f32[2,1536]{1,0:T(2,128)S(1)} %add_add_fusion.2), channel_id=1, source_target_pairs={{0,16},{4,20},{8,24},{12,28},{16,0},{20,4},{24,8},{28,12},{32,48},... | collective-permute-start | bytes 36872 | tf_op jit(solution)/shard_map/ppermute | solution.py:19
  46.8 5.2 %collective-permute-start.13 = (f32[2,1536]{1,0:T(2,128)S(1)}, f32[2,1536]{1,0:T(2,128)S(1)}, u32[]{:S(2)}, u32[]{:S(2)}) collective-permute-start(f32[2,1536]{1,0:T(2,128)S(1)} %add_add_fusion.2), channel_id=1, source_target_pairs={{0,32},{4,36},{8,40},{12,44},{16,48},{20,52},{24,56},{28,60},{32,0... | collective-permute-start | bytes 36872 | tf_op jit(solution)/shard_map/ppermute | solution.py:19
  49.5 4.9 %collective-permute-start.14 = (f32[2,1536]{1,0:T(2,128)S(1)}, f32[2,1536]{1,0:T(2,128)S(1)}, u32[]{:S(2)}, u32[]{:S(2)}) collective-permute-start(f32[2,1536]{1,0:T(2,128)S(1)} %add_add_fusion.2), channel_id=1, source_target_pairs={{0,48},{4,52},{8,56},{12,60},{16,32},{20,36},{24,40},{28,44},{32,1... | collective-permute-start | bytes 36872 | tf_op jit(solution)/shard_map/ppermute | solution.py:19
  67.1 5.8 %collective-permute-start = (f32[2,1024,8]{1,2,0:T(8,128)S(1)}, f32[2,1024,8]{1,2,0:T(8,128)S(1)}, u32[]{:S(2)}, u32[]{:S(2)}) collective-permute-start(f32[2,1024,8]{1,2,0:T(8,128)S(1)} %pad_maximum_fusion.4), channel_id=1, source_target_pairs={{0,64},{4,68},{8,72},{12,76},{16,80},{20,84},{24,88},{28,92},{32,9... | collective-permute-start | bytes 196616 | tf_op jit(solution)/shard_map/while/body/eval_jaxpr/ppermute | solution.py:19
  73.0 6.5 %collective-permute-start.1 = (f32[2,1024,8]{1,2,0:T(8,128)S(1)}, f32[2,1024,8]{1,2,0:T(8,128)S(1)}, u32[]{:S(2)}, u32[]{:S(2)}) collective-permute-start(f32[2,1024,8]{1,2,0:T(8,128)S(1)} %fusion.69), channel_id=1, source_target_pairs={{0,8},{4,12},{8,0},{12,4},{16,24},{20,28},{24,16},{28,20},{32,40},... | collective-permute-start | bytes 196616 | tf_op jit(solution)/shard_map/while/body/eval_jaxpr/ppermute | solution.py:19
  74.6 6.3 %collective-permute-start.2 = (f32[2,1024,8]{1,2,0:T(8,128)S(1)}, f32[2,1024,8]{1,2,0:T(8,128)S(1)}, u32[]{:S(2)}, u32[]{:S(2)}) collective-permute-start(f32[2,1024,8]{1,2,0:T(8,128)S(1)} %fusion.69), channel_id=1, source_target_pairs={{0,12},{4,8},{8,4},{12,0},{16,28},{20,24},{24,20},{28,16},{32,44},... | collective-permute-start | bytes 196616 | tf_op jit(solution)/shard_map/while/body/eval_jaxpr/ppermute | solution.py:19
  75.6 5.3 %collective-permute-start.3 = (f32[2,1024,8]{1,2,0:T(8,128)S(1)}, f32[2,1024,8]{1,2,0:T(8,128)S(1)}, u32[]{:S(2)}, u32[]{:S(2)}) collective-permute-start(f32[2,1024,8]{1,2,0:T(8,128)S(1)} %fusion.69), channel_id=1, source_target_pairs={{0,4},{4,0},{8,12},{12,8},{16,20},{20,16},{24,28},{28,24},{32,36},... | collective-permute-start | bytes 196616 | tf_op jit(solution)/shard_map/while/body/eval_jaxpr/ppermute | solution.py:19
  80.9 6.4 %collective-permute-start.4 = (f32[2,1024,8]{1,2,0:T(8,128)S(1)}, f32[2,1024,8]{1,2,0:T(8,128)S(1)}, u32[]{:S(2)}, u32[]{:S(2)}) collective-permute-start(f32[2,1024,8]{1,2,0:T(8,128)S(1)} %add_add_fusion.5), channel_id=1, source_target_pairs={{0,32},{4,36},{8,40},{12,44},{16,48},{20,52},{24,56},{28,60},{32,0... | collective-permute-start | bytes 196616 | tf_op jit(solution)/shard_map/while/body/eval_jaxpr/ppermute | solution.py:19
  81.0 6.8 %collective-permute-start.5 = (f32[2,1024,8]{1,2,0:T(8,128)S(1)}, f32[2,1024,8]{1,2,0:T(8,128)S(1)}, u32[]{:S(2)}, u32[]{:S(2)}) collective-permute-start(f32[2,1024,8]{1,2,0:T(8,128)S(1)} %add_add_fusion.5), channel_id=1, source_target_pairs={{0,48},{4,52},{8,56},{12,60},{16,32},{20,36},{24,40},{28,44},{32,1... | collective-permute-start | bytes 196616 | tf_op jit(solution)/shard_map/while/body/eval_jaxpr/ppermute | solution.py:19
  82.6 5.3 %collective-permute-start.6 = (f32[2,1024,8]{1,2,0:T(8,128)S(1)}, f32[2,1024,8]{1,2,0:T(8,128)S(1)}, u32[]{:S(2)}, u32[]{:S(2)}) collective-permute-start(f32[2,1024,8]{1,2,0:T(8,128)S(1)} %add_add_fusion.5), channel_id=1, source_target_pairs={{0,16},{4,20},{8,24},{12,28},{16,0},{20,4},{24,8},{28,12},{32,48},... | collective-permute-start | bytes 196616 | tf_op jit(solution)/shard_map/while/body/eval_jaxpr/ppermute | solution.py:19
  97.6 5.8 %collective-permute-start = (f32[2,1024,8]{1,2,0:T(8,128)S(1)}, f32[2,1024,8]{1,2,0:T(8,128)S(1)}, u32[]{:S(2)}, u32[]{:S(2)}) collective-permute-start(f32[2,1024,8]{1,2,0:T(8,128)S(1)} %pad_maximum_fusion.4), channel_id=1, source_target_pairs={{0,64},{4,68},{8,72},{12,76},{16,80},{20,84},{24,88},{28,92},{32,9... | collective-permute-start | bytes 196616 | tf_op jit(solution)/shard_map/while/body/eval_jaxpr/ppermute | solution.py:19
  103.5 6.4 %collective-permute-start.1 = (f32[2,1024,8]{1,2,0:T(8,128)S(1)}, f32[2,1024,8]{1,2,0:T(8,128)S(1)}, u32[]{:S(2)}, u32[]{:S(2)}) collective-permute-start(f32[2,1024,8]{1,2,0:T(8,128)S(1)} %fusion.69), channel_id=1, source_target_pairs={{0,8},{4,12},{8,0},{12,4},{16,24},{20,28},{24,16},{28,20},{32,40},... | collective-permute-start | bytes 196616 | tf_op jit(solution)/shard_map/while/body/eval_jaxpr/ppermute | solution.py:19
  105.3 5.5 %collective-permute-start.2 = (f32[2,1024,8]{1,2,0:T(8,128)S(1)}, f32[2,1024,8]{1,2,0:T(8,128)S(1)}, u32[]{:S(2)}, u32[]{:S(2)}) collective-permute-start(f32[2,1024,8]{1,2,0:T(8,128)S(1)} %fusion.69), channel_id=1, source_target_pairs={{0,12},{4,8},{8,4},{12,0},{16,28},{20,24},{24,20},{28,16},{32,44},... | collective-permute-start | bytes 196616 | tf_op jit(solution)/shard_map/while/body/eval_jaxpr/ppermute | solution.py:19
  106.2 4.6 %collective-permute-start.3 = (f32[2,1024,8]{1,2,0:T(8,128)S(1)}, f32[2,1024,8]{1,2,0:T(8,128)S(1)}, u32[]{:S(2)}, u32[]{:S(2)}) collective-permute-start(f32[2,1024,8]{1,2,0:T(8,128)S(1)} %fusion.69), channel_id=1, source_target_pairs={{0,4},{4,0},{8,12},{12,8},{16,20},{20,16},{24,28},{28,24},{32,36},... | collective-permute-start | bytes 196616 | tf_op jit(solution)/shard_map/while/body/eval_jaxpr/ppermute | solution.py:19
  110.8 5.8 %collective-permute-start.4 = (f32[2,1024,8]{1,2,0:T(8,128)S(1)}, f32[2,1024,8]{1,2,0:T(8,128)S(1)}, u32[]{:S(2)}, u32[]{:S(2)}) collective-permute-start(f32[2,1024,8]{1,2,0:T(8,128)S(1)} %add_add_fusion.5), channel_id=1, source_target_pairs={{0,32},{4,36},{8,40},{12,44},{16,48},{20,52},{24,56},{28,60},{32,0... | collective-permute-start | bytes 196616 | tf_op jit(solution)/shard_map/while/body/eval_jaxpr/ppermute | solution.py:19
  112.0 5.5 %collective-permute-start.5 = (f32[2,1024,8]{1,2,0:T(8,128)S(1)}, f32[2,1024,8]{1,2,0:T(8,128)S(1)}, u32[]{:S(2)}, u32[]{:S(2)}) collective-permute-start(f32[2,1024,8]{1,2,0:T(8,128)S(1)} %add_add_fusion.5), channel_id=1, source_target_pairs={{0,48},{4,52},{8,56},{12,60},{16,32},{20,36},{24,40},{28,44},{32,1... | collective-permute-start | bytes 196616 | tf_op jit(solution)/shard_map/while/body/eval_jaxpr/ppermute | solution.py:19
  128.4 5.8 %collective-permute-start = (f32[2,1024,8]{1,2,0:T(8,128)S(1)}, f32[2,1024,8]{1,2,0:T(8,128)S(1)}, u32[]{:S(2)}, u32[]{:S(2)}) collective-permute-start(f32[2,1024,8]{1,2,0:T(8,128)S(1)} %pad_maximum_fusion.4), channel_id=1, source_target_pairs={{0,64},{4,68},{8,72},{12,76},{16,80},{20,84},{24,88},{28,92},{32,9... | collective-permute-start | bytes 196616 | tf_op jit(solution)/shard_map/while/body/eval_jaxpr/ppermute | solution.py:19
  134.2 5.8 %collective-permute-start.1 = (f32[2,1024,8]{1,2,0:T(8,128)S(1)}, f32[2,1024,8]{1,2,0:T(8,128)S(1)}, u32[]{:S(2)}, u32[]{:S(2)}) collective-permute-start(f32[2,1024,8]{1,2,0:T(8,128)S(1)} %fusion.69), channel_id=1, source_target_pairs={{0,8},{4,12},{8,0},{12,4},{16,24},{20,28},{24,16},{28,20},{32,40},... | collective-permute-start | bytes 196616 | tf_op jit(solution)/shard_map/while/body/eval_jaxpr/ppermute | solution.py:19
  136.5 5.5 %collective-permute-start.2 = (f32[2,1024,8]{1,2,0:T(8,128)S(1)}, f32[2,1024,8]{1,2,0:T(8,128)S(1)}, u32[]{:S(2)}, u32[]{:S(2)}) collective-permute-start(f32[2,1024,8]{1,2,0:T(8,128)S(1)} %fusion.69), channel_id=1, source_target_pairs={{0,12},{4,8},{8,4},{12,0},{16,28},{20,24},{24,20},{28,16},{32,44},... | collective-permute-start | bytes 196616 | tf_op jit(solution)/shard_map/while/body/eval_jaxpr/ppermute | solution.py:19
  137.7 4.3 %collective-permute-start.3 = (f32[2,1024,8]{1,2,0:T(8,128)S(1)}, f32[2,1024,8]{1,2,0:T(8,128)S(1)}, u32[]{:S(2)}, u32[]{:S(2)}) collective-permute-start(f32[2,1024,8]{1,2,0:T(8,128)S(1)} %fusion.69), channel_id=1, source_target_pairs={{0,4},{4,0},{8,12},{12,8},{16,20},{20,16},{24,28},{28,24},{32,36},... | collective-permute-start | bytes 196616 | tf_op jit(solution)/shard_map/while/body/eval_jaxpr/ppermute | solution.py:19
  142.0 6.0 %collective-permute-start.4 = (f32[2,1024,8]{1,2,0:T(8,128)S(1)}, f32[2,1024,8]{1,2,0:T(8,128)S(1)}, u32[]{:S(2)}, u32[]{:S(2)}) collective-permute-start(f32[2,1024,8]{1,2,0:T(8,128)S(1)} %add_add_fusion.5), channel_id=1, source_target_pairs={{0,32},{4,36},{8,40},{12,44},{16,48},{20,52},{24,56},{28,60},{32,0... | collective-permute-start | bytes 196616 | tf_op jit(solution)/shard_map/while/body/eval_jaxpr/ppermute | solution.py:19
  142.3 6.2 %collective-permute-start.5 = (f32[2,1024,8]{1,2,0:T(8,128)S(1)}, f32[2,1024,8]{1,2,0:T(8,128)S(1)}, u32[]{:S(2)}, u32[]{:S(2)}) collective-permute-start(f32[2,1024,8]{1,2,0:T(8,128)S(1)} %add_add_fusion.5), channel_id=1, source_target_pairs={{0,48},{4,52},{8,56},{12,60},{16,32},{20,36},{24,40},{28,44},{32,1... | collective-permute-start | bytes 196616 | tf_op jit(solution)/shard_map/while/body/eval_jaxpr/ppermute | solution.py:19
  158.8 5.8 %collective-permute-start = (f32[2,1024,8]{1,2,0:T(8,128)S(1)}, f32[2,1024,8]{1,2,0:T(8,128)S(1)}, u32[]{:S(2)}, u32[]{:S(2)}) collective-permute-start(f32[2,1024,8]{1,2,0:T(8,128)S(1)} %pad_maximum_fusion.4), channel_id=1, source_target_pairs={{0,64},{4,68},{8,72},{12,76},{16,80},{20,84},{24,88},{28,92},{32,9... | collective-permute-start | bytes 196616 | tf_op jit(solution)/shard_map/while/body/eval_jaxpr/ppermute | solution.py:19
  164.6 5.8 %collective-permute-start.1 = (f32[2,1024,8]{1,2,0:T(8,128)S(1)}, f32[2,1024,8]{1,2,0:T(8,128)S(1)}, u32[]{:S(2)}, u32[]{:S(2)}) collective-permute-start(f32[2,1024,8]{1,2,0:T(8,128)S(1)} %fusion.69), channel_id=1, source_target_pairs={{0,8},{4,12},{8,0},{12,4},{16,24},{20,28},{24,16},{28,20},{32,40},... | collective-permute-start | bytes 196616 | tf_op jit(solution)/shard_map/while/body/eval_jaxpr/ppermute | solution.py:19
  166.3 5.5 %collective-permute-start.2 = (f32[2,1024,8]{1,2,0:T(8,128)S(1)}, f32[2,1024,8]{1,2,0:T(8,128)S(1)}, u32[]{:S(2)}, u32[]{:S(2)}) collective-permute-start(f32[2,1024,8]{1,2,0:T(8,128)S(1)} %fusion.69), channel_id=1, source_target_pairs={{0,12},{4,8},{8,4},{12,0},{16,28},{20,24},{24,20},{28,16},{32,44},... | collective-permute-start | bytes 196616 | tf_op jit(solution)/shard_map/while/body/eval_jaxpr/ppermute | solution.py:19
  171.8 5.8 %collective-permute-start.4 = (f32[2,1024,8]{1,2,0:T(8,128)S(1)}, f32[2,1024,8]{1,2,0:T(8,128)S(1)}, u32[]{:S(2)}, u32[]{:S(2)}) collective-permute-start(f32[2,1024,8]{1,2,0:T(8,128)S(1)} %add_add_fusion.5), channel_id=1, source_target_pairs={{0,32},{4,36},{8,40},{12,44},{16,48},{20,52},{24,56},{28,60},{32,0... | collective-permute-start | bytes 196616 | tf_op jit(solution)/shard_map/while/body/eval_jaxpr/ppermute | solution.py:19
  173.3 5.5 %collective-permute-start.5 = (f32[2,1024,8]{1,2,0:T(8,128)S(1)}, f32[2,1024,8]{1,2,0:T(8,128)S(1)}, u32[]{:S(2)}, u32[]{:S(2)}) collective-permute-start(f32[2,1024,8]{1,2,0:T(8,128)S(1)} %add_add_fusion.5), channel_id=1, source_target_pairs={{0,48},{4,52},{8,56},{12,60},{16,32},{20,36},{24,40},{28,44},{32,1... | collective-permute-start | bytes 196616 | tf_op jit(solution)/shard_map/while/body/eval_jaxpr/ppermute | solution.py:19
  189.4 5.8 %collective-permute-start = (f32[2,1024,8]{1,2,0:T(8,128)S(1)}, f32[2,1024,8]{1,2,0:T(8,128)S(1)}, u32[]{:S(2)}, u32[]{:S(2)}) collective-permute-start(f32[2,1024,8]{1,2,0:T(8,128)S(1)} %pad_maximum_fusion.4), channel_id=1, source_target_pairs={{0,64},{4,68},{8,72},{12,76},{16,80},{20,84},{24,88},{28,92},{32,9... | collective-permute-start | bytes 196616 | tf_op jit(solution)/shard_map/while/body/eval_jaxpr/ppermute | solution.py:19
  195.3 5.8 %collective-permute-start.1 = (f32[2,1024,8]{1,2,0:T(8,128)S(1)}, f32[2,1024,8]{1,2,0:T(8,128)S(1)}, u32[]{:S(2)}, u32[]{:S(2)}) collective-permute-start(f32[2,1024,8]{1,2,0:T(8,128)S(1)} %fusion.69), channel_id=1, source_target_pairs={{0,8},{4,12},{8,0},{12,4},{16,24},{20,28},{24,16},{28,20},{32,40},... | collective-permute-start | bytes 196616 | tf_op jit(solution)/shard_map/while/body/eval_jaxpr/ppermute | solution.py:19
  197.5 5.5 %collective-permute-start.2 = (f32[2,1024,8]{1,2,0:T(8,128)S(1)}, f32[2,1024,8]{1,2,0:T(8,128)S(1)}, u32[]{:S(2)}, u32[]{:S(2)}) collective-permute-start(f32[2,1024,8]{1,2,0:T(8,128)S(1)} %fusion.69), channel_id=1, source_target_pairs={{0,12},{4,8},{8,4},{12,0},{16,28},{20,24},{24,20},{28,16},{32,44},... | collective-permute-start | bytes 196616 | tf_op jit(solution)/shard_map/while/body/eval_jaxpr/ppermute | solution.py:19
  203.0 5.9 %collective-permute-start.4 = (f32[2,1024,8]{1,2,0:T(8,128)S(1)}, f32[2,1024,8]{1,2,0:T(8,128)S(1)}, u32[]{:S(2)}, u32[]{:S(2)}) collective-permute-start(f32[2,1024,8]{1,2,0:T(8,128)S(1)} %add_add_fusion.5), channel_id=1, source_target_pairs={{0,32},{4,36},{8,40},{12,44},{16,48},{20,52},{24,56},{28,60},{32,0... | collective-permute-start | bytes 196616 | tf_op jit(solution)/shard_map/while/body/eval_jaxpr/ppermute | solution.py:19
  203.8 5.8 %collective-permute-start.5 = (f32[2,1024,8]{1,2,0:T(8,128)S(1)}, f32[2,1024,8]{1,2,0:T(8,128)S(1)}, u32[]{:S(2)}, u32[]{:S(2)}) collective-permute-start(f32[2,1024,8]{1,2,0:T(8,128)S(1)} %add_add_fusion.5), channel_id=1, source_target_pairs={{0,48},{4,52},{8,56},{12,60},{16,32},{20,36},{24,40},{28,44},{32,1... | collective-permute-start | bytes 196616 | tf_op jit(solution)/shard_map/while/body/eval_jaxpr/ppermute | solution.py:19
  219.8 5.8 %collective-permute-start = (f32[2,1024,8]{1,2,0:T(8,128)S(1)}, f32[2,1024,8]{1,2,0:T(8,128)S(1)}, u32[]{:S(2)}, u32[]{:S(2)}) collective-permute-start(f32[2,1024,8]{1,2,0:T(8,128)S(1)} %pad_maximum_fusion.4), channel_id=1, source_target_pairs={{0,64},{4,68},{8,72},{12,76},{16,80},{20,84},{24,88},{28,92},{32,9... | collective-permute-start | bytes 196616 | tf_op jit(solution)/shard_map/while/body/eval_jaxpr/ppermute | solution.py:19
  225.7 5.8 %collective-permute-start.1 = (f32[2,1024,8]{1,2,0:T(8,128)S(1)}, f32[2,1024,8]{1,2,0:T(8,128)S(1)}, u32[]{:S(2)}, u32[]{:S(2)}) collective-permute-start(f32[2,1024,8]{1,2,0:T(8,128)S(1)} %fusion.69), channel_id=1, source_target_pairs={{0,8},{4,12},{8,0},{12,4},{16,24},{20,28},{24,16},{28,20},{32,40},... | collective-permute-start | bytes 196616 | tf_op jit(solution)/shard_map/while/body/eval_jaxpr/ppermute | solution.py:19
  227.4 5.5 %collective-permute-start.2 = (f32[2,1024,8]{1,2,0:T(8,128)S(1)}, f32[2,1024,8]{1,2,0:T(8,128)S(1)}, u32[]{:S(2)}, u32[]{:S(2)}) collective-permute-start(f32[2,1024,8]{1,2,0:T(8,128)S(1)} %fusion.69), channel_id=1, source_target_pairs={{0,12},{4,8},{8,4},{12,0},{16,28},{20,24},{24,20},{28,16},{32,44},... | collective-permute-start | bytes 196616 | tf_op jit(solution)/shard_map/while/body/eval_jaxpr/ppermute | solution.py:19
  232.9 5.8 %collective-permute-start.4 = (f32[2,1024,8]{1,2,0:T(8,128)S(1)}, f32[2,1024,8]{1,2,0:T(8,128)S(1)}, u32[]{:S(2)}, u32[]{:S(2)}) collective-permute-start(f32[2,1024,8]{1,2,0:T(8,128)S(1)} %add_add_fusion.5), channel_id=1, source_target_pairs={{0,32},{4,36},{8,40},{12,44},{16,48},{20,52},{24,56},{28,60},{32,0... | collective-permute-start | bytes 196616 | tf_op jit(solution)/shard_map/while/body/eval_jaxpr/ppermute | solution.py:19
  234.4 5.5 %collective-permute-start.5 = (f32[2,1024,8]{1,2,0:T(8,128)S(1)}, f32[2,1024,8]{1,2,0:T(8,128)S(1)}, u32[]{:S(2)}, u32[]{:S(2)}) collective-permute-start(f32[2,1024,8]{1,2,0:T(8,128)S(1)} %add_add_fusion.5), channel_id=1, source_target_pairs={{0,48},{4,52},{8,56},{12,60},{16,32},{20,36},{24,40},{28,44},{32,1... | collective-permute-start | bytes 196616 | tf_op jit(solution)/shard_map/while/body/eval_jaxpr/ppermute | solution.py:19
  249.4 9.5 %collective-permute-start.15 = (f32[16]{0:T(128)S(1)}, f32[16]{0:T(128)S(1)}, u32[]{:S(2)}, u32[]{:S(2)}) collective-permute-start(f32[16]{0:T(128)S(1)} %get-tuple-element.35), channel_id=1, source_target_pairs={{0,64},{4,68},{8,72},{12,76},{16,80},{20,84},{24,88},{28,92},{32,9... | collective-permute-start | bytes 200 | tf_op jit(solution)/shard_map/ppermute | solution.py:19
  259.0 4.7 %collective-permute-start.16 = (f32[16]{0:T(128)S(1)}, f32[16]{0:T(128)S(1)}, u32[]{:S(2)}, u32[]{:S(2)}) collective-permute-start(f32[16]{0:T(128)S(1)} %add.126), channel_id=1, source_target_pairs={{0,4},{4,0},{8,12},{12,8},{16,20},{20,16},{24,28},{28,24},{32,36},... | collective-permute-start | bytes 200 | tf_op jit(solution)/shard_map/ppermute | solution.py:19
  259.7 5.1 %collective-permute-start.17 = (f32[16]{0:T(128)S(1)}, f32[16]{0:T(128)S(1)}, u32[]{:S(2)}, u32[]{:S(2)}) collective-permute-start(f32[16]{0:T(128)S(1)} %add.126), channel_id=1, source_target_pairs={{0,8},{4,12},{8,0},{12,4},{16,24},{20,28},{24,16},{28,20},{32,40},... | collective-permute-start | bytes 200 | tf_op jit(solution)/shard_map/ppermute | solution.py:19
  262.4 4.8 %collective-permute-start.18 = (f32[16]{0:T(128)S(1)}, f32[16]{0:T(128)S(1)}, u32[]{:S(2)}, u32[]{:S(2)}) collective-permute-start(f32[16]{0:T(128)S(1)} %add.126), channel_id=1, source_target_pairs={{0,12},{4,8},{8,4},{12,0},{16,28},{20,24},{24,20},{28,16},{32,44},... | collective-permute-start | bytes 200 | tf_op jit(solution)/shard_map/ppermute | solution.py:19
  267.2 4.7 %collective-permute-start.19 = (f32[16]{0:T(128)S(1)}, f32[16]{0:T(128)S(1)}, u32[]{:S(2)}, u32[]{:S(2)}) collective-permute-start(f32[16]{0:T(128)S(1)} %add_add_fusion.3), channel_id=1, source_target_pairs={{0,16},{4,20},{8,24},{12,28},{16,0},{20,4},{24,8},{28,12},{32,48},... | collective-permute-start | bytes 200 | tf_op jit(solution)/shard_map/ppermute | solution.py:19
  267.3 5.1 %collective-permute-start.20 = (f32[16]{0:T(128)S(1)}, f32[16]{0:T(128)S(1)}, u32[]{:S(2)}, u32[]{:S(2)}) collective-permute-start(f32[16]{0:T(128)S(1)} %add_add_fusion.3), channel_id=1, source_target_pairs={{0,32},{4,36},{8,40},{12,44},{16,48},{20,52},{24,56},{28,60},{32,0... | collective-permute-start | bytes 200 | tf_op jit(solution)/shard_map/ppermute | solution.py:19
  269.9 4.8 %collective-permute-start.21 = (f32[16]{0:T(128)S(1)}, f32[16]{0:T(128)S(1)}, u32[]{:S(2)}, u32[]{:S(2)}) collective-permute-start(f32[16]{0:T(128)S(1)} %add_add_fusion.3), channel_id=1, source_target_pairs={{0,48},{4,52},{8,56},{12,60},{16,32},{20,36},{24,40},{28,44},{32,1... | collective-permute-start | bytes 200 | tf_op jit(solution)/shard_map/ppermute | solution.py:19
  (20 other events, 114.4 us)

commit v6 on v3

--- a/solution.py
+++ b/solution.py
@@ -85,7 +85,11 @@
     following = jnp.where(position == win_count - 1, tail, received)
     region = jnp.concatenate([dosage, following], axis=1)
     regionf = region.astype(jnp.float32)
-    stats = summed(jnp.stack([jnp.sum(regionf, axis=0), jnp.sum(regionf * regionf, axis=0)]), "ind")
+    ownf = dosage.astype(jnp.float32)
+    followf = following.astype(jnp.float32)
+    own_stats = jnp.stack([jnp.sum(ownf, axis=0), jnp.sum(ownf * ownf, axis=0)])
+    follow_stats = jnp.stack([jnp.sum(followf, axis=0), jnp.sum(followf * followf, axis=0)])
+    stats = summed(jnp.concatenate([own_stats, follow_stats], axis=1), "ind")
     mean = stats[0] / total
     var = stats[1] / total - mean * mean
     miss_here = lax.dynamic_slice_in_dim(missing, position * columns, columns + half_cols)

time: 275 us -> 274 us (level)
    reduce_sum x1 -> x2, other arithmetic: 1.89 us -> 5.89 us  [the longest x1 3.34 us: shards(): own_stats = jnp.stack([jnp.sum(ownf, axis=0), jnp.sum(ownf * ownf, axis=0)])]
    ppermute x1, waiting for transfers between devices: 23.5 us -> 20.2 us  [passed_along(): return lax.ppermute(array, axis, pairs)]
  transfers between devices with their start and end apart: 57 -> 57, of which waited for: 51 -> 51; matrix products, arithmetic and copies ran while one was open for 2% -> 3% of each run, Pallas kernels for 0% -> 0%
where the time goes in v6:
time: 274 us
  waiting for transfers between devices  98.6 us (36%)
  starting transfers between devices  88.4 us (32%)
  matrix products  48 us (18%)
  other arithmetic  32.8 us (12%)
  local copies, waits for them, and re-layouts  4.46 us (2%)
    ppermute x56, starting transfers between devices, swapped(): return lax.ppermute(value, axis, [(i, i ^ mask) for i in range(size)])  86.5 us
    ppermute x56, waiting for transfers between devices, swapped(): return lax.ppermute(value, axis, [(i, i ^ mask) for i in range(size)])  78.4 us
    dot_general x7, matrix products, project(): jnp.dot(stand, jnp.concatenate(pieces(wide), 1), preferred_element_type=j...  33.9 us
    ppermute x1, waiting for transfers between devices, passed_along(): return lax.ppermute(array, axis, pairs)  20.2 us
    another operation x24, other arithmetic, orthonormal(): factor = jnp.linalg.cholesky(gram)  9.76 us
    another operation x18, other arithmetic, orthonormal(): jax.scipy.linalg.solve_triangular(fac, rhs, lower=True)  8.03 us
    dot_general x6, matrix products, image_of(): lax.dot_general(stand, split, (((0,), (0,)), ((), ())), preferred_element...  6.76 us
    convert_element_type x1, other arithmetic, shards(): ((regionf - mean) / jnp.sqrt(var + 1e-05) * weight).astype(jnp.bfloat16)  6.37 us
  transfers between devices with their start and end apart: 57, of which 51 were waited for; matrix products, arithmetic and copies ran while one was open for 3% of the time, Pallas kernels for 0%

profile of v6, /device:TPU:32, one launch (start us, length us, event | category | flops | bytes accessed | tf_op | source)
XLA Modules:
  0.0 274.0 jit_solution(11884465601423899360)
XLA Ops:
  4.3 3.3 %convert_reduce_fusion = (f32[1024]{0:T(1024)S(1)}, f32[1024]{0:T(1024)S(1)}) fusion(bf16[2048,1024]{1,0:T(8,128)(2,1)} %param.6), kind=kLoop, calls=%fused_computation.53 | loop fusion | flops 8386560 | bytes 4202496 | tf_op jit(solution)/shard_map/reduce_sum | solution.py:90
  7.6 20.2 %collective-permute-done.7 = bf16[2048,512]{1,0:T(8,128)(2,1)} collective-permute-done((bf16[2048,512]{1,0:T(8,128)(2,1)S(1)}, bf16[2048,512]{1,0:T(8,128)(2,1)}, u32[]{:S(2)}, u32[]{:S(2)}) %collective-permute-start.7) | collective-permute-done | bytes 2097184 | tf_op jit(solution)/shard_map/ppermute | solution.py:14
  27.8 2.5 convert_reduce_fusion.1
  30.4 3.1 %collective-permute-start.10 = (f32[2,1536]{1,0:T(2,128)S(1)}, f32[2,1536]{1,0:T(2,128)S(1)}, u32[]{:S(2)}, u32[]{:S(2)}) collective-permute-start(f32[2,1536]{1,0:T(2,128)S(1)} %maximum_maximum_fusion), channel_id=1, source_target_pairs={{0,12},{4,8},{8,4},{12,0},{16,28},{20,24},{24,20},{28,16},{32,44},... | collective-permute-start | bytes 36872 | tf_op jit(solution)/shard_map/ppermute | solution.py:19
  40.6 2.7 collective-permute-start.12
  45.8 2.4 collective-permute-done.13
  48.2 3.1 %collective-permute-start.14 = (f32[2,1536]{1,0:T(2,128)S(1)}, f32[2,1536]{1,0:T(2,128)S(1)}, u32[]{:S(2)}, u32[]{:S(2)}) collective-permute-start(f32[2,1536]{1,0:T(2,128)S(1)} %add_add_fusion.2), channel_id=1, source_target_pairs={{0,64},{4,68},{8,72},{12,76},{16,80},{20,84},{24,88},{28,92},{32,9... | collective-permute-start | bytes 36872 | tf_op jit(solution)/shard_map/ppermute | solution.py:19
  53.6 6.4 %multiply_convert_fusion = bf16[2048,1536]{1,0:T(8,128)(2,1)} fusion(bf16[2048,512]{1,0:T(8,128)(2,1)S(1)} %get-tuple-element.39, bf16[2048,1024]{1,0:T(8,128)(2,1)} %param.6, f32[1536]{0:T(1024)S(1)} %multiply_sqrt_fusion, f32[1536]{0:T(1024)S(1)} %get-tuple-element.28, f32[1536]{0:T(1024)S(1)} %get-tuple-element.27), kind=kLoop, calls=%fused_computation.51 | loop fusion | flops 25165824 | bytes 12601344 | tf_op jit(solution)/shard_map/convert_element_type | solution.py:97
  60.0 184.9 %while.10 = (s32[]{:T(128)}, f32[2,1024,8]{1,2,0:T(8,128)S(1)}, bf16[2048,1536]{1,0:T(8,128)(2,1)}, s32[]{:T(128)}) while((s32[]{:T(128)}, f32[2,1024,8]{1,2,0:T(8,128)S(1)}, bf16[2048,1536]{1,0:T(8,128)(2,1)}, s32[]{:T(128)}) %tuple.56), condition=%wide.region_7.8_spmd, body=%wide.region_4.7_spmd.sunk | while | flops 609027072 | bytes 43456232 | solution.py:111
  60.0 4.9 %convolution_bitcast_fusion.4 = f32[2048,48]{0,1:T(8,128)S(1)} fusion(bf16[2048,1536]{1,0:T(8,128)(2,1)} %get-tuple-element.117, bf16[1536,16]{0,1:T(8,128)(2,1)S(1)} %get-tuple-element.98, bf16[1536,16]{0,1:T(8,128)(2,1)S(1)} %get-tuple-element.99, bf16[1536,16]{0,1:T(8,128)(2,1)S(1)} %get-tuple-element.100), kind=kOutput, calls=%fused_computation.1.clone.1 | convolution fusion | flops 302432256 | bytes 6832128 | tf_op jit(solution)/shard_map/while/body/eval_jaxpr/dot_general | solution.py:102
  67.8 3.0 %collective-permute-start.1 = (f32[2,1024,8]{1,2,0:T(8,128)S(1)}, f32[2,1024,8]{1,2,0:T(8,128)S(1)}, u32[]{:S(2)}, u32[]{:S(2)}) collective-permute-start(f32[2,1024,8]{1,2,0:T(8,128)S(1)} %pad_maximum_fusion.2), channel_id=1, source_target_pairs={{0,12},{4,8},{8,4},{12,0},{16,28},{20,24},{24,20},{28,16},{32,44},... | collective-permute-start | bytes 196616 | tf_op jit(solution)/shard_map/while/body/eval_jaxpr/ppermute | solution.py:19
  78.6 3.0 %collective-permute-done.3 = f32[2,1024,8]{1,2,0:T(8,128)S(1)} collective-permute-done((f32[2,1024,8]{1,2,0:T(8,128)S(1)}, f32[2,1024,8]{1,2,0:T(8,128)S(1)}, u32[]{:S(2)}, u32[]{:S(2)}) %collective-permute-start.3) | collective-permute-done | bytes 65568 | tf_op jit(solution)/shard_map/while/body/eval_jaxpr/ppermute | solution.py:19
  83.0 2.9 %collective-permute-start.6 = (f32[2,1024,8]{1,2,0:T(8,128)S(1)}, f32[2,1024,8]{1,2,0:T(8,128)S(1)}, u32[]{:S(2)}, u32[]{:S(2)}) collective-permute-start(f32[2,1024,8]{1,2,0:T(8,128)S(1)} %add_add_fusion.9), channel_id=1, source_target_pairs={{0,64},{4,68},{8,72},{12,76},{16,80},{20,84},{24,88},{28,92},{32,9... | collective-permute-start | bytes 196616 | tf_op jit(solution)/shard_map/while/body/eval_jaxpr/ppermute | solution.py:19
  85.9 2.9 %collective-permute-done.6 = f32[2,1024,8]{1,2,0:T(8,128)S(1)} collective-permute-done((f32[2,1024,8]{1,2,0:T(8,128)S(1)}, f32[2,1024,8]{1,2,0:T(8,128)S(1)}, u32[]{:S(2)}, u32[]{:S(2)}) %collective-permute-start.6) | collective-permute-done | bytes 65568 | tf_op jit(solution)/shard_map/while/body/eval_jaxpr/ppermute | solution.py:19
  92.4 4.9 %convolution_bitcast_fusion.4 = f32[2048,48]{0,1:T(8,128)S(1)} fusion(bf16[2048,1536]{1,0:T(8,128)(2,1)} %get-tuple-element.117, bf16[1536,16]{0,1:T(8,128)(2,1)S(1)} %get-tuple-element.98, bf16[1536,16]{0,1:T(8,128)(2,1)S(1)} %get-tuple-element.99, bf16[1536,16]{0,1:T(8,128)(2,1)S(1)} %get-tuple-element.100), kind=kOutput, calls=%fused_computation.1.clone.1 | convolution fusion | flops 302432256 | bytes 6832128 | tf_op jit(solution)/shard_map/while/body/eval_jaxpr/dot_general | solution.py:102
  98.7 2.8 %collective-permute-start.1 = (f32[2,1024,8]{1,2,0:T(8,128)S(1)}, f32[2,1024,8]{1,2,0:T(8,128)S(1)}, u32[]{:S(2)}, u32[]{:S(2)}) collective-permute-start(f32[2,1024,8]{1,2,0:T(8,128)S(1)} %pad_maximum_fusion.2), channel_id=1, source_target_pairs={{0,12},{4,8},{8,4},{12,0},{16,28},{20,24},{24,20},{28,16},{32,44},... | collective-permute-start | bytes 196616 | tf_op jit(solution)/shard_map/while/body/eval_jaxpr/ppermute | solution.py:19
  102.2 2.5 collective-permute-done
  106.8 2.3 collective-permute-start.4
  109.3 2.3 collective-permute-done.3
  113.4 2.9 %collective-permute-start.6 = (f32[2,1024,8]{1,2,0:T(8,128)S(1)}, f32[2,1024,8]{1,2,0:T(8,128)S(1)}, u32[]{:S(2)}, u32[]{:S(2)}) collective-permute-start(f32[2,1024,8]{1,2,0:T(8,128)S(1)} %add_add_fusion.9), channel_id=1, source_target_pairs={{0,64},{4,68},{8,72},{12,76},{16,80},{20,84},{24,88},{28,92},{32,9... | collective-permute-start | bytes 196616 | tf_op jit(solution)/shard_map/while/body/eval_jaxpr/ppermute | solution.py:19
  116.3 2.9 %collective-permute-done.6 = f32[2,1024,8]{1,2,0:T(8,128)S(1)} collective-permute-done((f32[2,1024,8]{1,2,0:T(8,128)S(1)}, f32[2,1024,8]{1,2,0:T(8,128)S(1)}, u32[]{:S(2)}, u32[]{:S(2)}) %collective-permute-start.6) | collective-permute-done | bytes 65568 | tf_op jit(solution)/shard_map/while/body/eval_jaxpr/ppermute | solution.py:19
  122.9 4.9 %convolution_bitcast_fusion.4 = f32[2048,48]{0,1:T(8,128)S(1)} fusion(bf16[2048,1536]{1,0:T(8,128)(2,1)} %get-tuple-element.117, bf16[1536,16]{0,1:T(8,128)(2,1)S(1)} %get-tuple-element.98, bf16[1536,16]{0,1:T(8,128)(2,1)S(1)} %get-tuple-element.99, bf16[1536,16]{0,1:T(8,128)(2,1)S(1)} %get-tuple-element.100), kind=kOutput, calls=%fused_computation.1.clone.1 | convolution fusion | flops 302432256 | bytes 6832128 | tf_op jit(solution)/shard_map/while/body/eval_jaxpr/dot_general | solution.py:102
  132.6 2.3 collective-permute-done
  137.3 2.4 collective-permute-start.4
  139.9 2.3 collective-permute-done.3
  144.0 2.9 %collective-permute-start.6 = (f32[2,1024,8]{1,2,0:T(8,128)S(1)}, f32[2,1024,8]{1,2,0:T(8,128)S(1)}, u32[]{:S(2)}, u32[]{:S(2)}) collective-permute-start(f32[2,1024,8]{1,2,0:T(8,128)S(1)} %add_add_fusion.9), channel_id=1, source_target_pairs={{0,64},{4,68},{8,72},{12,76},{16,80},{20,84},{24,88},{28,92},{32,9... | collective-permute-start | bytes 196616 | tf_op jit(solution)/shard_map/while/body/eval_jaxpr/ppermute | solution.py:19
  146.9 2.9 %collective-permute-done.6 = f32[2,1024,8]{1,2,0:T(8,128)S(1)} collective-permute-done((f32[2,1024,8]{1,2,0:T(8,128)S(1)}, f32[2,1024,8]{1,2,0:T(8,128)S(1)}, u32[]{:S(2)}, u32[]{:S(2)}) %collective-permute-start.6) | collective-permute-done | bytes 65568 | tf_op jit(solution)/shard_map/while/body/eval_jaxpr/ppermute | solution.py:19
  153.5 4.9 %convolution_bitcast_fusion.4 = f32[2048,48]{0,1:T(8,128)S(1)} fusion(bf16[2048,1536]{1,0:T(8,128)(2,1)} %get-tuple-element.117, bf16[1536,16]{0,1:T(8,128)(2,1)S(1)} %get-tuple-element.98, bf16[1536,16]{0,1:T(8,128)(2,1)S(1)} %get-tuple-element.99, bf16[1536,16]{0,1:T(8,128)(2,1)S(1)} %get-tuple-element.100), kind=kOutput, calls=%fused_computation.1.clone.1 | convolution fusion | flops 302432256 | bytes 6832128 | tf_op jit(solution)/shard_map/while/body/eval_jaxpr/dot_general | solution.py:102
  163.2 2.3 collective-permute-done
  170.4 2.3 collective-permute-done.3
  174.4 2.9 %collective-permute-start.6 = (f32[2,1024,8]{1,2,0:T(8,128)S(1)}, f32[2,1024,8]{1,2,0:T(8,128)S(1)}, u32[]{:S(2)}, u32[]{:S(2)}) collective-permute-start(f32[2,1024,8]{1,2,0:T(8,128)S(1)} %add_add_fusion.9), channel_id=1, source_target_pairs={{0,64},{4,68},{8,72},{12,76},{16,80},{20,84},{24,88},{28,92},{32,9... | collective-permute-start | bytes 196616 | tf_op jit(solution)/shard_map/while/body/eval_jaxpr/ppermute | solution.py:19
  177.4 2.9 %collective-permute-done.6 = f32[2,1024,8]{1,2,0:T(8,128)S(1)} collective-permute-done((f32[2,1024,8]{1,2,0:T(8,128)S(1)}, f32[2,1024,8]{1,2,0:T(8,128)S(1)}, u32[]{:S(2)}, u32[]{:S(2)}) %collective-permute-start.6) | collective-permute-done | bytes 65568 | tf_op jit(solution)/shard_map/while/body/eval_jaxpr/ppermute | solution.py:19
  183.9 4.9 %convolution_bitcast_fusion.4 = f32[2048,48]{0,1:T(8,128)S(1)} fusion(bf16[2048,1536]{1,0:T(8,128)(2,1)} %get-tuple-element.117, bf16[1536,16]{0,1:T(8,128)(2,1)S(1)} %get-tuple-element.98, bf16[1536,16]{0,1:T(8,128)(2,1)S(1)} %get-tuple-element.99, bf16[1536,16]{0,1:T(8,128)(2,1)S(1)} %get-tuple-element.100), kind=kOutput, calls=%fused_computation.1.clone.1 | convolution fusion | flops 302432256 | bytes 6832128 | tf_op jit(solution)/shard_map/while/body/eval_jaxpr/dot_general | solution.py:102
  193.6 2.3 collective-permute-done
  201.0 2.3 collective-permute-done.3
  205.0 2.9 %collective-permute-start.6 = (f32[2,1024,8]{1,2,0:T(8,128)S(1)}, f32[2,1024,8]{1,2,0:T(8,128)S(1)}, u32[]{:S(2)}, u32[]{:S(2)}) collective-permute-start(f32[2,1024,8]{1,2,0:T(8,128)S(1)} %add_add_fusion.9), channel_id=1, source_target_pairs={{0,64},{4,68},{8,72},{12,76},{16,80},{20,84},{24,88},{28,92},{32,9... | collective-permute-start | bytes 196616 | tf_op jit(solution)/shard_map/while/body/eval_jaxpr/ppermute | solution.py:19
  208.0 2.9 %collective-permute-done.6 = f32[2,1024,8]{1,2,0:T(8,128)S(1)} collective-permute-done((f32[2,1024,8]{1,2,0:T(8,128)S(1)}, f32[2,1024,8]{1,2,0:T(8,128)S(1)}, u32[]{:S(2)}, u32[]{:S(2)}) %collective-permute-start.6) | collective-permute-done | bytes 65568 | tf_op jit(solution)/shard_map/while/body/eval_jaxpr/ppermute | solution.py:19
  214.5 4.9 %convolution_bitcast_fusion.4 = f32[2048,48]{0,1:T(8,128)S(1)} fusion(bf16[2048,1536]{1,0:T(8,128)(2,1)} %get-tuple-element.117, bf16[1536,16]{0,1:T(8,128)(2,1)S(1)} %get-tuple-element.98, bf16[1536,16]{0,1:T(8,128)(2,1)S(1)} %get-tuple-element.99, bf16[1536,16]{0,1:T(8,128)(2,1)S(1)} %get-tuple-element.100), kind=kOutput, calls=%fused_computation.1.clone.1 | convolution fusion | flops 302432256 | bytes 6832128 | tf_op jit(solution)/shard_map/while/body/eval_jaxpr/dot_general | solution.py:102
  224.2 2.3 collective-permute-done
  231.4 2.3 collective-permute-done.3
  235.5 2.9 %collective-permute-start.6 = (f32[2,1024,8]{1,2,0:T(8,128)S(1)}, f32[2,1024,8]{1,2,0:T(8,128)S(1)}, u32[]{:S(2)}, u32[]{:S(2)}) collective-permute-start(f32[2,1024,8]{1,2,0:T(8,128)S(1)} %add_add_fusion.9), channel_id=1, source_target_pairs={{0,64},{4,68},{8,72},{12,76},{16,80},{20,84},{24,88},{28,92},{32,9... | collective-permute-start | bytes 196616 | tf_op jit(solution)/shard_map/while/body/eval_jaxpr/ppermute | solution.py:19
  238.4 2.9 %collective-permute-done.6 = f32[2,1024,8]{1,2,0:T(8,128)S(1)} collective-permute-done((f32[2,1024,8]{1,2,0:T(8,128)S(1)}, f32[2,1024,8]{1,2,0:T(8,128)S(1)}, u32[]{:S(2)}, u32[]{:S(2)}) %collective-permute-start.6) | collective-permute-done | bytes 65568 | tf_op jit(solution)/shard_map/while/body/eval_jaxpr/ppermute | solution.py:19
  245.0 4.7 %fusion.22 = f32[2048,48]{0,1:T(8,128)S(1)} fusion(bf16[2048,1536]{1,0:T(8,128)(2,1)} %get-tuple-element.119, bf16[1536,16]{0,1:T(8,128)(2,1)S(1)} %get-tuple-element.63, bf16[1536,16]{0,1:T(8,128)(2,1)S(1)} %get-tuple-element.62, bf16[1536,16]{0,1:T(8,128)(2,1)S(1)} %get-tuple-element.61), kind=kOutput, calls=%fused_computation.61 | convolution fusion | flops 302432256 | bytes 6832128 | tf_op jit(solution)/shard_map/dot_general | solution.py:102
  250.2 2.5 collective-permute-start.16
  257.7 3.0 %multiply_reduce_fusion.1 = (f32[2048]{0:T(1024)S(1)}, f32[2048]{0:T(1024)S(1)}) fusion(bf16[2048,1536]{1,0:T(8,128)(2,1)S(1)} %bitcast.84, f32[2048,1024]{1,0:T(8,128)S(1)} %fusion.36, bf16[2048,48]{0,1:T(8,128)(2,1)S(1)} %constant_dynamic-update-slice_fusion, bf16[1024,48]{0,1:T(8,128)(2,1)S(1)} %get-tuple-element.52), kind=kOutput, calls=%fused_computation.56 | convolution fusion | flops 218099712 | bytes 17088512 | tf_op jit(solution)/shard_map/dot_general | solution.py:67
  261.0 2.5 collective-permute-start.19
  266.1 2.2 collective-permute-done.20
  268.3 2.9 %collective-permute-start.21 = (f32[16]{0:T(128)S(1)}, f32[16]{0:T(128)S(1)}, u32[]{:S(2)}, u32[]{:S(2)}) collective-permute-start(f32[16]{0:T(128)S(1)} %add_add_fusion.4), channel_id=1, source_target_pairs={{0,64},{4,68},{8,72},{12,76},{16,80},{20,84},{24,88},{28,92},{32,9... | collective-permute-start | bytes 200 | tf_op jit(solution)/shard_map/ppermute | solution.py:19
  (259 shorter events, 110.1 us)
Async XLA Ops:
  2.4 25.5 %collective-permute-start.7 = (bf16[2048,512]{1,0:T(8,128)(2,1)S(1)}, bf16[2048,512]{1,0:T(8,128)(2,1)}, u32[]{:S(2)}, u32[]{:S(2)}) collective-permute-start(bf16[2048,512]{1,0:T(8,128)(2,1)S(1)} %slice.80), channel_id=1, source_target_pairs={{1,0},{2,1},{3,2},{5,4},{6,5},{7,6},{9,8},{10,9},{11,10},{13,12},{... | collective-permute-start | bytes 6291464 | tf_op jit(solution)/shard_map/ppermute | solution.py:14
  30.4 5.0 %collective-permute-start.10 = (f32[2,1536]{1,0:T(2,128)S(1)}, f32[2,1536]{1,0:T(2,128)S(1)}, u32[]{:S(2)}, u32[]{:S(2)}) collective-permute-start(f32[2,1536]{1,0:T(2,128)S(1)} %maximum_maximum_fusion), channel_id=1, source_target_pairs={{0,12},{4,8},{8,4},{12,0},{16,28},{20,24},{24,20},{28,16},{32,44},... | collective-permute-start | bytes 36872 | tf_op jit(solution)/shard_map/ppermute | solution.py:19
  33.6 5.2 %collective-permute-start.9 = (f32[2,1536]{1,0:T(2,128)S(1)}, f32[2,1536]{1,0:T(2,128)S(1)}, u32[]{:S(2)}, u32[]{:S(2)}) collective-permute-start(f32[2,1536]{1,0:T(2,128)S(1)} %maximum_maximum_fusion), channel_id=1, source_target_pairs={{0,8},{4,12},{8,0},{12,4},{16,24},{20,28},{24,16},{28,20},{32,40},... | collective-permute-start | bytes 36872 | tf_op jit(solution)/shard_map/ppermute | solution.py:19
  38.9 4.8 %collective-permute-start.11 = (f32[2,1536]{1,0:T(2,128)S(1)}, f32[2,1536]{1,0:T(2,128)S(1)}, u32[]{:S(2)}, u32[]{:S(2)}) collective-permute-start(f32[2,1536]{1,0:T(2,128)S(1)} %add_add_fusion.3), channel_id=1, source_target_pairs={{0,16},{4,20},{8,24},{12,28},{16,0},{20,4},{24,8},{28,12},{32,48},... | collective-permute-start | bytes 36872 | tf_op jit(solution)/shard_map/ppermute | solution.py:19
  40.6 5.2 %collective-permute-start.12 = (f32[2,1536]{1,0:T(2,128)S(1)}, f32[2,1536]{1,0:T(2,128)S(1)}, u32[]{:S(2)}, u32[]{:S(2)}) collective-permute-start(f32[2,1536]{1,0:T(2,128)S(1)} %add_add_fusion.3), channel_id=1, source_target_pairs={{0,32},{4,36},{8,40},{12,44},{16,48},{20,52},{24,56},{28,60},{32,0... | collective-permute-start | bytes 36872 | tf_op jit(solution)/shard_map/ppermute | solution.py:19
  43.3 4.9 %collective-permute-start.13 = (f32[2,1536]{1,0:T(2,128)S(1)}, f32[2,1536]{1,0:T(2,128)S(1)}, u32[]{:S(2)}, u32[]{:S(2)}) collective-permute-start(f32[2,1536]{1,0:T(2,128)S(1)} %add_add_fusion.3), channel_id=1, source_target_pairs={{0,48},{4,52},{8,56},{12,60},{16,32},{20,36},{24,40},{28,44},{32,1... | collective-permute-start | bytes 36872 | tf_op jit(solution)/shard_map/ppermute | solution.py:19
  48.2 5.3 %collective-permute-start.14 = (f32[2,1536]{1,0:T(2,128)S(1)}, f32[2,1536]{1,0:T(2,128)S(1)}, u32[]{:S(2)}, u32[]{:S(2)}) collective-permute-start(f32[2,1536]{1,0:T(2,128)S(1)} %add_add_fusion.2), channel_id=1, source_target_pairs={{0,64},{4,68},{8,72},{12,76},{16,80},{20,84},{24,88},{28,92},{32,9... | collective-permute-start | bytes 36872 | tf_op jit(solution)/shard_map/ppermute | solution.py:19
  66.1 5.8 %collective-permute-start = (f32[2,1024,8]{1,2,0:T(8,128)S(1)}, f32[2,1024,8]{1,2,0:T(8,128)S(1)}, u32[]{:S(2)}, u32[]{:S(2)}) collective-permute-start(f32[2,1024,8]{1,2,0:T(8,128)S(1)} %pad_maximum_fusion.2), channel_id=1, source_target_pairs={{0,8},{4,12},{8,0},{12,4},{16,24},{20,28},{24,16},{28,20},{32,40},... | collective-permute-start | bytes 196616 | tf_op jit(solution)/shard_map/while/body/eval_jaxpr/ppermute | solution.py:19
  67.8 5.5 %collective-permute-start.1 = (f32[2,1024,8]{1,2,0:T(8,128)S(1)}, f32[2,1024,8]{1,2,0:T(8,128)S(1)}, u32[]{:S(2)}, u32[]{:S(2)}) collective-permute-start(f32[2,1024,8]{1,2,0:T(8,128)S(1)} %pad_maximum_fusion.2), channel_id=1, source_target_pairs={{0,12},{4,8},{8,4},{12,0},{16,28},{20,24},{24,20},{28,16},{32,44},... | collective-permute-start | bytes 196616 | tf_op jit(solution)/shard_map/while/body/eval_jaxpr/ppermute | solution.py:19
  70.8 4.3 %collective-permute-start.2 = (f32[2,1024,8]{1,2,0:T(8,128)S(1)}, f32[2,1024,8]{1,2,0:T(8,128)S(1)}, u32[]{:S(2)}, u32[]{:S(2)}) collective-permute-start(f32[2,1024,8]{1,2,0:T(8,128)S(1)} %pad_maximum_fusion.2), channel_id=1, source_target_pairs={{0,4},{4,0},{8,12},{12,8},{16,20},{20,16},{24,28},{28,24},{32,36},... | collective-permute-start | bytes 196616 | tf_op jit(solution)/shard_map/while/body/eval_jaxpr/ppermute | solution.py:19
  75.1 6.6 %collective-permute-start.3 = (f32[2,1024,8]{1,2,0:T(8,128)S(1)}, f32[2,1024,8]{1,2,0:T(8,128)S(1)}, u32[]{:S(2)}, u32[]{:S(2)}) collective-permute-start(f32[2,1024,8]{1,2,0:T(8,128)S(1)} %add_add_fusion.8), channel_id=1, source_target_pairs={{0,32},{4,36},{8,40},{12,44},{16,48},{20,52},{24,56},{28,60},{32,0... | collective-permute-start | bytes 196616 | tf_op jit(solution)/shard_map/while/body/eval_jaxpr/ppermute | solution.py:19
  75.9 7.1 %collective-permute-start.4 = (f32[2,1024,8]{1,2,0:T(8,128)S(1)}, f32[2,1024,8]{1,2,0:T(8,128)S(1)}, u32[]{:S(2)}, u32[]{:S(2)}) collective-permute-start(f32[2,1024,8]{1,2,0:T(8,128)S(1)} %add_add_fusion.8), channel_id=1, source_target_pairs={{0,48},{4,52},{8,56},{12,60},{16,32},{20,36},{24,40},{28,44},{32,1... | collective-permute-start | bytes 196616 | tf_op jit(solution)/shard_map/while/body/eval_jaxpr/ppermute | solution.py:19
  76.8 6.1 %collective-permute-start.5 = (f32[2,1024,8]{1,2,0:T(8,128)S(1)}, f32[2,1024,8]{1,2,0:T(8,128)S(1)}, u32[]{:S(2)}, u32[]{:S(2)}) collective-permute-start(f32[2,1024,8]{1,2,0:T(8,128)S(1)} %add_add_fusion.8), channel_id=1, source_target_pairs={{0,16},{4,20},{8,24},{12,28},{16,0},{20,4},{24,8},{28,12},{32,48},... | collective-permute-start | bytes 196616 | tf_op jit(solution)/shard_map/while/body/eval_jaxpr/ppermute | solution.py:19
  83.0 5.8 %collective-permute-start.6 = (f32[2,1024,8]{1,2,0:T(8,128)S(1)}, f32[2,1024,8]{1,2,0:T(8,128)S(1)}, u32[]{:S(2)}, u32[]{:S(2)}) collective-permute-start(f32[2,1024,8]{1,2,0:T(8,128)S(1)} %add_add_fusion.9), channel_id=1, source_target_pairs={{0,64},{4,68},{8,72},{12,76},{16,80},{20,84},{24,88},{28,92},{32,9... | collective-permute-start | bytes 196616 | tf_op jit(solution)/shard_map/while/body/eval_jaxpr/ppermute | solution.py:19
  98.6 6.1 %collective-permute-start = (f32[2,1024,8]{1,2,0:T(8,128)S(1)}, f32[2,1024,8]{1,2,0:T(8,128)S(1)}, u32[]{:S(2)}, u32[]{:S(2)}) collective-permute-start(f32[2,1024,8]{1,2,0:T(8,128)S(1)} %pad_maximum_fusion.2), channel_id=1, source_target_pairs={{0,8},{4,12},{8,0},{12,4},{16,24},{20,28},{24,16},{28,20},{32,40},... | collective-permute-start | bytes 196616 | tf_op jit(solution)/shard_map/while/body/eval_jaxpr/ppermute | solution.py:19
  98.7 6.3 %collective-permute-start.1 = (f32[2,1024,8]{1,2,0:T(8,128)S(1)}, f32[2,1024,8]{1,2,0:T(8,128)S(1)}, u32[]{:S(2)}, u32[]{:S(2)}) collective-permute-start(f32[2,1024,8]{1,2,0:T(8,128)S(1)} %pad_maximum_fusion.2), channel_id=1, source_target_pairs={{0,12},{4,8},{8,4},{12,0},{16,28},{20,24},{24,20},{28,16},{32,44},... | collective-permute-start | bytes 196616 | tf_op jit(solution)/shard_map/while/body/eval_jaxpr/ppermute | solution.py:19
  105.8 5.8 %collective-permute-start.3 = (f32[2,1024,8]{1,2,0:T(8,128)S(1)}, f32[2,1024,8]{1,2,0:T(8,128)S(1)}, u32[]{:S(2)}, u32[]{:S(2)}) collective-permute-start(f32[2,1024,8]{1,2,0:T(8,128)S(1)} %add_add_fusion.8), channel_id=1, source_target_pairs={{0,32},{4,36},{8,40},{12,44},{16,48},{20,52},{24,56},{28,60},{32,0... | collective-permute-start | bytes 196616 | tf_op jit(solution)/shard_map/while/body/eval_jaxpr/ppermute | solution.py:19
  106.8 5.5 %collective-permute-start.4 = (f32[2,1024,8]{1,2,0:T(8,128)S(1)}, f32[2,1024,8]{1,2,0:T(8,128)S(1)}, u32[]{:S(2)}, u32[]{:S(2)}) collective-permute-start(f32[2,1024,8]{1,2,0:T(8,128)S(1)} %add_add_fusion.8), channel_id=1, source_target_pairs={{0,48},{4,52},{8,56},{12,60},{16,32},{20,36},{24,40},{28,44},{32,1... | collective-permute-start | bytes 196616 | tf_op jit(solution)/shard_map/while/body/eval_jaxpr/ppermute | solution.py:19
  113.4 5.8 %collective-permute-start.6 = (f32[2,1024,8]{1,2,0:T(8,128)S(1)}, f32[2,1024,8]{1,2,0:T(8,128)S(1)}, u32[]{:S(2)}, u32[]{:S(2)}) collective-permute-start(f32[2,1024,8]{1,2,0:T(8,128)S(1)} %add_add_fusion.9), channel_id=1, source_target_pairs={{0,64},{4,68},{8,72},{12,76},{16,80},{20,84},{24,88},{28,92},{32,9... | collective-permute-start | bytes 196616 | tf_op jit(solution)/shard_map/while/body/eval_jaxpr/ppermute | solution.py:19
  129.0 5.8 %collective-permute-start = (f32[2,1024,8]{1,2,0:T(8,128)S(1)}, f32[2,1024,8]{1,2,0:T(8,128)S(1)}, u32[]{:S(2)}, u32[]{:S(2)}) collective-permute-start(f32[2,1024,8]{1,2,0:T(8,128)S(1)} %pad_maximum_fusion.2), channel_id=1, source_target_pairs={{0,8},{4,12},{8,0},{12,4},{16,24},{20,28},{24,16},{28,20},{32,40},... | collective-permute-start | bytes 196616 | tf_op jit(solution)/shard_map/while/body/eval_jaxpr/ppermute | solution.py:19
  130.6 5.5 %collective-permute-start.1 = (f32[2,1024,8]{1,2,0:T(8,128)S(1)}, f32[2,1024,8]{1,2,0:T(8,128)S(1)}, u32[]{:S(2)}, u32[]{:S(2)}) collective-permute-start(f32[2,1024,8]{1,2,0:T(8,128)S(1)} %pad_maximum_fusion.2), channel_id=1, source_target_pairs={{0,12},{4,8},{8,4},{12,0},{16,28},{20,24},{24,20},{28,16},{32,44},... | collective-permute-start | bytes 196616 | tf_op jit(solution)/shard_map/while/body/eval_jaxpr/ppermute | solution.py:19
  132.1 4.3 %collective-permute-start.2 = (f32[2,1024,8]{1,2,0:T(8,128)S(1)}, f32[2,1024,8]{1,2,0:T(8,128)S(1)}, u32[]{:S(2)}, u32[]{:S(2)}) collective-permute-start(f32[2,1024,8]{1,2,0:T(8,128)S(1)} %pad_maximum_fusion.2), channel_id=1, source_target_pairs={{0,4},{4,0},{8,12},{12,8},{16,20},{20,16},{24,28},{28,24},{32,36},... | collective-permute-start | bytes 196616 | tf_op jit(solution)/shard_map/while/body/eval_jaxpr/ppermute | solution.py:19
  136.4 5.9 %collective-permute-start.3 = (f32[2,1024,8]{1,2,0:T(8,128)S(1)}, f32[2,1024,8]{1,2,0:T(8,128)S(1)}, u32[]{:S(2)}, u32[]{:S(2)}) collective-permute-start(f32[2,1024,8]{1,2,0:T(8,128)S(1)} %add_add_fusion.8), channel_id=1, source_target_pairs={{0,32},{4,36},{8,40},{12,44},{16,48},{20,52},{24,56},{28,60},{32,0... | collective-permute-start | bytes 196616 | tf_op jit(solution)/shard_map/while/body/eval_jaxpr/ppermute | solution.py:19
  137.3 5.6 %collective-permute-start.4 = (f32[2,1024,8]{1,2,0:T(8,128)S(1)}, f32[2,1024,8]{1,2,0:T(8,128)S(1)}, u32[]{:S(2)}, u32[]{:S(2)}) collective-permute-start(f32[2,1024,8]{1,2,0:T(8,128)S(1)} %add_add_fusion.8), channel_id=1, source_target_pairs={{0,48},{4,52},{8,56},{12,60},{16,32},{20,36},{24,40},{28,44},{32,1... | collective-permute-start | bytes 196616 | tf_op jit(solution)/shard_map/while/body/eval_jaxpr/ppermute | solution.py:19
  144.0 5.8 %collective-permute-start.6 = (f32[2,1024,8]{1,2,0:T(8,128)S(1)}, f32[2,1024,8]{1,2,0:T(8,128)S(1)}, u32[]{:S(2)}, u32[]{:S(2)}) collective-permute-start(f32[2,1024,8]{1,2,0:T(8,128)S(1)} %add_add_fusion.9), channel_id=1, source_target_pairs={{0,64},{4,68},{8,72},{12,76},{16,80},{20,84},{24,88},{28,92},{32,9... | collective-permute-start | bytes 196616 | tf_op jit(solution)/shard_map/while/body/eval_jaxpr/ppermute | solution.py:19
  159.6 5.8 %collective-permute-start = (f32[2,1024,8]{1,2,0:T(8,128)S(1)}, f32[2,1024,8]{1,2,0:T(8,128)S(1)}, u32[]{:S(2)}, u32[]{:S(2)}) collective-permute-start(f32[2,1024,8]{1,2,0:T(8,128)S(1)} %pad_maximum_fusion.2), channel_id=1, source_target_pairs={{0,8},{4,12},{8,0},{12,4},{16,24},{20,28},{24,16},{28,20},{32,40},... | collective-permute-start | bytes 196616 | tf_op jit(solution)/shard_map/while/body/eval_jaxpr/ppermute | solution.py:19
  160.7 5.5 %collective-permute-start.1 = (f32[2,1024,8]{1,2,0:T(8,128)S(1)}, f32[2,1024,8]{1,2,0:T(8,128)S(1)}, u32[]{:S(2)}, u32[]{:S(2)}) collective-permute-start(f32[2,1024,8]{1,2,0:T(8,128)S(1)} %pad_maximum_fusion.2), channel_id=1, source_target_pairs={{0,12},{4,8},{8,4},{12,0},{16,28},{20,24},{24,20},{28,16},{32,44},... | collective-permute-start | bytes 196616 | tf_op jit(solution)/shard_map/while/body/eval_jaxpr/ppermute | solution.py:19
  166.8 5.8 %collective-permute-start.3 = (f32[2,1024,8]{1,2,0:T(8,128)S(1)}, f32[2,1024,8]{1,2,0:T(8,128)S(1)}, u32[]{:S(2)}, u32[]{:S(2)}) collective-permute-start(f32[2,1024,8]{1,2,0:T(8,128)S(1)} %add_add_fusion.8), channel_id=1, source_target_pairs={{0,32},{4,36},{8,40},{12,44},{16,48},{20,52},{24,56},{28,60},{32,0... | collective-permute-start | bytes 196616 | tf_op jit(solution)/shard_map/while/body/eval_jaxpr/ppermute | solution.py:19
  168.1 5.5 %collective-permute-start.4 = (f32[2,1024,8]{1,2,0:T(8,128)S(1)}, f32[2,1024,8]{1,2,0:T(8,128)S(1)}, u32[]{:S(2)}, u32[]{:S(2)}) collective-permute-start(f32[2,1024,8]{1,2,0:T(8,128)S(1)} %add_add_fusion.8), channel_id=1, source_target_pairs={{0,48},{4,52},{8,56},{12,60},{16,32},{20,36},{24,40},{28,44},{32,1... | collective-permute-start | bytes 196616 | tf_op jit(solution)/shard_map/while/body/eval_jaxpr/ppermute | solution.py:19
  170.2 4.3 %collective-permute-start.5 = (f32[2,1024,8]{1,2,0:T(8,128)S(1)}, f32[2,1024,8]{1,2,0:T(8,128)S(1)}, u32[]{:S(2)}, u32[]{:S(2)}) collective-permute-start(f32[2,1024,8]{1,2,0:T(8,128)S(1)} %add_add_fusion.8), channel_id=1, source_target_pairs={{0,16},{4,20},{8,24},{12,28},{16,0},{20,4},{24,8},{28,12},{32,48},... | collective-permute-start | bytes 196616 | tf_op jit(solution)/shard_map/while/body/eval_jaxpr/ppermute | solution.py:19
  174.4 5.8 %collective-permute-start.6 = (f32[2,1024,8]{1,2,0:T(8,128)S(1)}, f32[2,1024,8]{1,2,0:T(8,128)S(1)}, u32[]{:S(2)}, u32[]{:S(2)}) collective-permute-start(f32[2,1024,8]{1,2,0:T(8,128)S(1)} %add_add_fusion.9), channel_id=1, source_target_pairs={{0,64},{4,68},{8,72},{12,76},{16,80},{20,84},{24,88},{28,92},{32,9... | collective-permute-start | bytes 196616 | tf_op jit(solution)/shard_map/while/body/eval_jaxpr/ppermute | solution.py:19
  190.1 5.8 %collective-permute-start = (f32[2,1024,8]{1,2,0:T(8,128)S(1)}, f32[2,1024,8]{1,2,0:T(8,128)S(1)}, u32[]{:S(2)}, u32[]{:S(2)}) collective-permute-start(f32[2,1024,8]{1,2,0:T(8,128)S(1)} %pad_maximum_fusion.2), channel_id=1, source_target_pairs={{0,8},{4,12},{8,0},{12,4},{16,24},{20,28},{24,16},{28,20},{32,40},... | collective-permute-start | bytes 196616 | tf_op jit(solution)/shard_map/while/body/eval_jaxpr/ppermute | solution.py:19
  191.6 5.5 %collective-permute-start.1 = (f32[2,1024,8]{1,2,0:T(8,128)S(1)}, f32[2,1024,8]{1,2,0:T(8,128)S(1)}, u32[]{:S(2)}, u32[]{:S(2)}) collective-permute-start(f32[2,1024,8]{1,2,0:T(8,128)S(1)} %pad_maximum_fusion.2), channel_id=1, source_target_pairs={{0,12},{4,8},{8,4},{12,0},{16,28},{20,24},{24,20},{28,16},{32,44},... | collective-permute-start | bytes 196616 | tf_op jit(solution)/shard_map/while/body/eval_jaxpr/ppermute | solution.py:19
  197.4 5.8 %collective-permute-start.3 = (f32[2,1024,8]{1,2,0:T(8,128)S(1)}, f32[2,1024,8]{1,2,0:T(8,128)S(1)}, u32[]{:S(2)}, u32[]{:S(2)}) collective-permute-start(f32[2,1024,8]{1,2,0:T(8,128)S(1)} %add_add_fusion.8), channel_id=1, source_target_pairs={{0,32},{4,36},{8,40},{12,44},{16,48},{20,52},{24,56},{28,60},{32,0... | collective-permute-start | bytes 196616 | tf_op jit(solution)/shard_map/while/body/eval_jaxpr/ppermute | solution.py:19
  198.7 5.5 %collective-permute-start.4 = (f32[2,1024,8]{1,2,0:T(8,128)S(1)}, f32[2,1024,8]{1,2,0:T(8,128)S(1)}, u32[]{:S(2)}, u32[]{:S(2)}) collective-permute-start(f32[2,1024,8]{1,2,0:T(8,128)S(1)} %add_add_fusion.8), channel_id=1, source_target_pairs={{0,48},{4,52},{8,56},{12,60},{16,32},{20,36},{24,40},{28,44},{32,1... | collective-permute-start | bytes 196616 | tf_op jit(solution)/shard_map/while/body/eval_jaxpr/ppermute | solution.py:19
  205.0 5.8 %collective-permute-start.6 = (f32[2,1024,8]{1,2,0:T(8,128)S(1)}, f32[2,1024,8]{1,2,0:T(8,128)S(1)}, u32[]{:S(2)}, u32[]{:S(2)}) collective-permute-start(f32[2,1024,8]{1,2,0:T(8,128)S(1)} %add_add_fusion.9), channel_id=1, source_target_pairs={{0,64},{4,68},{8,72},{12,76},{16,80},{20,84},{24,88},{28,92},{32,9... | collective-permute-start | bytes 196616 | tf_op jit(solution)/shard_map/while/body/eval_jaxpr/ppermute | solution.py:19
  220.7 5.8 %collective-permute-start = (f32[2,1024,8]{1,2,0:T(8,128)S(1)}, f32[2,1024,8]{1,2,0:T(8,128)S(1)}, u32[]{:S(2)}, u32[]{:S(2)}) collective-permute-start(f32[2,1024,8]{1,2,0:T(8,128)S(1)} %pad_maximum_fusion.2), channel_id=1, source_target_pairs={{0,8},{4,12},{8,0},{12,4},{16,24},{20,28},{24,16},{28,20},{32,40},... | collective-permute-start | bytes 196616 | tf_op jit(solution)/shard_map/while/body/eval_jaxpr/ppermute | solution.py:19
  221.7 5.5 %collective-permute-start.1 = (f32[2,1024,8]{1,2,0:T(8,128)S(1)}, f32[2,1024,8]{1,2,0:T(8,128)S(1)}, u32[]{:S(2)}, u32[]{:S(2)}) collective-permute-start(f32[2,1024,8]{1,2,0:T(8,128)S(1)} %pad_maximum_fusion.2), channel_id=1, source_target_pairs={{0,12},{4,8},{8,4},{12,0},{16,28},{20,24},{24,20},{28,16},{32,44},... | collective-permute-start | bytes 196616 | tf_op jit(solution)/shard_map/while/body/eval_jaxpr/ppermute | solution.py:19
  227.8 5.8 %collective-permute-start.3 = (f32[2,1024,8]{1,2,0:T(8,128)S(1)}, f32[2,1024,8]{1,2,0:T(8,128)S(1)}, u32[]{:S(2)}, u32[]{:S(2)}) collective-permute-start(f32[2,1024,8]{1,2,0:T(8,128)S(1)} %add_add_fusion.8), channel_id=1, source_target_pairs={{0,32},{4,36},{8,40},{12,44},{16,48},{20,52},{24,56},{28,60},{32,0... | collective-permute-start | bytes 196616 | tf_op jit(solution)/shard_map/while/body/eval_jaxpr/ppermute | solution.py:19
  229.2 5.5 %collective-permute-start.4 = (f32[2,1024,8]{1,2,0:T(8,128)S(1)}, f32[2,1024,8]{1,2,0:T(8,128)S(1)}, u32[]{:S(2)}, u32[]{:S(2)}) collective-permute-start(f32[2,1024,8]{1,2,0:T(8,128)S(1)} %add_add_fusion.8), channel_id=1, source_target_pairs={{0,48},{4,52},{8,56},{12,60},{16,32},{20,36},{24,40},{28,44},{32,1... | collective-permute-start | bytes 196616 | tf_op jit(solution)/shard_map/while/body/eval_jaxpr/ppermute | solution.py:19
  235.5 5.8 %collective-permute-start.6 = (f32[2,1024,8]{1,2,0:T(8,128)S(1)}, f32[2,1024,8]{1,2,0:T(8,128)S(1)}, u32[]{:S(2)}, u32[]{:S(2)}) collective-permute-start(f32[2,1024,8]{1,2,0:T(8,128)S(1)} %add_add_fusion.9), channel_id=1, source_target_pairs={{0,64},{4,68},{8,72},{12,76},{16,80},{20,84},{24,88},{28,92},{32,9... | collective-permute-start | bytes 196616 | tf_op jit(solution)/shard_map/while/body/eval_jaxpr/ppermute | solution.py:19
  249.8 10.9 %collective-permute-start.15 = (f32[16]{0:T(128)S(1)}, f32[16]{0:T(128)S(1)}, u32[]{:S(2)}, u32[]{:S(2)}) collective-permute-start(f32[16]{0:T(128)S(1)} %get-tuple-element.37), channel_id=1, source_target_pairs={{0,4},{4,0},{8,12},{12,8},{16,20},{20,16},{24,28},{28,24},{32,36},... | collective-permute-start | bytes 200 | tf_op jit(solution)/shard_map/ppermute | solution.py:19
  250.2 10.5 %collective-permute-start.16 = (f32[16]{0:T(128)S(1)}, f32[16]{0:T(128)S(1)}, u32[]{:S(2)}, u32[]{:S(2)}) collective-permute-start(f32[16]{0:T(128)S(1)} %get-tuple-element.37), channel_id=1, source_target_pairs={{0,8},{4,12},{8,0},{12,4},{16,24},{20,28},{24,16},{28,20},{32,40},... | collective-permute-start | bytes 200 | tf_op jit(solution)/shard_map/ppermute | solution.py:19
  252.7 8.1 %collective-permute-start.17 = (f32[16]{0:T(128)S(1)}, f32[16]{0:T(128)S(1)}, u32[]{:S(2)}, u32[]{:S(2)}) collective-permute-start(f32[16]{0:T(128)S(1)} %get-tuple-element.37), channel_id=1, source_target_pairs={{0,12},{4,8},{8,4},{12,0},{16,28},{20,24},{24,20},{28,16},{32,44},... | collective-permute-start | bytes 200 | tf_op jit(solution)/shard_map/ppermute | solution.py:19
  260.7 4.8 %collective-permute-start.18 = (f32[16]{0:T(128)S(1)}, f32[16]{0:T(128)S(1)}, u32[]{:S(2)}, u32[]{:S(2)}) collective-permute-start(f32[16]{0:T(128)S(1)} %add_add_fusion.5), channel_id=1, source_target_pairs={{0,16},{4,20},{8,24},{12,28},{16,0},{20,4},{24,8},{28,12},{32,48},... | collective-permute-start | bytes 200 | tf_op jit(solution)/shard_map/ppermute | solution.py:19
  261.0 5.1 %collective-permute-start.19 = (f32[16]{0:T(128)S(1)}, f32[16]{0:T(128)S(1)}, u32[]{:S(2)}, u32[]{:S(2)}) collective-permute-start(f32[16]{0:T(128)S(1)} %add_add_fusion.5), channel_id=1, source_target_pairs={{0,32},{4,36},{8,40},{12,44},{16,48},{20,52},{24,56},{28,60},{32,0... | collective-permute-start | bytes 200 | tf_op jit(solution)/shard_map/ppermute | solution.py:19
  263.5 4.8 %collective-permute-start.20 = (f32[16]{0:T(128)S(1)}, f32[16]{0:T(128)S(1)}, u32[]{:S(2)}, u32[]{:S(2)}) collective-permute-start(f32[16]{0:T(128)S(1)} %add_add_fusion.5), channel_id=1, source_target_pairs={{0,48},{4,52},{8,56},{12,60},{16,32},{20,36},{24,40},{28,44},{32,1... | collective-permute-start | bytes 200 | tf_op jit(solution)/shard_map/ppermute | solution.py:19
  268.3 5.1 %collective-permute-start.21 = (f32[16]{0:T(128)S(1)}, f32[16]{0:T(128)S(1)}, u32[]{:S(2)}, u32[]{:S(2)}) collective-permute-start(f32[16]{0:T(128)S(1)} %add_add_fusion.4), channel_id=1, source_target_pairs={{0,64},{4,68},{8,72},{12,76},{16,80},{20,84},{24,88},{28,92},{32,9... | collective-permute-start | bytes 200 | tf_op jit(solution)/shard_map/ppermute | solution.py:19
  (19 other events, 90.5 us)

commit v7 on v3

--- a/solution.py
+++ b/solution.py
@@ -23,17 +23,22 @@
     size = lax.axis_size(axis)
     if size & (size - 1):
         return lax.psum(value, axis)
-    bit = 1
-    while bit < size:
-        if bit * 4 <= size:
-            near = swapped(value, axis, bit)
-            mid = swapped(value, axis, 2 * bit)
-            far = swapped(value, axis, 3 * bit)
+    levels = size.bit_length() - 1
+    done = 0
+    for low in range(levels):
+        if done >> low & 1:
+            continue
+        high = low + 2
+        if high < levels and not done >> high & 1:
+            one, two = 1 << low, 1 << high
+            near = swapped(value, axis, one)
+            mid = swapped(value, axis, two)
+            far = swapped(value, axis, one | two)
             value = (value + near) + (mid + far)
-            bit *= 4
+            done |= one | two
         else:
-            value = value + swapped(value, axis, bit)
-            bit *= 2
+            value = value + swapped(value, axis, 1 << low)
+            done |= 1 << low
     return value
 
 

time: 275 us -> 299 us (1.087)
  starting transfers between devices: 89.6 us -> 109 us
  waiting for transfers between devices: 100 us -> 105 us
    ppermute x56, starting transfers between devices: 87.6 us -> 107 us  [swapped(): return lax.ppermute(value, axis, [(i, i ^ mask) for i in range(size)])]
    ppermute x56, waiting for transfers between devices: 76.8 us -> 81.1 us  [swapped(): return lax.ppermute(value, axis, [(i, i ^ mask) for i in range(size)])]
  transfers between devices with their start and end apart: 57 -> 57, of which waited for: 51 -> 45; matrix products, arithmetic and copies ran while one was open for 2% -> 2% of each run, Pallas kernels for 0% -> 0%
where the time goes in v7:
time: 299 us
  starting transfers between devices  109 us (36%)
  waiting for transfers between devices  105 us (35%)
  matrix products  48 us (16%)
  other arithmetic  30.7 us (10%)
  local copies, waits for them, and re-layouts  4.48 us (1%)
    ppermute x56, starting transfers between devices, swapped(): return lax.ppermute(value, axis, [(i, i ^ mask) for i in range(size)])  107 us
    ppermute x56, waiting for transfers between devices, swapped(): return lax.ppermute(value, axis, [(i, i ^ mask) for i in range(size)])  81.1 us
    dot_general x7, matrix products, project(): jnp.dot(stand, jnp.concatenate(pieces(wide), 1), preferred_element_type=j...  33.9 us
    ppermute x1, waiting for transfers between devices, passed_along(): return lax.ppermute(array, axis, pairs)  23.5 us
    another operation x24, other arithmetic, orthonormal(): factor = jnp.linalg.cholesky(gram)  9.76 us
    another operation x18, other arithmetic, orthonormal(): jax.scipy.linalg.solve_triangular(fac, rhs, lower=True)  8.03 us
    dot_general x6, matrix products, image_of(): lax.dot_general(stand, split, (((0,), (0,)), ((), ())), preferred_element...  6.76 us
    convert_element_type x1, other arithmetic, shards(): ((regionf - mean) / jnp.sqrt(var + 1e-05) * weight).astype(jnp.bfloat16)  6.38 us
  transfers between devices with their start and end apart: 57, of which 45 were waited for; matrix products, arithmetic and copies ran while one was open for 2% of the time, Pallas kernels for 0%

profile of v7, /device:TPU:32, one launch (start us, length us, event | category | flops | bytes accessed | tf_op | source)
XLA Modules:
  0.0 298.6 jit_solution(8071230127606890672)
XLA Ops:
  4.3 23.5 %collective-permute-done.7 = bf16[2048,512]{1,0:T(8,128)(2,1)} collective-permute-done((bf16[2048,512]{1,0:T(8,128)(2,1)S(1)}, bf16[2048,512]{1,0:T(8,128)(2,1)}, u32[]{:S(2)}, u32[]{:S(2)}) %collective-permute-start.7) | collective-permute-done | bytes 2097184 | tf_op jit(solution)/shard_map/ppermute | solution.py:14
  31.6 2.6 collective-permute-start.10
  38.4 3.3 %collective-permute-start.11 = (f32[2,1536]{1,0:T(2,128)S(1)}, f32[2,1536]{1,0:T(2,128)S(1)}, u32[]{:S(2)}, u32[]{:S(2)}) collective-permute-start(f32[2,1536]{1,0:T(2,128)S(1)} %add_add_fusion.3), channel_id=1, source_target_pairs={{0,8},{4,12},{8,0},{12,4},{16,24},{20,28},{24,16},{28,20},{32,40},... | collective-permute-start | bytes 36872 | tf_op jit(solution)/shard_map/ppermute | solution.py:19
  41.6 2.9 collective-permute-start.12
  46.8 5.3 %collective-permute-done.13 = f32[2,1536]{1,0:T(2,128)S(1)} collective-permute-done((f32[2,1536]{1,0:T(2,128)S(1)}, f32[2,1536]{1,0:T(2,128)S(1)}, u32[]{:S(2)}, u32[]{:S(2)}) %collective-permute-start.13) | collective-permute-done | bytes 12320 | tf_op jit(solution)/shard_map/ppermute | solution.py:19
  52.1 3.1 %collective-permute-start.14 = (f32[2,1536]{1,0:T(2,128)S(1)}, f32[2,1536]{1,0:T(2,128)S(1)}, u32[]{:S(2)}, u32[]{:S(2)}) collective-permute-start(f32[2,1536]{1,0:T(2,128)S(1)} %add_add_fusion.2), channel_id=1, source_target_pairs={{0,64},{4,68},{8,72},{12,76},{16,80},{20,84},{24,88},{28,92},{32,9... | collective-permute-start | bytes 36872 | tf_op jit(solution)/shard_map/ppermute | solution.py:19
  57.5 6.4 %fusion.23 = bf16[2048,1536]{1,0:T(8,128)(2,1)} fusion(f32[1536]{0:T(1024)S(1)} %multiply_sqrt_fusion, f32[1536]{0:T(1024)S(1)} %get-tuple-element.26, f32[1536]{0:T(1024)S(1)} %get-tuple-element.25, bf16[2048,512]{1,0:T(8,128)(2,1)S(1)} %broadcast_select_fusion, bf16[2048,1024]{1,0:T(8,128)(2,1)} %param.6), kind=kLoop, calls=%fused_computation.57 | loop fusion | flops 25165824 | bytes 12601344 | tf_op jit(solution)/shard_map/convert_element_type | solution.py:98
  63.9 203.1 %while.10 = (s32[]{:T(128)}, f32[2,1024,8]{1,2,0:T(8,128)S(1)}, bf16[2048,1536]{1,0:T(8,128)(2,1)}, s32[]{:T(128)}) while((s32[]{:T(128)}, f32[2,1024,8]{1,2,0:T(8,128)S(1)}, bf16[2048,1536]{1,0:T(8,128)(2,1)}, s32[]{:T(128)}) %tuple.54), condition=%wide.region_5.6_spmd, body=%wide.region_2.5_spmd.sunk | while | flops 609027072 | bytes 43456232 | solution.py:112
  63.9 4.9 %convolution_bitcast_fusion.4 = f32[2048,48]{0,1:T(8,128)S(1)} fusion(bf16[2048,1536]{1,0:T(8,128)(2,1)} %get-tuple-element.114, bf16[1536,16]{0,1:T(8,128)(2,1)S(1)} %get-tuple-element.95, bf16[1536,16]{0,1:T(8,128)(2,1)S(1)} %get-tuple-element.96, bf16[1536,16]{0,1:T(8,128)(2,1)S(1)} %get-tuple-element.97), kind=kOutput, calls=%fused_computation.1.clone.1 | convolution fusion | flops 302432256 | bytes 6832128 | tf_op jit(solution)/shard_map/while/body/eval_jaxpr/dot_general | solution.py:103
  77.9 3.6 %collective-permute-start.4 = (f32[2,1024,8]{1,2,0:T(8,128)S(1)}, f32[2,1024,8]{1,2,0:T(8,128)S(1)}, u32[]{:S(2)}, u32[]{:S(2)}) collective-permute-start(f32[2,1024,8]{1,2,0:T(8,128)S(1)} %add_add_fusion.8), channel_id=1, source_target_pairs={{0,40},{4,44},{8,32},{12,36},{16,56},{20,60},{24,48},{28,52},{32,8... | collective-permute-start | bytes 196616 | tf_op jit(solution)/shard_map/while/body/eval_jaxpr/ppermute | solution.py:19
  83.0 3.1 %collective-permute-done.4 = f32[2,1024,8]{1,2,0:T(8,128)S(1)} collective-permute-done((f32[2,1024,8]{1,2,0:T(8,128)S(1)}, f32[2,1024,8]{1,2,0:T(8,128)S(1)}, u32[]{:S(2)}, u32[]{:S(2)}) %collective-permute-start.4) | collective-permute-done | bytes 65568 | tf_op jit(solution)/shard_map/while/body/eval_jaxpr/ppermute | solution.py:19
  87.3 3.3 %collective-permute-start.6 = (f32[2,1024,8]{1,2,0:T(8,128)S(1)}, f32[2,1024,8]{1,2,0:T(8,128)S(1)}, u32[]{:S(2)}, u32[]{:S(2)}) collective-permute-start(f32[2,1024,8]{1,2,0:T(8,128)S(1)} %add_add_fusion.9), channel_id=1, source_target_pairs={{0,64},{4,68},{8,72},{12,76},{16,80},{20,84},{24,88},{28,92},{32,9... | collective-permute-start | bytes 196616 | tf_op jit(solution)/shard_map/while/body/eval_jaxpr/ppermute | solution.py:19
  90.6 2.6 collective-permute-done.6
  96.7 4.9 %convolution_bitcast_fusion.4 = f32[2048,48]{0,1:T(8,128)S(1)} fusion(bf16[2048,1536]{1,0:T(8,128)(2,1)} %get-tuple-element.114, bf16[1536,16]{0,1:T(8,128)(2,1)S(1)} %get-tuple-element.95, bf16[1536,16]{0,1:T(8,128)(2,1)S(1)} %get-tuple-element.96, bf16[1536,16]{0,1:T(8,128)(2,1)S(1)} %get-tuple-element.97), kind=kOutput, calls=%fused_computation.1.clone.1 | convolution fusion | flops 302432256 | bytes 6832128 | tf_op jit(solution)/shard_map/while/body/eval_jaxpr/dot_general | solution.py:103
  110.5 2.6 collective-permute-start.3
  113.1 3.8 %collective-permute-start.4 = (f32[2,1024,8]{1,2,0:T(8,128)S(1)}, f32[2,1024,8]{1,2,0:T(8,128)S(1)}, u32[]{:S(2)}, u32[]{:S(2)}) collective-permute-start(f32[2,1024,8]{1,2,0:T(8,128)S(1)} %add_add_fusion.8), channel_id=1, source_target_pairs={{0,40},{4,44},{8,32},{12,36},{16,56},{20,60},{24,48},{28,52},{32,8... | collective-permute-start | bytes 196616 | tf_op jit(solution)/shard_map/while/body/eval_jaxpr/ppermute | solution.py:19
  117.1 4.3 %collective-permute-done.4 = f32[2,1024,8]{1,2,0:T(8,128)S(1)} collective-permute-done((f32[2,1024,8]{1,2,0:T(8,128)S(1)}, f32[2,1024,8]{1,2,0:T(8,128)S(1)}, u32[]{:S(2)}, u32[]{:S(2)}) %collective-permute-start.4) | collective-permute-done | bytes 65568 | tf_op jit(solution)/shard_map/while/body/eval_jaxpr/ppermute | solution.py:19
  122.6 3.0 %collective-permute-start.6 = (f32[2,1024,8]{1,2,0:T(8,128)S(1)}, f32[2,1024,8]{1,2,0:T(8,128)S(1)}, u32[]{:S(2)}, u32[]{:S(2)}) collective-permute-start(f32[2,1024,8]{1,2,0:T(8,128)S(1)} %add_add_fusion.9), channel_id=1, source_target_pairs={{0,64},{4,68},{8,72},{12,76},{16,80},{20,84},{24,88},{28,92},{32,9... | collective-permute-start | bytes 196616 | tf_op jit(solution)/shard_map/while/body/eval_jaxpr/ppermute | solution.py:19
  125.7 2.8 collective-permute-done.6
  132.1 4.9 %convolution_bitcast_fusion.4 = f32[2048,48]{0,1:T(8,128)S(1)} fusion(bf16[2048,1536]{1,0:T(8,128)(2,1)} %get-tuple-element.114, bf16[1536,16]{0,1:T(8,128)(2,1)S(1)} %get-tuple-element.95, bf16[1536,16]{0,1:T(8,128)(2,1)S(1)} %get-tuple-element.96, bf16[1536,16]{0,1:T(8,128)(2,1)S(1)} %get-tuple-element.97), kind=kOutput, calls=%fused_computation.1.clone.1 | convolution fusion | flops 302432256 | bytes 6832128 | tf_op jit(solution)/shard_map/while/body/eval_jaxpr/dot_general | solution.py:103
  146.6 3.2 %collective-permute-start.4 = (f32[2,1024,8]{1,2,0:T(8,128)S(1)}, f32[2,1024,8]{1,2,0:T(8,128)S(1)}, u32[]{:S(2)}, u32[]{:S(2)}) collective-permute-start(f32[2,1024,8]{1,2,0:T(8,128)S(1)} %add_add_fusion.8), channel_id=1, source_target_pairs={{0,40},{4,44},{8,32},{12,36},{16,56},{20,60},{24,48},{28,52},{32,8... | collective-permute-start | bytes 196616 | tf_op jit(solution)/shard_map/while/body/eval_jaxpr/ppermute | solution.py:19
  151.2 3.6 %collective-permute-done.4 = f32[2,1024,8]{1,2,0:T(8,128)S(1)} collective-permute-done((f32[2,1024,8]{1,2,0:T(8,128)S(1)}, f32[2,1024,8]{1,2,0:T(8,128)S(1)}, u32[]{:S(2)}, u32[]{:S(2)}) %collective-permute-start.4) | collective-permute-done | bytes 65568 | tf_op jit(solution)/shard_map/while/body/eval_jaxpr/ppermute | solution.py:19
  155.6 3.4 %collective-permute-start.6 = (f32[2,1024,8]{1,2,0:T(8,128)S(1)}, f32[2,1024,8]{1,2,0:T(8,128)S(1)}, u32[]{:S(2)}, u32[]{:S(2)}) collective-permute-start(f32[2,1024,8]{1,2,0:T(8,128)S(1)} %add_add_fusion.9), channel_id=1, source_target_pairs={{0,64},{4,68},{8,72},{12,76},{16,80},{20,84},{24,88},{28,92},{32,9... | collective-permute-start | bytes 196616 | tf_op jit(solution)/shard_map/while/body/eval_jaxpr/ppermute | solution.py:19
  159.0 2.5 collective-permute-done.6
  165.1 4.9 %convolution_bitcast_fusion.4 = f32[2048,48]{0,1:T(8,128)S(1)} fusion(bf16[2048,1536]{1,0:T(8,128)(2,1)} %get-tuple-element.114, bf16[1536,16]{0,1:T(8,128)(2,1)S(1)} %get-tuple-element.95, bf16[1536,16]{0,1:T(8,128)(2,1)S(1)} %get-tuple-element.96, bf16[1536,16]{0,1:T(8,128)(2,1)S(1)} %get-tuple-element.97), kind=kOutput, calls=%fused_computation.1.clone.1 | convolution fusion | flops 302432256 | bytes 6832128 | tf_op jit(solution)/shard_map/while/body/eval_jaxpr/dot_general | solution.py:103
  177.6 4.3 %collective-permute-start.3 = (f32[2,1024,8]{1,2,0:T(8,128)S(1)}, f32[2,1024,8]{1,2,0:T(8,128)S(1)}, u32[]{:S(2)}, u32[]{:S(2)}) collective-permute-start(f32[2,1024,8]{1,2,0:T(8,128)S(1)} %add_add_fusion.8), channel_id=1, source_target_pairs={{0,32},{4,36},{8,40},{12,44},{16,48},{20,52},{24,56},{28,60},{32,0... | collective-permute-start | bytes 196616 | tf_op jit(solution)/shard_map/while/body/eval_jaxpr/ppermute | solution.py:19
  181.9 2.8 collective-permute-start.4
  185.0 5.1 %collective-permute-done.4 = f32[2,1024,8]{1,2,0:T(8,128)S(1)} collective-permute-done((f32[2,1024,8]{1,2,0:T(8,128)S(1)}, f32[2,1024,8]{1,2,0:T(8,128)S(1)}, u32[]{:S(2)}, u32[]{:S(2)}) %collective-permute-start.4) | collective-permute-done | bytes 65568 | tf_op jit(solution)/shard_map/while/body/eval_jaxpr/ppermute | solution.py:19
  190.8 3.0 %collective-permute-start.6 = (f32[2,1024,8]{1,2,0:T(8,128)S(1)}, f32[2,1024,8]{1,2,0:T(8,128)S(1)}, u32[]{:S(2)}, u32[]{:S(2)}) collective-permute-start(f32[2,1024,8]{1,2,0:T(8,128)S(1)} %add_add_fusion.9), channel_id=1, source_target_pairs={{0,64},{4,68},{8,72},{12,76},{16,80},{20,84},{24,88},{28,92},{32,9... | collective-permute-start | bytes 196616 | tf_op jit(solution)/shard_map/while/body/eval_jaxpr/ppermute | solution.py:19
  193.8 2.8 collective-permute-done.6
  200.3 4.9 %convolution_bitcast_fusion.4 = f32[2048,48]{0,1:T(8,128)S(1)} fusion(bf16[2048,1536]{1,0:T(8,128)(2,1)} %get-tuple-element.114, bf16[1536,16]{0,1:T(8,128)(2,1)S(1)} %get-tuple-element.95, bf16[1536,16]{0,1:T(8,128)(2,1)S(1)} %get-tuple-element.96, bf16[1536,16]{0,1:T(8,128)(2,1)S(1)} %get-tuple-element.97), kind=kOutput, calls=%fused_computation.1.clone.1 | convolution fusion | flops 302432256 | bytes 6832128 | tf_op jit(solution)/shard_map/while/body/eval_jaxpr/dot_general | solution.py:103
  207.5 2.5 collective-permute-start.2
  214.4 2.9 collective-permute-start.4
  219.4 3.2 %collective-permute-done.4 = f32[2,1024,8]{1,2,0:T(8,128)S(1)} collective-permute-done((f32[2,1024,8]{1,2,0:T(8,128)S(1)}, f32[2,1024,8]{1,2,0:T(8,128)S(1)}, u32[]{:S(2)}, u32[]{:S(2)}) %collective-permute-start.4) | collective-permute-done | bytes 65568 | tf_op jit(solution)/shard_map/while/body/eval_jaxpr/ppermute | solution.py:19
  223.3 3.5 %collective-permute-start.6 = (f32[2,1024,8]{1,2,0:T(8,128)S(1)}, f32[2,1024,8]{1,2,0:T(8,128)S(1)}, u32[]{:S(2)}, u32[]{:S(2)}) collective-permute-start(f32[2,1024,8]{1,2,0:T(8,128)S(1)} %add_add_fusion.9), channel_id=1, source_target_pairs={{0,64},{4,68},{8,72},{12,76},{16,80},{20,84},{24,88},{28,92},{32,9... | collective-permute-start | bytes 196616 | tf_op jit(solution)/shard_map/while/body/eval_jaxpr/ppermute | solution.py:19
  226.8 2.3 collective-permute-done.6
  232.8 4.9 %convolution_bitcast_fusion.4 = f32[2048,48]{0,1:T(8,128)S(1)} fusion(bf16[2048,1536]{1,0:T(8,128)(2,1)} %get-tuple-element.114, bf16[1536,16]{0,1:T(8,128)(2,1)S(1)} %get-tuple-element.95, bf16[1536,16]{0,1:T(8,128)(2,1)S(1)} %get-tuple-element.96, bf16[1536,16]{0,1:T(8,128)(2,1)S(1)} %get-tuple-element.97), kind=kOutput, calls=%fused_computation.1.clone.1 | convolution fusion | flops 302432256 | bytes 6832128 | tf_op jit(solution)/shard_map/while/body/eval_jaxpr/dot_general | solution.py:103
  245.1 3.4 %collective-permute-start.3 = (f32[2,1024,8]{1,2,0:T(8,128)S(1)}, f32[2,1024,8]{1,2,0:T(8,128)S(1)}, u32[]{:S(2)}, u32[]{:S(2)}) collective-permute-start(f32[2,1024,8]{1,2,0:T(8,128)S(1)} %add_add_fusion.8), channel_id=1, source_target_pairs={{0,32},{4,36},{8,40},{12,44},{16,48},{20,52},{24,56},{28,60},{32,0... | collective-permute-start | bytes 196616 | tf_op jit(solution)/shard_map/while/body/eval_jaxpr/ppermute | solution.py:19
  248.5 3.3 %collective-permute-start.4 = (f32[2,1024,8]{1,2,0:T(8,128)S(1)}, f32[2,1024,8]{1,2,0:T(8,128)S(1)}, u32[]{:S(2)}, u32[]{:S(2)}) collective-permute-start(f32[2,1024,8]{1,2,0:T(8,128)S(1)} %add_add_fusion.8), channel_id=1, source_target_pairs={{0,40},{4,44},{8,32},{12,36},{16,56},{20,60},{24,48},{28,52},{32,8... | collective-permute-start | bytes 196616 | tf_op jit(solution)/shard_map/while/body/eval_jaxpr/ppermute | solution.py:19
  251.8 4.9 %collective-permute-done.4 = f32[2,1024,8]{1,2,0:T(8,128)S(1)} collective-permute-done((f32[2,1024,8]{1,2,0:T(8,128)S(1)}, f32[2,1024,8]{1,2,0:T(8,128)S(1)}, u32[]{:S(2)}, u32[]{:S(2)}) %collective-permute-start.4) | collective-permute-done | bytes 65568 | tf_op jit(solution)/shard_map/while/body/eval_jaxpr/ppermute | solution.py:19
  257.6 3.0 %collective-permute-start.6 = (f32[2,1024,8]{1,2,0:T(8,128)S(1)}, f32[2,1024,8]{1,2,0:T(8,128)S(1)}, u32[]{:S(2)}, u32[]{:S(2)}) collective-permute-start(f32[2,1024,8]{1,2,0:T(8,128)S(1)} %add_add_fusion.9), channel_id=1, source_target_pairs={{0,64},{4,68},{8,72},{12,76},{16,80},{20,84},{24,88},{28,92},{32,9... | collective-permute-start | bytes 196616 | tf_op jit(solution)/shard_map/while/body/eval_jaxpr/ppermute | solution.py:19
  260.6 2.8 collective-permute-done.6
  267.0 4.7 %fusion.24 = f32[2048,48]{0,1:T(8,128)S(1)} fusion(bf16[2048,1536]{1,0:T(8,128)(2,1)} %get-tuple-element.116, bf16[1536,16]{0,1:T(8,128)(2,1)S(1)} %get-tuple-element.60, bf16[1536,16]{0,1:T(8,128)(2,1)S(1)} %get-tuple-element.59, bf16[1536,16]{0,1:T(8,128)(2,1)S(1)} %get-tuple-element.58), kind=kOutput, calls=%fused_computation.62 | convolution fusion | flops 302432256 | bytes 6832128 | tf_op jit(solution)/shard_map/dot_general | solution.py:103
  278.6 3.0 multiply_reduce_fusion.1
  282.3 3.1 %collective-permute-start.19 = (f32[16]{0:T(128)S(1)}, f32[16]{0:T(128)S(1)}, u32[]{:S(2)}, u32[]{:S(2)}) collective-permute-start(f32[16]{0:T(128)S(1)} %add_add_fusion.5), channel_id=1, source_target_pairs={{0,32},{4,36},{8,40},{12,44},{16,48},{20,52},{24,56},{28,60},{32,0... | collective-permute-start | bytes 200 | tf_op jit(solution)/shard_map/ppermute | solution.py:19
  285.4 2.8 collective-permute-start.20
  288.2 4.6 %collective-permute-done.20 = f32[16]{0:T(128)S(1)} collective-permute-done((f32[16]{0:T(128)S(1)}, f32[16]{0:T(128)S(1)}, u32[]{:S(2)}, u32[]{:S(2)}) %collective-permute-start.20) | collective-permute-done | bytes 96 | tf_op jit(solution)/shard_map/ppermute | solution.py:19
  292.8 3.0 collective-permute-start.21
  (263 shorter events, 108.1 us)
Async XLA Ops:
  2.4 25.5 %collective-permute-start.7 = (bf16[2048,512]{1,0:T(8,128)(2,1)S(1)}, bf16[2048,512]{1,0:T(8,128)(2,1)}, u32[]{:S(2)}, u32[]{:S(2)}) collective-permute-start(bf16[2048,512]{1,0:T(8,128)(2,1)S(1)} %slice.80), channel_id=1, source_target_pairs={{1,0},{2,1},{3,2},{5,4},{6,5},{7,6},{9,8},{10,9},{11,10},{13,12},{... | collective-permute-start | bytes 6291464 | tf_op jit(solution)/shard_map/ppermute | solution.py:14
  31.6 4.7 %collective-permute-start.10 = (f32[2,1536]{1,0:T(2,128)S(1)}, f32[2,1536]{1,0:T(2,128)S(1)}, u32[]{:S(2)}, u32[]{:S(2)}) collective-permute-start(f32[2,1536]{1,0:T(2,128)S(1)} %pad_maximum_fusion.2), channel_id=1, source_target_pairs={{0,20},{4,16},{8,28},{12,24},{16,4},{20,0},{24,12},{28,8},{32,52},... | collective-permute-start | bytes 36872 | tf_op jit(solution)/shard_map/ppermute | solution.py:19
  38.4 6.6 %collective-permute-start.11 = (f32[2,1536]{1,0:T(2,128)S(1)}, f32[2,1536]{1,0:T(2,128)S(1)}, u32[]{:S(2)}, u32[]{:S(2)}) collective-permute-start(f32[2,1536]{1,0:T(2,128)S(1)} %add_add_fusion.3), channel_id=1, source_target_pairs={{0,8},{4,12},{8,0},{12,4},{16,24},{20,28},{24,16},{28,20},{32,40},... | collective-permute-start | bytes 36872 | tf_op jit(solution)/shard_map/ppermute | solution.py:19
  41.6 5.2 %collective-permute-start.12 = (f32[2,1536]{1,0:T(2,128)S(1)}, f32[2,1536]{1,0:T(2,128)S(1)}, u32[]{:S(2)}, u32[]{:S(2)}) collective-permute-start(f32[2,1536]{1,0:T(2,128)S(1)} %add_add_fusion.3), channel_id=1, source_target_pairs={{0,32},{4,36},{8,40},{12,44},{16,48},{20,52},{24,56},{28,60},{32,0... | collective-permute-start | bytes 36872 | tf_op jit(solution)/shard_map/ppermute | solution.py:19
  44.5 7.6 %collective-permute-start.13 = (f32[2,1536]{1,0:T(2,128)S(1)}, f32[2,1536]{1,0:T(2,128)S(1)}, u32[]{:S(2)}, u32[]{:S(2)}) collective-permute-start(f32[2,1536]{1,0:T(2,128)S(1)} %add_add_fusion.3), channel_id=1, source_target_pairs={{0,40},{4,44},{8,32},{12,36},{16,56},{20,60},{24,48},{28,52},{32,8... | collective-permute-start | bytes 36872 | tf_op jit(solution)/shard_map/ppermute | solution.py:19
  52.1 5.3 %collective-permute-start.14 = (f32[2,1536]{1,0:T(2,128)S(1)}, f32[2,1536]{1,0:T(2,128)S(1)}, u32[]{:S(2)}, u32[]{:S(2)}) collective-permute-start(f32[2,1536]{1,0:T(2,128)S(1)} %add_add_fusion.2), channel_id=1, source_target_pairs={{0,64},{4,68},{8,72},{12,76},{16,80},{20,84},{24,88},{28,92},{32,9... | collective-permute-start | bytes 36872 | tf_op jit(solution)/shard_map/ppermute | solution.py:19
  70.5 5.2 %collective-permute-start.1 = (f32[2,1024,8]{1,2,0:T(8,128)S(1)}, f32[2,1024,8]{1,2,0:T(8,128)S(1)}, u32[]{:S(2)}, u32[]{:S(2)}) collective-permute-start(f32[2,1024,8]{1,2,0:T(8,128)S(1)} %pad_maximum_fusion.4), channel_id=1, source_target_pairs={{0,20},{4,16},{8,28},{12,24},{16,4},{20,0},{24,12},{28,8},{32,52},... | collective-permute-start | bytes 196616 | tf_op jit(solution)/shard_map/while/body/eval_jaxpr/ppermute | solution.py:19
  76.4 6.6 %collective-permute-start.3 = (f32[2,1024,8]{1,2,0:T(8,128)S(1)}, f32[2,1024,8]{1,2,0:T(8,128)S(1)}, u32[]{:S(2)}, u32[]{:S(2)}) collective-permute-start(f32[2,1024,8]{1,2,0:T(8,128)S(1)} %add_add_fusion.8), channel_id=1, source_target_pairs={{0,32},{4,36},{8,40},{12,44},{16,48},{20,52},{24,56},{28,60},{32,0... | collective-permute-start | bytes 196616 | tf_op jit(solution)/shard_map/while/body/eval_jaxpr/ppermute | solution.py:19
  77.9 8.2 %collective-permute-start.4 = (f32[2,1024,8]{1,2,0:T(8,128)S(1)}, f32[2,1024,8]{1,2,0:T(8,128)S(1)}, u32[]{:S(2)}, u32[]{:S(2)}) collective-permute-start(f32[2,1024,8]{1,2,0:T(8,128)S(1)} %add_add_fusion.8), channel_id=1, source_target_pairs={{0,40},{4,44},{8,32},{12,36},{16,56},{20,60},{24,48},{28,52},{32,8... | collective-permute-start | bytes 196616 | tf_op jit(solution)/shard_map/while/body/eval_jaxpr/ppermute | solution.py:19
  81.5 5.8 %collective-permute-start.5 = (f32[2,1024,8]{1,2,0:T(8,128)S(1)}, f32[2,1024,8]{1,2,0:T(8,128)S(1)}, u32[]{:S(2)}, u32[]{:S(2)}) collective-permute-start(f32[2,1024,8]{1,2,0:T(8,128)S(1)} %add_add_fusion.8), channel_id=1, source_target_pairs={{0,8},{4,12},{8,0},{12,4},{16,24},{20,28},{24,16},{28,20},{32,40},... | collective-permute-start | bytes 196616 | tf_op jit(solution)/shard_map/while/body/eval_jaxpr/ppermute | solution.py:19
  87.3 5.8 %collective-permute-start.6 = (f32[2,1024,8]{1,2,0:T(8,128)S(1)}, f32[2,1024,8]{1,2,0:T(8,128)S(1)}, u32[]{:S(2)}, u32[]{:S(2)}) collective-permute-start(f32[2,1024,8]{1,2,0:T(8,128)S(1)} %add_add_fusion.9), channel_id=1, source_target_pairs={{0,64},{4,68},{8,72},{12,76},{16,80},{20,84},{24,88},{28,92},{32,9... | collective-permute-start | bytes 196616 | tf_op jit(solution)/shard_map/while/body/eval_jaxpr/ppermute | solution.py:19
  102.9 4.6 %collective-permute-start = (f32[2,1024,8]{1,2,0:T(8,128)S(1)}, f32[2,1024,8]{1,2,0:T(8,128)S(1)}, u32[]{:S(2)}, u32[]{:S(2)}) collective-permute-start(f32[2,1024,8]{1,2,0:T(8,128)S(1)} %pad_maximum_fusion.4), channel_id=1, source_target_pairs={{0,16},{4,20},{8,24},{12,28},{16,0},{20,4},{24,8},{28,12},{32,48},... | collective-permute-start | bytes 196616 | tf_op jit(solution)/shard_map/while/body/eval_jaxpr/ppermute | solution.py:19
  103.1 6.0 %collective-permute-start.1 = (f32[2,1024,8]{1,2,0:T(8,128)S(1)}, f32[2,1024,8]{1,2,0:T(8,128)S(1)}, u32[]{:S(2)}, u32[]{:S(2)}) collective-permute-start(f32[2,1024,8]{1,2,0:T(8,128)S(1)} %pad_maximum_fusion.4), channel_id=1, source_target_pairs={{0,20},{4,16},{8,28},{12,24},{16,4},{20,0},{24,12},{28,8},{32,52},... | collective-permute-start | bytes 196616 | tf_op jit(solution)/shard_map/while/body/eval_jaxpr/ppermute | solution.py:19
  104.8 5.7 %collective-permute-start.2 = (f32[2,1024,8]{1,2,0:T(8,128)S(1)}, f32[2,1024,8]{1,2,0:T(8,128)S(1)}, u32[]{:S(2)}, u32[]{:S(2)}) collective-permute-start(f32[2,1024,8]{1,2,0:T(8,128)S(1)} %pad_maximum_fusion.4), channel_id=1, source_target_pairs={{0,4},{4,0},{8,12},{12,8},{16,20},{20,16},{24,28},{28,24},{32,36},... | collective-permute-start | bytes 196616 | tf_op jit(solution)/shard_map/while/body/eval_jaxpr/ppermute | solution.py:19
  110.5 6.6 %collective-permute-start.3 = (f32[2,1024,8]{1,2,0:T(8,128)S(1)}, f32[2,1024,8]{1,2,0:T(8,128)S(1)}, u32[]{:S(2)}, u32[]{:S(2)}) collective-permute-start(f32[2,1024,8]{1,2,0:T(8,128)S(1)} %add_add_fusion.8), channel_id=1, source_target_pairs={{0,32},{4,36},{8,40},{12,44},{16,48},{20,52},{24,56},{28,60},{32,0... | collective-permute-start | bytes 196616 | tf_op jit(solution)/shard_map/while/body/eval_jaxpr/ppermute | solution.py:19
  113.1 8.3 %collective-permute-start.4 = (f32[2,1024,8]{1,2,0:T(8,128)S(1)}, f32[2,1024,8]{1,2,0:T(8,128)S(1)}, u32[]{:S(2)}, u32[]{:S(2)}) collective-permute-start(f32[2,1024,8]{1,2,0:T(8,128)S(1)} %add_add_fusion.8), channel_id=1, source_target_pairs={{0,40},{4,44},{8,32},{12,36},{16,56},{20,60},{24,48},{28,52},{32,8... | collective-permute-start | bytes 196616 | tf_op jit(solution)/shard_map/while/body/eval_jaxpr/ppermute | solution.py:19
  116.9 5.8 %collective-permute-start.5 = (f32[2,1024,8]{1,2,0:T(8,128)S(1)}, f32[2,1024,8]{1,2,0:T(8,128)S(1)}, u32[]{:S(2)}, u32[]{:S(2)}) collective-permute-start(f32[2,1024,8]{1,2,0:T(8,128)S(1)} %add_add_fusion.8), channel_id=1, source_target_pairs={{0,8},{4,12},{8,0},{12,4},{16,24},{20,28},{24,16},{28,20},{32,40},... | collective-permute-start | bytes 196616 | tf_op jit(solution)/shard_map/while/body/eval_jaxpr/ppermute | solution.py:19
  122.6 5.8 %collective-permute-start.6 = (f32[2,1024,8]{1,2,0:T(8,128)S(1)}, f32[2,1024,8]{1,2,0:T(8,128)S(1)}, u32[]{:S(2)}, u32[]{:S(2)}) collective-permute-start(f32[2,1024,8]{1,2,0:T(8,128)S(1)} %add_add_fusion.9), channel_id=1, source_target_pairs={{0,64},{4,68},{8,72},{12,76},{16,80},{20,84},{24,88},{28,92},{32,9... | collective-permute-start | bytes 196616 | tf_op jit(solution)/shard_map/while/body/eval_jaxpr/ppermute | solution.py:19
  138.7 5.2 %collective-permute-start.1 = (f32[2,1024,8]{1,2,0:T(8,128)S(1)}, f32[2,1024,8]{1,2,0:T(8,128)S(1)}, u32[]{:S(2)}, u32[]{:S(2)}) collective-permute-start(f32[2,1024,8]{1,2,0:T(8,128)S(1)} %pad_maximum_fusion.4), channel_id=1, source_target_pairs={{0,20},{4,16},{8,28},{12,24},{16,4},{20,0},{24,12},{28,8},{32,52},... | collective-permute-start | bytes 196616 | tf_op jit(solution)/shard_map/while/body/eval_jaxpr/ppermute | solution.py:19
  140.1 4.5 %collective-permute-start.2 = (f32[2,1024,8]{1,2,0:T(8,128)S(1)}, f32[2,1024,8]{1,2,0:T(8,128)S(1)}, u32[]{:S(2)}, u32[]{:S(2)}) collective-permute-start(f32[2,1024,8]{1,2,0:T(8,128)S(1)} %pad_maximum_fusion.4), channel_id=1, source_target_pairs={{0,4},{4,0},{8,12},{12,8},{16,20},{20,16},{24,28},{28,24},{32,36},... | collective-permute-start | bytes 196616 | tf_op jit(solution)/shard_map/while/body/eval_jaxpr/ppermute | solution.py:19
  144.6 6.6 %collective-permute-start.3 = (f32[2,1024,8]{1,2,0:T(8,128)S(1)}, f32[2,1024,8]{1,2,0:T(8,128)S(1)}, u32[]{:S(2)}, u32[]{:S(2)}) collective-permute-start(f32[2,1024,8]{1,2,0:T(8,128)S(1)} %add_add_fusion.8), channel_id=1, source_target_pairs={{0,32},{4,36},{8,40},{12,44},{16,48},{20,52},{24,56},{28,60},{32,0... | collective-permute-start | bytes 196616 | tf_op jit(solution)/shard_map/while/body/eval_jaxpr/ppermute | solution.py:19
  146.6 8.2 %collective-permute-start.4 = (f32[2,1024,8]{1,2,0:T(8,128)S(1)}, f32[2,1024,8]{1,2,0:T(8,128)S(1)}, u32[]{:S(2)}, u32[]{:S(2)}) collective-permute-start(f32[2,1024,8]{1,2,0:T(8,128)S(1)} %add_add_fusion.8), channel_id=1, source_target_pairs={{0,40},{4,44},{8,32},{12,36},{16,56},{20,60},{24,48},{28,52},{32,8... | collective-permute-start | bytes 196616 | tf_op jit(solution)/shard_map/while/body/eval_jaxpr/ppermute | solution.py:19
  149.8 5.8 %collective-permute-start.5 = (f32[2,1024,8]{1,2,0:T(8,128)S(1)}, f32[2,1024,8]{1,2,0:T(8,128)S(1)}, u32[]{:S(2)}, u32[]{:S(2)}) collective-permute-start(f32[2,1024,8]{1,2,0:T(8,128)S(1)} %add_add_fusion.8), channel_id=1, source_target_pairs={{0,8},{4,12},{8,0},{12,4},{16,24},{20,28},{24,16},{28,20},{32,40},... | collective-permute-start | bytes 196616 | tf_op jit(solution)/shard_map/while/body/eval_jaxpr/ppermute | solution.py:19
  155.6 5.8 %collective-permute-start.6 = (f32[2,1024,8]{1,2,0:T(8,128)S(1)}, f32[2,1024,8]{1,2,0:T(8,128)S(1)}, u32[]{:S(2)}, u32[]{:S(2)}) collective-permute-start(f32[2,1024,8]{1,2,0:T(8,128)S(1)} %add_add_fusion.9), channel_id=1, source_target_pairs={{0,64},{4,68},{8,72},{12,76},{16,80},{20,84},{24,88},{28,92},{32,9... | collective-permute-start | bytes 196616 | tf_op jit(solution)/shard_map/while/body/eval_jaxpr/ppermute | solution.py:19
  171.7 5.3 %collective-permute-start.1 = (f32[2,1024,8]{1,2,0:T(8,128)S(1)}, f32[2,1024,8]{1,2,0:T(8,128)S(1)}, u32[]{:S(2)}, u32[]{:S(2)}) collective-permute-start(f32[2,1024,8]{1,2,0:T(8,128)S(1)} %pad_maximum_fusion.4), channel_id=1, source_target_pairs={{0,20},{4,16},{8,28},{12,24},{16,4},{20,0},{24,12},{28,8},{32,52},... | collective-permute-start | bytes 196616 | tf_op jit(solution)/shard_map/while/body/eval_jaxpr/ppermute | solution.py:19
  177.6 7.3 %collective-permute-start.3 = (f32[2,1024,8]{1,2,0:T(8,128)S(1)}, f32[2,1024,8]{1,2,0:T(8,128)S(1)}, u32[]{:S(2)}, u32[]{:S(2)}) collective-permute-start(f32[2,1024,8]{1,2,0:T(8,128)S(1)} %add_add_fusion.8), channel_id=1, source_target_pairs={{0,32},{4,36},{8,40},{12,44},{16,48},{20,52},{24,56},{28,60},{32,0... | collective-permute-start | bytes 196616 | tf_op jit(solution)/shard_map/while/body/eval_jaxpr/ppermute | solution.py:19
  181.9 8.2 %collective-permute-start.4 = (f32[2,1024,8]{1,2,0:T(8,128)S(1)}, f32[2,1024,8]{1,2,0:T(8,128)S(1)}, u32[]{:S(2)}, u32[]{:S(2)}) collective-permute-start(f32[2,1024,8]{1,2,0:T(8,128)S(1)} %add_add_fusion.8), channel_id=1, source_target_pairs={{0,40},{4,44},{8,32},{12,36},{16,56},{20,60},{24,48},{28,52},{32,8... | collective-permute-start | bytes 196616 | tf_op jit(solution)/shard_map/while/body/eval_jaxpr/ppermute | solution.py:19
  184.7 6.1 %collective-permute-start.5 = (f32[2,1024,8]{1,2,0:T(8,128)S(1)}, f32[2,1024,8]{1,2,0:T(8,128)S(1)}, u32[]{:S(2)}, u32[]{:S(2)}) collective-permute-start(f32[2,1024,8]{1,2,0:T(8,128)S(1)} %add_add_fusion.8), channel_id=1, source_target_pairs={{0,8},{4,12},{8,0},{12,4},{16,24},{20,28},{24,16},{28,20},{32,40},... | collective-permute-start | bytes 196616 | tf_op jit(solution)/shard_map/while/body/eval_jaxpr/ppermute | solution.py:19
  190.8 5.8 %collective-permute-start.6 = (f32[2,1024,8]{1,2,0:T(8,128)S(1)}, f32[2,1024,8]{1,2,0:T(8,128)S(1)}, u32[]{:S(2)}, u32[]{:S(2)}) collective-permute-start(f32[2,1024,8]{1,2,0:T(8,128)S(1)} %add_add_fusion.9), channel_id=1, source_target_pairs={{0,64},{4,68},{8,72},{12,76},{16,80},{20,84},{24,88},{28,92},{32,9... | collective-permute-start | bytes 196616 | tf_op jit(solution)/shard_map/while/body/eval_jaxpr/ppermute | solution.py:19
  207.0 5.2 %collective-permute-start.1 = (f32[2,1024,8]{1,2,0:T(8,128)S(1)}, f32[2,1024,8]{1,2,0:T(8,128)S(1)}, u32[]{:S(2)}, u32[]{:S(2)}) collective-permute-start(f32[2,1024,8]{1,2,0:T(8,128)S(1)} %pad_maximum_fusion.4), channel_id=1, source_target_pairs={{0,20},{4,16},{8,28},{12,24},{16,4},{20,0},{24,12},{28,8},{32,52},... | collective-permute-start | bytes 196616 | tf_op jit(solution)/shard_map/while/body/eval_jaxpr/ppermute | solution.py:19
  207.5 5.3 %collective-permute-start.2 = (f32[2,1024,8]{1,2,0:T(8,128)S(1)}, f32[2,1024,8]{1,2,0:T(8,128)S(1)}, u32[]{:S(2)}, u32[]{:S(2)}) collective-permute-start(f32[2,1024,8]{1,2,0:T(8,128)S(1)} %pad_maximum_fusion.4), channel_id=1, source_target_pairs={{0,4},{4,0},{8,12},{12,8},{16,20},{20,16},{24,28},{28,24},{32,36},... | collective-permute-start | bytes 196616 | tf_op jit(solution)/shard_map/while/body/eval_jaxpr/ppermute | solution.py:19
  212.9 6.6 %collective-permute-start.3 = (f32[2,1024,8]{1,2,0:T(8,128)S(1)}, f32[2,1024,8]{1,2,0:T(8,128)S(1)}, u32[]{:S(2)}, u32[]{:S(2)}) collective-permute-start(f32[2,1024,8]{1,2,0:T(8,128)S(1)} %add_add_fusion.8), channel_id=1, source_target_pairs={{0,32},{4,36},{8,40},{12,44},{16,48},{20,52},{24,56},{28,60},{32,0... | collective-permute-start | bytes 196616 | tf_op jit(solution)/shard_map/while/body/eval_jaxpr/ppermute | solution.py:19
  214.4 8.2 %collective-permute-start.4 = (f32[2,1024,8]{1,2,0:T(8,128)S(1)}, f32[2,1024,8]{1,2,0:T(8,128)S(1)}, u32[]{:S(2)}, u32[]{:S(2)}) collective-permute-start(f32[2,1024,8]{1,2,0:T(8,128)S(1)} %add_add_fusion.8), channel_id=1, source_target_pairs={{0,40},{4,44},{8,32},{12,36},{16,56},{20,60},{24,48},{28,52},{32,8... | collective-permute-start | bytes 196616 | tf_op jit(solution)/shard_map/while/body/eval_jaxpr/ppermute | solution.py:19
  217.3 6.0 %collective-permute-start.5 = (f32[2,1024,8]{1,2,0:T(8,128)S(1)}, f32[2,1024,8]{1,2,0:T(8,128)S(1)}, u32[]{:S(2)}, u32[]{:S(2)}) collective-permute-start(f32[2,1024,8]{1,2,0:T(8,128)S(1)} %add_add_fusion.8), channel_id=1, source_target_pairs={{0,8},{4,12},{8,0},{12,4},{16,24},{20,28},{24,16},{28,20},{32,40},... | collective-permute-start | bytes 196616 | tf_op jit(solution)/shard_map/while/body/eval_jaxpr/ppermute | solution.py:19
  223.3 5.8 %collective-permute-start.6 = (f32[2,1024,8]{1,2,0:T(8,128)S(1)}, f32[2,1024,8]{1,2,0:T(8,128)S(1)}, u32[]{:S(2)}, u32[]{:S(2)}) collective-permute-start(f32[2,1024,8]{1,2,0:T(8,128)S(1)} %add_add_fusion.9), channel_id=1, source_target_pairs={{0,64},{4,68},{8,72},{12,76},{16,80},{20,84},{24,88},{28,92},{32,9... | collective-permute-start | bytes 196616 | tf_op jit(solution)/shard_map/while/body/eval_jaxpr/ppermute | solution.py:19
  239.2 5.2 %collective-permute-start.1 = (f32[2,1024,8]{1,2,0:T(8,128)S(1)}, f32[2,1024,8]{1,2,0:T(8,128)S(1)}, u32[]{:S(2)}, u32[]{:S(2)}) collective-permute-start(f32[2,1024,8]{1,2,0:T(8,128)S(1)} %pad_maximum_fusion.4), channel_id=1, source_target_pairs={{0,20},{4,16},{8,28},{12,24},{16,4},{20,0},{24,12},{28,8},{32,52},... | collective-permute-start | bytes 196616 | tf_op jit(solution)/shard_map/while/body/eval_jaxpr/ppermute | solution.py:19
  240.6 4.5 %collective-permute-start.2 = (f32[2,1024,8]{1,2,0:T(8,128)S(1)}, f32[2,1024,8]{1,2,0:T(8,128)S(1)}, u32[]{:S(2)}, u32[]{:S(2)}) collective-permute-start(f32[2,1024,8]{1,2,0:T(8,128)S(1)} %pad_maximum_fusion.4), channel_id=1, source_target_pairs={{0,4},{4,0},{8,12},{12,8},{16,20},{20,16},{24,28},{28,24},{32,36},... | collective-permute-start | bytes 196616 | tf_op jit(solution)/shard_map/while/body/eval_jaxpr/ppermute | solution.py:19
  245.1 6.7 %collective-permute-start.3 = (f32[2,1024,8]{1,2,0:T(8,128)S(1)}, f32[2,1024,8]{1,2,0:T(8,128)S(1)}, u32[]{:S(2)}, u32[]{:S(2)}) collective-permute-start(f32[2,1024,8]{1,2,0:T(8,128)S(1)} %add_add_fusion.8), channel_id=1, source_target_pairs={{0,32},{4,36},{8,40},{12,44},{16,48},{20,52},{24,56},{28,60},{32,0... | collective-permute-start | bytes 196616 | tf_op jit(solution)/shard_map/while/body/eval_jaxpr/ppermute | solution.py:19
  248.5 8.2 %collective-permute-start.4 = (f32[2,1024,8]{1,2,0:T(8,128)S(1)}, f32[2,1024,8]{1,2,0:T(8,128)S(1)}, u32[]{:S(2)}, u32[]{:S(2)}) collective-permute-start(f32[2,1024,8]{1,2,0:T(8,128)S(1)} %add_add_fusion.8), channel_id=1, source_target_pairs={{0,40},{4,44},{8,32},{12,36},{16,56},{20,60},{24,48},{28,52},{32,8... | collective-permute-start | bytes 196616 | tf_op jit(solution)/shard_map/while/body/eval_jaxpr/ppermute | solution.py:19
  251.8 5.8 %collective-permute-start.5 = (f32[2,1024,8]{1,2,0:T(8,128)S(1)}, f32[2,1024,8]{1,2,0:T(8,128)S(1)}, u32[]{:S(2)}, u32[]{:S(2)}) collective-permute-start(f32[2,1024,8]{1,2,0:T(8,128)S(1)} %add_add_fusion.8), channel_id=1, source_target_pairs={{0,8},{4,12},{8,0},{12,4},{16,24},{20,28},{24,16},{28,20},{32,40},... | collective-permute-start | bytes 196616 | tf_op jit(solution)/shard_map/while/body/eval_jaxpr/ppermute | solution.py:19
  257.6 5.8 %collective-permute-start.6 = (f32[2,1024,8]{1,2,0:T(8,128)S(1)}, f32[2,1024,8]{1,2,0:T(8,128)S(1)}, u32[]{:S(2)}, u32[]{:S(2)}) collective-permute-start(f32[2,1024,8]{1,2,0:T(8,128)S(1)} %add_add_fusion.9), channel_id=1, source_target_pairs={{0,64},{4,68},{8,72},{12,76},{16,80},{20,84},{24,88},{28,92},{32,9... | collective-permute-start | bytes 196616 | tf_op jit(solution)/shard_map/while/body/eval_jaxpr/ppermute | solution.py:19
  271.9 9.7 %collective-permute-start.15 = (f32[16]{0:T(128)S(1)}, f32[16]{0:T(128)S(1)}, u32[]{:S(2)}, u32[]{:S(2)}) collective-permute-start(f32[16]{0:T(128)S(1)} %get-tuple-element.35), channel_id=1, source_target_pairs={{0,4},{4,0},{8,12},{12,8},{16,20},{20,16},{24,28},{28,24},{32,36},... | collective-permute-start | bytes 200 | tf_op jit(solution)/shard_map/ppermute | solution.py:19
  272.4 9.2 %collective-permute-start.16 = (f32[16]{0:T(128)S(1)}, f32[16]{0:T(128)S(1)}, u32[]{:S(2)}, u32[]{:S(2)}) collective-permute-start(f32[16]{0:T(128)S(1)} %get-tuple-element.35), channel_id=1, source_target_pairs={{0,16},{4,20},{8,24},{12,28},{16,0},{20,4},{24,8},{28,12},{32,48},... | collective-permute-start | bytes 200 | tf_op jit(solution)/shard_map/ppermute | solution.py:19
  273.1 8.4 %collective-permute-start.17 = (f32[16]{0:T(128)S(1)}, f32[16]{0:T(128)S(1)}, u32[]{:S(2)}, u32[]{:S(2)}) collective-permute-start(f32[16]{0:T(128)S(1)} %get-tuple-element.35), channel_id=1, source_target_pairs={{0,20},{4,16},{8,28},{12,24},{16,4},{20,0},{24,12},{28,8},{32,52},... | collective-permute-start | bytes 200 | tf_op jit(solution)/shard_map/ppermute | solution.py:19
  281.6 6.6 %collective-permute-start.18 = (f32[16]{0:T(128)S(1)}, f32[16]{0:T(128)S(1)}, u32[]{:S(2)}, u32[]{:S(2)}) collective-permute-start(f32[16]{0:T(128)S(1)} %add_add_fusion.5), channel_id=1, source_target_pairs={{0,8},{4,12},{8,0},{12,4},{16,24},{20,28},{24,16},{28,20},{32,40},... | collective-permute-start | bytes 200 | tf_op jit(solution)/shard_map/ppermute | solution.py:19
  282.3 5.9 %collective-permute-start.19 = (f32[16]{0:T(128)S(1)}, f32[16]{0:T(128)S(1)}, u32[]{:S(2)}, u32[]{:S(2)}) collective-permute-start(f32[16]{0:T(128)S(1)} %add_add_fusion.5), channel_id=1, source_target_pairs={{0,32},{4,36},{8,40},{12,44},{16,48},{20,52},{24,56},{28,60},{32,0... | collective-permute-start | bytes 200 | tf_op jit(solution)/shard_map/ppermute | solution.py:19
  285.4 7.5 %collective-permute-start.20 = (f32[16]{0:T(128)S(1)}, f32[16]{0:T(128)S(1)}, u32[]{:S(2)}, u32[]{:S(2)}) collective-permute-start(f32[16]{0:T(128)S(1)} %add_add_fusion.5), channel_id=1, source_target_pairs={{0,40},{4,44},{8,32},{12,36},{16,56},{20,60},{24,48},{28,52},{32,8... | collective-permute-start | bytes 200 | tf_op jit(solution)/shard_map/ppermute | solution.py:19
  292.8 5.1 %collective-permute-start.21 = (f32[16]{0:T(128)S(1)}, f32[16]{0:T(128)S(1)}, u32[]{:S(2)}, u32[]{:S(2)}) collective-permute-start(f32[16]{0:T(128)S(1)} %add_add_fusion.4), channel_id=1, source_target_pairs={{0,64},{4,68},{8,72},{12,76},{16,80},{20,84},{24,88},{28,92},{32,9... | collective-permute-start | bytes 200 | tf_op jit(solution)/shard_map/ppermute | solution.py:19
  (20 other events, 114.5 us)

commit v8 on v3

--- a/solution.py
+++ b/solution.py
@@ -39,11 +39,20 @@
 
 def orthonormal(image):
     gram = jnp.einsum("swk,swl->skl", image, image, precision=HIGHEST)
-    factor = jnp.linalg.cholesky(gram)
-    solved = jax.vmap(lambda fac, rhs: jax.scipy.linalg.solve_triangular(fac, rhs, lower=True))(
-        factor, jnp.swapaxes(image, 1, 2)
-    )
-    return jnp.swapaxes(solved, 1, 2)
+    size = gram.shape[1]
+    index = jnp.arange(size)
+    factor = jnp.zeros_like(gram)
+    for k in range(size):
+        column = jnp.where(index >= k, gram[:, :, k] / jnp.sqrt(gram[:, k, k])[:, None], 0.0)
+        factor = factor + column[:, :, None] * (index == k)[None, None, :]
+        gram = gram - column[:, :, None] * column[:, None, :]
+    inverse = jnp.zeros_like(factor)
+    rest = jnp.broadcast_to(jnp.eye(size, dtype=factor.dtype), factor.shape)
+    for k in range(size):
+        row = rest[:, k, :] / factor[:, k, k][:, None]
+        inverse = inverse + (index == k)[None, :, None] * row[:, None, :]
+        rest = rest - factor[:, :, k][:, :, None] * row[:, None, :]
+    return jnp.einsum("swk,sck->swc", image, inverse, precision=HIGHEST)
 
 
 def pieces(value):

time: 275 us -> 286 us (1.040)
  local copies, waits for them, and re-layouts: 4.48 us -> 13.9 us
    another operation x42 -> x0, other arithmetic: 17.8 us -> none  [the longest x24 9.76 us: orthonormal(): factor = jnp.linalg.cholesky(gram)]
    sqrt x0 -> x48, local copies, waits for them, and re-layouts: none -> 8.3 us  [orthonormal(): jnp.sqrt(gram[:, k, k])[:, None]]
    sub x0 -> x78, other arithmetic: none -> 6.39 us  [the longest x42 3.54 us: orthonormal(): gram = gram - column[:, :, None] * column[:, None, :]]
    select_n x0 -> x78, other arithmetic: none -> 5.91 us  [orthonormal(): jnp.where(index >= k, gram[:, :, k] / jnp.sqrt(gram[:, k, k])[:, None], 0.0)]
    div x6 -> x60, other arithmetic: 0.05 us -> 4.6 us  [the longest x48 3.71 us: orthonormal(): row = rest[:, k, :] / factor[:, k, k][:, None]]
where the time goes in v8:
time: 286 us; the launch traced here: 285 us
  waiting for transfers between devices  100 us (35%)
  starting transfers between devices  89.9 us (31%)
  matrix products  48 us (17%)
  other arithmetic  30.6 us (11%)
  local copies, waits for them, and re-layouts  13.9 us (5%)
    ppermute x56, starting transfers between devices, swapped(): return lax.ppermute(value, axis, [(i, i ^ mask) for i in range(size)])  88 us
    ppermute x56, waiting for transfers between devices, swapped(): return lax.ppermute(value, axis, [(i, i ^ mask) for i in range(size)])  76.6 us
    dot_general x7, matrix products, project(): jnp.dot(stand, jnp.concatenate(pieces(wide), 1), preferred_element_type=j...  33.9 us
    ppermute x1, waiting for transfers between devices, passed_along(): return lax.ppermute(array, axis, pairs)  23.5 us
    sqrt x48, local copies, waits for them, and re-layouts, orthonormal(): jnp.sqrt(gram[:, k, k])[:, None]  8.3 us
    dot_general x6, matrix products, image_of(): lax.dot_general(stand, split, (((0,), (0,)), ((), ())), preferred_element...  6.76 us
    convert_element_type x1, other arithmetic, shards(): ((regionf - mean) / jnp.sqrt(var + 1e-05) * weight).astype(jnp.bfloat16)  6.36 us
    select_n x78, other arithmetic, orthonormal(): jnp.where(index >= k, gram[:, :, k] / jnp.sqrt(gram[:, k, k])[:, None], 0.0)  5.91 us
  transfers between devices with their start and end apart: 57, of which 51 were waited for; matrix products, arithmetic and copies ran while one was open for 2% of the time, Pallas kernels for 0%

profile of v8, /device:TPU:32, one launch (start us, length us, event | category | flops | bytes accessed | tf_op | source)
XLA Modules:
  0.0 285.1 jit_solution(13983360311231335699)
XLA Ops:
  4.3 23.5 %collective-permute-done.7 = bf16[2048,512]{1,0:T(8,128)(2,1)} collective-permute-done((bf16[2048,512]{1,0:T(8,128)(2,1)S(1)}, bf16[2048,512]{1,0:T(8,128)(2,1)}, u32[]{:S(2)}, u32[]{:S(2)}) %collective-permute-start.7) | collective-permute-done | bytes 2097184 | tf_op jit(solution)/shard_map/ppermute | solution.py:14
  31.6 3.1 %collective-permute-start.10 = (f32[2,1536]{1,0:T(2,128)S(1)}, f32[2,1536]{1,0:T(2,128)S(1)}, u32[]{:S(2)}, u32[]{:S(2)}) collective-permute-start(f32[2,1536]{1,0:T(2,128)S(1)} %pad_maximum_fusion.2), channel_id=1, source_target_pairs={{0,12},{4,8},{8,4},{12,0},{16,28},{20,24},{24,20},{28,16},{32,44},... | collective-permute-start | bytes 36872 | tf_op jit(solution)/shard_map/ppermute | solution.py:19
  41.8 2.7 collective-permute-start.12
  47.0 2.4 collective-permute-done.13
  49.4 3.1 %collective-permute-start.14 = (f32[2,1536]{1,0:T(2,128)S(1)}, f32[2,1536]{1,0:T(2,128)S(1)}, u32[]{:S(2)}, u32[]{:S(2)}) collective-permute-start(f32[2,1536]{1,0:T(2,128)S(1)} %add_add_fusion.2), channel_id=1, source_target_pairs={{0,64},{4,68},{8,72},{12,76},{16,80},{20,84},{24,88},{28,92},{32,9... | collective-permute-start | bytes 36872 | tf_op jit(solution)/shard_map/ppermute | solution.py:19
  54.8 6.4 %fusion.62 = bf16[2048,1536]{1,0:T(8,128)(2,1)} fusion(f32[1536]{0:T(1024)S(1)} %multiply_sqrt_fusion, f32[1536]{0:T(1024)S(1)} %get-tuple-element.34, f32[1536]{0:T(1024)S(1)} %get-tuple-element.33, bf16[2048,512]{1,0:T(8,128)(2,1)S(1)} %broadcast_select_fusion.7, bf16[2048,1024]{1,0:T(8,128)(2,1)} %param.6), kind=kLoop, calls=%fused_computation.161 | loop fusion | flops 25165824 | bytes 12601344 | tf_op jit(solution)/shard_map/convert_element_type | solution.py:102
  61.1 194.8 %while.10 = (s32[]{:T(128)}, f32[2,1024,8]{1,2,0:T(8,128)S(1)}, bf16[2048,1536]{1,0:T(8,128)(2,1)}, s32[]{:T(128)}) while((s32[]{:T(128)}, f32[2,1024,8]{1,2,0:T(8,128)S(1)}, bf16[2048,1536]{1,0:T(8,128)(2,1)}, s32[]{:T(128)}) %tuple.104), condition=%wide.region_3.4_spmd, body=%wide.region_2.3_spmd.sunk | while | flops 609042624 | bytes 43476856 | solution.py:116
  61.2 4.9 %convolution_bitcast_fusion.4 = f32[2048,48]{0,1:T(8,128)S(1)} fusion(bf16[2048,1536]{1,0:T(8,128)(2,1)} %get-tuple-element.225, bf16[1536,16]{0,1:T(8,128)(2,1)S(1)} %get-tuple-element.169, bf16[1536,16]{0,1:T(8,128)(2,1)S(1)} %get-tuple-element.170, bf16[1536,16]{0,1:T(8,128)(2,1)S(1)} %get-tuple-element.171), kind=kOutput, calls=%fused_computation.1.clone.1 | convolution fusion | flops 302432256 | bytes 6832128 | tf_op jit(solution)/shard_map/while/body/eval_jaxpr/dot_general | solution.py:107
  68.8 3.2 %collective-permute-start.1 = (f32[2,1024,8]{1,2,0:T(8,128)S(1)}, f32[2,1024,8]{1,2,0:T(8,128)S(1)}, u32[]{:S(2)}, u32[]{:S(2)}) collective-permute-start(f32[2,1024,8]{1,2,0:T(8,128)S(1)} %pad_maximum_fusion.4), channel_id=1, source_target_pairs={{0,12},{4,8},{8,4},{12,0},{16,28},{20,24},{24,20},{28,16},{32,44},... | collective-permute-start | bytes 196616 | tf_op jit(solution)/shard_map/while/body/eval_jaxpr/ppermute | solution.py:19
  74.3 2.3 collective-permute-done.2
  78.0 2.2 collective-permute-start.5
  80.2 2.6 collective-permute-done.3
  84.2 3.2 %collective-permute-start.6 = (f32[2,1024,8]{1,2,0:T(8,128)S(1)}, f32[2,1024,8]{1,2,0:T(8,128)S(1)}, u32[]{:S(2)}, u32[]{:S(2)}) collective-permute-start(f32[2,1024,8]{1,2,0:T(8,128)S(1)} %add_add_fusion.9), channel_id=1, source_target_pairs={{0,64},{4,68},{8,72},{12,76},{16,80},{20,84},{24,88},{28,92},{32,9... | collective-permute-start | bytes 196616 | tf_op jit(solution)/shard_map/while/body/eval_jaxpr/ppermute | solution.py:19
  87.4 2.7 collective-permute-done.6
  95.3 4.9 %convolution_bitcast_fusion.4 = f32[2048,48]{0,1:T(8,128)S(1)} fusion(bf16[2048,1536]{1,0:T(8,128)(2,1)} %get-tuple-element.225, bf16[1536,16]{0,1:T(8,128)(2,1)S(1)} %get-tuple-element.169, bf16[1536,16]{0,1:T(8,128)(2,1)S(1)} %get-tuple-element.170, bf16[1536,16]{0,1:T(8,128)(2,1)S(1)} %get-tuple-element.171), kind=kOutput, calls=%fused_computation.1.clone.1 | convolution fusion | flops 302432256 | bytes 6832128 | tf_op jit(solution)/shard_map/while/body/eval_jaxpr/dot_general | solution.py:107
  101.5 2.8 collective-permute-start.1
  105.1 2.6 collective-permute-done
  110.1 2.2 collective-permute-start.4
  112.3 2.2 collective-permute-done.3
  116.5 3.1 %collective-permute-start.6 = (f32[2,1024,8]{1,2,0:T(8,128)S(1)}, f32[2,1024,8]{1,2,0:T(8,128)S(1)}, u32[]{:S(2)}, u32[]{:S(2)}) collective-permute-start(f32[2,1024,8]{1,2,0:T(8,128)S(1)} %add_add_fusion.9), channel_id=1, source_target_pairs={{0,64},{4,68},{8,72},{12,76},{16,80},{20,84},{24,88},{28,92},{32,9... | collective-permute-start | bytes 196616 | tf_op jit(solution)/shard_map/while/body/eval_jaxpr/ppermute | solution.py:19
  119.7 2.7 collective-permute-done.6
  127.6 4.9 %convolution_bitcast_fusion.4 = f32[2048,48]{0,1:T(8,128)S(1)} fusion(bf16[2048,1536]{1,0:T(8,128)(2,1)} %get-tuple-element.225, bf16[1536,16]{0,1:T(8,128)(2,1)S(1)} %get-tuple-element.169, bf16[1536,16]{0,1:T(8,128)(2,1)S(1)} %get-tuple-element.170, bf16[1536,16]{0,1:T(8,128)(2,1)S(1)} %get-tuple-element.171), kind=kOutput, calls=%fused_computation.1.clone.1 | convolution fusion | flops 302432256 | bytes 6832128 | tf_op jit(solution)/shard_map/while/body/eval_jaxpr/dot_general | solution.py:107
  134.5 2.6 collective-permute-start.1
  137.4 2.2 collective-permute-done
  141.9 2.3 collective-permute-start.4
  145.0 2.3 collective-permute-done.3
  148.5 3.1 %collective-permute-start.6 = (f32[2,1024,8]{1,2,0:T(8,128)S(1)}, f32[2,1024,8]{1,2,0:T(8,128)S(1)}, u32[]{:S(2)}, u32[]{:S(2)}) collective-permute-start(f32[2,1024,8]{1,2,0:T(8,128)S(1)} %add_add_fusion.9), channel_id=1, source_target_pairs={{0,64},{4,68},{8,72},{12,76},{16,80},{20,84},{24,88},{28,92},{32,9... | collective-permute-start | bytes 196616 | tf_op jit(solution)/shard_map/while/body/eval_jaxpr/ppermute | solution.py:19
  151.6 2.7 collective-permute-done.6
  159.6 4.9 %convolution_bitcast_fusion.4 = f32[2048,48]{0,1:T(8,128)S(1)} fusion(bf16[2048,1536]{1,0:T(8,128)(2,1)} %get-tuple-element.225, bf16[1536,16]{0,1:T(8,128)(2,1)S(1)} %get-tuple-element.169, bf16[1536,16]{0,1:T(8,128)(2,1)S(1)} %get-tuple-element.170, bf16[1536,16]{0,1:T(8,128)(2,1)S(1)} %get-tuple-element.171), kind=kOutput, calls=%fused_computation.1.clone.1 | convolution fusion | flops 302432256 | bytes 6832128 | tf_op jit(solution)/shard_map/while/body/eval_jaxpr/dot_general | solution.py:107
  169.4 2.2 collective-permute-done
  176.5 2.3 collective-permute-done.3
  180.8 3.1 %collective-permute-start.6 = (f32[2,1024,8]{1,2,0:T(8,128)S(1)}, f32[2,1024,8]{1,2,0:T(8,128)S(1)}, u32[]{:S(2)}, u32[]{:S(2)}) collective-permute-start(f32[2,1024,8]{1,2,0:T(8,128)S(1)} %add_add_fusion.9), channel_id=1, source_target_pairs={{0,64},{4,68},{8,72},{12,76},{16,80},{20,84},{24,88},{28,92},{32,9... | collective-permute-start | bytes 196616 | tf_op jit(solution)/shard_map/while/body/eval_jaxpr/ppermute | solution.py:19
  183.9 2.7 collective-permute-done.6
  191.8 4.9 %convolution_bitcast_fusion.4 = f32[2048,48]{0,1:T(8,128)S(1)} fusion(bf16[2048,1536]{1,0:T(8,128)(2,1)} %get-tuple-element.225, bf16[1536,16]{0,1:T(8,128)(2,1)S(1)} %get-tuple-element.169, bf16[1536,16]{0,1:T(8,128)(2,1)S(1)} %get-tuple-element.170, bf16[1536,16]{0,1:T(8,128)(2,1)S(1)} %get-tuple-element.171), kind=kOutput, calls=%fused_computation.1.clone.1 | convolution fusion | flops 302432256 | bytes 6832128 | tf_op jit(solution)/shard_map/while/body/eval_jaxpr/dot_general | solution.py:107
  201.7 2.2 collective-permute-done
  209.3 2.3 collective-permute-done.3
  212.7 3.1 %collective-permute-start.6 = (f32[2,1024,8]{1,2,0:T(8,128)S(1)}, f32[2,1024,8]{1,2,0:T(8,128)S(1)}, u32[]{:S(2)}, u32[]{:S(2)}) collective-permute-start(f32[2,1024,8]{1,2,0:T(8,128)S(1)} %add_add_fusion.9), channel_id=1, source_target_pairs={{0,64},{4,68},{8,72},{12,76},{16,80},{20,84},{24,88},{28,92},{32,9... | collective-permute-start | bytes 196616 | tf_op jit(solution)/shard_map/while/body/eval_jaxpr/ppermute | solution.py:19
  215.8 2.7 collective-permute-done.6
  223.8 4.9 %convolution_bitcast_fusion.4 = f32[2048,48]{0,1:T(8,128)S(1)} fusion(bf16[2048,1536]{1,0:T(8,128)(2,1)} %get-tuple-element.225, bf16[1536,16]{0,1:T(8,128)(2,1)S(1)} %get-tuple-element.169, bf16[1536,16]{0,1:T(8,128)(2,1)S(1)} %get-tuple-element.170, bf16[1536,16]{0,1:T(8,128)(2,1)S(1)} %get-tuple-element.171), kind=kOutput, calls=%fused_computation.1.clone.1 | convolution fusion | flops 302432256 | bytes 6832128 | tf_op jit(solution)/shard_map/while/body/eval_jaxpr/dot_general | solution.py:107
  233.6 2.2 collective-permute-done
  240.7 2.3 collective-permute-done.3
  245.0 3.1 %collective-permute-start.6 = (f32[2,1024,8]{1,2,0:T(8,128)S(1)}, f32[2,1024,8]{1,2,0:T(8,128)S(1)}, u32[]{:S(2)}, u32[]{:S(2)}) collective-permute-start(f32[2,1024,8]{1,2,0:T(8,128)S(1)} %add_add_fusion.9), channel_id=1, source_target_pairs={{0,64},{4,68},{8,72},{12,76},{16,80},{20,84},{24,88},{28,92},{32,9... | collective-permute-start | bytes 196616 | tf_op jit(solution)/shard_map/while/body/eval_jaxpr/ppermute | solution.py:19
  248.1 2.7 collective-permute-done.6
  256.1 4.7 %fusion.63 = f32[2048,48]{0,1:T(8,128)S(1)} fusion(bf16[2048,1536]{1,0:T(8,128)(2,1)} %get-tuple-element.227, bf16[1536,16]{0,1:T(8,128)(2,1)S(1)} %get-tuple-element.97, bf16[1536,16]{0,1:T(8,128)(2,1)S(1)} %get-tuple-element.96, bf16[1536,16]{0,1:T(8,128)(2,1)S(1)} %get-tuple-element.95), kind=kOutput, calls=%fused_computation.166 | convolution fusion | flops 302432256 | bytes 6832128 | tf_op jit(solution)/shard_map/dot_general | solution.py:107
  268.8 3.0 %multiply_reduce_fusion.1 = (f32[2048]{0:T(1024)S(1)}, f32[2048]{0:T(1024)S(1)}) fusion(bf16[2048,1536]{1,0:T(8,128)(2,1)S(1)} %bitcast.153, f32[2048,1024]{1,0:T(8,128)S(1)} %fusion.78, bf16[2048,48]{0,1:T(8,128)(2,1)S(1)} %constant_dynamic-update-slice_fusion, bf16[1024,48]{0,1:T(8,128)(2,1)S(1)} %get-tuple-element.86), kind=kOutput, calls=%fused_computation.163 | convolution fusion | flops 218099712 | bytes 17088512 | tf_op jit(solution)/shard_map/dot_general | solution.py:76
  271.9 2.7 collective-permute-start.19
  277.1 2.3 collective-permute-done.20
  279.4 3.1 %collective-permute-start.21 = (f32[16]{0:T(128)S(1)}, f32[16]{0:T(128)S(1)}, u32[]{:S(2)}, u32[]{:S(2)}) collective-permute-start(f32[16]{0:T(128)S(1)} %add_add_fusion.4), channel_id=1, source_target_pairs={{0,64},{4,68},{8,72},{12,76},{16,80},{20,84},{24,88},{28,92},{32,9... | collective-permute-start | bytes 200 | tf_op jit(solution)/shard_map/ppermute | solution.py:19
  (575 shorter events, 118.5 us)
Async XLA Ops:
  2.4 25.5 %collective-permute-start.7 = (bf16[2048,512]{1,0:T(8,128)(2,1)S(1)}, bf16[2048,512]{1,0:T(8,128)(2,1)}, u32[]{:S(2)}, u32[]{:S(2)}) collective-permute-start(bf16[2048,512]{1,0:T(8,128)(2,1)S(1)} %slice.186), channel_id=1, source_target_pairs={{1,0},{2,1},{3,2},{5,4},{6,5},{7,6},{9,8},{10,9},{11,10},{13,12},{... | collective-permute-start | bytes 6291464 | tf_op jit(solution)/shard_map/ppermute | solution.py:14
  31.6 5.0 %collective-permute-start.10 = (f32[2,1536]{1,0:T(2,128)S(1)}, f32[2,1536]{1,0:T(2,128)S(1)}, u32[]{:S(2)}, u32[]{:S(2)}) collective-permute-start(f32[2,1536]{1,0:T(2,128)S(1)} %pad_maximum_fusion.2), channel_id=1, source_target_pairs={{0,12},{4,8},{8,4},{12,0},{16,28},{20,24},{24,20},{28,16},{32,44},... | collective-permute-start | bytes 36872 | tf_op jit(solution)/shard_map/ppermute | solution.py:19
  34.8 5.2 %collective-permute-start.9 = (f32[2,1536]{1,0:T(2,128)S(1)}, f32[2,1536]{1,0:T(2,128)S(1)}, u32[]{:S(2)}, u32[]{:S(2)}) collective-permute-start(f32[2,1536]{1,0:T(2,128)S(1)} %pad_maximum_fusion.2), channel_id=1, source_target_pairs={{0,8},{4,12},{8,0},{12,4},{16,24},{20,28},{24,16},{28,20},{32,40},... | collective-permute-start | bytes 36872 | tf_op jit(solution)/shard_map/ppermute | solution.py:19
  40.1 4.8 %collective-permute-start.11 = (f32[2,1536]{1,0:T(2,128)S(1)}, f32[2,1536]{1,0:T(2,128)S(1)}, u32[]{:S(2)}, u32[]{:S(2)}) collective-permute-start(f32[2,1536]{1,0:T(2,128)S(1)} %add_add_fusion.3), channel_id=1, source_target_pairs={{0,16},{4,20},{8,24},{12,28},{16,0},{20,4},{24,8},{28,12},{32,48},... | collective-permute-start | bytes 36872 | tf_op jit(solution)/shard_map/ppermute | solution.py:19
  41.8 5.2 %collective-permute-start.12 = (f32[2,1536]{1,0:T(2,128)S(1)}, f32[2,1536]{1,0:T(2,128)S(1)}, u32[]{:S(2)}, u32[]{:S(2)}) collective-permute-start(f32[2,1536]{1,0:T(2,128)S(1)} %add_add_fusion.3), channel_id=1, source_target_pairs={{0,32},{4,36},{8,40},{12,44},{16,48},{20,52},{24,56},{28,60},{32,0... | collective-permute-start | bytes 36872 | tf_op jit(solution)/shard_map/ppermute | solution.py:19
  44.5 4.9 %collective-permute-start.13 = (f32[2,1536]{1,0:T(2,128)S(1)}, f32[2,1536]{1,0:T(2,128)S(1)}, u32[]{:S(2)}, u32[]{:S(2)}) collective-permute-start(f32[2,1536]{1,0:T(2,128)S(1)} %add_add_fusion.3), channel_id=1, source_target_pairs={{0,48},{4,52},{8,56},{12,60},{16,32},{20,36},{24,40},{28,44},{32,1... | collective-permute-start | bytes 36872 | tf_op jit(solution)/shard_map/ppermute | solution.py:19
  49.4 5.3 %collective-permute-start.14 = (f32[2,1536]{1,0:T(2,128)S(1)}, f32[2,1536]{1,0:T(2,128)S(1)}, u32[]{:S(2)}, u32[]{:S(2)}) collective-permute-start(f32[2,1536]{1,0:T(2,128)S(1)} %add_add_fusion.2), channel_id=1, source_target_pairs={{0,64},{4,68},{8,72},{12,76},{16,80},{20,84},{24,88},{28,92},{32,9... | collective-permute-start | bytes 36872 | tf_op jit(solution)/shard_map/ppermute | solution.py:19
  67.3 5.8 %collective-permute-start = (f32[2,1024,8]{1,2,0:T(8,128)S(1)}, f32[2,1024,8]{1,2,0:T(8,128)S(1)}, u32[]{:S(2)}, u32[]{:S(2)}) collective-permute-start(f32[2,1024,8]{1,2,0:T(8,128)S(1)} %pad_maximum_fusion.4), channel_id=1, source_target_pairs={{0,8},{4,12},{8,0},{12,4},{16,24},{20,28},{24,16},{28,20},{32,40},... | collective-permute-start | bytes 196616 | tf_op jit(solution)/shard_map/while/body/eval_jaxpr/ppermute | solution.py:19
  68.8 5.5 %collective-permute-start.1 = (f32[2,1024,8]{1,2,0:T(8,128)S(1)}, f32[2,1024,8]{1,2,0:T(8,128)S(1)}, u32[]{:S(2)}, u32[]{:S(2)}) collective-permute-start(f32[2,1024,8]{1,2,0:T(8,128)S(1)} %pad_maximum_fusion.4), channel_id=1, source_target_pairs={{0,12},{4,8},{8,4},{12,0},{16,28},{20,24},{24,20},{28,16},{32,44},... | collective-permute-start | bytes 196616 | tf_op jit(solution)/shard_map/while/body/eval_jaxpr/ppermute | solution.py:19
  72.0 4.7 %collective-permute-start.2 = (f32[2,1024,8]{1,2,0:T(8,128)S(1)}, f32[2,1024,8]{1,2,0:T(8,128)S(1)}, u32[]{:S(2)}, u32[]{:S(2)}) collective-permute-start(f32[2,1024,8]{1,2,0:T(8,128)S(1)} %pad_maximum_fusion.4), channel_id=1, source_target_pairs={{0,4},{4,0},{8,12},{12,8},{16,20},{20,16},{24,28},{28,24},{32,36},... | collective-permute-start | bytes 196616 | tf_op jit(solution)/shard_map/while/body/eval_jaxpr/ppermute | solution.py:19
  76.7 6.2 %collective-permute-start.3 = (f32[2,1024,8]{1,2,0:T(8,128)S(1)}, f32[2,1024,8]{1,2,0:T(8,128)S(1)}, u32[]{:S(2)}, u32[]{:S(2)}) collective-permute-start(f32[2,1024,8]{1,2,0:T(8,128)S(1)} %add_add_fusion.8), channel_id=1, source_target_pairs={{0,32},{4,36},{8,40},{12,44},{16,48},{20,52},{24,56},{28,60},{32,0... | collective-permute-start | bytes 196616 | tf_op jit(solution)/shard_map/while/body/eval_jaxpr/ppermute | solution.py:19
  76.9 7.3 %collective-permute-start.4 = (f32[2,1024,8]{1,2,0:T(8,128)S(1)}, f32[2,1024,8]{1,2,0:T(8,128)S(1)}, u32[]{:S(2)}, u32[]{:S(2)}) collective-permute-start(f32[2,1024,8]{1,2,0:T(8,128)S(1)} %add_add_fusion.8), channel_id=1, source_target_pairs={{0,48},{4,52},{8,56},{12,60},{16,32},{20,36},{24,40},{28,44},{32,1... | collective-permute-start | bytes 196616 | tf_op jit(solution)/shard_map/while/body/eval_jaxpr/ppermute | solution.py:19
  78.0 6.2 %collective-permute-start.5 = (f32[2,1024,8]{1,2,0:T(8,128)S(1)}, f32[2,1024,8]{1,2,0:T(8,128)S(1)}, u32[]{:S(2)}, u32[]{:S(2)}) collective-permute-start(f32[2,1024,8]{1,2,0:T(8,128)S(1)} %add_add_fusion.8), channel_id=1, source_target_pairs={{0,16},{4,20},{8,24},{12,28},{16,0},{20,4},{24,8},{28,12},{32,48},... | collective-permute-start | bytes 196616 | tf_op jit(solution)/shard_map/while/body/eval_jaxpr/ppermute | solution.py:19
  84.2 5.8 %collective-permute-start.6 = (f32[2,1024,8]{1,2,0:T(8,128)S(1)}, f32[2,1024,8]{1,2,0:T(8,128)S(1)}, u32[]{:S(2)}, u32[]{:S(2)}) collective-permute-start(f32[2,1024,8]{1,2,0:T(8,128)S(1)} %add_add_fusion.9), channel_id=1, source_target_pairs={{0,64},{4,68},{8,72},{12,76},{16,80},{20,84},{24,88},{28,92},{32,9... | collective-permute-start | bytes 196616 | tf_op jit(solution)/shard_map/while/body/eval_jaxpr/ppermute | solution.py:19
  101.4 6.3 %collective-permute-start = (f32[2,1024,8]{1,2,0:T(8,128)S(1)}, f32[2,1024,8]{1,2,0:T(8,128)S(1)}, u32[]{:S(2)}, u32[]{:S(2)}) collective-permute-start(f32[2,1024,8]{1,2,0:T(8,128)S(1)} %pad_maximum_fusion.4), channel_id=1, source_target_pairs={{0,8},{4,12},{8,0},{12,4},{16,24},{20,28},{24,16},{28,20},{32,40},... | collective-permute-start | bytes 196616 | tf_op jit(solution)/shard_map/while/body/eval_jaxpr/ppermute | solution.py:19
  101.5 6.3 %collective-permute-start.1 = (f32[2,1024,8]{1,2,0:T(8,128)S(1)}, f32[2,1024,8]{1,2,0:T(8,128)S(1)}, u32[]{:S(2)}, u32[]{:S(2)}) collective-permute-start(f32[2,1024,8]{1,2,0:T(8,128)S(1)} %pad_maximum_fusion.4), channel_id=1, source_target_pairs={{0,12},{4,8},{8,4},{12,0},{16,28},{20,24},{24,20},{28,16},{32,44},... | collective-permute-start | bytes 196616 | tf_op jit(solution)/shard_map/while/body/eval_jaxpr/ppermute | solution.py:19
  104.3 4.3 %collective-permute-start.2 = (f32[2,1024,8]{1,2,0:T(8,128)S(1)}, f32[2,1024,8]{1,2,0:T(8,128)S(1)}, u32[]{:S(2)}, u32[]{:S(2)}) collective-permute-start(f32[2,1024,8]{1,2,0:T(8,128)S(1)} %pad_maximum_fusion.4), channel_id=1, source_target_pairs={{0,4},{4,0},{8,12},{12,8},{16,20},{20,16},{24,28},{28,24},{32,36},... | collective-permute-start | bytes 196616 | tf_op jit(solution)/shard_map/while/body/eval_jaxpr/ppermute | solution.py:19
  108.6 5.8 %collective-permute-start.3 = (f32[2,1024,8]{1,2,0:T(8,128)S(1)}, f32[2,1024,8]{1,2,0:T(8,128)S(1)}, u32[]{:S(2)}, u32[]{:S(2)}) collective-permute-start(f32[2,1024,8]{1,2,0:T(8,128)S(1)} %add_add_fusion.8), channel_id=1, source_target_pairs={{0,32},{4,36},{8,40},{12,44},{16,48},{20,52},{24,56},{28,60},{32,0... | collective-permute-start | bytes 196616 | tf_op jit(solution)/shard_map/while/body/eval_jaxpr/ppermute | solution.py:19
  110.1 5.5 %collective-permute-start.4 = (f32[2,1024,8]{1,2,0:T(8,128)S(1)}, f32[2,1024,8]{1,2,0:T(8,128)S(1)}, u32[]{:S(2)}, u32[]{:S(2)}) collective-permute-start(f32[2,1024,8]{1,2,0:T(8,128)S(1)} %add_add_fusion.8), channel_id=1, source_target_pairs={{0,48},{4,52},{8,56},{12,60},{16,32},{20,36},{24,40},{28,44},{32,1... | collective-permute-start | bytes 196616 | tf_op jit(solution)/shard_map/while/body/eval_jaxpr/ppermute | solution.py:19
  116.5 5.8 %collective-permute-start.6 = (f32[2,1024,8]{1,2,0:T(8,128)S(1)}, f32[2,1024,8]{1,2,0:T(8,128)S(1)}, u32[]{:S(2)}, u32[]{:S(2)}) collective-permute-start(f32[2,1024,8]{1,2,0:T(8,128)S(1)} %add_add_fusion.9), channel_id=1, source_target_pairs={{0,64},{4,68},{8,72},{12,76},{16,80},{20,84},{24,88},{28,92},{32,9... | collective-permute-start | bytes 196616 | tf_op jit(solution)/shard_map/while/body/eval_jaxpr/ppermute | solution.py:19
  133.8 5.9 %collective-permute-start = (f32[2,1024,8]{1,2,0:T(8,128)S(1)}, f32[2,1024,8]{1,2,0:T(8,128)S(1)}, u32[]{:S(2)}, u32[]{:S(2)}) collective-permute-start(f32[2,1024,8]{1,2,0:T(8,128)S(1)} %pad_maximum_fusion.4), channel_id=1, source_target_pairs={{0,8},{4,12},{8,0},{12,4},{16,24},{20,28},{24,16},{28,20},{32,40},... | collective-permute-start | bytes 196616 | tf_op jit(solution)/shard_map/while/body/eval_jaxpr/ppermute | solution.py:19
  134.5 5.8 %collective-permute-start.1 = (f32[2,1024,8]{1,2,0:T(8,128)S(1)}, f32[2,1024,8]{1,2,0:T(8,128)S(1)}, u32[]{:S(2)}, u32[]{:S(2)}) collective-permute-start(f32[2,1024,8]{1,2,0:T(8,128)S(1)} %pad_maximum_fusion.4), channel_id=1, source_target_pairs={{0,12},{4,8},{8,4},{12,0},{16,28},{20,24},{24,20},{28,16},{32,44},... | collective-permute-start | bytes 196616 | tf_op jit(solution)/shard_map/while/body/eval_jaxpr/ppermute | solution.py:19
  137.2 4.3 %collective-permute-start.2 = (f32[2,1024,8]{1,2,0:T(8,128)S(1)}, f32[2,1024,8]{1,2,0:T(8,128)S(1)}, u32[]{:S(2)}, u32[]{:S(2)}) collective-permute-start(f32[2,1024,8]{1,2,0:T(8,128)S(1)} %pad_maximum_fusion.4), channel_id=1, source_target_pairs={{0,4},{4,0},{8,12},{12,8},{16,20},{20,16},{24,28},{28,24},{32,36},... | collective-permute-start | bytes 196616 | tf_op jit(solution)/shard_map/while/body/eval_jaxpr/ppermute | solution.py:19
  141.5 5.9 %collective-permute-start.3 = (f32[2,1024,8]{1,2,0:T(8,128)S(1)}, f32[2,1024,8]{1,2,0:T(8,128)S(1)}, u32[]{:S(2)}, u32[]{:S(2)}) collective-permute-start(f32[2,1024,8]{1,2,0:T(8,128)S(1)} %add_add_fusion.8), channel_id=1, source_target_pairs={{0,32},{4,36},{8,40},{12,44},{16,48},{20,52},{24,56},{28,60},{32,0... | collective-permute-start | bytes 196616 | tf_op jit(solution)/shard_map/while/body/eval_jaxpr/ppermute | solution.py:19
  141.9 6.1 %collective-permute-start.4 = (f32[2,1024,8]{1,2,0:T(8,128)S(1)}, f32[2,1024,8]{1,2,0:T(8,128)S(1)}, u32[]{:S(2)}, u32[]{:S(2)}) collective-permute-start(f32[2,1024,8]{1,2,0:T(8,128)S(1)} %add_add_fusion.8), channel_id=1, source_target_pairs={{0,48},{4,52},{8,56},{12,60},{16,32},{20,36},{24,40},{28,44},{32,1... | collective-permute-start | bytes 196616 | tf_op jit(solution)/shard_map/while/body/eval_jaxpr/ppermute | solution.py:19
  148.5 5.8 %collective-permute-start.6 = (f32[2,1024,8]{1,2,0:T(8,128)S(1)}, f32[2,1024,8]{1,2,0:T(8,128)S(1)}, u32[]{:S(2)}, u32[]{:S(2)}) collective-permute-start(f32[2,1024,8]{1,2,0:T(8,128)S(1)} %add_add_fusion.9), channel_id=1, source_target_pairs={{0,64},{4,68},{8,72},{12,76},{16,80},{20,84},{24,88},{28,92},{32,9... | collective-permute-start | bytes 196616 | tf_op jit(solution)/shard_map/while/body/eval_jaxpr/ppermute | solution.py:19
  165.7 5.9 %collective-permute-start = (f32[2,1024,8]{1,2,0:T(8,128)S(1)}, f32[2,1024,8]{1,2,0:T(8,128)S(1)}, u32[]{:S(2)}, u32[]{:S(2)}) collective-permute-start(f32[2,1024,8]{1,2,0:T(8,128)S(1)} %pad_maximum_fusion.4), channel_id=1, source_target_pairs={{0,8},{4,12},{8,0},{12,4},{16,24},{20,28},{24,16},{28,20},{32,40},... | collective-permute-start | bytes 196616 | tf_op jit(solution)/shard_map/while/body/eval_jaxpr/ppermute | solution.py:19
  166.6 5.7 %collective-permute-start.1 = (f32[2,1024,8]{1,2,0:T(8,128)S(1)}, f32[2,1024,8]{1,2,0:T(8,128)S(1)}, u32[]{:S(2)}, u32[]{:S(2)}) collective-permute-start(f32[2,1024,8]{1,2,0:T(8,128)S(1)} %pad_maximum_fusion.4), channel_id=1, source_target_pairs={{0,12},{4,8},{8,4},{12,0},{16,28},{20,24},{24,20},{28,16},{32,44},... | collective-permute-start | bytes 196616 | tf_op jit(solution)/shard_map/while/body/eval_jaxpr/ppermute | solution.py:19
  172.9 5.8 %collective-permute-start.3 = (f32[2,1024,8]{1,2,0:T(8,128)S(1)}, f32[2,1024,8]{1,2,0:T(8,128)S(1)}, u32[]{:S(2)}, u32[]{:S(2)}) collective-permute-start(f32[2,1024,8]{1,2,0:T(8,128)S(1)} %add_add_fusion.8), channel_id=1, source_target_pairs={{0,32},{4,36},{8,40},{12,44},{16,48},{20,52},{24,56},{28,60},{32,0... | collective-permute-start | bytes 196616 | tf_op jit(solution)/shard_map/while/body/eval_jaxpr/ppermute | solution.py:19
  174.5 5.5 %collective-permute-start.4 = (f32[2,1024,8]{1,2,0:T(8,128)S(1)}, f32[2,1024,8]{1,2,0:T(8,128)S(1)}, u32[]{:S(2)}, u32[]{:S(2)}) collective-permute-start(f32[2,1024,8]{1,2,0:T(8,128)S(1)} %add_add_fusion.8), channel_id=1, source_target_pairs={{0,48},{4,52},{8,56},{12,60},{16,32},{20,36},{24,40},{28,44},{32,1... | collective-permute-start | bytes 196616 | tf_op jit(solution)/shard_map/while/body/eval_jaxpr/ppermute | solution.py:19
  180.8 5.8 %collective-permute-start.6 = (f32[2,1024,8]{1,2,0:T(8,128)S(1)}, f32[2,1024,8]{1,2,0:T(8,128)S(1)}, u32[]{:S(2)}, u32[]{:S(2)}) collective-permute-start(f32[2,1024,8]{1,2,0:T(8,128)S(1)} %add_add_fusion.9), channel_id=1, source_target_pairs={{0,64},{4,68},{8,72},{12,76},{16,80},{20,84},{24,88},{28,92},{32,9... | collective-permute-start | bytes 196616 | tf_op jit(solution)/shard_map/while/body/eval_jaxpr/ppermute | solution.py:19
  198.0 5.8 %collective-permute-start = (f32[2,1024,8]{1,2,0:T(8,128)S(1)}, f32[2,1024,8]{1,2,0:T(8,128)S(1)}, u32[]{:S(2)}, u32[]{:S(2)}) collective-permute-start(f32[2,1024,8]{1,2,0:T(8,128)S(1)} %pad_maximum_fusion.4), channel_id=1, source_target_pairs={{0,8},{4,12},{8,0},{12,4},{16,24},{20,28},{24,16},{28,20},{32,40},... | collective-permute-start | bytes 196616 | tf_op jit(solution)/shard_map/while/body/eval_jaxpr/ppermute | solution.py:19
  199.4 5.5 %collective-permute-start.1 = (f32[2,1024,8]{1,2,0:T(8,128)S(1)}, f32[2,1024,8]{1,2,0:T(8,128)S(1)}, u32[]{:S(2)}, u32[]{:S(2)}) collective-permute-start(f32[2,1024,8]{1,2,0:T(8,128)S(1)} %pad_maximum_fusion.4), channel_id=1, source_target_pairs={{0,12},{4,8},{8,4},{12,0},{16,28},{20,24},{24,20},{28,16},{32,44},... | collective-permute-start | bytes 196616 | tf_op jit(solution)/shard_map/while/body/eval_jaxpr/ppermute | solution.py:19
  205.7 5.9 %collective-permute-start.3 = (f32[2,1024,8]{1,2,0:T(8,128)S(1)}, f32[2,1024,8]{1,2,0:T(8,128)S(1)}, u32[]{:S(2)}, u32[]{:S(2)}) collective-permute-start(f32[2,1024,8]{1,2,0:T(8,128)S(1)} %add_add_fusion.8), channel_id=1, source_target_pairs={{0,32},{4,36},{8,40},{12,44},{16,48},{20,52},{24,56},{28,60},{32,0... | collective-permute-start | bytes 196616 | tf_op jit(solution)/shard_map/while/body/eval_jaxpr/ppermute | solution.py:19
  206.4 5.8 %collective-permute-start.4 = (f32[2,1024,8]{1,2,0:T(8,128)S(1)}, f32[2,1024,8]{1,2,0:T(8,128)S(1)}, u32[]{:S(2)}, u32[]{:S(2)}) collective-permute-start(f32[2,1024,8]{1,2,0:T(8,128)S(1)} %add_add_fusion.8), channel_id=1, source_target_pairs={{0,48},{4,52},{8,56},{12,60},{16,32},{20,36},{24,40},{28,44},{32,1... | collective-permute-start | bytes 196616 | tf_op jit(solution)/shard_map/while/body/eval_jaxpr/ppermute | solution.py:19
  212.7 5.8 %collective-permute-start.6 = (f32[2,1024,8]{1,2,0:T(8,128)S(1)}, f32[2,1024,8]{1,2,0:T(8,128)S(1)}, u32[]{:S(2)}, u32[]{:S(2)}) collective-permute-start(f32[2,1024,8]{1,2,0:T(8,128)S(1)} %add_add_fusion.9), channel_id=1, source_target_pairs={{0,64},{4,68},{8,72},{12,76},{16,80},{20,84},{24,88},{28,92},{32,9... | collective-permute-start | bytes 196616 | tf_op jit(solution)/shard_map/while/body/eval_jaxpr/ppermute | solution.py:19
  229.9 5.9 %collective-permute-start = (f32[2,1024,8]{1,2,0:T(8,128)S(1)}, f32[2,1024,8]{1,2,0:T(8,128)S(1)}, u32[]{:S(2)}, u32[]{:S(2)}) collective-permute-start(f32[2,1024,8]{1,2,0:T(8,128)S(1)} %pad_maximum_fusion.4), channel_id=1, source_target_pairs={{0,8},{4,12},{8,0},{12,4},{16,24},{20,28},{24,16},{28,20},{32,40},... | collective-permute-start | bytes 196616 | tf_op jit(solution)/shard_map/while/body/eval_jaxpr/ppermute | solution.py:19
  230.8 5.7 %collective-permute-start.1 = (f32[2,1024,8]{1,2,0:T(8,128)S(1)}, f32[2,1024,8]{1,2,0:T(8,128)S(1)}, u32[]{:S(2)}, u32[]{:S(2)}) collective-permute-start(f32[2,1024,8]{1,2,0:T(8,128)S(1)} %pad_maximum_fusion.4), channel_id=1, source_target_pairs={{0,12},{4,8},{8,4},{12,0},{16,28},{20,24},{24,20},{28,16},{32,44},... | collective-permute-start | bytes 196616 | tf_op jit(solution)/shard_map/while/body/eval_jaxpr/ppermute | solution.py:19
  237.1 5.8 %collective-permute-start.3 = (f32[2,1024,8]{1,2,0:T(8,128)S(1)}, f32[2,1024,8]{1,2,0:T(8,128)S(1)}, u32[]{:S(2)}, u32[]{:S(2)}) collective-permute-start(f32[2,1024,8]{1,2,0:T(8,128)S(1)} %add_add_fusion.8), channel_id=1, source_target_pairs={{0,32},{4,36},{8,40},{12,44},{16,48},{20,52},{24,56},{28,60},{32,0... | collective-permute-start | bytes 196616 | tf_op jit(solution)/shard_map/while/body/eval_jaxpr/ppermute | solution.py:19
  238.7 5.5 %collective-permute-start.4 = (f32[2,1024,8]{1,2,0:T(8,128)S(1)}, f32[2,1024,8]{1,2,0:T(8,128)S(1)}, u32[]{:S(2)}, u32[]{:S(2)}) collective-permute-start(f32[2,1024,8]{1,2,0:T(8,128)S(1)} %add_add_fusion.8), channel_id=1, source_target_pairs={{0,48},{4,52},{8,56},{12,60},{16,32},{20,36},{24,40},{28,44},{32,1... | collective-permute-start | bytes 196616 | tf_op jit(solution)/shard_map/while/body/eval_jaxpr/ppermute | solution.py:19
  245.0 5.8 %collective-permute-start.6 = (f32[2,1024,8]{1,2,0:T(8,128)S(1)}, f32[2,1024,8]{1,2,0:T(8,128)S(1)}, u32[]{:S(2)}, u32[]{:S(2)}) collective-permute-start(f32[2,1024,8]{1,2,0:T(8,128)S(1)} %add_add_fusion.9), channel_id=1, source_target_pairs={{0,64},{4,68},{8,72},{12,76},{16,80},{20,84},{24,88},{28,92},{32,9... | collective-permute-start | bytes 196616 | tf_op jit(solution)/shard_map/while/body/eval_jaxpr/ppermute | solution.py:19
  260.9 10.9 %collective-permute-start.15 = (f32[16]{0:T(128)S(1)}, f32[16]{0:T(128)S(1)}, u32[]{:S(2)}, u32[]{:S(2)}) collective-permute-start(f32[16]{0:T(128)S(1)} %get-tuple-element.43), channel_id=1, source_target_pairs={{0,4},{4,0},{8,12},{12,8},{16,20},{20,16},{24,28},{28,24},{32,36},... | collective-permute-start | bytes 200 | tf_op jit(solution)/shard_map/ppermute | solution.py:19
  261.7 10.1 %collective-permute-start.16 = (f32[16]{0:T(128)S(1)}, f32[16]{0:T(128)S(1)}, u32[]{:S(2)}, u32[]{:S(2)}) collective-permute-start(f32[16]{0:T(128)S(1)} %get-tuple-element.43), channel_id=1, source_target_pairs={{0,8},{4,12},{8,0},{12,4},{16,24},{20,28},{24,16},{28,20},{32,40},... | collective-permute-start | bytes 200 | tf_op jit(solution)/shard_map/ppermute | solution.py:19
  263.7 8.1 %collective-permute-start.17 = (f32[16]{0:T(128)S(1)}, f32[16]{0:T(128)S(1)}, u32[]{:S(2)}, u32[]{:S(2)}) collective-permute-start(f32[16]{0:T(128)S(1)} %get-tuple-element.43), channel_id=1, source_target_pairs={{0,12},{4,8},{8,4},{12,0},{16,28},{20,24},{24,20},{28,16},{32,44},... | collective-permute-start | bytes 200 | tf_op jit(solution)/shard_map/ppermute | solution.py:19
  271.8 4.8 %collective-permute-start.18 = (f32[16]{0:T(128)S(1)}, f32[16]{0:T(128)S(1)}, u32[]{:S(2)}, u32[]{:S(2)}) collective-permute-start(f32[16]{0:T(128)S(1)} %add_add_fusion.5), channel_id=1, source_target_pairs={{0,16},{4,20},{8,24},{12,28},{16,0},{20,4},{24,8},{28,12},{32,48},... | collective-permute-start | bytes 200 | tf_op jit(solution)/shard_map/ppermute | solution.py:19
  271.9 5.1 %collective-permute-start.19 = (f32[16]{0:T(128)S(1)}, f32[16]{0:T(128)S(1)}, u32[]{:S(2)}, u32[]{:S(2)}) collective-permute-start(f32[16]{0:T(128)S(1)} %add_add_fusion.5), channel_id=1, source_target_pairs={{0,32},{4,36},{8,40},{12,44},{16,48},{20,52},{24,56},{28,60},{32,0... | collective-permute-start | bytes 200 | tf_op jit(solution)/shard_map/ppermute | solution.py:19
  274.6 4.8 %collective-permute-start.20 = (f32[16]{0:T(128)S(1)}, f32[16]{0:T(128)S(1)}, u32[]{:S(2)}, u32[]{:S(2)}) collective-permute-start(f32[16]{0:T(128)S(1)} %add_add_fusion.5), channel_id=1, source_target_pairs={{0,48},{4,52},{8,56},{12,60},{16,32},{20,36},{24,40},{28,44},{32,1... | collective-permute-start | bytes 200 | tf_op jit(solution)/shard_map/ppermute | solution.py:19
  279.4 5.1 %collective-permute-start.21 = (f32[16]{0:T(128)S(1)}, f32[16]{0:T(128)S(1)}, u32[]{:S(2)}, u32[]{:S(2)}) collective-permute-start(f32[16]{0:T(128)S(1)} %add_add_fusion.4), channel_id=1, source_target_pairs={{0,64},{4,68},{8,72},{12,76},{16,80},{20,84},{24,88},{28,92},{32,9... | collective-permute-start | bytes 200 | tf_op jit(solution)/shard_map/ppermute | solution.py:19
  (20 other events, 115.8 us)

commit v9 on v3

--- a/solution.py
+++ b/solution.py
@@ -85,7 +85,11 @@
     following = jnp.where(position == win_count - 1, tail, received)
     region = jnp.concatenate([dosage, following], axis=1)
     regionf = region.astype(jnp.float32)
-    stats = summed(jnp.stack([jnp.sum(regionf, axis=0), jnp.sum(regionf * regionf, axis=0)]), "ind")
+    ownf = jnp.concatenate([dosage, tail], axis=1).astype(jnp.float32)
+    reduced = summed(jnp.stack([jnp.sum(ownf, axis=0), jnp.sum(ownf * ownf, axis=0)]), "ind")
+    from_next = passed_along(reduced[:, :half_cols], "win", -1)
+    follow_stats = jnp.where(position == win_count - 1, reduced[:, columns:], from_next)
+    stats = jnp.concatenate([reduced[:, :columns], follow_stats], axis=1)
     mean = stats[0] / total
     var = stats[1] / total - mean * mean
     miss_here = lax.dynamic_slice_in_dim(missing, position * columns, columns + half_cols)

time: 275 us -> 259 us (0.942)
  starting transfers between devices: 89.6 us -> 77.5 us
  waiting for transfers between devices: 100 us -> 94.3 us
    ppermute x1 -> x2, waiting for transfers between devices: 23.5 us -> 0.49 us  [passed_along(): return lax.ppermute(array, axis, pairs)]
    ppermute x56, waiting for transfers between devices: 76.8 us -> 93.8 us  [swapped(): return lax.ppermute(value, axis, [(i, i ^ mask) for i in range(size)])]
    ppermute x56, starting transfers between devices: 87.6 us -> 73.5 us  [swapped(): return lax.ppermute(value, axis, [(i, i ^ mask) for i in range(size)])]
  transfers between devices with their start and end apart: 57 -> 58, of which waited for: 51 -> 40; matrix products, arithmetic and copies ran while one was open for 2% -> 4% of each run, Pallas kernels for 0% -> 0%
where the time goes in v9:
time: 259 us
  waiting for transfers between devices  94.3 us (36%)
  starting transfers between devices  77.5 us (30%)
  matrix products  48 us (19%)
  other arithmetic  31.3 us (12%)
  local copies, waits for them, and re-layouts  6.1 us (2%)
    ppermute x56, waiting for transfers between devices, swapped(): return lax.ppermute(value, axis, [(i, i ^ mask) for i in range(size)])  93.8 us
    ppermute x56, starting transfers between devices, swapped(): return lax.ppermute(value, axis, [(i, i ^ mask) for i in range(size)])  73.5 us
    dot_general x7, matrix products, project(): jnp.dot(stand, jnp.concatenate(pieces(wide), 1), preferred_element_type=j...  33.9 us
    another operation x24, other arithmetic, orthonormal(): factor = jnp.linalg.cholesky(gram)  9.76 us
    another operation x18, other arithmetic, orthonormal(): jax.scipy.linalg.solve_triangular(fac, rhs, lower=True)  8.03 us
    dot_general x6, matrix products, image_of(): lax.dot_general(stand, split, (((0,), (0,)), ((), ())), preferred_element...  6.76 us
  transfers between devices with their start and end apart: 58, of which 40 were waited for; matrix products, arithmetic and copies ran while one was open for 4% of the time, Pallas kernels for 0%

profile of v9, /device:TPU:32, one launch (start us, length us, event | category | flops | bytes accessed | tf_op | source)
XLA Modules:
  0.0 258.8 jit_solution(14543656197228352573)
XLA Ops:
  0.7 3.2 %slice.89 = bf16[2048,512]{1,0:T(8,128)(2,1)} slice(bf16[2048,1024]{1,0:T(8,128)(2,1)} %param.6), slice={[0:2048], [0:512]} | slice | bytes 4194304 | tf_op jit(solution)/shard_map/slice | solution.py:84
  3.9 2.0 collective-permute-start.7
  5.9 3.5 %convert_reduce_fusion = (f32[1536]{0:T(1024)S(1)}, f32[1536]{0:T(1024)S(1)}) fusion(bf16[2048,512]{1,0:T(8,128)(2,1)} %param.7, bf16[2048,1024]{1,0:T(8,128)(2,1)S(1)} %copy-done.1), kind=kLoop, calls=%fused_computation.52 | loop fusion | flops 22017024 | bytes 6303744 | tf_op jit(solution)/shard_map/reduce_sum | solution.py:89
  9.5 3.1 %collective-permute-start.10 = (f32[2,1536]{1,0:T(2,128)S(1)}, f32[2,1536]{1,0:T(2,128)S(1)}, u32[]{:S(2)}, u32[]{:S(2)}) collective-permute-start(f32[2,1536]{1,0:T(2,128)S(1)} %pad_maximum_fusion.3), channel_id=1, source_target_pairs={{0,12},{4,8},{8,4},{12,0},{16,28},{20,24},{24,20},{28,16},{32,44},... | collective-permute-start | bytes 36872 | tf_op jit(solution)/shard_map/ppermute | solution.py:19
  19.5 2.7 %collective-permute-start.12 = (f32[2,1536]{1,0:T(2,128)S(1)}, f32[2,1536]{1,0:T(2,128)S(1)}, u32[]{:S(2)}, u32[]{:S(2)}) collective-permute-start(f32[2,1536]{1,0:T(2,128)S(1)} %add_add_fusion.3), channel_id=1, source_target_pairs={{0,32},{4,36},{8,40},{12,44},{16,48},{20,52},{24,56},{28,60},{32,0... | collective-permute-start | bytes 36872 | tf_op jit(solution)/shard_map/ppermute | solution.py:19
  22.7 2.0 collective-permute-done.12
  24.7 2.4 collective-permute-done.13
  27.2 3.1 %collective-permute-start.14 = (f32[2,1536]{1,0:T(2,128)S(1)}, f32[2,1536]{1,0:T(2,128)S(1)}, u32[]{:S(2)}, u32[]{:S(2)}) collective-permute-start(f32[2,1536]{1,0:T(2,128)S(1)} %add_add_fusion.2), channel_id=1, source_target_pairs={{0,64},{4,68},{8,72},{12,76},{16,80},{20,84},{24,88},{28,92},{32,9... | collective-permute-start | bytes 36872 | tf_op jit(solution)/shard_map/ppermute | solution.py:19
  30.2 3.1 %collective-permute-done.14 = f32[2,1536]{1,0:T(2,128)S(1)} collective-permute-done((f32[2,1536]{1,0:T(2,128)S(1)}, f32[2,1536]{1,0:T(2,128)S(1)}, u32[]{:S(2)}, u32[]{:S(2)}) %collective-permute-start.14) | collective-permute-done | bytes 12320 | tf_op jit(solution)/shard_map/ppermute | solution.py:19
  36.7 2.1 broadcast_select_fusion
  38.9 5.1 %multiply_convert_fusion = bf16[2048,1536]{1,0:T(8,128)(2,1)} fusion(bf16[2048,1024]{1,0:T(8,128)(2,1)S(1)} %copy-done.2, bf16[2048,512]{1,0:T(8,128)(2,1)S(1)} %broadcast_select_fusion, f32[1536]{0:T(1024)S(1)} %multiply_sqrt_fusion, f32[1536]{0:T(1024)S(1)} %get-tuple-element.26, f32[1536]{0:T(1024)S(1)} %get-tuple-element.25), kind=kLoop, calls=%fused_computation.54 | loop fusion | flops 25165824 | bytes 12601344 | tf_op jit(solution)/shard_map/convert_element_type | solution.py:97
  44.1 184.8 %while.10 = (s32[]{:T(128)}, f32[2,1024,8]{1,2,0:T(8,128)S(1)}, bf16[2048,1536]{1,0:T(8,128)(2,1)}, s32[]{:T(128)}) while((s32[]{:T(128)}, f32[2,1024,8]{1,2,0:T(8,128)S(1)}, bf16[2048,1536]{1,0:T(8,128)(2,1)}, s32[]{:T(128)}) %tuple.54), condition=%wide.region_5.6_spmd, body=%wide.region_2.5_spmd.sunk | while | flops 609027072 | bytes 43456232 | solution.py:111
  44.1 4.9 %convolution_bitcast_fusion.4 = f32[2048,48]{0,1:T(8,128)S(1)} fusion(bf16[2048,1536]{1,0:T(8,128)(2,1)} %get-tuple-element.114, bf16[1536,16]{0,1:T(8,128)(2,1)S(1)} %get-tuple-element.95, bf16[1536,16]{0,1:T(8,128)(2,1)S(1)} %get-tuple-element.96, bf16[1536,16]{0,1:T(8,128)(2,1)S(1)} %get-tuple-element.97), kind=kOutput, calls=%fused_computation.1.clone.1 | convolution fusion | flops 302432256 | bytes 6832128 | tf_op jit(solution)/shard_map/while/body/eval_jaxpr/dot_general | solution.py:102
  50.3 3.3 %collective-permute-start = (f32[2,1024,8]{1,2,0:T(8,128)S(1)}, f32[2,1024,8]{1,2,0:T(8,128)S(1)}, u32[]{:S(2)}, u32[]{:S(2)}) collective-permute-start(f32[2,1024,8]{1,2,0:T(8,128)S(1)} %pad_maximum_fusion.6), channel_id=1, source_target_pairs={{0,8},{4,12},{8,0},{12,4},{16,24},{20,28},{24,16},{28,20},{32,40},... | collective-permute-start | bytes 196616 | tf_op jit(solution)/shard_map/while/body/eval_jaxpr/ppermute | solution.py:19
  56.1 2.9 %collective-permute-done.1 = f32[2,1024,8]{1,2,0:T(8,128)S(1)} collective-permute-done((f32[2,1024,8]{1,2,0:T(8,128)S(1)}, f32[2,1024,8]{1,2,0:T(8,128)S(1)}, u32[]{:S(2)}, u32[]{:S(2)}) %collective-permute-start.1) | collective-permute-done | bytes 65568 | tf_op jit(solution)/shard_map/while/body/eval_jaxpr/ppermute | solution.py:19
  59.0 3.1 %collective-permute-start.3 = (f32[2,1024,8]{1,2,0:T(8,128)S(1)}, f32[2,1024,8]{1,2,0:T(8,128)S(1)}, u32[]{:S(2)}, u32[]{:S(2)}) collective-permute-start(f32[2,1024,8]{1,2,0:T(8,128)S(1)} %add_add_fusion.8), channel_id=1, source_target_pairs={{0,32},{4,36},{8,40},{12,44},{16,48},{20,52},{24,56},{28,60},{32,0... | collective-permute-start | bytes 196616 | tf_op jit(solution)/shard_map/while/body/eval_jaxpr/ppermute | solution.py:19
  65.0 2.6 %collective-permute-done.4 = f32[2,1024,8]{1,2,0:T(8,128)S(1)} collective-permute-done((f32[2,1024,8]{1,2,0:T(8,128)S(1)}, f32[2,1024,8]{1,2,0:T(8,128)S(1)}, u32[]{:S(2)}, u32[]{:S(2)}) %collective-permute-start.4) | collective-permute-done | bytes 65568 | tf_op jit(solution)/shard_map/while/body/eval_jaxpr/ppermute | solution.py:19
  68.3 5.2 %collective-permute-done.6 = f32[2,1024,8]{1,2,0:T(8,128)S(1)} collective-permute-done((f32[2,1024,8]{1,2,0:T(8,128)S(1)}, f32[2,1024,8]{1,2,0:T(8,128)S(1)}, u32[]{:S(2)}, u32[]{:S(2)}) %collective-permute-start.6) | collective-permute-done | bytes 65568 | tf_op jit(solution)/shard_map/while/body/eval_jaxpr/ppermute | solution.py:19
  77.1 4.9 %convolution_bitcast_fusion.4 = f32[2048,48]{0,1:T(8,128)S(1)} fusion(bf16[2048,1536]{1,0:T(8,128)(2,1)} %get-tuple-element.114, bf16[1536,16]{0,1:T(8,128)(2,1)S(1)} %get-tuple-element.95, bf16[1536,16]{0,1:T(8,128)(2,1)S(1)} %get-tuple-element.96, bf16[1536,16]{0,1:T(8,128)(2,1)S(1)} %get-tuple-element.97), kind=kOutput, calls=%fused_computation.1.clone.1 | convolution fusion | flops 302432256 | bytes 6832128 | tf_op jit(solution)/shard_map/while/body/eval_jaxpr/dot_general | solution.py:102
  86.8 2.3 collective-permute-done
  94.0 2.3 collective-permute-done.3
  98.9 4.4 %collective-permute-done.6 = f32[2,1024,8]{1,2,0:T(8,128)S(1)} collective-permute-done((f32[2,1024,8]{1,2,0:T(8,128)S(1)}, f32[2,1024,8]{1,2,0:T(8,128)S(1)}, u32[]{:S(2)}, u32[]{:S(2)}) %collective-permute-start.6) | collective-permute-done | bytes 65568 | tf_op jit(solution)/shard_map/while/body/eval_jaxpr/ppermute | solution.py:19
  106.9 4.9 %convolution_bitcast_fusion.4 = f32[2048,48]{0,1:T(8,128)S(1)} fusion(bf16[2048,1536]{1,0:T(8,128)(2,1)} %get-tuple-element.114, bf16[1536,16]{0,1:T(8,128)(2,1)S(1)} %get-tuple-element.95, bf16[1536,16]{0,1:T(8,128)(2,1)S(1)} %get-tuple-element.96, bf16[1536,16]{0,1:T(8,128)(2,1)S(1)} %get-tuple-element.97), kind=kOutput, calls=%fused_computation.1.clone.1 | convolution fusion | flops 302432256 | bytes 6832128 | tf_op jit(solution)/shard_map/while/body/eval_jaxpr/dot_general | solution.py:102
  113.0 2.3 collective-permute-start
  116.6 2.3 collective-permute-done
  120.8 2.4 collective-permute-start.3
  124.4 2.3 collective-permute-done.3
  129.4 5.1 %collective-permute-done.6 = f32[2,1024,8]{1,2,0:T(8,128)S(1)} collective-permute-done((f32[2,1024,8]{1,2,0:T(8,128)S(1)}, f32[2,1024,8]{1,2,0:T(8,128)S(1)}, u32[]{:S(2)}, u32[]{:S(2)}) %collective-permute-start.6) | collective-permute-done | bytes 65568 | tf_op jit(solution)/shard_map/while/body/eval_jaxpr/ppermute | solution.py:19
  138.2 4.9 %convolution_bitcast_fusion.4 = f32[2048,48]{0,1:T(8,128)S(1)} fusion(bf16[2048,1536]{1,0:T(8,128)(2,1)} %get-tuple-element.114, bf16[1536,16]{0,1:T(8,128)(2,1)S(1)} %get-tuple-element.95, bf16[1536,16]{0,1:T(8,128)(2,1)S(1)} %get-tuple-element.96, bf16[1536,16]{0,1:T(8,128)(2,1)S(1)} %get-tuple-element.97), kind=kOutput, calls=%fused_computation.1.clone.1 | convolution fusion | flops 302432256 | bytes 6832128 | tf_op jit(solution)/shard_map/while/body/eval_jaxpr/dot_general | solution.py:102
  147.9 2.3 collective-permute-done
  155.0 2.3 collective-permute-done.3
  159.9 4.4 %collective-permute-done.6 = f32[2,1024,8]{1,2,0:T(8,128)S(1)} collective-permute-done((f32[2,1024,8]{1,2,0:T(8,128)S(1)}, f32[2,1024,8]{1,2,0:T(8,128)S(1)}, u32[]{:S(2)}, u32[]{:S(2)}) %collective-permute-start.6) | collective-permute-done | bytes 65568 | tf_op jit(solution)/shard_map/while/body/eval_jaxpr/ppermute | solution.py:19
  167.9 4.9 %convolution_bitcast_fusion.4 = f32[2048,48]{0,1:T(8,128)S(1)} fusion(bf16[2048,1536]{1,0:T(8,128)(2,1)} %get-tuple-element.114, bf16[1536,16]{0,1:T(8,128)(2,1)S(1)} %get-tuple-element.95, bf16[1536,16]{0,1:T(8,128)(2,1)S(1)} %get-tuple-element.96, bf16[1536,16]{0,1:T(8,128)(2,1)S(1)} %get-tuple-element.97), kind=kOutput, calls=%fused_computation.1.clone.1 | convolution fusion | flops 302432256 | bytes 6832128 | tf_op jit(solution)/shard_map/while/body/eval_jaxpr/dot_general | solution.py:102
  174.1 2.3 collective-permute-start
  177.7 2.3 collective-permute-done
  181.9 2.4 collective-permute-start.3
  185.5 2.3 collective-permute-done.3
  190.5 5.1 %collective-permute-done.6 = f32[2,1024,8]{1,2,0:T(8,128)S(1)} collective-permute-done((f32[2,1024,8]{1,2,0:T(8,128)S(1)}, f32[2,1024,8]{1,2,0:T(8,128)S(1)}, u32[]{:S(2)}, u32[]{:S(2)}) %collective-permute-start.6) | collective-permute-done | bytes 65568 | tf_op jit(solution)/shard_map/while/body/eval_jaxpr/ppermute | solution.py:19
  199.2 4.9 %convolution_bitcast_fusion.4 = f32[2048,48]{0,1:T(8,128)S(1)} fusion(bf16[2048,1536]{1,0:T(8,128)(2,1)} %get-tuple-element.114, bf16[1536,16]{0,1:T(8,128)(2,1)S(1)} %get-tuple-element.95, bf16[1536,16]{0,1:T(8,128)(2,1)S(1)} %get-tuple-element.96, bf16[1536,16]{0,1:T(8,128)(2,1)S(1)} %get-tuple-element.97), kind=kOutput, calls=%fused_computation.1.clone.1 | convolution fusion | flops 302432256 | bytes 6832128 | tf_op jit(solution)/shard_map/while/body/eval_jaxpr/dot_general | solution.py:102
  208.9 2.3 collective-permute-done
  216.1 2.3 collective-permute-done.3
  221.0 4.4 %collective-permute-done.6 = f32[2,1024,8]{1,2,0:T(8,128)S(1)} collective-permute-done((f32[2,1024,8]{1,2,0:T(8,128)S(1)}, f32[2,1024,8]{1,2,0:T(8,128)S(1)}, u32[]{:S(2)}, u32[]{:S(2)}) %collective-permute-start.6) | collective-permute-done | bytes 65568 | tf_op jit(solution)/shard_map/while/body/eval_jaxpr/ppermute | solution.py:19
  229.0 4.7 %fusion.21 = f32[2048,48]{0,1:T(8,128)S(1)} fusion(bf16[2048,1536]{1,0:T(8,128)(2,1)} %get-tuple-element.116, bf16[1536,16]{0,1:T(8,128)(2,1)S(1)} %get-tuple-element.60, bf16[1536,16]{0,1:T(8,128)(2,1)S(1)} %get-tuple-element.59, bf16[1536,16]{0,1:T(8,128)(2,1)S(1)} %get-tuple-element.58), kind=kOutput, calls=%fused_computation.60 | convolution fusion | flops 302432256 | bytes 6832128 | tf_op jit(solution)/shard_map/dot_general | solution.py:102
  234.7 2.7 %collective-permute-start.17 = (f32[16]{0:T(128)S(1)}, f32[16]{0:T(128)S(1)}, u32[]{:S(2)}, u32[]{:S(2)}) collective-permute-start(f32[16]{0:T(128)S(1)} %get-tuple-element.35), channel_id=1, source_target_pairs={{0,8},{4,12},{8,0},{12,4},{16,24},{20,28},{24,16},{28,20},{32,40},... | collective-permute-start | bytes 200 | tf_op jit(solution)/shard_map/ppermute | solution.py:19
  241.8 3.0 %multiply_reduce_fusion.1 = (f32[2048]{0:T(1024)S(1)}, f32[2048]{0:T(1024)S(1)}) fusion(bf16[2048,1536]{1,0:T(8,128)(2,1)S(1)} %bitcast.80, f32[2048,1024]{1,0:T(8,128)S(1)} %fusion.38, bf16[2048,48]{0,1:T(8,128)(2,1)S(1)} %constant_dynamic-update-slice_fusion, bf16[1024,48]{0,1:T(8,128)(2,1)S(1)} %get-tuple-element.49), kind=kOutput, calls=%fused_computation.56 | convolution fusion | flops 218099712 | bytes 17088512 | tf_op jit(solution)/shard_map/dot_general | solution.py:67
  245.7 2.7 %collective-permute-start.20 = (f32[16]{0:T(128)S(1)}, f32[16]{0:T(128)S(1)}, u32[]{:S(2)}, u32[]{:S(2)}) collective-permute-start(f32[16]{0:T(128)S(1)} %add_add_fusion.5), channel_id=1, source_target_pairs={{0,32},{4,36},{8,40},{12,44},{16,48},{20,52},{24,56},{28,60},{32,0... | collective-permute-start | bytes 200 | tf_op jit(solution)/shard_map/ppermute | solution.py:19
  250.7 2.4 collective-permute-done.21
  254.3 3.9 %collective-permute-done.22 = f32[16]{0:T(128)S(1)} collective-permute-done((f32[16]{0:T(128)S(1)}, f32[16]{0:T(128)S(1)}, u32[]{:S(2)}, u32[]{:S(2)}) %collective-permute-start.22) | collective-permute-done | bytes 96 | tf_op jit(solution)/shard_map/ppermute | solution.py:19
  (272 shorter events, 103.6 us)
Async XLA Ops:
  3.9 32.8 %collective-permute-start.7 = (bf16[2048,512]{1,0:T(8,128)(2,1)}, bf16[2048,512]{1,0:T(8,128)(2,1)}, u32[]{:S(2)}, u32[]{:S(2)}) collective-permute-start(bf16[2048,512]{1,0:T(8,128)(2,1)} %slice.89), channel_id=1, source_target_pairs={{1,0},{2,1},{3,2},{5,4},{6,5},{7,6},{9,8},{10,9},{11,10},{13,12},{... | collective-permute-start | bytes 6291464 | tf_op jit(solution)/shard_map/ppermute | solution.py:14
  9.5 5.0 %collective-permute-start.10 = (f32[2,1536]{1,0:T(2,128)S(1)}, f32[2,1536]{1,0:T(2,128)S(1)}, u32[]{:S(2)}, u32[]{:S(2)}) collective-permute-start(f32[2,1536]{1,0:T(2,128)S(1)} %pad_maximum_fusion.3), channel_id=1, source_target_pairs={{0,12},{4,8},{8,4},{12,0},{16,28},{20,24},{24,20},{28,16},{32,44},... | collective-permute-start | bytes 36872 | tf_op jit(solution)/shard_map/ppermute | solution.py:19
  12.7 5.2 %collective-permute-start.9 = (f32[2,1536]{1,0:T(2,128)S(1)}, f32[2,1536]{1,0:T(2,128)S(1)}, u32[]{:S(2)}, u32[]{:S(2)}) collective-permute-start(f32[2,1536]{1,0:T(2,128)S(1)} %pad_maximum_fusion.3), channel_id=1, source_target_pairs={{0,8},{4,12},{8,0},{12,4},{16,24},{20,28},{24,16},{28,20},{32,40},... | collective-permute-start | bytes 36872 | tf_op jit(solution)/shard_map/ppermute | solution.py:19
  17.9 4.8 %collective-permute-start.11 = (f32[2,1536]{1,0:T(2,128)S(1)}, f32[2,1536]{1,0:T(2,128)S(1)}, u32[]{:S(2)}, u32[]{:S(2)}) collective-permute-start(f32[2,1536]{1,0:T(2,128)S(1)} %add_add_fusion.3), channel_id=1, source_target_pairs={{0,16},{4,20},{8,24},{12,28},{16,0},{20,4},{24,8},{28,12},{32,48},... | collective-permute-start | bytes 36872 | tf_op jit(solution)/shard_map/ppermute | solution.py:19
  19.5 5.2 %collective-permute-start.12 = (f32[2,1536]{1,0:T(2,128)S(1)}, f32[2,1536]{1,0:T(2,128)S(1)}, u32[]{:S(2)}, u32[]{:S(2)}) collective-permute-start(f32[2,1536]{1,0:T(2,128)S(1)} %add_add_fusion.3), channel_id=1, source_target_pairs={{0,32},{4,36},{8,40},{12,44},{16,48},{20,52},{24,56},{28,60},{32,0... | collective-permute-start | bytes 36872 | tf_op jit(solution)/shard_map/ppermute | solution.py:19
  22.2 4.9 %collective-permute-start.13 = (f32[2,1536]{1,0:T(2,128)S(1)}, f32[2,1536]{1,0:T(2,128)S(1)}, u32[]{:S(2)}, u32[]{:S(2)}) collective-permute-start(f32[2,1536]{1,0:T(2,128)S(1)} %add_add_fusion.3), channel_id=1, source_target_pairs={{0,48},{4,52},{8,56},{12,60},{16,32},{20,36},{24,40},{28,44},{32,1... | collective-permute-start | bytes 36872 | tf_op jit(solution)/shard_map/ppermute | solution.py:19
  27.2 6.2 %collective-permute-start.14 = (f32[2,1536]{1,0:T(2,128)S(1)}, f32[2,1536]{1,0:T(2,128)S(1)}, u32[]{:S(2)}, u32[]{:S(2)}) collective-permute-start(f32[2,1536]{1,0:T(2,128)S(1)} %add_add_fusion.2), channel_id=1, source_target_pairs={{0,64},{4,68},{8,72},{12,76},{16,80},{20,84},{24,88},{28,92},{32,9... | collective-permute-start | bytes 36872 | tf_op jit(solution)/shard_map/ppermute | solution.py:19
  50.3 5.8 %collective-permute-start = (f32[2,1024,8]{1,2,0:T(8,128)S(1)}, f32[2,1024,8]{1,2,0:T(8,128)S(1)}, u32[]{:S(2)}, u32[]{:S(2)}) collective-permute-start(f32[2,1024,8]{1,2,0:T(8,128)S(1)} %pad_maximum_fusion.6), channel_id=1, source_target_pairs={{0,8},{4,12},{8,0},{12,4},{16,24},{20,28},{24,16},{28,20},{32,40},... | collective-permute-start | bytes 196616 | tf_op jit(solution)/shard_map/while/body/eval_jaxpr/ppermute | solution.py:19
  53.5 5.5 %collective-permute-start.1 = (f32[2,1024,8]{1,2,0:T(8,128)S(1)}, f32[2,1024,8]{1,2,0:T(8,128)S(1)}, u32[]{:S(2)}, u32[]{:S(2)}) collective-permute-start(f32[2,1024,8]{1,2,0:T(8,128)S(1)} %pad_maximum_fusion.6), channel_id=1, source_target_pairs={{0,12},{4,8},{8,4},{12,0},{16,28},{20,24},{24,20},{28,16},{32,44},... | collective-permute-start | bytes 196616 | tf_op jit(solution)/shard_map/while/body/eval_jaxpr/ppermute | solution.py:19
  54.6 4.4 %collective-permute-start.2 = (f32[2,1024,8]{1,2,0:T(8,128)S(1)}, f32[2,1024,8]{1,2,0:T(8,128)S(1)}, u32[]{:S(2)}, u32[]{:S(2)}) collective-permute-start(f32[2,1024,8]{1,2,0:T(8,128)S(1)} %pad_maximum_fusion.6), channel_id=1, source_target_pairs={{0,4},{4,0},{8,12},{12,8},{16,20},{20,16},{24,28},{28,24},{32,36},... | collective-permute-start | bytes 196616 | tf_op jit(solution)/shard_map/while/body/eval_jaxpr/ppermute | solution.py:19
  59.0 6.0 %collective-permute-start.3 = (f32[2,1024,8]{1,2,0:T(8,128)S(1)}, f32[2,1024,8]{1,2,0:T(8,128)S(1)}, u32[]{:S(2)}, u32[]{:S(2)}) collective-permute-start(f32[2,1024,8]{1,2,0:T(8,128)S(1)} %add_add_fusion.8), channel_id=1, source_target_pairs={{0,32},{4,36},{8,40},{12,44},{16,48},{20,52},{24,56},{28,60},{32,0... | collective-permute-start | bytes 196616 | tf_op jit(solution)/shard_map/while/body/eval_jaxpr/ppermute | solution.py:19
  62.1 5.5 %collective-permute-start.4 = (f32[2,1024,8]{1,2,0:T(8,128)S(1)}, f32[2,1024,8]{1,2,0:T(8,128)S(1)}, u32[]{:S(2)}, u32[]{:S(2)}) collective-permute-start(f32[2,1024,8]{1,2,0:T(8,128)S(1)} %add_add_fusion.8), channel_id=1, source_target_pairs={{0,48},{4,52},{8,56},{12,60},{16,32},{20,36},{24,40},{28,44},{32,1... | collective-permute-start | bytes 196616 | tf_op jit(solution)/shard_map/while/body/eval_jaxpr/ppermute | solution.py:19
  63.3 4.3 %collective-permute-start.5 = (f32[2,1024,8]{1,2,0:T(8,128)S(1)}, f32[2,1024,8]{1,2,0:T(8,128)S(1)}, u32[]{:S(2)}, u32[]{:S(2)}) collective-permute-start(f32[2,1024,8]{1,2,0:T(8,128)S(1)} %add_add_fusion.8), channel_id=1, source_target_pairs={{0,16},{4,20},{8,24},{12,28},{16,0},{20,4},{24,8},{28,12},{32,48},... | collective-permute-start | bytes 196616 | tf_op jit(solution)/shard_map/while/body/eval_jaxpr/ppermute | solution.py:19
  67.6 5.8 %collective-permute-start.6 = (f32[2,1024,8]{1,2,0:T(8,128)S(1)}, f32[2,1024,8]{1,2,0:T(8,128)S(1)}, u32[]{:S(2)}, u32[]{:S(2)}) collective-permute-start(f32[2,1024,8]{1,2,0:T(8,128)S(1)} %add_add_fusion.9), channel_id=1, source_target_pairs={{0,64},{4,68},{8,72},{12,76},{16,80},{20,84},{24,88},{28,92},{32,9... | collective-permute-start | bytes 196616 | tf_op jit(solution)/shard_map/while/body/eval_jaxpr/ppermute | solution.py:19
  83.3 5.8 %collective-permute-start = (f32[2,1024,8]{1,2,0:T(8,128)S(1)}, f32[2,1024,8]{1,2,0:T(8,128)S(1)}, u32[]{:S(2)}, u32[]{:S(2)}) collective-permute-start(f32[2,1024,8]{1,2,0:T(8,128)S(1)} %pad_maximum_fusion.6), channel_id=1, source_target_pairs={{0,8},{4,12},{8,0},{12,4},{16,24},{20,28},{24,16},{28,20},{32,40},... | collective-permute-start | bytes 196616 | tf_op jit(solution)/shard_map/while/body/eval_jaxpr/ppermute | solution.py:19
  84.9 5.5 %collective-permute-start.1 = (f32[2,1024,8]{1,2,0:T(8,128)S(1)}, f32[2,1024,8]{1,2,0:T(8,128)S(1)}, u32[]{:S(2)}, u32[]{:S(2)}) collective-permute-start(f32[2,1024,8]{1,2,0:T(8,128)S(1)} %pad_maximum_fusion.6), channel_id=1, source_target_pairs={{0,12},{4,8},{8,4},{12,0},{16,28},{20,24},{24,20},{28,16},{32,44},... | collective-permute-start | bytes 196616 | tf_op jit(solution)/shard_map/while/body/eval_jaxpr/ppermute | solution.py:19
  85.9 4.5 %collective-permute-start.2 = (f32[2,1024,8]{1,2,0:T(8,128)S(1)}, f32[2,1024,8]{1,2,0:T(8,128)S(1)}, u32[]{:S(2)}, u32[]{:S(2)}) collective-permute-start(f32[2,1024,8]{1,2,0:T(8,128)S(1)} %pad_maximum_fusion.6), channel_id=1, source_target_pairs={{0,4},{4,0},{8,12},{12,8},{16,20},{20,16},{24,28},{28,24},{32,36},... | collective-permute-start | bytes 196616 | tf_op jit(solution)/shard_map/while/body/eval_jaxpr/ppermute | solution.py:19
  90.4 5.8 %collective-permute-start.3 = (f32[2,1024,8]{1,2,0:T(8,128)S(1)}, f32[2,1024,8]{1,2,0:T(8,128)S(1)}, u32[]{:S(2)}, u32[]{:S(2)}) collective-permute-start(f32[2,1024,8]{1,2,0:T(8,128)S(1)} %add_add_fusion.8), channel_id=1, source_target_pairs={{0,32},{4,36},{8,40},{12,44},{16,48},{20,52},{24,56},{28,60},{32,0... | collective-permute-start | bytes 196616 | tf_op jit(solution)/shard_map/while/body/eval_jaxpr/ppermute | solution.py:19
  91.9 5.5 %collective-permute-start.4 = (f32[2,1024,8]{1,2,0:T(8,128)S(1)}, f32[2,1024,8]{1,2,0:T(8,128)S(1)}, u32[]{:S(2)}, u32[]{:S(2)}) collective-permute-start(f32[2,1024,8]{1,2,0:T(8,128)S(1)} %add_add_fusion.8), channel_id=1, source_target_pairs={{0,48},{4,52},{8,56},{12,60},{16,32},{20,36},{24,40},{28,44},{32,1... | collective-permute-start | bytes 196616 | tf_op jit(solution)/shard_map/while/body/eval_jaxpr/ppermute | solution.py:19
  93.1 4.3 %collective-permute-start.5 = (f32[2,1024,8]{1,2,0:T(8,128)S(1)}, f32[2,1024,8]{1,2,0:T(8,128)S(1)}, u32[]{:S(2)}, u32[]{:S(2)}) collective-permute-start(f32[2,1024,8]{1,2,0:T(8,128)S(1)} %add_add_fusion.8), channel_id=1, source_target_pairs={{0,16},{4,20},{8,24},{12,28},{16,0},{20,4},{24,8},{28,12},{32,48},... | collective-permute-start | bytes 196616 | tf_op jit(solution)/shard_map/while/body/eval_jaxpr/ppermute | solution.py:19
  97.4 5.8 %collective-permute-start.6 = (f32[2,1024,8]{1,2,0:T(8,128)S(1)}, f32[2,1024,8]{1,2,0:T(8,128)S(1)}, u32[]{:S(2)}, u32[]{:S(2)}) collective-permute-start(f32[2,1024,8]{1,2,0:T(8,128)S(1)} %add_add_fusion.9), channel_id=1, source_target_pairs={{0,64},{4,68},{8,72},{12,76},{16,80},{20,84},{24,88},{28,92},{32,9... | collective-permute-start | bytes 196616 | tf_op jit(solution)/shard_map/while/body/eval_jaxpr/ppermute | solution.py:19
  113.0 5.8 %collective-permute-start = (f32[2,1024,8]{1,2,0:T(8,128)S(1)}, f32[2,1024,8]{1,2,0:T(8,128)S(1)}, u32[]{:S(2)}, u32[]{:S(2)}) collective-permute-start(f32[2,1024,8]{1,2,0:T(8,128)S(1)} %pad_maximum_fusion.6), channel_id=1, source_target_pairs={{0,8},{4,12},{8,0},{12,4},{16,24},{20,28},{24,16},{28,20},{32,40},... | collective-permute-start | bytes 196616 | tf_op jit(solution)/shard_map/while/body/eval_jaxpr/ppermute | solution.py:19
  115.3 5.5 %collective-permute-start.1 = (f32[2,1024,8]{1,2,0:T(8,128)S(1)}, f32[2,1024,8]{1,2,0:T(8,128)S(1)}, u32[]{:S(2)}, u32[]{:S(2)}) collective-permute-start(f32[2,1024,8]{1,2,0:T(8,128)S(1)} %pad_maximum_fusion.6), channel_id=1, source_target_pairs={{0,12},{4,8},{8,4},{12,0},{16,28},{20,24},{24,20},{28,16},{32,44},... | collective-permute-start | bytes 196616 | tf_op jit(solution)/shard_map/while/body/eval_jaxpr/ppermute | solution.py:19
  120.8 5.8 %collective-permute-start.3 = (f32[2,1024,8]{1,2,0:T(8,128)S(1)}, f32[2,1024,8]{1,2,0:T(8,128)S(1)}, u32[]{:S(2)}, u32[]{:S(2)}) collective-permute-start(f32[2,1024,8]{1,2,0:T(8,128)S(1)} %add_add_fusion.8), channel_id=1, source_target_pairs={{0,32},{4,36},{8,40},{12,44},{16,48},{20,52},{24,56},{28,60},{32,0... | collective-permute-start | bytes 196616 | tf_op jit(solution)/shard_map/while/body/eval_jaxpr/ppermute | solution.py:19
  123.2 5.5 %collective-permute-start.4 = (f32[2,1024,8]{1,2,0:T(8,128)S(1)}, f32[2,1024,8]{1,2,0:T(8,128)S(1)}, u32[]{:S(2)}, u32[]{:S(2)}) collective-permute-start(f32[2,1024,8]{1,2,0:T(8,128)S(1)} %add_add_fusion.8), channel_id=1, source_target_pairs={{0,48},{4,52},{8,56},{12,60},{16,32},{20,36},{24,40},{28,44},{32,1... | collective-permute-start | bytes 196616 | tf_op jit(solution)/shard_map/while/body/eval_jaxpr/ppermute | solution.py:19
  128.7 5.8 %collective-permute-start.6 = (f32[2,1024,8]{1,2,0:T(8,128)S(1)}, f32[2,1024,8]{1,2,0:T(8,128)S(1)}, u32[]{:S(2)}, u32[]{:S(2)}) collective-permute-start(f32[2,1024,8]{1,2,0:T(8,128)S(1)} %add_add_fusion.9), channel_id=1, source_target_pairs={{0,64},{4,68},{8,72},{12,76},{16,80},{20,84},{24,88},{28,92},{32,9... | collective-permute-start | bytes 196616 | tf_op jit(solution)/shard_map/while/body/eval_jaxpr/ppermute | solution.py:19
  144.3 5.8 %collective-permute-start = (f32[2,1024,8]{1,2,0:T(8,128)S(1)}, f32[2,1024,8]{1,2,0:T(8,128)S(1)}, u32[]{:S(2)}, u32[]{:S(2)}) collective-permute-start(f32[2,1024,8]{1,2,0:T(8,128)S(1)} %pad_maximum_fusion.6), channel_id=1, source_target_pairs={{0,8},{4,12},{8,0},{12,4},{16,24},{20,28},{24,16},{28,20},{32,40},... | collective-permute-start | bytes 196616 | tf_op jit(solution)/shard_map/while/body/eval_jaxpr/ppermute | solution.py:19
  145.9 5.5 %collective-permute-start.1 = (f32[2,1024,8]{1,2,0:T(8,128)S(1)}, f32[2,1024,8]{1,2,0:T(8,128)S(1)}, u32[]{:S(2)}, u32[]{:S(2)}) collective-permute-start(f32[2,1024,8]{1,2,0:T(8,128)S(1)} %pad_maximum_fusion.6), channel_id=1, source_target_pairs={{0,12},{4,8},{8,4},{12,0},{16,28},{20,24},{24,20},{28,16},{32,44},... | collective-permute-start | bytes 196616 | tf_op jit(solution)/shard_map/while/body/eval_jaxpr/ppermute | solution.py:19
  151.4 5.8 %collective-permute-start.3 = (f32[2,1024,8]{1,2,0:T(8,128)S(1)}, f32[2,1024,8]{1,2,0:T(8,128)S(1)}, u32[]{:S(2)}, u32[]{:S(2)}) collective-permute-start(f32[2,1024,8]{1,2,0:T(8,128)S(1)} %add_add_fusion.8), channel_id=1, source_target_pairs={{0,32},{4,36},{8,40},{12,44},{16,48},{20,52},{24,56},{28,60},{32,0... | collective-permute-start | bytes 196616 | tf_op jit(solution)/shard_map/while/body/eval_jaxpr/ppermute | solution.py:19
  153.0 5.5 %collective-permute-start.4 = (f32[2,1024,8]{1,2,0:T(8,128)S(1)}, f32[2,1024,8]{1,2,0:T(8,128)S(1)}, u32[]{:S(2)}, u32[]{:S(2)}) collective-permute-start(f32[2,1024,8]{1,2,0:T(8,128)S(1)} %add_add_fusion.8), channel_id=1, source_target_pairs={{0,48},{4,52},{8,56},{12,60},{16,32},{20,36},{24,40},{28,44},{32,1... | collective-permute-start | bytes 196616 | tf_op jit(solution)/shard_map/while/body/eval_jaxpr/ppermute | solution.py:19
  158.5 5.8 %collective-permute-start.6 = (f32[2,1024,8]{1,2,0:T(8,128)S(1)}, f32[2,1024,8]{1,2,0:T(8,128)S(1)}, u32[]{:S(2)}, u32[]{:S(2)}) collective-permute-start(f32[2,1024,8]{1,2,0:T(8,128)S(1)} %add_add_fusion.9), channel_id=1, source_target_pairs={{0,64},{4,68},{8,72},{12,76},{16,80},{20,84},{24,88},{28,92},{32,9... | collective-permute-start | bytes 196616 | tf_op jit(solution)/shard_map/while/body/eval_jaxpr/ppermute | solution.py:19
  174.1 5.8 %collective-permute-start = (f32[2,1024,8]{1,2,0:T(8,128)S(1)}, f32[2,1024,8]{1,2,0:T(8,128)S(1)}, u32[]{:S(2)}, u32[]{:S(2)}) collective-permute-start(f32[2,1024,8]{1,2,0:T(8,128)S(1)} %pad_maximum_fusion.6), channel_id=1, source_target_pairs={{0,8},{4,12},{8,0},{12,4},{16,24},{20,28},{24,16},{28,20},{32,40},... | collective-permute-start | bytes 196616 | tf_op jit(solution)/shard_map/while/body/eval_jaxpr/ppermute | solution.py:19
  176.4 5.5 %collective-permute-start.1 = (f32[2,1024,8]{1,2,0:T(8,128)S(1)}, f32[2,1024,8]{1,2,0:T(8,128)S(1)}, u32[]{:S(2)}, u32[]{:S(2)}) collective-permute-start(f32[2,1024,8]{1,2,0:T(8,128)S(1)} %pad_maximum_fusion.6), channel_id=1, source_target_pairs={{0,12},{4,8},{8,4},{12,0},{16,28},{20,24},{24,20},{28,16},{32,44},... | collective-permute-start | bytes 196616 | tf_op jit(solution)/shard_map/while/body/eval_jaxpr/ppermute | solution.py:19
  181.9 5.8 %collective-permute-start.3 = (f32[2,1024,8]{1,2,0:T(8,128)S(1)}, f32[2,1024,8]{1,2,0:T(8,128)S(1)}, u32[]{:S(2)}, u32[]{:S(2)}) collective-permute-start(f32[2,1024,8]{1,2,0:T(8,128)S(1)} %add_add_fusion.8), channel_id=1, source_target_pairs={{0,32},{4,36},{8,40},{12,44},{16,48},{20,52},{24,56},{28,60},{32,0... | collective-permute-start | bytes 196616 | tf_op jit(solution)/shard_map/while/body/eval_jaxpr/ppermute | solution.py:19
  184.2 5.5 %collective-permute-start.4 = (f32[2,1024,8]{1,2,0:T(8,128)S(1)}, f32[2,1024,8]{1,2,0:T(8,128)S(1)}, u32[]{:S(2)}, u32[]{:S(2)}) collective-permute-start(f32[2,1024,8]{1,2,0:T(8,128)S(1)} %add_add_fusion.8), channel_id=1, source_target_pairs={{0,48},{4,52},{8,56},{12,60},{16,32},{20,36},{24,40},{28,44},{32,1... | collective-permute-start | bytes 196616 | tf_op jit(solution)/shard_map/while/body/eval_jaxpr/ppermute | solution.py:19
  189.7 5.8 %collective-permute-start.6 = (f32[2,1024,8]{1,2,0:T(8,128)S(1)}, f32[2,1024,8]{1,2,0:T(8,128)S(1)}, u32[]{:S(2)}, u32[]{:S(2)}) collective-permute-start(f32[2,1024,8]{1,2,0:T(8,128)S(1)} %add_add_fusion.9), channel_id=1, source_target_pairs={{0,64},{4,68},{8,72},{12,76},{16,80},{20,84},{24,88},{28,92},{32,9... | collective-permute-start | bytes 196616 | tf_op jit(solution)/shard_map/while/body/eval_jaxpr/ppermute | solution.py:19
  205.4 5.8 %collective-permute-start = (f32[2,1024,8]{1,2,0:T(8,128)S(1)}, f32[2,1024,8]{1,2,0:T(8,128)S(1)}, u32[]{:S(2)}, u32[]{:S(2)}) collective-permute-start(f32[2,1024,8]{1,2,0:T(8,128)S(1)} %pad_maximum_fusion.6), channel_id=1, source_target_pairs={{0,8},{4,12},{8,0},{12,4},{16,24},{20,28},{24,16},{28,20},{32,40},... | collective-permute-start | bytes 196616 | tf_op jit(solution)/shard_map/while/body/eval_jaxpr/ppermute | solution.py:19
  207.0 5.5 %collective-permute-start.1 = (f32[2,1024,8]{1,2,0:T(8,128)S(1)}, f32[2,1024,8]{1,2,0:T(8,128)S(1)}, u32[]{:S(2)}, u32[]{:S(2)}) collective-permute-start(f32[2,1024,8]{1,2,0:T(8,128)S(1)} %pad_maximum_fusion.6), channel_id=1, source_target_pairs={{0,12},{4,8},{8,4},{12,0},{16,28},{20,24},{24,20},{28,16},{32,44},... | collective-permute-start | bytes 196616 | tf_op jit(solution)/shard_map/while/body/eval_jaxpr/ppermute | solution.py:19
  212.5 5.8 %collective-permute-start.3 = (f32[2,1024,8]{1,2,0:T(8,128)S(1)}, f32[2,1024,8]{1,2,0:T(8,128)S(1)}, u32[]{:S(2)}, u32[]{:S(2)}) collective-permute-start(f32[2,1024,8]{1,2,0:T(8,128)S(1)} %add_add_fusion.8), channel_id=1, source_target_pairs={{0,32},{4,36},{8,40},{12,44},{16,48},{20,52},{24,56},{28,60},{32,0... | collective-permute-start | bytes 196616 | tf_op jit(solution)/shard_map/while/body/eval_jaxpr/ppermute | solution.py:19
  214.0 5.5 %collective-permute-start.4 = (f32[2,1024,8]{1,2,0:T(8,128)S(1)}, f32[2,1024,8]{1,2,0:T(8,128)S(1)}, u32[]{:S(2)}, u32[]{:S(2)}) collective-permute-start(f32[2,1024,8]{1,2,0:T(8,128)S(1)} %add_add_fusion.8), channel_id=1, source_target_pairs={{0,48},{4,52},{8,56},{12,60},{16,32},{20,36},{24,40},{28,44},{32,1... | collective-permute-start | bytes 196616 | tf_op jit(solution)/shard_map/while/body/eval_jaxpr/ppermute | solution.py:19
  219.5 5.8 %collective-permute-start.6 = (f32[2,1024,8]{1,2,0:T(8,128)S(1)}, f32[2,1024,8]{1,2,0:T(8,128)S(1)}, u32[]{:S(2)}, u32[]{:S(2)}) collective-permute-start(f32[2,1024,8]{1,2,0:T(8,128)S(1)} %add_add_fusion.9), channel_id=1, source_target_pairs={{0,64},{4,68},{8,72},{12,76},{16,80},{20,84},{24,88},{28,92},{32,9... | collective-permute-start | bytes 196616 | tf_op jit(solution)/shard_map/while/body/eval_jaxpr/ppermute | solution.py:19
  233.9 10.9 %collective-permute-start.16 = (f32[16]{0:T(128)S(1)}, f32[16]{0:T(128)S(1)}, u32[]{:S(2)}, u32[]{:S(2)}) collective-permute-start(f32[16]{0:T(128)S(1)} %get-tuple-element.35), channel_id=1, source_target_pairs={{0,4},{4,0},{8,12},{12,8},{16,20},{20,16},{24,28},{28,24},{32,36},... | collective-permute-start | bytes 200 | tf_op jit(solution)/shard_map/ppermute | solution.py:19
  234.7 10.1 %collective-permute-start.17 = (f32[16]{0:T(128)S(1)}, f32[16]{0:T(128)S(1)}, u32[]{:S(2)}, u32[]{:S(2)}) collective-permute-start(f32[16]{0:T(128)S(1)} %get-tuple-element.35), channel_id=1, source_target_pairs={{0,8},{4,12},{8,0},{12,4},{16,24},{20,28},{24,16},{28,20},{32,40},... | collective-permute-start | bytes 200 | tf_op jit(solution)/shard_map/ppermute | solution.py:19
  237.4 7.3 %collective-permute-start.18 = (f32[16]{0:T(128)S(1)}, f32[16]{0:T(128)S(1)}, u32[]{:S(2)}, u32[]{:S(2)}) collective-permute-start(f32[16]{0:T(128)S(1)} %get-tuple-element.35), channel_id=1, source_target_pairs={{0,12},{4,8},{8,4},{12,0},{16,28},{20,24},{24,20},{28,16},{32,44},... | collective-permute-start | bytes 200 | tf_op jit(solution)/shard_map/ppermute | solution.py:19
  244.8 4.8 %collective-permute-start.19 = (f32[16]{0:T(128)S(1)}, f32[16]{0:T(128)S(1)}, u32[]{:S(2)}, u32[]{:S(2)}) collective-permute-start(f32[16]{0:T(128)S(1)} %add_add_fusion.5), channel_id=1, source_target_pairs={{0,16},{4,20},{8,24},{12,28},{16,0},{20,4},{24,8},{28,12},{32,48},... | collective-permute-start | bytes 200 | tf_op jit(solution)/shard_map/ppermute | solution.py:19
  245.7 5.1 %collective-permute-start.20 = (f32[16]{0:T(128)S(1)}, f32[16]{0:T(128)S(1)}, u32[]{:S(2)}, u32[]{:S(2)}) collective-permute-start(f32[16]{0:T(128)S(1)} %add_add_fusion.5), channel_id=1, source_target_pairs={{0,32},{4,36},{8,40},{12,44},{16,48},{20,52},{24,56},{28,60},{32,0... | collective-permute-start | bytes 200 | tf_op jit(solution)/shard_map/ppermute | solution.py:19
  248.3 4.8 %collective-permute-start.21 = (f32[16]{0:T(128)S(1)}, f32[16]{0:T(128)S(1)}, u32[]{:S(2)}, u32[]{:S(2)}) collective-permute-start(f32[16]{0:T(128)S(1)} %add_add_fusion.5), channel_id=1, source_target_pairs={{0,48},{4,52},{8,56},{12,60},{16,32},{20,36},{24,40},{28,44},{32,1... | collective-permute-start | bytes 200 | tf_op jit(solution)/shard_map/ppermute | solution.py:19
  253.1 5.1 %collective-permute-start.22 = (f32[16]{0:T(128)S(1)}, f32[16]{0:T(128)S(1)}, u32[]{:S(2)}, u32[]{:S(2)}) collective-permute-start(f32[16]{0:T(128)S(1)} %add_add_fusion.4), channel_id=1, source_target_pairs={{0,64},{4,68},{8,72},{12,76},{16,80},{20,84},{24,88},{28,92},{32,9... | collective-permute-start | bytes 200 | tf_op jit(solution)/shard_map/ppermute | solution.py:19
  (23 other events, 136.7 us)

commit v10 on v9

--- a/solution.py
+++ b/solution.py
@@ -81,8 +81,8 @@
     half_cols = columns // 2
     comps = start.shape[2]
     total = dosage.shape[0] * lax.axis_size("ind")
-    received = passed_along(dosage[:, :half_cols], "win", -1)
-    following = jnp.where(position == win_count - 1, tail, received)
+    outgoing = jnp.where(position == 0, tail, dosage[:, :half_cols])
+    following = lax.ppermute(outgoing, "win", [(i, (i - 1) % win_count) for i in range(win_count)])
     region = jnp.concatenate([dosage, following], axis=1)
     regionf = region.astype(jnp.float32)
     ownf = jnp.concatenate([dosage, tail], axis=1).astype(jnp.float32)

time: 259 us -> 259 us (level)
  starting transfers between devices: 77.5 us -> 73 us
  waiting for transfers between devices: 94.3 us -> 97.5 us
    slice x1 -> x0, local copies, waits for them, and re-layouts: 3.22 us -> none  [shards(): received = passed_along(dosage[:, :half_cols], 'win', -1)]
    ppermute x56, waiting for transfers between devices: 93.8 us -> 97 us  [swapped(): return lax.ppermute(value, axis, [(i, i ^ mask) for i in range(size)])]
  transfers between devices with their start and end apart: 58 -> 58, of which waited for: 40 -> 40; matrix products, arithmetic and copies ran while one was open for 4% -> 3% of each run, Pallas kernels for 0% -> 0%
where the time goes in v10:
time: 259 us; the launch traced here: 257 us
  waiting for transfers between devices  97.5 us (38%)
  starting transfers between devices  73 us (28%)
  matrix products  48 us (19%)
  other arithmetic  33 us (13%)
  local copies, waits for them, and re-layouts  3.65 us (1%)
    ppermute x56, waiting for transfers between devices, swapped(): return lax.ppermute(value, axis, [(i, i ^ mask) for i in range(size)])  97 us
    ppermute x56, starting transfers between devices, swapped(): return lax.ppermute(value, axis, [(i, i ^ mask) for i in range(size)])  71 us
    dot_general x7, matrix products, project(): jnp.dot(stand, jnp.concatenate(pieces(wide), 1), preferred_element_type=j...  33.9 us
    another operation x24, other arithmetic, orthonormal(): factor = jnp.linalg.cholesky(gram)  9.76 us
    another operation x18, other arithmetic, orthonormal(): jax.scipy.linalg.solve_triangular(fac, rhs, lower=True)  8.03 us
    convert_element_type x1, other arithmetic, shards(): ((regionf - mean) / jnp.sqrt(var + 1e-05) * weight).astype(jnp.bfloat16)  7.23 us
    dot_general x6, matrix products, image_of(): lax.dot_general(stand, split, (((0,), (0,)), ((), ())), preferred_element...  6.76 us
  transfers between devices with their start and end apart: 58, of which 40 were waited for; matrix products, arithmetic and copies ran while one was open for 3% of the time, Pallas kernels for 0%

profile of v10, /device:TPU:32, one launch (start us, length us, event | category | flops | bytes accessed | tf_op | source)
XLA Modules:
  0.0 256.8 jit_solution(9582542079307235827)
XLA Ops:
  0.7 3.3 %slice_select_fusion = bf16[2048,512]{1,0:T(8,128)(2,1)} fusion(bf16[2048,512]{1,0:T(8,128)(2,1)} %param.7, bf16[2048,1024]{1,0:T(8,128)(2,1)} %param.6, pred[]{:T(512)S(6)} %eq.6), kind=kLoop, calls=%fused_computation.59 | loop fusion | flops 1048576 | bytes 6291457 | tf_op jit(solution)/shard_map/jit(_where)/select_n | solution.py:84
  6.8 3.1 %collective-permute-start.10 = (f32[2,1536]{1,0:T(2,128)S(1)}, f32[2,1536]{1,0:T(2,128)S(1)}, u32[]{:S(2)}, u32[]{:S(2)}) collective-permute-start(f32[2,1536]{1,0:T(2,128)S(1)} %pad_maximum_fusion.3), channel_id=1, source_target_pairs={{0,12},{4,8},{8,4},{12,0},{16,28},{20,24},{24,20},{28,16},{32,44},... | collective-permute-start | bytes 36872 | tf_op jit(solution)/shard_map/ppermute | solution.py:19
  16.8 2.7 %collective-permute-start.12 = (f32[2,1536]{1,0:T(2,128)S(1)}, f32[2,1536]{1,0:T(2,128)S(1)}, u32[]{:S(2)}, u32[]{:S(2)}) collective-permute-start(f32[2,1536]{1,0:T(2,128)S(1)} %add_add_fusion.3), channel_id=1, source_target_pairs={{0,32},{4,36},{8,40},{12,44},{16,48},{20,52},{24,56},{28,60},{32,0... | collective-permute-start | bytes 36872 | tf_op jit(solution)/shard_map/ppermute | solution.py:19
  20.0 2.0 collective-permute-done.12
  22.0 2.4 collective-permute-done.13
  24.5 3.1 %collective-permute-start.14 = (f32[2,1536]{1,0:T(2,128)S(1)}, f32[2,1536]{1,0:T(2,128)S(1)}, u32[]{:S(2)}, u32[]{:S(2)}) collective-permute-start(f32[2,1536]{1,0:T(2,128)S(1)} %add_add_fusion.2), channel_id=1, source_target_pairs={{0,64},{4,68},{8,72},{12,76},{16,80},{20,84},{24,88},{28,92},{32,9... | collective-permute-start | bytes 36872 | tf_op jit(solution)/shard_map/ppermute | solution.py:19
  27.5 3.9 %collective-permute-done.14 = f32[2,1536]{1,0:T(2,128)S(1)} collective-permute-done((f32[2,1536]{1,0:T(2,128)S(1)}, f32[2,1536]{1,0:T(2,128)S(1)}, u32[]{:S(2)}, u32[]{:S(2)}) %collective-permute-start.14) | collective-permute-done | bytes 12320 | tf_op jit(solution)/shard_map/ppermute | solution.py:19
  31.4 1.9 collective-permute-start.15
  34.8 7.2 %multiply_convert_fusion = bf16[2048,1536]{1,0:T(8,128)(2,1)} fusion(bf16[2048,1024]{1,0:T(8,128)(2,1)} %param.6, bf16[2048,512]{1,0:T(8,128)(2,1)} %collective-permute-done.7, f32[1536]{0:T(1024)S(1)} %multiply_sqrt_fusion, f32[1536]{0:T(1024)S(1)} %get-tuple-element.26, f32[1536]{0:T(1024)S(1)} %get-tuple-element.25), kind=kLoop, calls=%fused_computation.54 | loop fusion | flops 25165824 | bytes 12601344 | tf_op jit(solution)/shard_map/convert_element_type | solution.py:97
  42.0 184.8 %while.10 = (s32[]{:T(128)}, f32[2,1024,8]{1,2,0:T(8,128)S(1)}, bf16[2048,1536]{1,0:T(8,128)(2,1)}, s32[]{:T(128)}) while((s32[]{:T(128)}, f32[2,1024,8]{1,2,0:T(8,128)S(1)}, bf16[2048,1536]{1,0:T(8,128)(2,1)}, s32[]{:T(128)}) %tuple.54), condition=%wide.region_5.6_spmd, body=%wide.region_2.5_spmd.sunk | while | flops 609027072 | bytes 43456232 | solution.py:111
  42.0 4.9 %convolution_bitcast_fusion.4 = f32[2048,48]{0,1:T(8,128)S(1)} fusion(bf16[2048,1536]{1,0:T(8,128)(2,1)} %get-tuple-element.114, bf16[1536,16]{0,1:T(8,128)(2,1)S(1)} %get-tuple-element.95, bf16[1536,16]{0,1:T(8,128)(2,1)S(1)} %get-tuple-element.96, bf16[1536,16]{0,1:T(8,128)(2,1)S(1)} %get-tuple-element.97), kind=kOutput, calls=%fused_computation.1.clone.1 | convolution fusion | flops 302432256 | bytes 6832128 | tf_op jit(solution)/shard_map/while/body/eval_jaxpr/dot_general | solution.py:102
  48.2 3.3 %collective-permute-start = (f32[2,1024,8]{1,2,0:T(8,128)S(1)}, f32[2,1024,8]{1,2,0:T(8,128)S(1)}, u32[]{:S(2)}, u32[]{:S(2)}) collective-permute-start(f32[2,1024,8]{1,2,0:T(8,128)S(1)} %pad_maximum_fusion.6), channel_id=1, source_target_pairs={{0,8},{4,12},{8,0},{12,4},{16,24},{20,28},{24,16},{28,20},{32,40},... | collective-permute-start | bytes 196616 | tf_op jit(solution)/shard_map/while/body/eval_jaxpr/ppermute | solution.py:19
  54.0 2.9 %collective-permute-done.1 = f32[2,1024,8]{1,2,0:T(8,128)S(1)} collective-permute-done((f32[2,1024,8]{1,2,0:T(8,128)S(1)}, f32[2,1024,8]{1,2,0:T(8,128)S(1)}, u32[]{:S(2)}, u32[]{:S(2)}) %collective-permute-start.1) | collective-permute-done | bytes 65568 | tf_op jit(solution)/shard_map/while/body/eval_jaxpr/ppermute | solution.py:19
  57.0 3.1 %collective-permute-start.3 = (f32[2,1024,8]{1,2,0:T(8,128)S(1)}, f32[2,1024,8]{1,2,0:T(8,128)S(1)}, u32[]{:S(2)}, u32[]{:S(2)}) collective-permute-start(f32[2,1024,8]{1,2,0:T(8,128)S(1)} %add_add_fusion.8), channel_id=1, source_target_pairs={{0,32},{4,36},{8,40},{12,44},{16,48},{20,52},{24,56},{28,60},{32,0... | collective-permute-start | bytes 196616 | tf_op jit(solution)/shard_map/while/body/eval_jaxpr/ppermute | solution.py:19
  62.9 2.7 %collective-permute-done.4 = f32[2,1024,8]{1,2,0:T(8,128)S(1)} collective-permute-done((f32[2,1024,8]{1,2,0:T(8,128)S(1)}, f32[2,1024,8]{1,2,0:T(8,128)S(1)}, u32[]{:S(2)}, u32[]{:S(2)}) %collective-permute-start.4) | collective-permute-done | bytes 65568 | tf_op jit(solution)/shard_map/while/body/eval_jaxpr/ppermute | solution.py:19
  66.2 5.2 %collective-permute-done.6 = f32[2,1024,8]{1,2,0:T(8,128)S(1)} collective-permute-done((f32[2,1024,8]{1,2,0:T(8,128)S(1)}, f32[2,1024,8]{1,2,0:T(8,128)S(1)}, u32[]{:S(2)}, u32[]{:S(2)}) %collective-permute-start.6) | collective-permute-done | bytes 65568 | tf_op jit(solution)/shard_map/while/body/eval_jaxpr/ppermute | solution.py:19
  75.0 4.9 %convolution_bitcast_fusion.4 = f32[2048,48]{0,1:T(8,128)S(1)} fusion(bf16[2048,1536]{1,0:T(8,128)(2,1)} %get-tuple-element.114, bf16[1536,16]{0,1:T(8,128)(2,1)S(1)} %get-tuple-element.95, bf16[1536,16]{0,1:T(8,128)(2,1)S(1)} %get-tuple-element.96, bf16[1536,16]{0,1:T(8,128)(2,1)S(1)} %get-tuple-element.97), kind=kOutput, calls=%fused_computation.1.clone.1 | convolution fusion | flops 302432256 | bytes 6832128 | tf_op jit(solution)/shard_map/while/body/eval_jaxpr/dot_general | solution.py:102
  84.8 2.3 collective-permute-done
  91.9 2.3 collective-permute-done.3
  96.1 5.1 %collective-permute-done.6 = f32[2,1024,8]{1,2,0:T(8,128)S(1)} collective-permute-done((f32[2,1024,8]{1,2,0:T(8,128)S(1)}, f32[2,1024,8]{1,2,0:T(8,128)S(1)}, u32[]{:S(2)}, u32[]{:S(2)}) %collective-permute-start.6) | collective-permute-done | bytes 65568 | tf_op jit(solution)/shard_map/while/body/eval_jaxpr/ppermute | solution.py:19
  104.8 4.9 %convolution_bitcast_fusion.4 = f32[2048,48]{0,1:T(8,128)S(1)} fusion(bf16[2048,1536]{1,0:T(8,128)(2,1)} %get-tuple-element.114, bf16[1536,16]{0,1:T(8,128)(2,1)S(1)} %get-tuple-element.95, bf16[1536,16]{0,1:T(8,128)(2,1)S(1)} %get-tuple-element.96, bf16[1536,16]{0,1:T(8,128)(2,1)S(1)} %get-tuple-element.97), kind=kOutput, calls=%fused_computation.1.clone.1 | convolution fusion | flops 302432256 | bytes 6832128 | tf_op jit(solution)/shard_map/while/body/eval_jaxpr/dot_general | solution.py:102
  111.0 2.3 collective-permute-start
  114.5 2.3 collective-permute-done
  118.7 2.4 collective-permute-start.3
  122.3 2.3 collective-permute-done.3
  124.6 2.0 collective-permute-done.4
  127.2 5.2 %collective-permute-done.6 = f32[2,1024,8]{1,2,0:T(8,128)S(1)} collective-permute-done((f32[2,1024,8]{1,2,0:T(8,128)S(1)}, f32[2,1024,8]{1,2,0:T(8,128)S(1)}, u32[]{:S(2)}, u32[]{:S(2)}) %collective-permute-start.6) | collective-permute-done | bytes 65568 | tf_op jit(solution)/shard_map/while/body/eval_jaxpr/ppermute | solution.py:19
  136.1 4.9 %convolution_bitcast_fusion.4 = f32[2048,48]{0,1:T(8,128)S(1)} fusion(bf16[2048,1536]{1,0:T(8,128)(2,1)} %get-tuple-element.114, bf16[1536,16]{0,1:T(8,128)(2,1)S(1)} %get-tuple-element.95, bf16[1536,16]{0,1:T(8,128)(2,1)S(1)} %get-tuple-element.96, bf16[1536,16]{0,1:T(8,128)(2,1)S(1)} %get-tuple-element.97), kind=kOutput, calls=%fused_computation.1.clone.1 | convolution fusion | flops 302432256 | bytes 6832128 | tf_op jit(solution)/shard_map/while/body/eval_jaxpr/dot_general | solution.py:102
  145.8 2.3 collective-permute-done
  152.9 2.3 collective-permute-done.3
  157.1 5.1 %collective-permute-done.6 = f32[2,1024,8]{1,2,0:T(8,128)S(1)} collective-permute-done((f32[2,1024,8]{1,2,0:T(8,128)S(1)}, f32[2,1024,8]{1,2,0:T(8,128)S(1)}, u32[]{:S(2)}, u32[]{:S(2)}) %collective-permute-start.6) | collective-permute-done | bytes 65568 | tf_op jit(solution)/shard_map/while/body/eval_jaxpr/ppermute | solution.py:19
  165.9 4.9 %convolution_bitcast_fusion.4 = f32[2048,48]{0,1:T(8,128)S(1)} fusion(bf16[2048,1536]{1,0:T(8,128)(2,1)} %get-tuple-element.114, bf16[1536,16]{0,1:T(8,128)(2,1)S(1)} %get-tuple-element.95, bf16[1536,16]{0,1:T(8,128)(2,1)S(1)} %get-tuple-element.96, bf16[1536,16]{0,1:T(8,128)(2,1)S(1)} %get-tuple-element.97), kind=kOutput, calls=%fused_computation.1.clone.1 | convolution fusion | flops 302432256 | bytes 6832128 | tf_op jit(solution)/shard_map/while/body/eval_jaxpr/dot_general | solution.py:102
  172.0 2.3 collective-permute-start
  175.6 2.3 collective-permute-done
  179.8 2.4 collective-permute-start.3
  183.4 2.3 collective-permute-done.3
  185.6 2.0 collective-permute-done.4
  188.3 5.2 %collective-permute-done.6 = f32[2,1024,8]{1,2,0:T(8,128)S(1)} collective-permute-done((f32[2,1024,8]{1,2,0:T(8,128)S(1)}, f32[2,1024,8]{1,2,0:T(8,128)S(1)}, u32[]{:S(2)}, u32[]{:S(2)}) %collective-permute-start.6) | collective-permute-done | bytes 65568 | tf_op jit(solution)/shard_map/while/body/eval_jaxpr/ppermute | solution.py:19
  197.1 4.9 %convolution_bitcast_fusion.4 = f32[2048,48]{0,1:T(8,128)S(1)} fusion(bf16[2048,1536]{1,0:T(8,128)(2,1)} %get-tuple-element.114, bf16[1536,16]{0,1:T(8,128)(2,1)S(1)} %get-tuple-element.95, bf16[1536,16]{0,1:T(8,128)(2,1)S(1)} %get-tuple-element.96, bf16[1536,16]{0,1:T(8,128)(2,1)S(1)} %get-tuple-element.97), kind=kOutput, calls=%fused_computation.1.clone.1 | convolution fusion | flops 302432256 | bytes 6832128 | tf_op jit(solution)/shard_map/while/body/eval_jaxpr/dot_general | solution.py:102
  206.8 2.3 collective-permute-done
  214.0 2.3 collective-permute-done.3
  218.2 5.1 %collective-permute-done.6 = f32[2,1024,8]{1,2,0:T(8,128)S(1)} collective-permute-done((f32[2,1024,8]{1,2,0:T(8,128)S(1)}, f32[2,1024,8]{1,2,0:T(8,128)S(1)}, u32[]{:S(2)}, u32[]{:S(2)}) %collective-permute-start.6) | collective-permute-done | bytes 65568 | tf_op jit(solution)/shard_map/while/body/eval_jaxpr/ppermute | solution.py:19
  226.9 4.7 %fusion.21 = f32[2048,48]{0,1:T(8,128)S(1)} fusion(bf16[2048,1536]{1,0:T(8,128)(2,1)} %get-tuple-element.116, bf16[1536,16]{0,1:T(8,128)(2,1)S(1)} %get-tuple-element.60, bf16[1536,16]{0,1:T(8,128)(2,1)S(1)} %get-tuple-element.59, bf16[1536,16]{0,1:T(8,128)(2,1)S(1)} %get-tuple-element.58), kind=kOutput, calls=%fused_computation.60 | convolution fusion | flops 302432256 | bytes 6832128 | tf_op jit(solution)/shard_map/dot_general | solution.py:102
  232.6 2.7 %collective-permute-start.17 = (f32[16]{0:T(128)S(1)}, f32[16]{0:T(128)S(1)}, u32[]{:S(2)}, u32[]{:S(2)}) collective-permute-start(f32[16]{0:T(128)S(1)} %get-tuple-element.35), channel_id=1, source_target_pairs={{0,8},{4,12},{8,0},{12,4},{16,24},{20,28},{24,16},{28,20},{32,40},... | collective-permute-start | bytes 200 | tf_op jit(solution)/shard_map/ppermute | solution.py:19
  239.7 3.0 %multiply_reduce_fusion.1 = (f32[2048]{0:T(1024)S(1)}, f32[2048]{0:T(1024)S(1)}) fusion(bf16[2048,1536]{1,0:T(8,128)(2,1)S(1)} %bitcast.80, f32[2048,1024]{1,0:T(8,128)S(1)} %fusion.38, bf16[2048,48]{0,1:T(8,128)(2,1)S(1)} %constant_dynamic-update-slice_fusion, bf16[1024,48]{0,1:T(8,128)(2,1)S(1)} %get-tuple-element.49), kind=kOutput, calls=%fused_computation.56 | convolution fusion | flops 218099712 | bytes 17088512 | tf_op jit(solution)/shard_map/dot_general | solution.py:67
  243.6 2.7 %collective-permute-start.20 = (f32[16]{0:T(128)S(1)}, f32[16]{0:T(128)S(1)}, u32[]{:S(2)}, u32[]{:S(2)}) collective-permute-start(f32[16]{0:T(128)S(1)} %add_add_fusion.5), channel_id=1, source_target_pairs={{0,32},{4,36},{8,40},{12,44},{16,48},{20,52},{24,56},{28,60},{32,0... | collective-permute-start | bytes 200 | tf_op jit(solution)/shard_map/ppermute | solution.py:19
  248.7 2.4 collective-permute-done.21
  252.2 3.9 %collective-permute-done.22 = f32[16]{0:T(128)S(1)} collective-permute-done((f32[16]{0:T(128)S(1)}, f32[16]{0:T(128)S(1)}, u32[]{:S(2)}, u32[]{:S(2)}) %collective-permute-start.22) | collective-permute-done | bytes 96 | tf_op jit(solution)/shard_map/ppermute | solution.py:19
  (269 shorter events, 97.9 us)
Async XLA Ops:
  4.0 30.8 %collective-permute-start.7 = (bf16[2048,512]{1,0:T(8,128)(2,1)}, bf16[2048,512]{1,0:T(8,128)(2,1)}, u32[]{:S(2)}, u32[]{:S(2)}) collective-permute-start(bf16[2048,512]{1,0:T(8,128)(2,1)} %slice_select_fusion), channel_id=1, source_target_pairs={{0,3},{1,0},{2,1},{3,2},{4,7},{5,4},{6,5},{7,6},{8,11},{9,8},{10,9... | collective-permute-start | bytes 6291464 | tf_op jit(solution)/shard_map/ppermute | solution.py:85
  6.8 5.0 %collective-permute-start.10 = (f32[2,1536]{1,0:T(2,128)S(1)}, f32[2,1536]{1,0:T(2,128)S(1)}, u32[]{:S(2)}, u32[]{:S(2)}) collective-permute-start(f32[2,1536]{1,0:T(2,128)S(1)} %pad_maximum_fusion.3), channel_id=1, source_target_pairs={{0,12},{4,8},{8,4},{12,0},{16,28},{20,24},{24,20},{28,16},{32,44},... | collective-permute-start | bytes 36872 | tf_op jit(solution)/shard_map/ppermute | solution.py:19
  10.0 5.2 %collective-permute-start.9 = (f32[2,1536]{1,0:T(2,128)S(1)}, f32[2,1536]{1,0:T(2,128)S(1)}, u32[]{:S(2)}, u32[]{:S(2)}) collective-permute-start(f32[2,1536]{1,0:T(2,128)S(1)} %pad_maximum_fusion.3), channel_id=1, source_target_pairs={{0,8},{4,12},{8,0},{12,4},{16,24},{20,28},{24,16},{28,20},{32,40},... | collective-permute-start | bytes 36872 | tf_op jit(solution)/shard_map/ppermute | solution.py:19
  15.2 4.8 %collective-permute-start.11 = (f32[2,1536]{1,0:T(2,128)S(1)}, f32[2,1536]{1,0:T(2,128)S(1)}, u32[]{:S(2)}, u32[]{:S(2)}) collective-permute-start(f32[2,1536]{1,0:T(2,128)S(1)} %add_add_fusion.3), channel_id=1, source_target_pairs={{0,16},{4,20},{8,24},{12,28},{16,0},{20,4},{24,8},{28,12},{32,48},... | collective-permute-start | bytes 36872 | tf_op jit(solution)/shard_map/ppermute | solution.py:19
  16.8 5.2 %collective-permute-start.12 = (f32[2,1536]{1,0:T(2,128)S(1)}, f32[2,1536]{1,0:T(2,128)S(1)}, u32[]{:S(2)}, u32[]{:S(2)}) collective-permute-start(f32[2,1536]{1,0:T(2,128)S(1)} %add_add_fusion.3), channel_id=1, source_target_pairs={{0,32},{4,36},{8,40},{12,44},{16,48},{20,52},{24,56},{28,60},{32,0... | collective-permute-start | bytes 36872 | tf_op jit(solution)/shard_map/ppermute | solution.py:19
  19.5 4.9 %collective-permute-start.13 = (f32[2,1536]{1,0:T(2,128)S(1)}, f32[2,1536]{1,0:T(2,128)S(1)}, u32[]{:S(2)}, u32[]{:S(2)}) collective-permute-start(f32[2,1536]{1,0:T(2,128)S(1)} %add_add_fusion.3), channel_id=1, source_target_pairs={{0,48},{4,52},{8,56},{12,60},{16,32},{20,36},{24,40},{28,44},{32,1... | collective-permute-start | bytes 36872 | tf_op jit(solution)/shard_map/ppermute | solution.py:19
  24.5 7.0 %collective-permute-start.14 = (f32[2,1536]{1,0:T(2,128)S(1)}, f32[2,1536]{1,0:T(2,128)S(1)}, u32[]{:S(2)}, u32[]{:S(2)}) collective-permute-start(f32[2,1536]{1,0:T(2,128)S(1)} %add_add_fusion.2), channel_id=1, source_target_pairs={{0,64},{4,68},{8,72},{12,76},{16,80},{20,84},{24,88},{28,92},{32,9... | collective-permute-start | bytes 36872 | tf_op jit(solution)/shard_map/ppermute | solution.py:19
  48.2 5.8 %collective-permute-start = (f32[2,1024,8]{1,2,0:T(8,128)S(1)}, f32[2,1024,8]{1,2,0:T(8,128)S(1)}, u32[]{:S(2)}, u32[]{:S(2)}) collective-permute-start(f32[2,1024,8]{1,2,0:T(8,128)S(1)} %pad_maximum_fusion.6), channel_id=1, source_target_pairs={{0,8},{4,12},{8,0},{12,4},{16,24},{20,28},{24,16},{28,20},{32,40},... | collective-permute-start | bytes 196616 | tf_op jit(solution)/shard_map/while/body/eval_jaxpr/ppermute | solution.py:19
  51.5 5.5 %collective-permute-start.1 = (f32[2,1024,8]{1,2,0:T(8,128)S(1)}, f32[2,1024,8]{1,2,0:T(8,128)S(1)}, u32[]{:S(2)}, u32[]{:S(2)}) collective-permute-start(f32[2,1024,8]{1,2,0:T(8,128)S(1)} %pad_maximum_fusion.6), channel_id=1, source_target_pairs={{0,12},{4,8},{8,4},{12,0},{16,28},{20,24},{24,20},{28,16},{32,44},... | collective-permute-start | bytes 196616 | tf_op jit(solution)/shard_map/while/body/eval_jaxpr/ppermute | solution.py:19
  52.5 4.4 %collective-permute-start.2 = (f32[2,1024,8]{1,2,0:T(8,128)S(1)}, f32[2,1024,8]{1,2,0:T(8,128)S(1)}, u32[]{:S(2)}, u32[]{:S(2)}) collective-permute-start(f32[2,1024,8]{1,2,0:T(8,128)S(1)} %pad_maximum_fusion.6), channel_id=1, source_target_pairs={{0,4},{4,0},{8,12},{12,8},{16,20},{20,16},{24,28},{28,24},{32,36},... | collective-permute-start | bytes 196616 | tf_op jit(solution)/shard_map/while/body/eval_jaxpr/ppermute | solution.py:19
  57.0 5.9 %collective-permute-start.3 = (f32[2,1024,8]{1,2,0:T(8,128)S(1)}, f32[2,1024,8]{1,2,0:T(8,128)S(1)}, u32[]{:S(2)}, u32[]{:S(2)}) collective-permute-start(f32[2,1024,8]{1,2,0:T(8,128)S(1)} %add_add_fusion.8), channel_id=1, source_target_pairs={{0,32},{4,36},{8,40},{12,44},{16,48},{20,52},{24,56},{28,60},{32,0... | collective-permute-start | bytes 196616 | tf_op jit(solution)/shard_map/while/body/eval_jaxpr/ppermute | solution.py:19
  60.1 5.5 %collective-permute-start.4 = (f32[2,1024,8]{1,2,0:T(8,128)S(1)}, f32[2,1024,8]{1,2,0:T(8,128)S(1)}, u32[]{:S(2)}, u32[]{:S(2)}) collective-permute-start(f32[2,1024,8]{1,2,0:T(8,128)S(1)} %add_add_fusion.8), channel_id=1, source_target_pairs={{0,48},{4,52},{8,56},{12,60},{16,32},{20,36},{24,40},{28,44},{32,1... | collective-permute-start | bytes 196616 | tf_op jit(solution)/shard_map/while/body/eval_jaxpr/ppermute | solution.py:19
  61.2 4.3 %collective-permute-start.5 = (f32[2,1024,8]{1,2,0:T(8,128)S(1)}, f32[2,1024,8]{1,2,0:T(8,128)S(1)}, u32[]{:S(2)}, u32[]{:S(2)}) collective-permute-start(f32[2,1024,8]{1,2,0:T(8,128)S(1)} %add_add_fusion.8), channel_id=1, source_target_pairs={{0,16},{4,20},{8,24},{12,28},{16,0},{20,4},{24,8},{28,12},{32,48},... | collective-permute-start | bytes 196616 | tf_op jit(solution)/shard_map/while/body/eval_jaxpr/ppermute | solution.py:19
  65.6 5.8 %collective-permute-start.6 = (f32[2,1024,8]{1,2,0:T(8,128)S(1)}, f32[2,1024,8]{1,2,0:T(8,128)S(1)}, u32[]{:S(2)}, u32[]{:S(2)}) collective-permute-start(f32[2,1024,8]{1,2,0:T(8,128)S(1)} %add_add_fusion.9), channel_id=1, source_target_pairs={{0,64},{4,68},{8,72},{12,76},{16,80},{20,84},{24,88},{28,92},{32,9... | collective-permute-start | bytes 196616 | tf_op jit(solution)/shard_map/while/body/eval_jaxpr/ppermute | solution.py:19
  81.2 5.8 %collective-permute-start = (f32[2,1024,8]{1,2,0:T(8,128)S(1)}, f32[2,1024,8]{1,2,0:T(8,128)S(1)}, u32[]{:S(2)}, u32[]{:S(2)}) collective-permute-start(f32[2,1024,8]{1,2,0:T(8,128)S(1)} %pad_maximum_fusion.6), channel_id=1, source_target_pairs={{0,8},{4,12},{8,0},{12,4},{16,24},{20,28},{24,16},{28,20},{32,40},... | collective-permute-start | bytes 196616 | tf_op jit(solution)/shard_map/while/body/eval_jaxpr/ppermute | solution.py:19
  82.8 5.5 %collective-permute-start.1 = (f32[2,1024,8]{1,2,0:T(8,128)S(1)}, f32[2,1024,8]{1,2,0:T(8,128)S(1)}, u32[]{:S(2)}, u32[]{:S(2)}) collective-permute-start(f32[2,1024,8]{1,2,0:T(8,128)S(1)} %pad_maximum_fusion.6), channel_id=1, source_target_pairs={{0,12},{4,8},{8,4},{12,0},{16,28},{20,24},{24,20},{28,16},{32,44},... | collective-permute-start | bytes 196616 | tf_op jit(solution)/shard_map/while/body/eval_jaxpr/ppermute | solution.py:19
  83.9 4.3 %collective-permute-start.2 = (f32[2,1024,8]{1,2,0:T(8,128)S(1)}, f32[2,1024,8]{1,2,0:T(8,128)S(1)}, u32[]{:S(2)}, u32[]{:S(2)}) collective-permute-start(f32[2,1024,8]{1,2,0:T(8,128)S(1)} %pad_maximum_fusion.6), channel_id=1, source_target_pairs={{0,4},{4,0},{8,12},{12,8},{16,20},{20,16},{24,28},{28,24},{32,36},... | collective-permute-start | bytes 196616 | tf_op jit(solution)/shard_map/while/body/eval_jaxpr/ppermute | solution.py:19
  88.3 5.8 %collective-permute-start.3 = (f32[2,1024,8]{1,2,0:T(8,128)S(1)}, f32[2,1024,8]{1,2,0:T(8,128)S(1)}, u32[]{:S(2)}, u32[]{:S(2)}) collective-permute-start(f32[2,1024,8]{1,2,0:T(8,128)S(1)} %add_add_fusion.8), channel_id=1, source_target_pairs={{0,32},{4,36},{8,40},{12,44},{16,48},{20,52},{24,56},{28,60},{32,0... | collective-permute-start | bytes 196616 | tf_op jit(solution)/shard_map/while/body/eval_jaxpr/ppermute | solution.py:19
  89.8 5.5 %collective-permute-start.4 = (f32[2,1024,8]{1,2,0:T(8,128)S(1)}, f32[2,1024,8]{1,2,0:T(8,128)S(1)}, u32[]{:S(2)}, u32[]{:S(2)}) collective-permute-start(f32[2,1024,8]{1,2,0:T(8,128)S(1)} %add_add_fusion.8), channel_id=1, source_target_pairs={{0,48},{4,52},{8,56},{12,60},{16,32},{20,36},{24,40},{28,44},{32,1... | collective-permute-start | bytes 196616 | tf_op jit(solution)/shard_map/while/body/eval_jaxpr/ppermute | solution.py:19
  91.0 4.3 %collective-permute-start.5 = (f32[2,1024,8]{1,2,0:T(8,128)S(1)}, f32[2,1024,8]{1,2,0:T(8,128)S(1)}, u32[]{:S(2)}, u32[]{:S(2)}) collective-permute-start(f32[2,1024,8]{1,2,0:T(8,128)S(1)} %add_add_fusion.8), channel_id=1, source_target_pairs={{0,16},{4,20},{8,24},{12,28},{16,0},{20,4},{24,8},{28,12},{32,48},... | collective-permute-start | bytes 196616 | tf_op jit(solution)/shard_map/while/body/eval_jaxpr/ppermute | solution.py:19
  95.3 5.8 %collective-permute-start.6 = (f32[2,1024,8]{1,2,0:T(8,128)S(1)}, f32[2,1024,8]{1,2,0:T(8,128)S(1)}, u32[]{:S(2)}, u32[]{:S(2)}) collective-permute-start(f32[2,1024,8]{1,2,0:T(8,128)S(1)} %add_add_fusion.9), channel_id=1, source_target_pairs={{0,64},{4,68},{8,72},{12,76},{16,80},{20,84},{24,88},{28,92},{32,9... | collective-permute-start | bytes 196616 | tf_op jit(solution)/shard_map/while/body/eval_jaxpr/ppermute | solution.py:19
  111.0 5.8 %collective-permute-start = (f32[2,1024,8]{1,2,0:T(8,128)S(1)}, f32[2,1024,8]{1,2,0:T(8,128)S(1)}, u32[]{:S(2)}, u32[]{:S(2)}) collective-permute-start(f32[2,1024,8]{1,2,0:T(8,128)S(1)} %pad_maximum_fusion.6), channel_id=1, source_target_pairs={{0,8},{4,12},{8,0},{12,4},{16,24},{20,28},{24,16},{28,20},{32,40},... | collective-permute-start | bytes 196616 | tf_op jit(solution)/shard_map/while/body/eval_jaxpr/ppermute | solution.py:19
  113.2 5.5 %collective-permute-start.1 = (f32[2,1024,8]{1,2,0:T(8,128)S(1)}, f32[2,1024,8]{1,2,0:T(8,128)S(1)}, u32[]{:S(2)}, u32[]{:S(2)}) collective-permute-start(f32[2,1024,8]{1,2,0:T(8,128)S(1)} %pad_maximum_fusion.6), channel_id=1, source_target_pairs={{0,12},{4,8},{8,4},{12,0},{16,28},{20,24},{24,20},{28,16},{32,44},... | collective-permute-start | bytes 196616 | tf_op jit(solution)/shard_map/while/body/eval_jaxpr/ppermute | solution.py:19
  118.7 5.8 %collective-permute-start.3 = (f32[2,1024,8]{1,2,0:T(8,128)S(1)}, f32[2,1024,8]{1,2,0:T(8,128)S(1)}, u32[]{:S(2)}, u32[]{:S(2)}) collective-permute-start(f32[2,1024,8]{1,2,0:T(8,128)S(1)} %add_add_fusion.8), channel_id=1, source_target_pairs={{0,32},{4,36},{8,40},{12,44},{16,48},{20,52},{24,56},{28,60},{32,0... | collective-permute-start | bytes 196616 | tf_op jit(solution)/shard_map/while/body/eval_jaxpr/ppermute | solution.py:19
  121.1 5.5 %collective-permute-start.4 = (f32[2,1024,8]{1,2,0:T(8,128)S(1)}, f32[2,1024,8]{1,2,0:T(8,128)S(1)}, u32[]{:S(2)}, u32[]{:S(2)}) collective-permute-start(f32[2,1024,8]{1,2,0:T(8,128)S(1)} %add_add_fusion.8), channel_id=1, source_target_pairs={{0,48},{4,52},{8,56},{12,60},{16,32},{20,36},{24,40},{28,44},{32,1... | collective-permute-start | bytes 196616 | tf_op jit(solution)/shard_map/while/body/eval_jaxpr/ppermute | solution.py:19
  126.6 5.8 %collective-permute-start.6 = (f32[2,1024,8]{1,2,0:T(8,128)S(1)}, f32[2,1024,8]{1,2,0:T(8,128)S(1)}, u32[]{:S(2)}, u32[]{:S(2)}) collective-permute-start(f32[2,1024,8]{1,2,0:T(8,128)S(1)} %add_add_fusion.9), channel_id=1, source_target_pairs={{0,64},{4,68},{8,72},{12,76},{16,80},{20,84},{24,88},{28,92},{32,9... | collective-permute-start | bytes 196616 | tf_op jit(solution)/shard_map/while/body/eval_jaxpr/ppermute | solution.py:19
  142.2 5.8 %collective-permute-start = (f32[2,1024,8]{1,2,0:T(8,128)S(1)}, f32[2,1024,8]{1,2,0:T(8,128)S(1)}, u32[]{:S(2)}, u32[]{:S(2)}) collective-permute-start(f32[2,1024,8]{1,2,0:T(8,128)S(1)} %pad_maximum_fusion.6), channel_id=1, source_target_pairs={{0,8},{4,12},{8,0},{12,4},{16,24},{20,28},{24,16},{28,20},{32,40},... | collective-permute-start | bytes 196616 | tf_op jit(solution)/shard_map/while/body/eval_jaxpr/ppermute | solution.py:19
  143.8 5.5 %collective-permute-start.1 = (f32[2,1024,8]{1,2,0:T(8,128)S(1)}, f32[2,1024,8]{1,2,0:T(8,128)S(1)}, u32[]{:S(2)}, u32[]{:S(2)}) collective-permute-start(f32[2,1024,8]{1,2,0:T(8,128)S(1)} %pad_maximum_fusion.6), channel_id=1, source_target_pairs={{0,12},{4,8},{8,4},{12,0},{16,28},{20,24},{24,20},{28,16},{32,44},... | collective-permute-start | bytes 196616 | tf_op jit(solution)/shard_map/while/body/eval_jaxpr/ppermute | solution.py:19
  149.3 5.8 %collective-permute-start.3 = (f32[2,1024,8]{1,2,0:T(8,128)S(1)}, f32[2,1024,8]{1,2,0:T(8,128)S(1)}, u32[]{:S(2)}, u32[]{:S(2)}) collective-permute-start(f32[2,1024,8]{1,2,0:T(8,128)S(1)} %add_add_fusion.8), channel_id=1, source_target_pairs={{0,32},{4,36},{8,40},{12,44},{16,48},{20,52},{24,56},{28,60},{32,0... | collective-permute-start | bytes 196616 | tf_op jit(solution)/shard_map/while/body/eval_jaxpr/ppermute | solution.py:19
  150.9 5.5 %collective-permute-start.4 = (f32[2,1024,8]{1,2,0:T(8,128)S(1)}, f32[2,1024,8]{1,2,0:T(8,128)S(1)}, u32[]{:S(2)}, u32[]{:S(2)}) collective-permute-start(f32[2,1024,8]{1,2,0:T(8,128)S(1)} %add_add_fusion.8), channel_id=1, source_target_pairs={{0,48},{4,52},{8,56},{12,60},{16,32},{20,36},{24,40},{28,44},{32,1... | collective-permute-start | bytes 196616 | tf_op jit(solution)/shard_map/while/body/eval_jaxpr/ppermute | solution.py:19
  156.4 5.8 %collective-permute-start.6 = (f32[2,1024,8]{1,2,0:T(8,128)S(1)}, f32[2,1024,8]{1,2,0:T(8,128)S(1)}, u32[]{:S(2)}, u32[]{:S(2)}) collective-permute-start(f32[2,1024,8]{1,2,0:T(8,128)S(1)} %add_add_fusion.9), channel_id=1, source_target_pairs={{0,64},{4,68},{8,72},{12,76},{16,80},{20,84},{24,88},{28,92},{32,9... | collective-permute-start | bytes 196616 | tf_op jit(solution)/shard_map/while/body/eval_jaxpr/ppermute | solution.py:19
  172.0 5.8 %collective-permute-start = (f32[2,1024,8]{1,2,0:T(8,128)S(1)}, f32[2,1024,8]{1,2,0:T(8,128)S(1)}, u32[]{:S(2)}, u32[]{:S(2)}) collective-permute-start(f32[2,1024,8]{1,2,0:T(8,128)S(1)} %pad_maximum_fusion.6), channel_id=1, source_target_pairs={{0,8},{4,12},{8,0},{12,4},{16,24},{20,28},{24,16},{28,20},{32,40},... | collective-permute-start | bytes 196616 | tf_op jit(solution)/shard_map/while/body/eval_jaxpr/ppermute | solution.py:19
  174.3 5.5 %collective-permute-start.1 = (f32[2,1024,8]{1,2,0:T(8,128)S(1)}, f32[2,1024,8]{1,2,0:T(8,128)S(1)}, u32[]{:S(2)}, u32[]{:S(2)}) collective-permute-start(f32[2,1024,8]{1,2,0:T(8,128)S(1)} %pad_maximum_fusion.6), channel_id=1, source_target_pairs={{0,12},{4,8},{8,4},{12,0},{16,28},{20,24},{24,20},{28,16},{32,44},... | collective-permute-start | bytes 196616 | tf_op jit(solution)/shard_map/while/body/eval_jaxpr/ppermute | solution.py:19
  179.8 5.8 %collective-permute-start.3 = (f32[2,1024,8]{1,2,0:T(8,128)S(1)}, f32[2,1024,8]{1,2,0:T(8,128)S(1)}, u32[]{:S(2)}, u32[]{:S(2)}) collective-permute-start(f32[2,1024,8]{1,2,0:T(8,128)S(1)} %add_add_fusion.8), channel_id=1, source_target_pairs={{0,32},{4,36},{8,40},{12,44},{16,48},{20,52},{24,56},{28,60},{32,0... | collective-permute-start | bytes 196616 | tf_op jit(solution)/shard_map/while/body/eval_jaxpr/ppermute | solution.py:19
  182.1 5.5 %collective-permute-start.4 = (f32[2,1024,8]{1,2,0:T(8,128)S(1)}, f32[2,1024,8]{1,2,0:T(8,128)S(1)}, u32[]{:S(2)}, u32[]{:S(2)}) collective-permute-start(f32[2,1024,8]{1,2,0:T(8,128)S(1)} %add_add_fusion.8), channel_id=1, source_target_pairs={{0,48},{4,52},{8,56},{12,60},{16,32},{20,36},{24,40},{28,44},{32,1... | collective-permute-start | bytes 196616 | tf_op jit(solution)/shard_map/while/body/eval_jaxpr/ppermute | solution.py:19
  187.6 5.8 %collective-permute-start.6 = (f32[2,1024,8]{1,2,0:T(8,128)S(1)}, f32[2,1024,8]{1,2,0:T(8,128)S(1)}, u32[]{:S(2)}, u32[]{:S(2)}) collective-permute-start(f32[2,1024,8]{1,2,0:T(8,128)S(1)} %add_add_fusion.9), channel_id=1, source_target_pairs={{0,64},{4,68},{8,72},{12,76},{16,80},{20,84},{24,88},{28,92},{32,9... | collective-permute-start | bytes 196616 | tf_op jit(solution)/shard_map/while/body/eval_jaxpr/ppermute | solution.py:19
  203.3 5.8 %collective-permute-start = (f32[2,1024,8]{1,2,0:T(8,128)S(1)}, f32[2,1024,8]{1,2,0:T(8,128)S(1)}, u32[]{:S(2)}, u32[]{:S(2)}) collective-permute-start(f32[2,1024,8]{1,2,0:T(8,128)S(1)} %pad_maximum_fusion.6), channel_id=1, source_target_pairs={{0,8},{4,12},{8,0},{12,4},{16,24},{20,28},{24,16},{28,20},{32,40},... | collective-permute-start | bytes 196616 | tf_op jit(solution)/shard_map/while/body/eval_jaxpr/ppermute | solution.py:19
  204.9 5.5 %collective-permute-start.1 = (f32[2,1024,8]{1,2,0:T(8,128)S(1)}, f32[2,1024,8]{1,2,0:T(8,128)S(1)}, u32[]{:S(2)}, u32[]{:S(2)}) collective-permute-start(f32[2,1024,8]{1,2,0:T(8,128)S(1)} %pad_maximum_fusion.6), channel_id=1, source_target_pairs={{0,12},{4,8},{8,4},{12,0},{16,28},{20,24},{24,20},{28,16},{32,44},... | collective-permute-start | bytes 196616 | tf_op jit(solution)/shard_map/while/body/eval_jaxpr/ppermute | solution.py:19
  210.4 5.8 %collective-permute-start.3 = (f32[2,1024,8]{1,2,0:T(8,128)S(1)}, f32[2,1024,8]{1,2,0:T(8,128)S(1)}, u32[]{:S(2)}, u32[]{:S(2)}) collective-permute-start(f32[2,1024,8]{1,2,0:T(8,128)S(1)} %add_add_fusion.8), channel_id=1, source_target_pairs={{0,32},{4,36},{8,40},{12,44},{16,48},{20,52},{24,56},{28,60},{32,0... | collective-permute-start | bytes 196616 | tf_op jit(solution)/shard_map/while/body/eval_jaxpr/ppermute | solution.py:19
  211.9 5.5 %collective-permute-start.4 = (f32[2,1024,8]{1,2,0:T(8,128)S(1)}, f32[2,1024,8]{1,2,0:T(8,128)S(1)}, u32[]{:S(2)}, u32[]{:S(2)}) collective-permute-start(f32[2,1024,8]{1,2,0:T(8,128)S(1)} %add_add_fusion.8), channel_id=1, source_target_pairs={{0,48},{4,52},{8,56},{12,60},{16,32},{20,36},{24,40},{28,44},{32,1... | collective-permute-start | bytes 196616 | tf_op jit(solution)/shard_map/while/body/eval_jaxpr/ppermute | solution.py:19
  217.4 5.8 %collective-permute-start.6 = (f32[2,1024,8]{1,2,0:T(8,128)S(1)}, f32[2,1024,8]{1,2,0:T(8,128)S(1)}, u32[]{:S(2)}, u32[]{:S(2)}) collective-permute-start(f32[2,1024,8]{1,2,0:T(8,128)S(1)} %add_add_fusion.9), channel_id=1, source_target_pairs={{0,64},{4,68},{8,72},{12,76},{16,80},{20,84},{24,88},{28,92},{32,9... | collective-permute-start | bytes 196616 | tf_op jit(solution)/shard_map/while/body/eval_jaxpr/ppermute | solution.py:19
  231.8 10.9 %collective-permute-start.16 = (f32[16]{0:T(128)S(1)}, f32[16]{0:T(128)S(1)}, u32[]{:S(2)}, u32[]{:S(2)}) collective-permute-start(f32[16]{0:T(128)S(1)} %get-tuple-element.35), channel_id=1, source_target_pairs={{0,4},{4,0},{8,12},{12,8},{16,20},{20,16},{24,28},{28,24},{32,36},... | collective-permute-start | bytes 200 | tf_op jit(solution)/shard_map/ppermute | solution.py:19
  232.6 10.1 %collective-permute-start.17 = (f32[16]{0:T(128)S(1)}, f32[16]{0:T(128)S(1)}, u32[]{:S(2)}, u32[]{:S(2)}) collective-permute-start(f32[16]{0:T(128)S(1)} %get-tuple-element.35), channel_id=1, source_target_pairs={{0,8},{4,12},{8,0},{12,4},{16,24},{20,28},{24,16},{28,20},{32,40},... | collective-permute-start | bytes 200 | tf_op jit(solution)/shard_map/ppermute | solution.py:19
  235.3 7.3 %collective-permute-start.18 = (f32[16]{0:T(128)S(1)}, f32[16]{0:T(128)S(1)}, u32[]{:S(2)}, u32[]{:S(2)}) collective-permute-start(f32[16]{0:T(128)S(1)} %get-tuple-element.35), channel_id=1, source_target_pairs={{0,12},{4,8},{8,4},{12,0},{16,28},{20,24},{24,20},{28,16},{32,44},... | collective-permute-start | bytes 200 | tf_op jit(solution)/shard_map/ppermute | solution.py:19
  242.7 4.8 %collective-permute-start.19 = (f32[16]{0:T(128)S(1)}, f32[16]{0:T(128)S(1)}, u32[]{:S(2)}, u32[]{:S(2)}) collective-permute-start(f32[16]{0:T(128)S(1)} %add_add_fusion.5), channel_id=1, source_target_pairs={{0,16},{4,20},{8,24},{12,28},{16,0},{20,4},{24,8},{28,12},{32,48},... | collective-permute-start | bytes 200 | tf_op jit(solution)/shard_map/ppermute | solution.py:19
  243.6 5.1 %collective-permute-start.20 = (f32[16]{0:T(128)S(1)}, f32[16]{0:T(128)S(1)}, u32[]{:S(2)}, u32[]{:S(2)}) collective-permute-start(f32[16]{0:T(128)S(1)} %add_add_fusion.5), channel_id=1, source_target_pairs={{0,32},{4,36},{8,40},{12,44},{16,48},{20,52},{24,56},{28,60},{32,0... | collective-permute-start | bytes 200 | tf_op jit(solution)/shard_map/ppermute | solution.py:19
  246.2 4.8 %collective-permute-start.21 = (f32[16]{0:T(128)S(1)}, f32[16]{0:T(128)S(1)}, u32[]{:S(2)}, u32[]{:S(2)}) collective-permute-start(f32[16]{0:T(128)S(1)} %add_add_fusion.5), channel_id=1, source_target_pairs={{0,48},{4,52},{8,56},{12,60},{16,32},{20,36},{24,40},{28,44},{32,1... | collective-permute-start | bytes 200 | tf_op jit(solution)/shard_map/ppermute | solution.py:19
  251.0 5.1 %collective-permute-start.22 = (f32[16]{0:T(128)S(1)}, f32[16]{0:T(128)S(1)}, u32[]{:S(2)}, u32[]{:S(2)}) collective-permute-start(f32[16]{0:T(128)S(1)} %add_add_fusion.4), channel_id=1, source_target_pairs={{0,64},{4,68},{8,72},{12,76},{16,80},{20,84},{24,88},{28,92},{32,9... | collective-permute-start | bytes 200 | tf_op jit(solution)/shard_map/ppermute | solution.py:19
  (22 other events, 102.1 us)

commit v11 on v9

--- a/solution.py
+++ b/solution.py
@@ -108,7 +108,7 @@
         parts = jnp.stack([back[:columns, :comps], back[half_cols:, comps:]], 0)
         return summed(parts, "ind") / total
 
-    basis = lax.fori_loop(0, ITERS, lambda step, basis: orthonormal(image_of(basis)), start)
+    basis = lax.fori_loop(0, ITERS, lambda step, basis: orthonormal(image_of(basis)), start, unroll=2)
     proj = project(basis)
     variances = summed(jnp.sum(proj * proj, axis=0), "ind").reshape(2, comps) / total
     first = stand[:, :columns].astype(jnp.float32) - product(proj[:, :comps], basis[0])

time: 259 us -> 267 us (1.031)
  matrix products: 48 us -> 55.9 us
    dot_general x6, matrix products: 6.76 us -> 15.1 us  [image_of(): lax.dot_general(stand, split, (((0,), (0,)), ((), ())), preferred_element...]
    another operation x24 -> x21, other arithmetic: 9.76 us -> 9.74 us  [orthonormal(): factor = jnp.linalg.cholesky(gram)]
    another operation x18 -> x15, other arithmetic: 8.03 us -> 8.01 us  [orthonormal(): jax.scipy.linalg.solve_triangular(fac, rhs, lower=True)]
  transfers between devices with their start and end apart: 58 -> 58, of which waited for: 40 -> 39; matrix products, arithmetic and copies ran while one was open for 4% -> 4% of each run, Pallas kernels for 0% -> 0%
where the time goes in v11:
time: 267 us
  waiting for transfers between devices  94.6 us (35%)
  starting transfers between devices  77 us (29%)
  matrix products  55.9 us (21%)
  other arithmetic  31.2 us (12%)
  local copies, waits for them, and re-layouts  6.37 us (2%)
    ppermute x56, waiting for transfers between devices, swapped(): return lax.ppermute(value, axis, [(i, i ^ mask) for i in range(size)])  94.3 us
    ppermute x56, starting transfers between devices, swapped(): return lax.ppermute(value, axis, [(i, i ^ mask) for i in range(size)])  73 us
    dot_general x7, matrix products, project(): jnp.dot(stand, jnp.concatenate(pieces(wide), 1), preferred_element_type=j...  33.5 us
    dot_general x6, matrix products, image_of(): lax.dot_general(stand, split, (((0,), (0,)), ((), ())), preferred_element...  15.1 us
    another operation x21, other arithmetic, orthonormal(): factor = jnp.linalg.cholesky(gram)  9.74 us
    another operation x15, other arithmetic, orthonormal(): jax.scipy.linalg.solve_triangular(fac, rhs, lower=True)  8.01 us
  transfers between devices with their start and end apart: 58, of which 39 were waited for; matrix products, arithmetic and copies ran while one was open for 4% of the time, Pallas kernels for 0%

profile of v11, /device:TPU:32, one launch (start us, length us, event | category | flops | bytes accessed | tf_op | source)
XLA Modules:
  0.0 266.8 jit_solution(18419295036300034898)
XLA Ops:
  0.7 3.2 %slice.115 = bf16[2048,512]{1,0:T(8,128)(2,1)} slice(bf16[2048,1024]{1,0:T(8,128)(2,1)} %param.9), slice={[0:2048], [0:512]} | slice | bytes 4194304 | tf_op jit(solution)/shard_map/slice | solution.py:84
  5.8 3.5 %convert_reduce_fusion = (f32[1536]{0:T(1024)S(1)}, f32[1536]{0:T(1024)S(1)}) fusion(bf16[2048,512]{1,0:T(8,128)(2,1)} %param.10, bf16[2048,1024]{1,0:T(8,128)(2,1)S(1)} %copy-done.1), kind=kLoop, calls=%fused_computation.101 | loop fusion | flops 22017024 | bytes 6303744 | tf_op jit(solution)/shard_map/reduce_sum | solution.py:89
  11.0 2.9 %collective-permute-start.16 = (f32[2,1536]{1,0:T(2,128)S(1)}, f32[2,1536]{1,0:T(2,128)S(1)}, u32[]{:S(2)}, u32[]{:S(2)}) collective-permute-start(f32[2,1536]{1,0:T(2,128)S(1)} %pad_maximum_fusion.4), channel_id=1, source_target_pairs={{0,8},{4,12},{8,0},{12,4},{16,24},{20,28},{24,16},{28,20},{32,40},... | collective-permute-start | bytes 36872 | tf_op jit(solution)/shard_map/ppermute | solution.py:19
  16.2 2.6 collective-permute-done.17
  20.4 2.7 %collective-permute-start.19 = (f32[2,1536]{1,0:T(2,128)S(1)}, f32[2,1536]{1,0:T(2,128)S(1)}, u32[]{:S(2)}, u32[]{:S(2)}) collective-permute-start(f32[2,1536]{1,0:T(2,128)S(1)} %add_add_fusion.5), channel_id=1, source_target_pairs={{0,32},{4,36},{8,40},{12,44},{16,48},{20,52},{24,56},{28,60},{32,0... | collective-permute-start | bytes 36872 | tf_op jit(solution)/shard_map/ppermute | solution.py:19
  25.6 2.4 collective-permute-done.20
  28.1 3.1 %collective-permute-start.21 = (f32[2,1536]{1,0:T(2,128)S(1)}, f32[2,1536]{1,0:T(2,128)S(1)}, u32[]{:S(2)}, u32[]{:S(2)}) collective-permute-start(f32[2,1536]{1,0:T(2,128)S(1)} %add_add_fusion.4), channel_id=1, source_target_pairs={{0,64},{4,68},{8,72},{12,76},{16,80},{20,84},{24,88},{28,92},{32,9... | collective-permute-start | bytes 36872 | tf_op jit(solution)/shard_map/ppermute | solution.py:19
  39.1 5.2 %multiply_convert_fusion = bf16[2048,1536]{1,0:T(8,128)(2,1)} fusion(bf16[2048,1024]{1,0:T(8,128)(2,1)S(1)} %copy-done.2, bf16[2048,512]{1,0:T(8,128)(2,1)S(1)} %broadcast_select_fusion, f32[1536]{0:T(1024)S(1)} %multiply_sqrt_fusion, f32[1536]{0:T(1024)S(1)} %get-tuple-element.28, f32[1536]{0:T(1024)S(1)} %get-tuple-element.27), kind=kLoop, calls=%fused_computation.103 | loop fusion | flops 25165824 | bytes 12601344 | tf_op jit(solution)/shard_map/convert_element_type | solution.py:97
  44.3 192.6 %while.10 = (s32[]{:T(128)}, f32[2,1024,8]{1,2,0:T(8,128)S(1)}, bf16[2048,1536]{1,0:T(8,128)(2,1)}, s32[]{:T(128)}) while((s32[]{:T(128)}, f32[2,1024,8]{1,2,0:T(8,128)S(1)}, bf16[2048,1536]{1,0:T(8,128)(2,1)}, s32[]{:T(128)}) %tuple.72), condition=%wide.region_5.8_spmd, body=%wide.region_2.0_spmd.sunk | while | flops 1218054016 | bytes 61746432 | solution.py:111
  44.3 4.9 %convolution_bitcast_fusion.12 = f32[2048,48]{0,1:T(8,128)S(1)} fusion(bf16[2048,1536]{1,0:T(8,128)(2,1)} %get-tuple-element.149, bf16[1536,16]{0,1:T(8,128)(2,1)S(1)} %get-tuple-element.119, bf16[1536,16]{0,1:T(8,128)(2,1)S(1)} %get-tuple-element.120, bf16[1536,16]{0,1:T(8,128)(2,1)S(1)} %get-tuple-element.121), kind=kOutput, calls=%fused_computation.3.clone.1 | convolution fusion | flops 302432256 | bytes 6832128 | tf_op jit(solution)/shard_map/while/body/eval_jaxpr/dot_general | solution.py:102
  50.5 3.2 %collective-permute-start = (f32[2,1024,8]{1,2,0:T(8,128)S(1)}, f32[2,1024,8]{1,2,0:T(8,128)S(1)}, u32[]{:S(2)}, u32[]{:S(2)}) collective-permute-start(f32[2,1024,8]{1,2,0:T(8,128)S(1)} %pad_maximum_fusion.8), channel_id=1, source_target_pairs={{0,8},{4,12},{8,0},{12,4},{16,24},{20,28},{24,16},{28,20},{32,40},... | collective-permute-start | bytes 196616 | tf_op jit(solution)/shard_map/while/body/eval_jaxpr/ppermute | solution.py:19
  56.3 2.8 %collective-permute-done.1 = f32[2,1024,8]{1,2,0:T(8,128)S(1)} collective-permute-done((f32[2,1024,8]{1,2,0:T(8,128)S(1)}, f32[2,1024,8]{1,2,0:T(8,128)S(1)}, u32[]{:S(2)}, u32[]{:S(2)}) %collective-permute-start.1) | collective-permute-done | bytes 65568 | tf_op jit(solution)/shard_map/while/body/eval_jaxpr/ppermute | solution.py:19
  59.1 3.1 %collective-permute-start.3 = (f32[2,1024,8]{1,2,0:T(8,128)S(1)}, f32[2,1024,8]{1,2,0:T(8,128)S(1)}, u32[]{:S(2)}, u32[]{:S(2)}) collective-permute-start(f32[2,1024,8]{1,2,0:T(8,128)S(1)} %add_add_fusion.12), channel_id=1, source_target_pairs={{0,32},{4,36},{8,40},{12,44},{16,48},{20,52},{24,56},{28,60},{32,0... | collective-permute-start | bytes 196616 | tf_op jit(solution)/shard_map/while/body/eval_jaxpr/ppermute | solution.py:19
  65.1 2.6 collective-permute-done.4
  68.4 5.2 %collective-permute-done.6 = f32[2,1024,8]{1,2,0:T(8,128)S(1)} collective-permute-done((f32[2,1024,8]{1,2,0:T(8,128)S(1)}, f32[2,1024,8]{1,2,0:T(8,128)S(1)}, u32[]{:S(2)}, u32[]{:S(2)}) %collective-permute-start.6) | collective-permute-done | bytes 65568 | tf_op jit(solution)/shard_map/while/body/eval_jaxpr/ppermute | solution.py:19
  77.2 4.7 %convolution_bitcast_fusion.15 = f32[2048,48]{0,1:T(8,128)S(1)} fusion(bf16[2048,1536]{1,0:T(8,128)(2,1)} %get-tuple-element.149, bf16[1536,16]{0,1:T(8,128)(2,1)S(1)} %get-tuple-element.130, bf16[1536,16]{0,1:T(8,128)(2,1)S(1)} %get-tuple-element.131, bf16[1536,16]{0,1:T(8,128)(2,1)S(1)} %get-tuple-element.132), kind=kOutput, calls=%fused_computation.1.clone.1 | convolution fusion | flops 302432256 | bytes 6832128 | tf_op jit(solution)/shard_map/while/body/eval_jaxpr/dot_general | solution.py:102
  82.0 3.9 %convolution_bitcast_fusion.16 = f32[1536,48]{0,1:T(8,128)S(1)} fusion(bf16[2048,1536]{1,0:T(8,128)(2,1)} %get-tuple-element.149, bf16[2048,16]{0,1:T(8,128)(2,1)S(1)} %get-tuple-element.134, bf16[2048,16]{0,1:T(8,128)(2,1)S(1)} %get-tuple-element.135, bf16[2048,16]{0,1:T(8,128)(2,1)S(1)} %get-tuple-element.136), kind=kOutput, calls=%fused_computation.clone.1 | convolution fusion | flops 302579712 | bytes 6782976 | tf_op jit(solution)/shard_map/while/body/eval_jaxpr/dot_general | solution.py:107
  89.5 2.3 collective-permute-done.7
  96.7 2.3 collective-permute-done.10
  101.6 4.4 %collective-permute-done.13 = f32[2,1024,8]{1,2,0:T(8,128)S(1)} collective-permute-done((f32[2,1024,8]{1,2,0:T(8,128)S(1)}, f32[2,1024,8]{1,2,0:T(8,128)S(1)}, u32[]{:S(2)}, u32[]{:S(2)}) %collective-permute-start.13) | collective-permute-done | bytes 65568 | tf_op jit(solution)/shard_map/while/body/eval_jaxpr/ppermute | solution.py:19
  109.6 4.9 %convolution_bitcast_fusion.12 = f32[2048,48]{0,1:T(8,128)S(1)} fusion(bf16[2048,1536]{1,0:T(8,128)(2,1)} %get-tuple-element.149, bf16[1536,16]{0,1:T(8,128)(2,1)S(1)} %get-tuple-element.119, bf16[1536,16]{0,1:T(8,128)(2,1)S(1)} %get-tuple-element.120, bf16[1536,16]{0,1:T(8,128)(2,1)S(1)} %get-tuple-element.121), kind=kOutput, calls=%fused_computation.3.clone.1 | convolution fusion | flops 302432256 | bytes 6832128 | tf_op jit(solution)/shard_map/while/body/eval_jaxpr/dot_general | solution.py:102
  115.8 2.3 collective-permute-start
  119.3 2.3 collective-permute-done
  123.5 2.3 collective-permute-start.3
  127.1 2.3 collective-permute-done.3
  132.0 5.2 %collective-permute-done.6 = f32[2,1024,8]{1,2,0:T(8,128)S(1)} collective-permute-done((f32[2,1024,8]{1,2,0:T(8,128)S(1)}, f32[2,1024,8]{1,2,0:T(8,128)S(1)}, u32[]{:S(2)}, u32[]{:S(2)}) %collective-permute-start.6) | collective-permute-done | bytes 65568 | tf_op jit(solution)/shard_map/while/body/eval_jaxpr/ppermute | solution.py:19
  140.9 4.7 %convolution_bitcast_fusion.15 = f32[2048,48]{0,1:T(8,128)S(1)} fusion(bf16[2048,1536]{1,0:T(8,128)(2,1)} %get-tuple-element.149, bf16[1536,16]{0,1:T(8,128)(2,1)S(1)} %get-tuple-element.130, bf16[1536,16]{0,1:T(8,128)(2,1)S(1)} %get-tuple-element.131, bf16[1536,16]{0,1:T(8,128)(2,1)S(1)} %get-tuple-element.132), kind=kOutput, calls=%fused_computation.1.clone.1 | convolution fusion | flops 302432256 | bytes 6832128 | tf_op jit(solution)/shard_map/while/body/eval_jaxpr/dot_general | solution.py:102
  145.6 3.9 %convolution_bitcast_fusion.16 = f32[1536,48]{0,1:T(8,128)S(1)} fusion(bf16[2048,1536]{1,0:T(8,128)(2,1)} %get-tuple-element.149, bf16[2048,16]{0,1:T(8,128)(2,1)S(1)} %get-tuple-element.134, bf16[2048,16]{0,1:T(8,128)(2,1)S(1)} %get-tuple-element.135, bf16[2048,16]{0,1:T(8,128)(2,1)S(1)} %get-tuple-element.136), kind=kOutput, calls=%fused_computation.clone.1 | convolution fusion | flops 302579712 | bytes 6782976 | tf_op jit(solution)/shard_map/while/body/eval_jaxpr/dot_general | solution.py:107
  153.2 2.3 collective-permute-done.7
  160.3 2.3 collective-permute-done.10
  165.2 4.4 %collective-permute-done.13 = f32[2,1024,8]{1,2,0:T(8,128)S(1)} collective-permute-done((f32[2,1024,8]{1,2,0:T(8,128)S(1)}, f32[2,1024,8]{1,2,0:T(8,128)S(1)}, u32[]{:S(2)}, u32[]{:S(2)}) %collective-permute-start.13) | collective-permute-done | bytes 65568 | tf_op jit(solution)/shard_map/while/body/eval_jaxpr/ppermute | solution.py:19
  173.3 4.9 %convolution_bitcast_fusion.12 = f32[2048,48]{0,1:T(8,128)S(1)} fusion(bf16[2048,1536]{1,0:T(8,128)(2,1)} %get-tuple-element.149, bf16[1536,16]{0,1:T(8,128)(2,1)S(1)} %get-tuple-element.119, bf16[1536,16]{0,1:T(8,128)(2,1)S(1)} %get-tuple-element.120, bf16[1536,16]{0,1:T(8,128)(2,1)S(1)} %get-tuple-element.121), kind=kOutput, calls=%fused_computation.3.clone.1 | convolution fusion | flops 302432256 | bytes 6832128 | tf_op jit(solution)/shard_map/while/body/eval_jaxpr/dot_general | solution.py:102
  179.4 2.3 collective-permute-start
  183.0 2.3 collective-permute-done
  187.2 2.3 collective-permute-start.3
  190.8 2.3 collective-permute-done.3
  195.7 5.2 %collective-permute-done.6 = f32[2,1024,8]{1,2,0:T(8,128)S(1)} collective-permute-done((f32[2,1024,8]{1,2,0:T(8,128)S(1)}, f32[2,1024,8]{1,2,0:T(8,128)S(1)}, u32[]{:S(2)}, u32[]{:S(2)}) %collective-permute-start.6) | collective-permute-done | bytes 65568 | tf_op jit(solution)/shard_map/while/body/eval_jaxpr/ppermute | solution.py:19
  204.5 4.7 %convolution_bitcast_fusion.15 = f32[2048,48]{0,1:T(8,128)S(1)} fusion(bf16[2048,1536]{1,0:T(8,128)(2,1)} %get-tuple-element.149, bf16[1536,16]{0,1:T(8,128)(2,1)S(1)} %get-tuple-element.130, bf16[1536,16]{0,1:T(8,128)(2,1)S(1)} %get-tuple-element.131, bf16[1536,16]{0,1:T(8,128)(2,1)S(1)} %get-tuple-element.132), kind=kOutput, calls=%fused_computation.1.clone.1 | convolution fusion | flops 302432256 | bytes 6832128 | tf_op jit(solution)/shard_map/while/body/eval_jaxpr/dot_general | solution.py:102
  209.3 3.9 %convolution_bitcast_fusion.16 = f32[1536,48]{0,1:T(8,128)S(1)} fusion(bf16[2048,1536]{1,0:T(8,128)(2,1)} %get-tuple-element.149, bf16[2048,16]{0,1:T(8,128)(2,1)S(1)} %get-tuple-element.134, bf16[2048,16]{0,1:T(8,128)(2,1)S(1)} %get-tuple-element.135, bf16[2048,16]{0,1:T(8,128)(2,1)S(1)} %get-tuple-element.136), kind=kOutput, calls=%fused_computation.clone.1 | convolution fusion | flops 302579712 | bytes 6782976 | tf_op jit(solution)/shard_map/while/body/eval_jaxpr/dot_general | solution.py:107
  216.8 2.3 collective-permute-done.7
  224.0 2.3 collective-permute-done.10
  228.8 4.4 %collective-permute-done.13 = f32[2,1024,8]{1,2,0:T(8,128)S(1)} collective-permute-done((f32[2,1024,8]{1,2,0:T(8,128)S(1)}, f32[2,1024,8]{1,2,0:T(8,128)S(1)}, u32[]{:S(2)}, u32[]{:S(2)}) %collective-permute-start.13) | collective-permute-done | bytes 65568 | tf_op jit(solution)/shard_map/while/body/eval_jaxpr/ppermute | solution.py:19
  236.9 4.7 %fusion.41 = f32[2048,48]{0,1:T(8,128)S(1)} fusion(bf16[2048,1536]{1,0:T(8,128)(2,1)} %get-tuple-element.151, bf16[1536,16]{0,1:T(8,128)(2,1)S(1)} %get-tuple-element.73, bf16[1536,16]{0,1:T(8,128)(2,1)S(1)} %get-tuple-element.72, bf16[1536,16]{0,1:T(8,128)(2,1)S(1)} %get-tuple-element.71), kind=kOutput, calls=%fused_computation.109 | convolution fusion | flops 302432256 | bytes 6832128 | tf_op jit(solution)/shard_map/dot_general | solution.py:102
  242.6 2.7 %collective-permute-start.24 = (f32[16]{0:T(128)S(1)}, f32[16]{0:T(128)S(1)}, u32[]{:S(2)}, u32[]{:S(2)}) collective-permute-start(f32[16]{0:T(128)S(1)} %get-tuple-element.39), channel_id=1, source_target_pairs={{0,8},{4,12},{8,0},{12,4},{16,24},{20,28},{24,16},{28,20},{32,40},... | collective-permute-start | bytes 200 | tf_op jit(solution)/shard_map/ppermute | solution.py:19
  249.7 3.0 %multiply_reduce_fusion.1 = (f32[2048]{0:T(1024)S(1)}, f32[2048]{0:T(1024)S(1)}) fusion(bf16[2048,1536]{1,0:T(8,128)(2,1)S(1)} %bitcast.142, f32[2048,1024]{1,0:T(8,128)S(1)} %fusion.58, bf16[2048,48]{0,1:T(8,128)(2,1)S(1)} %constant_dynamic-update-slice_fusion, bf16[1024,48]{0,1:T(8,128)(2,1)S(1)} %get-tuple-element.62), kind=kOutput, calls=%fused_computation.105 | convolution fusion | flops 218099712 | bytes 17088512 | tf_op jit(solution)/shard_map/dot_general | solution.py:67
  253.6 2.7 %collective-permute-start.27 = (f32[16]{0:T(128)S(1)}, f32[16]{0:T(128)S(1)}, u32[]{:S(2)}, u32[]{:S(2)}) collective-permute-start(f32[16]{0:T(128)S(1)} %add_add_fusion.7), channel_id=1, source_target_pairs={{0,32},{4,36},{8,40},{12,44},{16,48},{20,52},{24,56},{28,60},{32,0... | collective-permute-start | bytes 200 | tf_op jit(solution)/shard_map/ppermute | solution.py:19
  258.7 2.4 collective-permute-done.28
  262.2 3.9 %collective-permute-done.29 = f32[16]{0:T(128)S(1)} collective-permute-done((f32[16]{0:T(128)S(1)}, f32[16]{0:T(128)S(1)}, u32[]{:S(2)}, u32[]{:S(2)}) %collective-permute-start.29) | collective-permute-done | bytes 96 | tf_op jit(solution)/shard_map/ppermute | solution.py:19
  (260 shorter events, 107.0 us)
Async XLA Ops:
  3.9 32.8 %collective-permute-start.14 = (bf16[2048,512]{1,0:T(8,128)(2,1)}, bf16[2048,512]{1,0:T(8,128)(2,1)}, u32[]{:S(2)}, u32[]{:S(2)}) collective-permute-start(bf16[2048,512]{1,0:T(8,128)(2,1)} %slice.115), channel_id=1, source_target_pairs={{1,0},{2,1},{3,2},{5,4},{6,5},{7,6},{9,8},{10,9},{11,10},{13,12},{... | collective-permute-start | bytes 6291464 | tf_op jit(solution)/shard_map/ppermute | solution.py:14
  9.4 4.8 %collective-permute-start.15 = (f32[2,1536]{1,0:T(2,128)S(1)}, f32[2,1536]{1,0:T(2,128)S(1)}, u32[]{:S(2)}, u32[]{:S(2)}) collective-permute-start(f32[2,1536]{1,0:T(2,128)S(1)} %pad_maximum_fusion.4), channel_id=1, source_target_pairs={{0,4},{4,0},{8,12},{12,8},{16,20},{20,16},{24,28},{28,24},{32,36},... | collective-permute-start | bytes 36872 | tf_op jit(solution)/shard_map/ppermute | solution.py:19
  11.0 5.2 %collective-permute-start.16 = (f32[2,1536]{1,0:T(2,128)S(1)}, f32[2,1536]{1,0:T(2,128)S(1)}, u32[]{:S(2)}, u32[]{:S(2)}) collective-permute-start(f32[2,1536]{1,0:T(2,128)S(1)} %pad_maximum_fusion.4), channel_id=1, source_target_pairs={{0,8},{4,12},{8,0},{12,4},{16,24},{20,28},{24,16},{28,20},{32,40},... | collective-permute-start | bytes 36872 | tf_op jit(solution)/shard_map/ppermute | solution.py:19
  13.9 4.9 %collective-permute-start.17 = (f32[2,1536]{1,0:T(2,128)S(1)}, f32[2,1536]{1,0:T(2,128)S(1)}, u32[]{:S(2)}, u32[]{:S(2)}) collective-permute-start(f32[2,1536]{1,0:T(2,128)S(1)} %pad_maximum_fusion.4), channel_id=1, source_target_pairs={{0,12},{4,8},{8,4},{12,0},{16,28},{20,24},{24,20},{28,16},{32,44},... | collective-permute-start | bytes 36872 | tf_op jit(solution)/shard_map/ppermute | solution.py:19
  18.8 4.8 %collective-permute-start.18 = (f32[2,1536]{1,0:T(2,128)S(1)}, f32[2,1536]{1,0:T(2,128)S(1)}, u32[]{:S(2)}, u32[]{:S(2)}) collective-permute-start(f32[2,1536]{1,0:T(2,128)S(1)} %add_add_fusion.5), channel_id=1, source_target_pairs={{0,16},{4,20},{8,24},{12,28},{16,0},{20,4},{24,8},{28,12},{32,48},... | collective-permute-start | bytes 36872 | tf_op jit(solution)/shard_map/ppermute | solution.py:19
  20.4 5.2 %collective-permute-start.19 = (f32[2,1536]{1,0:T(2,128)S(1)}, f32[2,1536]{1,0:T(2,128)S(1)}, u32[]{:S(2)}, u32[]{:S(2)}) collective-permute-start(f32[2,1536]{1,0:T(2,128)S(1)} %add_add_fusion.5), channel_id=1, source_target_pairs={{0,32},{4,36},{8,40},{12,44},{16,48},{20,52},{24,56},{28,60},{32,0... | collective-permute-start | bytes 36872 | tf_op jit(solution)/shard_map/ppermute | solution.py:19
  23.1 4.9 %collective-permute-start.20 = (f32[2,1536]{1,0:T(2,128)S(1)}, f32[2,1536]{1,0:T(2,128)S(1)}, u32[]{:S(2)}, u32[]{:S(2)}) collective-permute-start(f32[2,1536]{1,0:T(2,128)S(1)} %add_add_fusion.5), channel_id=1, source_target_pairs={{0,48},{4,52},{8,56},{12,60},{16,32},{20,36},{24,40},{28,44},{32,1... | collective-permute-start | bytes 36872 | tf_op jit(solution)/shard_map/ppermute | solution.py:19
  28.1 5.3 %collective-permute-start.21 = (f32[2,1536]{1,0:T(2,128)S(1)}, f32[2,1536]{1,0:T(2,128)S(1)}, u32[]{:S(2)}, u32[]{:S(2)}) collective-permute-start(f32[2,1536]{1,0:T(2,128)S(1)} %add_add_fusion.4), channel_id=1, source_target_pairs={{0,64},{4,68},{8,72},{12,76},{16,80},{20,84},{24,88},{28,92},{32,9... | collective-permute-start | bytes 36872 | tf_op jit(solution)/shard_map/ppermute | solution.py:19
  50.5 5.8 %collective-permute-start = (f32[2,1024,8]{1,2,0:T(8,128)S(1)}, f32[2,1024,8]{1,2,0:T(8,128)S(1)}, u32[]{:S(2)}, u32[]{:S(2)}) collective-permute-start(f32[2,1024,8]{1,2,0:T(8,128)S(1)} %pad_maximum_fusion.8), channel_id=1, source_target_pairs={{0,8},{4,12},{8,0},{12,4},{16,24},{20,28},{24,16},{28,20},{32,40},... | collective-permute-start | bytes 196616 | tf_op jit(solution)/shard_map/while/body/eval_jaxpr/ppermute | solution.py:19
  53.6 5.5 %collective-permute-start.1 = (f32[2,1024,8]{1,2,0:T(8,128)S(1)}, f32[2,1024,8]{1,2,0:T(8,128)S(1)}, u32[]{:S(2)}, u32[]{:S(2)}) collective-permute-start(f32[2,1024,8]{1,2,0:T(8,128)S(1)} %pad_maximum_fusion.8), channel_id=1, source_target_pairs={{0,12},{4,8},{8,4},{12,0},{16,28},{20,24},{24,20},{28,16},{32,44},... | collective-permute-start | bytes 196616 | tf_op jit(solution)/shard_map/while/body/eval_jaxpr/ppermute | solution.py:19
  54.7 4.4 %collective-permute-start.2 = (f32[2,1024,8]{1,2,0:T(8,128)S(1)}, f32[2,1024,8]{1,2,0:T(8,128)S(1)}, u32[]{:S(2)}, u32[]{:S(2)}) collective-permute-start(f32[2,1024,8]{1,2,0:T(8,128)S(1)} %pad_maximum_fusion.8), channel_id=1, source_target_pairs={{0,4},{4,0},{8,12},{12,8},{16,20},{20,16},{24,28},{28,24},{32,36},... | collective-permute-start | bytes 196616 | tf_op jit(solution)/shard_map/while/body/eval_jaxpr/ppermute | solution.py:19
  59.1 6.0 %collective-permute-start.3 = (f32[2,1024,8]{1,2,0:T(8,128)S(1)}, f32[2,1024,8]{1,2,0:T(8,128)S(1)}, u32[]{:S(2)}, u32[]{:S(2)}) collective-permute-start(f32[2,1024,8]{1,2,0:T(8,128)S(1)} %add_add_fusion.12), channel_id=1, source_target_pairs={{0,32},{4,36},{8,40},{12,44},{16,48},{20,52},{24,56},{28,60},{32,0... | collective-permute-start | bytes 196616 | tf_op jit(solution)/shard_map/while/body/eval_jaxpr/ppermute | solution.py:19
  62.2 5.5 %collective-permute-start.4 = (f32[2,1024,8]{1,2,0:T(8,128)S(1)}, f32[2,1024,8]{1,2,0:T(8,128)S(1)}, u32[]{:S(2)}, u32[]{:S(2)}) collective-permute-start(f32[2,1024,8]{1,2,0:T(8,128)S(1)} %add_add_fusion.12), channel_id=1, source_target_pairs={{0,48},{4,52},{8,56},{12,60},{16,32},{20,36},{24,40},{28,44},{32,1... | collective-permute-start | bytes 196616 | tf_op jit(solution)/shard_map/while/body/eval_jaxpr/ppermute | solution.py:19
  67.7 5.8 %collective-permute-start.6 = (f32[2,1024,8]{1,2,0:T(8,128)S(1)}, f32[2,1024,8]{1,2,0:T(8,128)S(1)}, u32[]{:S(2)}, u32[]{:S(2)}) collective-permute-start(f32[2,1024,8]{1,2,0:T(8,128)S(1)} %add_add_fusion.13), channel_id=1, source_target_pairs={{0,64},{4,68},{8,72},{12,76},{16,80},{20,84},{24,88},{28,92},{32,9... | collective-permute-start | bytes 196616 | tf_op jit(solution)/shard_map/while/body/eval_jaxpr/ppermute | solution.py:19
  86.0 5.8 %collective-permute-start.7 = (f32[2,1024,8]{1,2,0:T(8,128)S(1)}, f32[2,1024,8]{1,2,0:T(8,128)S(1)}, u32[]{:S(2)}, u32[]{:S(2)}) collective-permute-start(f32[2,1024,8]{1,2,0:T(8,128)S(1)} %pad_maximum_fusion.9), channel_id=1, source_target_pairs={{0,8},{4,12},{8,0},{12,4},{16,24},{20,28},{24,16},{28,20},{32,40},... | collective-permute-start | bytes 196616 | tf_op jit(solution)/shard_map/while/body/eval_jaxpr/ppermute | solution.py:19
  87.6 5.5 %collective-permute-start.8 = (f32[2,1024,8]{1,2,0:T(8,128)S(1)}, f32[2,1024,8]{1,2,0:T(8,128)S(1)}, u32[]{:S(2)}, u32[]{:S(2)}) collective-permute-start(f32[2,1024,8]{1,2,0:T(8,128)S(1)} %pad_maximum_fusion.9), channel_id=1, source_target_pairs={{0,12},{4,8},{8,4},{12,0},{16,28},{20,24},{24,20},{28,16},{32,44},... | collective-permute-start | bytes 196616 | tf_op jit(solution)/shard_map/while/body/eval_jaxpr/ppermute | solution.py:19
  88.6 4.5 %collective-permute-start.9 = (f32[2,1024,8]{1,2,0:T(8,128)S(1)}, f32[2,1024,8]{1,2,0:T(8,128)S(1)}, u32[]{:S(2)}, u32[]{:S(2)}) collective-permute-start(f32[2,1024,8]{1,2,0:T(8,128)S(1)} %pad_maximum_fusion.9), channel_id=1, source_target_pairs={{0,4},{4,0},{8,12},{12,8},{16,20},{20,16},{24,28},{28,24},{32,36},... | collective-permute-start | bytes 196616 | tf_op jit(solution)/shard_map/while/body/eval_jaxpr/ppermute | solution.py:19
  93.1 5.8 %collective-permute-start.10 = (f32[2,1024,8]{1,2,0:T(8,128)S(1)}, f32[2,1024,8]{1,2,0:T(8,128)S(1)}, u32[]{:S(2)}, u32[]{:S(2)}) collective-permute-start(f32[2,1024,8]{1,2,0:T(8,128)S(1)} %add_add_fusion.14), channel_id=1, source_target_pairs={{0,32},{4,36},{8,40},{12,44},{16,48},{20,52},{24,56},{28,60},{32,0... | collective-permute-start | bytes 196616 | tf_op jit(solution)/shard_map/while/body/eval_jaxpr/ppermute | solution.py:19
  94.6 5.5 %collective-permute-start.11 = (f32[2,1024,8]{1,2,0:T(8,128)S(1)}, f32[2,1024,8]{1,2,0:T(8,128)S(1)}, u32[]{:S(2)}, u32[]{:S(2)}) collective-permute-start(f32[2,1024,8]{1,2,0:T(8,128)S(1)} %add_add_fusion.14), channel_id=1, source_target_pairs={{0,48},{4,52},{8,56},{12,60},{16,32},{20,36},{24,40},{28,44},{32,1... | collective-permute-start | bytes 196616 | tf_op jit(solution)/shard_map/while/body/eval_jaxpr/ppermute | solution.py:19
  95.8 4.3 %collective-permute-start.12 = (f32[2,1024,8]{1,2,0:T(8,128)S(1)}, f32[2,1024,8]{1,2,0:T(8,128)S(1)}, u32[]{:S(2)}, u32[]{:S(2)}) collective-permute-start(f32[2,1024,8]{1,2,0:T(8,128)S(1)} %add_add_fusion.14), channel_id=1, source_target_pairs={{0,16},{4,20},{8,24},{12,28},{16,0},{20,4},{24,8},{28,12},{32,48},... | collective-permute-start | bytes 196616 | tf_op jit(solution)/shard_map/while/body/eval_jaxpr/ppermute | solution.py:19
  100.1 5.8 %collective-permute-start.13 = (f32[2,1024,8]{1,2,0:T(8,128)S(1)}, f32[2,1024,8]{1,2,0:T(8,128)S(1)}, u32[]{:S(2)}, u32[]{:S(2)}) collective-permute-start(f32[2,1024,8]{1,2,0:T(8,128)S(1)} %add_add_fusion.15), channel_id=1, source_target_pairs={{0,64},{4,68},{8,72},{12,76},{16,80},{20,84},{24,88},{28,92},{32,9... | collective-permute-start | bytes 196616 | tf_op jit(solution)/shard_map/while/body/eval_jaxpr/ppermute | solution.py:19
  115.8 5.8 %collective-permute-start = (f32[2,1024,8]{1,2,0:T(8,128)S(1)}, f32[2,1024,8]{1,2,0:T(8,128)S(1)}, u32[]{:S(2)}, u32[]{:S(2)}) collective-permute-start(f32[2,1024,8]{1,2,0:T(8,128)S(1)} %pad_maximum_fusion.8), channel_id=1, source_target_pairs={{0,8},{4,12},{8,0},{12,4},{16,24},{20,28},{24,16},{28,20},{32,40},... | collective-permute-start | bytes 196616 | tf_op jit(solution)/shard_map/while/body/eval_jaxpr/ppermute | solution.py:19
  118.0 5.5 %collective-permute-start.1 = (f32[2,1024,8]{1,2,0:T(8,128)S(1)}, f32[2,1024,8]{1,2,0:T(8,128)S(1)}, u32[]{:S(2)}, u32[]{:S(2)}) collective-permute-start(f32[2,1024,8]{1,2,0:T(8,128)S(1)} %pad_maximum_fusion.8), channel_id=1, source_target_pairs={{0,12},{4,8},{8,4},{12,0},{16,28},{20,24},{24,20},{28,16},{32,44},... | collective-permute-start | bytes 196616 | tf_op jit(solution)/shard_map/while/body/eval_jaxpr/ppermute | solution.py:19
  123.5 5.8 %collective-permute-start.3 = (f32[2,1024,8]{1,2,0:T(8,128)S(1)}, f32[2,1024,8]{1,2,0:T(8,128)S(1)}, u32[]{:S(2)}, u32[]{:S(2)}) collective-permute-start(f32[2,1024,8]{1,2,0:T(8,128)S(1)} %add_add_fusion.12), channel_id=1, source_target_pairs={{0,32},{4,36},{8,40},{12,44},{16,48},{20,52},{24,56},{28,60},{32,0... | collective-permute-start | bytes 196616 | tf_op jit(solution)/shard_map/while/body/eval_jaxpr/ppermute | solution.py:19
  125.9 5.5 %collective-permute-start.4 = (f32[2,1024,8]{1,2,0:T(8,128)S(1)}, f32[2,1024,8]{1,2,0:T(8,128)S(1)}, u32[]{:S(2)}, u32[]{:S(2)}) collective-permute-start(f32[2,1024,8]{1,2,0:T(8,128)S(1)} %add_add_fusion.12), channel_id=1, source_target_pairs={{0,48},{4,52},{8,56},{12,60},{16,32},{20,36},{24,40},{28,44},{32,1... | collective-permute-start | bytes 196616 | tf_op jit(solution)/shard_map/while/body/eval_jaxpr/ppermute | solution.py:19
  131.4 5.8 %collective-permute-start.6 = (f32[2,1024,8]{1,2,0:T(8,128)S(1)}, f32[2,1024,8]{1,2,0:T(8,128)S(1)}, u32[]{:S(2)}, u32[]{:S(2)}) collective-permute-start(f32[2,1024,8]{1,2,0:T(8,128)S(1)} %add_add_fusion.13), channel_id=1, source_target_pairs={{0,64},{4,68},{8,72},{12,76},{16,80},{20,84},{24,88},{28,92},{32,9... | collective-permute-start | bytes 196616 | tf_op jit(solution)/shard_map/while/body/eval_jaxpr/ppermute | solution.py:19
  149.6 5.8 %collective-permute-start.7 = (f32[2,1024,8]{1,2,0:T(8,128)S(1)}, f32[2,1024,8]{1,2,0:T(8,128)S(1)}, u32[]{:S(2)}, u32[]{:S(2)}) collective-permute-start(f32[2,1024,8]{1,2,0:T(8,128)S(1)} %pad_maximum_fusion.9), channel_id=1, source_target_pairs={{0,8},{4,12},{8,0},{12,4},{16,24},{20,28},{24,16},{28,20},{32,40},... | collective-permute-start | bytes 196616 | tf_op jit(solution)/shard_map/while/body/eval_jaxpr/ppermute | solution.py:19
  151.2 5.5 %collective-permute-start.8 = (f32[2,1024,8]{1,2,0:T(8,128)S(1)}, f32[2,1024,8]{1,2,0:T(8,128)S(1)}, u32[]{:S(2)}, u32[]{:S(2)}) collective-permute-start(f32[2,1024,8]{1,2,0:T(8,128)S(1)} %pad_maximum_fusion.9), channel_id=1, source_target_pairs={{0,12},{4,8},{8,4},{12,0},{16,28},{20,24},{24,20},{28,16},{32,44},... | collective-permute-start | bytes 196616 | tf_op jit(solution)/shard_map/while/body/eval_jaxpr/ppermute | solution.py:19
  156.7 5.8 %collective-permute-start.10 = (f32[2,1024,8]{1,2,0:T(8,128)S(1)}, f32[2,1024,8]{1,2,0:T(8,128)S(1)}, u32[]{:S(2)}, u32[]{:S(2)}) collective-permute-start(f32[2,1024,8]{1,2,0:T(8,128)S(1)} %add_add_fusion.14), channel_id=1, source_target_pairs={{0,32},{4,36},{8,40},{12,44},{16,48},{20,52},{24,56},{28,60},{32,0... | collective-permute-start | bytes 196616 | tf_op jit(solution)/shard_map/while/body/eval_jaxpr/ppermute | solution.py:19
  158.3 5.5 %collective-permute-start.11 = (f32[2,1024,8]{1,2,0:T(8,128)S(1)}, f32[2,1024,8]{1,2,0:T(8,128)S(1)}, u32[]{:S(2)}, u32[]{:S(2)}) collective-permute-start(f32[2,1024,8]{1,2,0:T(8,128)S(1)} %add_add_fusion.14), channel_id=1, source_target_pairs={{0,48},{4,52},{8,56},{12,60},{16,32},{20,36},{24,40},{28,44},{32,1... | collective-permute-start | bytes 196616 | tf_op jit(solution)/shard_map/while/body/eval_jaxpr/ppermute | solution.py:19
  163.8 5.8 %collective-permute-start.13 = (f32[2,1024,8]{1,2,0:T(8,128)S(1)}, f32[2,1024,8]{1,2,0:T(8,128)S(1)}, u32[]{:S(2)}, u32[]{:S(2)}) collective-permute-start(f32[2,1024,8]{1,2,0:T(8,128)S(1)} %add_add_fusion.15), channel_id=1, source_target_pairs={{0,64},{4,68},{8,72},{12,76},{16,80},{20,84},{24,88},{28,92},{32,9... | collective-permute-start | bytes 196616 | tf_op jit(solution)/shard_map/while/body/eval_jaxpr/ppermute | solution.py:19
  179.4 5.8 %collective-permute-start = (f32[2,1024,8]{1,2,0:T(8,128)S(1)}, f32[2,1024,8]{1,2,0:T(8,128)S(1)}, u32[]{:S(2)}, u32[]{:S(2)}) collective-permute-start(f32[2,1024,8]{1,2,0:T(8,128)S(1)} %pad_maximum_fusion.8), channel_id=1, source_target_pairs={{0,8},{4,12},{8,0},{12,4},{16,24},{20,28},{24,16},{28,20},{32,40},... | collective-permute-start | bytes 196616 | tf_op jit(solution)/shard_map/while/body/eval_jaxpr/ppermute | solution.py:19
  181.7 5.5 %collective-permute-start.1 = (f32[2,1024,8]{1,2,0:T(8,128)S(1)}, f32[2,1024,8]{1,2,0:T(8,128)S(1)}, u32[]{:S(2)}, u32[]{:S(2)}) collective-permute-start(f32[2,1024,8]{1,2,0:T(8,128)S(1)} %pad_maximum_fusion.8), channel_id=1, source_target_pairs={{0,12},{4,8},{8,4},{12,0},{16,28},{20,24},{24,20},{28,16},{32,44},... | collective-permute-start | bytes 196616 | tf_op jit(solution)/shard_map/while/body/eval_jaxpr/ppermute | solution.py:19
  187.2 5.8 %collective-permute-start.3 = (f32[2,1024,8]{1,2,0:T(8,128)S(1)}, f32[2,1024,8]{1,2,0:T(8,128)S(1)}, u32[]{:S(2)}, u32[]{:S(2)}) collective-permute-start(f32[2,1024,8]{1,2,0:T(8,128)S(1)} %add_add_fusion.12), channel_id=1, source_target_pairs={{0,32},{4,36},{8,40},{12,44},{16,48},{20,52},{24,56},{28,60},{32,0... | collective-permute-start | bytes 196616 | tf_op jit(solution)/shard_map/while/body/eval_jaxpr/ppermute | solution.py:19
  189.5 5.5 %collective-permute-start.4 = (f32[2,1024,8]{1,2,0:T(8,128)S(1)}, f32[2,1024,8]{1,2,0:T(8,128)S(1)}, u32[]{:S(2)}, u32[]{:S(2)}) collective-permute-start(f32[2,1024,8]{1,2,0:T(8,128)S(1)} %add_add_fusion.12), channel_id=1, source_target_pairs={{0,48},{4,52},{8,56},{12,60},{16,32},{20,36},{24,40},{28,44},{32,1... | collective-permute-start | bytes 196616 | tf_op jit(solution)/shard_map/while/body/eval_jaxpr/ppermute | solution.py:19
  195.0 5.8 %collective-permute-start.6 = (f32[2,1024,8]{1,2,0:T(8,128)S(1)}, f32[2,1024,8]{1,2,0:T(8,128)S(1)}, u32[]{:S(2)}, u32[]{:S(2)}) collective-permute-start(f32[2,1024,8]{1,2,0:T(8,128)S(1)} %add_add_fusion.13), channel_id=1, source_target_pairs={{0,64},{4,68},{8,72},{12,76},{16,80},{20,84},{24,88},{28,92},{32,9... | collective-permute-start | bytes 196616 | tf_op jit(solution)/shard_map/while/body/eval_jaxpr/ppermute | solution.py:19
  213.3 5.8 %collective-permute-start.7 = (f32[2,1024,8]{1,2,0:T(8,128)S(1)}, f32[2,1024,8]{1,2,0:T(8,128)S(1)}, u32[]{:S(2)}, u32[]{:S(2)}) collective-permute-start(f32[2,1024,8]{1,2,0:T(8,128)S(1)} %pad_maximum_fusion.9), channel_id=1, source_target_pairs={{0,8},{4,12},{8,0},{12,4},{16,24},{20,28},{24,16},{28,20},{32,40},... | collective-permute-start | bytes 196616 | tf_op jit(solution)/shard_map/while/body/eval_jaxpr/ppermute | solution.py:19
  214.9 5.5 %collective-permute-start.8 = (f32[2,1024,8]{1,2,0:T(8,128)S(1)}, f32[2,1024,8]{1,2,0:T(8,128)S(1)}, u32[]{:S(2)}, u32[]{:S(2)}) collective-permute-start(f32[2,1024,8]{1,2,0:T(8,128)S(1)} %pad_maximum_fusion.9), channel_id=1, source_target_pairs={{0,12},{4,8},{8,4},{12,0},{16,28},{20,24},{24,20},{28,16},{32,44},... | collective-permute-start | bytes 196616 | tf_op jit(solution)/shard_map/while/body/eval_jaxpr/ppermute | solution.py:19
  220.4 5.8 %collective-permute-start.10 = (f32[2,1024,8]{1,2,0:T(8,128)S(1)}, f32[2,1024,8]{1,2,0:T(8,128)S(1)}, u32[]{:S(2)}, u32[]{:S(2)}) collective-permute-start(f32[2,1024,8]{1,2,0:T(8,128)S(1)} %add_add_fusion.14), channel_id=1, source_target_pairs={{0,32},{4,36},{8,40},{12,44},{16,48},{20,52},{24,56},{28,60},{32,0... | collective-permute-start | bytes 196616 | tf_op jit(solution)/shard_map/while/body/eval_jaxpr/ppermute | solution.py:19
  221.9 5.5 %collective-permute-start.11 = (f32[2,1024,8]{1,2,0:T(8,128)S(1)}, f32[2,1024,8]{1,2,0:T(8,128)S(1)}, u32[]{:S(2)}, u32[]{:S(2)}) collective-permute-start(f32[2,1024,8]{1,2,0:T(8,128)S(1)} %add_add_fusion.14), channel_id=1, source_target_pairs={{0,48},{4,52},{8,56},{12,60},{16,32},{20,36},{24,40},{28,44},{32,1... | collective-permute-start | bytes 196616 | tf_op jit(solution)/shard_map/while/body/eval_jaxpr/ppermute | solution.py:19
  227.4 5.8 %collective-permute-start.13 = (f32[2,1024,8]{1,2,0:T(8,128)S(1)}, f32[2,1024,8]{1,2,0:T(8,128)S(1)}, u32[]{:S(2)}, u32[]{:S(2)}) collective-permute-start(f32[2,1024,8]{1,2,0:T(8,128)S(1)} %add_add_fusion.15), channel_id=1, source_target_pairs={{0,64},{4,68},{8,72},{12,76},{16,80},{20,84},{24,88},{28,92},{32,9... | collective-permute-start | bytes 196616 | tf_op jit(solution)/shard_map/while/body/eval_jaxpr/ppermute | solution.py:19
  241.8 10.9 %collective-permute-start.23 = (f32[16]{0:T(128)S(1)}, f32[16]{0:T(128)S(1)}, u32[]{:S(2)}, u32[]{:S(2)}) collective-permute-start(f32[16]{0:T(128)S(1)} %get-tuple-element.39), channel_id=1, source_target_pairs={{0,4},{4,0},{8,12},{12,8},{16,20},{20,16},{24,28},{28,24},{32,36},... | collective-permute-start | bytes 200 | tf_op jit(solution)/shard_map/ppermute | solution.py:19
  242.6 10.1 %collective-permute-start.24 = (f32[16]{0:T(128)S(1)}, f32[16]{0:T(128)S(1)}, u32[]{:S(2)}, u32[]{:S(2)}) collective-permute-start(f32[16]{0:T(128)S(1)} %get-tuple-element.39), channel_id=1, source_target_pairs={{0,8},{4,12},{8,0},{12,4},{16,24},{20,28},{24,16},{28,20},{32,40},... | collective-permute-start | bytes 200 | tf_op jit(solution)/shard_map/ppermute | solution.py:19
  245.3 7.3 %collective-permute-start.25 = (f32[16]{0:T(128)S(1)}, f32[16]{0:T(128)S(1)}, u32[]{:S(2)}, u32[]{:S(2)}) collective-permute-start(f32[16]{0:T(128)S(1)} %get-tuple-element.39), channel_id=1, source_target_pairs={{0,12},{4,8},{8,4},{12,0},{16,28},{20,24},{24,20},{28,16},{32,44},... | collective-permute-start | bytes 200 | tf_op jit(solution)/shard_map/ppermute | solution.py:19
  252.7 4.8 %collective-permute-start.26 = (f32[16]{0:T(128)S(1)}, f32[16]{0:T(128)S(1)}, u32[]{:S(2)}, u32[]{:S(2)}) collective-permute-start(f32[16]{0:T(128)S(1)} %add_add_fusion.7), channel_id=1, source_target_pairs={{0,16},{4,20},{8,24},{12,28},{16,0},{20,4},{24,8},{28,12},{32,48},... | collective-permute-start | bytes 200 | tf_op jit(solution)/shard_map/ppermute | solution.py:19
  253.6 5.1 %collective-permute-start.27 = (f32[16]{0:T(128)S(1)}, f32[16]{0:T(128)S(1)}, u32[]{:S(2)}, u32[]{:S(2)}) collective-permute-start(f32[16]{0:T(128)S(1)} %add_add_fusion.7), channel_id=1, source_target_pairs={{0,32},{4,36},{8,40},{12,44},{16,48},{20,52},{24,56},{28,60},{32,0... | collective-permute-start | bytes 200 | tf_op jit(solution)/shard_map/ppermute | solution.py:19
  256.3 4.8 %collective-permute-start.28 = (f32[16]{0:T(128)S(1)}, f32[16]{0:T(128)S(1)}, u32[]{:S(2)}, u32[]{:S(2)}) collective-permute-start(f32[16]{0:T(128)S(1)} %add_add_fusion.7), channel_id=1, source_target_pairs={{0,48},{4,52},{8,56},{12,60},{16,32},{20,36},{24,40},{28,44},{32,1... | collective-permute-start | bytes 200 | tf_op jit(solution)/shard_map/ppermute | solution.py:19
  261.0 5.1 %collective-permute-start.29 = (f32[16]{0:T(128)S(1)}, f32[16]{0:T(128)S(1)}, u32[]{:S(2)}, u32[]{:S(2)}) collective-permute-start(f32[16]{0:T(128)S(1)} %add_add_fusion.6), channel_id=1, source_target_pairs={{0,64},{4,68},{8,72},{12,76},{16,80},{20,84},{24,88},{28,92},{32,9... | collective-permute-start | bytes 200 | tf_op jit(solution)/shard_map/ppermute | solution.py:19
  (20 other events, 122.2 us)

commit v12 on v9

--- a/solution.py
+++ b/solution.py
@@ -105,8 +105,8 @@
         proj = project(basis)
         split = jnp.concatenate(pieces(proj), 1)
         back = thirds(lax.dot_general(stand, split, (((0,), (0,)), ((), ())), preferred_element_type=jnp.float32))
-        parts = jnp.stack([back[:columns, :comps], back[half_cols:, comps:]], 0)
-        return summed(parts, "ind") / total
+        back = summed(back, "ind") / total
+        return jnp.stack([back[:columns, :comps], back[half_cols:, comps:]], 0)
 
     basis = lax.fori_loop(0, ITERS, lambda step, basis: orthonormal(image_of(basis)), start)
     proj = project(basis)

time: 259 us -> 267 us (1.031)
  waiting for transfers between devices: 94.3 us -> 104 us
    ppermute x56, waiting for transfers between devices: 93.8 us -> 104 us  [swapped(): return lax.ppermute(value, axis, [(i, i ^ mask) for i in range(size)])]
  transfers between devices with their start and end apart: 58 -> 58, of which waited for: 40 -> 50; matrix products, arithmetic and copies ran while one was open for 4% -> 4% of each run, Pallas kernels for 0% -> 0%
where the time goes in v12:
time: 267 us
  waiting for transfers between devices  104 us (39%)
  starting transfers between devices  75.4 us (28%)
  matrix products  47.9 us (18%)
  other arithmetic  31.5 us (12%)
  local copies, waits for them, and re-layouts  6.1 us (2%)
    ppermute x56, waiting for transfers between devices, swapped(): return lax.ppermute(value, axis, [(i, i ^ mask) for i in range(size)])  104 us
    ppermute x56, starting transfers between devices, swapped(): return lax.ppermute(value, axis, [(i, i ^ mask) for i in range(size)])  71.4 us
    dot_general x7, matrix products, project(): jnp.dot(stand, jnp.concatenate(pieces(wide), 1), preferred_element_type=j...  33.9 us
    another operation x24, other arithmetic, orthonormal(): factor = jnp.linalg.cholesky(gram)  9.75 us
    another operation x18, other arithmetic, orthonormal(): jax.scipy.linalg.solve_triangular(fac, rhs, lower=True)  8.03 us
    dot_general x6, matrix products, image_of(): lax.dot_general(stand, split, (((0,), (0,)), ((), ())), preferred_element...  6.76 us
  transfers between devices with their start and end apart: 58, of which 50 were waited for; matrix products, arithmetic and copies ran while one was open for 4% of the time, Pallas kernels for 0%

profile of v12, /device:TPU:32, one launch (start us, length us, event | category | flops | bytes accessed | tf_op | source)
XLA Modules:
  0.0 266.6 jit_solution(6606675562579579076)
XLA Ops:
  0.7 3.2 %slice.89 = bf16[2048,512]{1,0:T(8,128)(2,1)} slice(bf16[2048,1024]{1,0:T(8,128)(2,1)} %param.6), slice={[0:2048], [0:512]} | slice | bytes 4194304 | tf_op jit(solution)/shard_map/slice | solution.py:84
  3.9 2.0 collective-permute-start.7
  5.9 3.5 %convert_reduce_fusion = (f32[1536]{0:T(1024)S(1)}, f32[1536]{0:T(1024)S(1)}) fusion(bf16[2048,512]{1,0:T(8,128)(2,1)} %param.7, bf16[2048,1024]{1,0:T(8,128)(2,1)S(1)} %copy-done.1), kind=kLoop, calls=%fused_computation.52 | loop fusion | flops 22017024 | bytes 6303744 | tf_op jit(solution)/shard_map/reduce_sum | solution.py:89
  9.5 3.1 %collective-permute-start.10 = (f32[2,1536]{1,0:T(2,128)S(1)}, f32[2,1536]{1,0:T(2,128)S(1)}, u32[]{:S(2)}, u32[]{:S(2)}) collective-permute-start(f32[2,1536]{1,0:T(2,128)S(1)} %pad_maximum_fusion.5), channel_id=1, source_target_pairs={{0,12},{4,8},{8,4},{12,0},{16,28},{20,24},{24,20},{28,16},{32,44},... | collective-permute-start | bytes 36872 | tf_op jit(solution)/shard_map/ppermute | solution.py:19
  19.5 2.7 %collective-permute-start.12 = (f32[2,1536]{1,0:T(2,128)S(1)}, f32[2,1536]{1,0:T(2,128)S(1)}, u32[]{:S(2)}, u32[]{:S(2)}) collective-permute-start(f32[2,1536]{1,0:T(2,128)S(1)} %add_add_fusion.3), channel_id=1, source_target_pairs={{0,32},{4,36},{8,40},{12,44},{16,48},{20,52},{24,56},{28,60},{32,0... | collective-permute-start | bytes 36872 | tf_op jit(solution)/shard_map/ppermute | solution.py:19
  22.7 2.0 collective-permute-done.12
  24.7 2.4 collective-permute-done.13
  27.2 3.1 %collective-permute-start.14 = (f32[2,1536]{1,0:T(2,128)S(1)}, f32[2,1536]{1,0:T(2,128)S(1)}, u32[]{:S(2)}, u32[]{:S(2)}) collective-permute-start(f32[2,1536]{1,0:T(2,128)S(1)} %add_add_fusion.2), channel_id=1, source_target_pairs={{0,64},{4,68},{8,72},{12,76},{16,80},{20,84},{24,88},{28,92},{32,9... | collective-permute-start | bytes 36872 | tf_op jit(solution)/shard_map/ppermute | solution.py:19
  30.2 3.1 %collective-permute-done.14 = f32[2,1536]{1,0:T(2,128)S(1)} collective-permute-done((f32[2,1536]{1,0:T(2,128)S(1)}, f32[2,1536]{1,0:T(2,128)S(1)}, u32[]{:S(2)}, u32[]{:S(2)}) %collective-permute-start.14) | collective-permute-done | bytes 12320 | tf_op jit(solution)/shard_map/ppermute | solution.py:19
  36.7 2.1 broadcast_select_fusion
  38.9 5.1 %multiply_convert_fusion = bf16[2048,1536]{1,0:T(8,128)(2,1)} fusion(bf16[2048,1024]{1,0:T(8,128)(2,1)S(1)} %copy-done.2, bf16[2048,512]{1,0:T(8,128)(2,1)S(1)} %broadcast_select_fusion, f32[1536]{0:T(1024)S(1)} %multiply_sqrt_fusion, f32[1536]{0:T(1024)S(1)} %get-tuple-element.26, f32[1536]{0:T(1024)S(1)} %get-tuple-element.25), kind=kLoop, calls=%fused_computation.54 | loop fusion | flops 25165824 | bytes 12601344 | tf_op jit(solution)/shard_map/convert_element_type | solution.py:97
  44.1 192.9 %while.10 = (s32[]{:T(128)}, f32[2,1024,8]{1,2,0:T(8,128)S(1)}, bf16[2048,1536]{1,0:T(8,128)(2,1)}, s32[]{:T(128)}) while((s32[]{:T(128)}, f32[2,1024,8]{1,2,0:T(8,128)S(1)}, bf16[2048,1536]{1,0:T(8,128)(2,1)}, s32[]{:T(128)}) %tuple.54), condition=%wide.region_5.6_spmd, body=%wide.region_2.5_spmd.sunk | while | flops 609108992 | bytes 44930792 | solution.py:111
  44.1 4.9 %convolution_bitcast_fusion.4 = f32[2048,48]{0,1:T(8,128)S(1)} fusion(bf16[2048,1536]{1,0:T(8,128)(2,1)} %get-tuple-element.114, bf16[1536,16]{0,1:T(8,128)(2,1)S(1)} %get-tuple-element.95, bf16[1536,16]{0,1:T(8,128)(2,1)S(1)} %get-tuple-element.96, bf16[1536,16]{0,1:T(8,128)(2,1)S(1)} %get-tuple-element.97), kind=kOutput, calls=%fused_computation.1.clone.1 | convolution fusion | flops 302432256 | bytes 6832128 | tf_op jit(solution)/shard_map/while/body/eval_jaxpr/dot_general | solution.py:102
  50.2 3.3 %collective-permute-start = (f32[1536,16]{0,1:T(8,128)S(1)}, f32[1536,16]{0,1:T(8,128)S(1)}, u32[]{:S(2)}, u32[]{:S(2)}) collective-permute-start(f32[1536,16]{0,1:T(8,128)S(1)} %slice_add_fusion.9), channel_id=1, source_target_pairs={{0,8},{4,12},{8,0},{12,4},{16,24},{20,28},{24,16},{28,20},{32,40},... | collective-permute-start | bytes 294920 | tf_op jit(solution)/shard_map/while/body/eval_jaxpr/ppermute | solution.py:19
  54.6 2.1 collective-permute-done
  56.7 2.6 collective-permute-done.1
  59.4 3.1 %collective-permute-start.3 = (f32[1536,16]{0,1:T(8,128)S(1)}, f32[1536,16]{0,1:T(8,128)S(1)}, u32[]{:S(2)}, u32[]{:S(2)}) collective-permute-start(f32[1536,16]{0,1:T(8,128)S(1)} %add_add_fusion.8), channel_id=1, source_target_pairs={{0,32},{4,36},{8,40},{12,44},{16,48},{20,52},{24,56},{28,60},{32,0... | collective-permute-start | bytes 294920 | tf_op jit(solution)/shard_map/while/body/eval_jaxpr/ppermute | solution.py:19
  63.6 2.1 collective-permute-done.3
  65.7 2.6 collective-permute-done.4
  69.4 5.1 %collective-permute-done.6 = f32[1536,16]{0,1:T(8,128)S(1)} collective-permute-done((f32[1536,16]{0,1:T(8,128)S(1)}, f32[1536,16]{0,1:T(8,128)S(1)}, u32[]{:S(2)}, u32[]{:S(2)}) %collective-permute-start.6) | collective-permute-done | bytes 98336 | tf_op jit(solution)/shard_map/while/body/eval_jaxpr/ppermute | solution.py:19
  78.2 4.9 %convolution_bitcast_fusion.4 = f32[2048,48]{0,1:T(8,128)S(1)} fusion(bf16[2048,1536]{1,0:T(8,128)(2,1)} %get-tuple-element.114, bf16[1536,16]{0,1:T(8,128)(2,1)S(1)} %get-tuple-element.95, bf16[1536,16]{0,1:T(8,128)(2,1)S(1)} %get-tuple-element.96, bf16[1536,16]{0,1:T(8,128)(2,1)S(1)} %get-tuple-element.97), kind=kOutput, calls=%fused_computation.1.clone.1 | convolution fusion | flops 302432256 | bytes 6832128 | tf_op jit(solution)/shard_map/while/body/eval_jaxpr/dot_general | solution.py:102
  85.9 2.0 collective-permute-start.1
  87.9 2.6 collective-permute-done
  94.1 2.1 collective-permute-start.4
  96.3 2.5 collective-permute-done.3
  101.5 5.6 %collective-permute-done.6 = f32[1536,16]{0,1:T(8,128)S(1)} collective-permute-done((f32[1536,16]{0,1:T(8,128)S(1)}, f32[1536,16]{0,1:T(8,128)S(1)}, u32[]{:S(2)}, u32[]{:S(2)}) %collective-permute-start.6) | collective-permute-done | bytes 98336 | tf_op jit(solution)/shard_map/while/body/eval_jaxpr/ppermute | solution.py:19
  110.7 4.9 %convolution_bitcast_fusion.4 = f32[2048,48]{0,1:T(8,128)S(1)} fusion(bf16[2048,1536]{1,0:T(8,128)(2,1)} %get-tuple-element.114, bf16[1536,16]{0,1:T(8,128)(2,1)S(1)} %get-tuple-element.95, bf16[1536,16]{0,1:T(8,128)(2,1)S(1)} %get-tuple-element.96, bf16[1536,16]{0,1:T(8,128)(2,1)S(1)} %get-tuple-element.97), kind=kOutput, calls=%fused_computation.1.clone.1 | convolution fusion | flops 302432256 | bytes 6832128 | tf_op jit(solution)/shard_map/while/body/eval_jaxpr/dot_general | solution.py:102
  120.4 2.6 collective-permute-done
  128.1 2.6 collective-permute-done.3
  132.7 5.6 %collective-permute-done.6 = f32[1536,16]{0,1:T(8,128)S(1)} collective-permute-done((f32[1536,16]{0,1:T(8,128)S(1)}, f32[1536,16]{0,1:T(8,128)S(1)}, u32[]{:S(2)}, u32[]{:S(2)}) %collective-permute-start.6) | collective-permute-done | bytes 98336 | tf_op jit(solution)/shard_map/while/body/eval_jaxpr/ppermute | solution.py:19
  141.9 4.9 %convolution_bitcast_fusion.4 = f32[2048,48]{0,1:T(8,128)S(1)} fusion(bf16[2048,1536]{1,0:T(8,128)(2,1)} %get-tuple-element.114, bf16[1536,16]{0,1:T(8,128)(2,1)S(1)} %get-tuple-element.95, bf16[1536,16]{0,1:T(8,128)(2,1)S(1)} %get-tuple-element.96, bf16[1536,16]{0,1:T(8,128)(2,1)S(1)} %get-tuple-element.97), kind=kOutput, calls=%fused_computation.1.clone.1 | convolution fusion | flops 302432256 | bytes 6832128 | tf_op jit(solution)/shard_map/while/body/eval_jaxpr/dot_general | solution.py:102
  151.6 2.6 collective-permute-done
  159.6 2.6 collective-permute-done.3
  164.7 5.6 %collective-permute-done.6 = f32[1536,16]{0,1:T(8,128)S(1)} collective-permute-done((f32[1536,16]{0,1:T(8,128)S(1)}, f32[1536,16]{0,1:T(8,128)S(1)}, u32[]{:S(2)}, u32[]{:S(2)}) %collective-permute-start.6) | collective-permute-done | bytes 98336 | tf_op jit(solution)/shard_map/while/body/eval_jaxpr/ppermute | solution.py:19
  173.9 4.9 %convolution_bitcast_fusion.4 = f32[2048,48]{0,1:T(8,128)S(1)} fusion(bf16[2048,1536]{1,0:T(8,128)(2,1)} %get-tuple-element.114, bf16[1536,16]{0,1:T(8,128)(2,1)S(1)} %get-tuple-element.95, bf16[1536,16]{0,1:T(8,128)(2,1)S(1)} %get-tuple-element.96, bf16[1536,16]{0,1:T(8,128)(2,1)S(1)} %get-tuple-element.97), kind=kOutput, calls=%fused_computation.1.clone.1 | convolution fusion | flops 302432256 | bytes 6832128 | tf_op jit(solution)/shard_map/while/body/eval_jaxpr/dot_general | solution.py:102
  183.6 2.6 collective-permute-done
  191.3 2.6 collective-permute-done.3
  195.8 5.6 %collective-permute-done.6 = f32[1536,16]{0,1:T(8,128)S(1)} collective-permute-done((f32[1536,16]{0,1:T(8,128)S(1)}, f32[1536,16]{0,1:T(8,128)S(1)}, u32[]{:S(2)}, u32[]{:S(2)}) %collective-permute-start.6) | collective-permute-done | bytes 98336 | tf_op jit(solution)/shard_map/while/body/eval_jaxpr/ppermute | solution.py:19
  205.0 4.9 %convolution_bitcast_fusion.4 = f32[2048,48]{0,1:T(8,128)S(1)} fusion(bf16[2048,1536]{1,0:T(8,128)(2,1)} %get-tuple-element.114, bf16[1536,16]{0,1:T(8,128)(2,1)S(1)} %get-tuple-element.95, bf16[1536,16]{0,1:T(8,128)(2,1)S(1)} %get-tuple-element.96, bf16[1536,16]{0,1:T(8,128)(2,1)S(1)} %get-tuple-element.97), kind=kOutput, calls=%fused_computation.1.clone.1 | convolution fusion | flops 302432256 | bytes 6832128 | tf_op jit(solution)/shard_map/while/body/eval_jaxpr/dot_general | solution.py:102
  214.7 2.6 collective-permute-done
  222.7 2.6 collective-permute-done.3
  227.8 5.6 %collective-permute-done.6 = f32[1536,16]{0,1:T(8,128)S(1)} collective-permute-done((f32[1536,16]{0,1:T(8,128)S(1)}, f32[1536,16]{0,1:T(8,128)S(1)}, u32[]{:S(2)}, u32[]{:S(2)}) %collective-permute-start.6) | collective-permute-done | bytes 98336 | tf_op jit(solution)/shard_map/while/body/eval_jaxpr/ppermute | solution.py:19
  237.1 4.7 %fusion.21 = f32[2048,48]{0,1:T(8,128)S(1)} fusion(bf16[2048,1536]{1,0:T(8,128)(2,1)} %get-tuple-element.116, bf16[1536,16]{0,1:T(8,128)(2,1)S(1)} %get-tuple-element.60, bf16[1536,16]{0,1:T(8,128)(2,1)S(1)} %get-tuple-element.59, bf16[1536,16]{0,1:T(8,128)(2,1)S(1)} %get-tuple-element.58), kind=kOutput, calls=%fused_computation.60 | convolution fusion | flops 302432256 | bytes 6832128 | tf_op jit(solution)/shard_map/dot_general | solution.py:102
  242.3 2.9 %collective-permute-start.17 = (f32[16]{0:T(128)S(1)}, f32[16]{0:T(128)S(1)}, u32[]{:S(2)}, u32[]{:S(2)}) collective-permute-start(f32[16]{0:T(128)S(1)} %get-tuple-element.35), channel_id=1, source_target_pairs={{0,8},{4,12},{8,0},{12,4},{16,24},{20,28},{24,16},{28,20},{32,40},... | collective-permute-start | bytes 200 | tf_op jit(solution)/shard_map/ppermute | solution.py:19
  249.8 3.0 %multiply_reduce_fusion.1 = (f32[2048]{0:T(1024)S(1)}, f32[2048]{0:T(1024)S(1)}) fusion(bf16[2048,1536]{1,0:T(8,128)(2,1)S(1)} %bitcast.80, f32[2048,1024]{1,0:T(8,128)S(1)} %fusion.38, bf16[2048,48]{0,1:T(8,128)(2,1)S(1)} %constant_dynamic-update-slice_fusion, bf16[1024,48]{0,1:T(8,128)(2,1)S(1)} %get-tuple-element.49), kind=kOutput, calls=%fused_computation.56 | convolution fusion | flops 218099712 | bytes 17088512 | tf_op jit(solution)/shard_map/dot_general | solution.py:67
  253.1 3.0 %collective-permute-start.20 = (f32[16]{0:T(128)S(1)}, f32[16]{0:T(128)S(1)}, u32[]{:S(2)}, u32[]{:S(2)}) collective-permute-start(f32[16]{0:T(128)S(1)} %add_add_fusion.5), channel_id=1, source_target_pairs={{0,32},{4,36},{8,40},{12,44},{16,48},{20,52},{24,56},{28,60},{32,0... | collective-permute-start | bytes 200 | tf_op jit(solution)/shard_map/ppermute | solution.py:19
  258.1 2.7 %collective-permute-done.21 = f32[16]{0:T(128)S(1)} collective-permute-done((f32[16]{0:T(128)S(1)}, f32[16]{0:T(128)S(1)}, u32[]{:S(2)}, u32[]{:S(2)}) %collective-permute-start.21) | collective-permute-done | bytes 96 | tf_op jit(solution)/shard_map/ppermute | solution.py:19
  262.0 3.9 %collective-permute-done.22 = f32[16]{0:T(128)S(1)} collective-permute-done((f32[16]{0:T(128)S(1)}, f32[16]{0:T(128)S(1)}, u32[]{:S(2)}, u32[]{:S(2)}) %collective-permute-start.22) | collective-permute-done | bytes 96 | tf_op jit(solution)/shard_map/ppermute | solution.py:19
  (272 shorter events, 104.1 us)
Async XLA Ops:
  3.9 32.8 %collective-permute-start.7 = (bf16[2048,512]{1,0:T(8,128)(2,1)}, bf16[2048,512]{1,0:T(8,128)(2,1)}, u32[]{:S(2)}, u32[]{:S(2)}) collective-permute-start(bf16[2048,512]{1,0:T(8,128)(2,1)} %slice.89), channel_id=1, source_target_pairs={{1,0},{2,1},{3,2},{5,4},{6,5},{7,6},{9,8},{10,9},{11,10},{13,12},{... | collective-permute-start | bytes 6291464 | tf_op jit(solution)/shard_map/ppermute | solution.py:14
  9.5 5.0 %collective-permute-start.10 = (f32[2,1536]{1,0:T(2,128)S(1)}, f32[2,1536]{1,0:T(2,128)S(1)}, u32[]{:S(2)}, u32[]{:S(2)}) collective-permute-start(f32[2,1536]{1,0:T(2,128)S(1)} %pad_maximum_fusion.5), channel_id=1, source_target_pairs={{0,12},{4,8},{8,4},{12,0},{16,28},{20,24},{24,20},{28,16},{32,44},... | collective-permute-start | bytes 36872 | tf_op jit(solution)/shard_map/ppermute | solution.py:19
  12.7 5.2 %collective-permute-start.9 = (f32[2,1536]{1,0:T(2,128)S(1)}, f32[2,1536]{1,0:T(2,128)S(1)}, u32[]{:S(2)}, u32[]{:S(2)}) collective-permute-start(f32[2,1536]{1,0:T(2,128)S(1)} %pad_maximum_fusion.5), channel_id=1, source_target_pairs={{0,8},{4,12},{8,0},{12,4},{16,24},{20,28},{24,16},{28,20},{32,40},... | collective-permute-start | bytes 36872 | tf_op jit(solution)/shard_map/ppermute | solution.py:19
  17.9 4.8 %collective-permute-start.11 = (f32[2,1536]{1,0:T(2,128)S(1)}, f32[2,1536]{1,0:T(2,128)S(1)}, u32[]{:S(2)}, u32[]{:S(2)}) collective-permute-start(f32[2,1536]{1,0:T(2,128)S(1)} %add_add_fusion.3), channel_id=1, source_target_pairs={{0,16},{4,20},{8,24},{12,28},{16,0},{20,4},{24,8},{28,12},{32,48},... | collective-permute-start | bytes 36872 | tf_op jit(solution)/shard_map/ppermute | solution.py:19
  19.5 5.2 %collective-permute-start.12 = (f32[2,1536]{1,0:T(2,128)S(1)}, f32[2,1536]{1,0:T(2,128)S(1)}, u32[]{:S(2)}, u32[]{:S(2)}) collective-permute-start(f32[2,1536]{1,0:T(2,128)S(1)} %add_add_fusion.3), channel_id=1, source_target_pairs={{0,32},{4,36},{8,40},{12,44},{16,48},{20,52},{24,56},{28,60},{32,0... | collective-permute-start | bytes 36872 | tf_op jit(solution)/shard_map/ppermute | solution.py:19
  22.2 4.9 %collective-permute-start.13 = (f32[2,1536]{1,0:T(2,128)S(1)}, f32[2,1536]{1,0:T(2,128)S(1)}, u32[]{:S(2)}, u32[]{:S(2)}) collective-permute-start(f32[2,1536]{1,0:T(2,128)S(1)} %add_add_fusion.3), channel_id=1, source_target_pairs={{0,48},{4,52},{8,56},{12,60},{16,32},{20,36},{24,40},{28,44},{32,1... | collective-permute-start | bytes 36872 | tf_op jit(solution)/shard_map/ppermute | solution.py:19
  27.2 6.2 %collective-permute-start.14 = (f32[2,1536]{1,0:T(2,128)S(1)}, f32[2,1536]{1,0:T(2,128)S(1)}, u32[]{:S(2)}, u32[]{:S(2)}) collective-permute-start(f32[2,1536]{1,0:T(2,128)S(1)} %add_add_fusion.2), channel_id=1, source_target_pairs={{0,64},{4,68},{8,72},{12,76},{16,80},{20,84},{24,88},{28,92},{32,9... | collective-permute-start | bytes 36872 | tf_op jit(solution)/shard_map/ppermute | solution.py:19
  50.2 6.5 %collective-permute-start = (f32[1536,16]{0,1:T(8,128)S(1)}, f32[1536,16]{0,1:T(8,128)S(1)}, u32[]{:S(2)}, u32[]{:S(2)}) collective-permute-start(f32[1536,16]{0,1:T(8,128)S(1)} %slice_add_fusion.9), channel_id=1, source_target_pairs={{0,8},{4,12},{8,0},{12,4},{16,24},{20,28},{24,16},{28,20},{32,40},... | collective-permute-start | bytes 294920 | tf_op jit(solution)/shard_map/while/body/eval_jaxpr/ppermute | solution.py:19
  53.5 5.8 %collective-permute-start.1 = (f32[1536,16]{0,1:T(8,128)S(1)}, f32[1536,16]{0,1:T(8,128)S(1)}, u32[]{:S(2)}, u32[]{:S(2)}) collective-permute-start(f32[1536,16]{0,1:T(8,128)S(1)} %slice_add_fusion.9), channel_id=1, source_target_pairs={{0,12},{4,8},{8,4},{12,0},{16,28},{20,24},{24,20},{28,16},{32,44},... | collective-permute-start | bytes 294920 | tf_op jit(solution)/shard_map/while/body/eval_jaxpr/ppermute | solution.py:19
  54.6 4.8 %collective-permute-start.2 = (f32[1536,16]{0,1:T(8,128)S(1)}, f32[1536,16]{0,1:T(8,128)S(1)}, u32[]{:S(2)}, u32[]{:S(2)}) collective-permute-start(f32[1536,16]{0,1:T(8,128)S(1)} %slice_add_fusion.9), channel_id=1, source_target_pairs={{0,4},{4,0},{8,12},{12,8},{16,20},{20,16},{24,28},{28,24},{32,36},... | collective-permute-start | bytes 294920 | tf_op jit(solution)/shard_map/while/body/eval_jaxpr/ppermute | solution.py:19
  59.4 6.3 %collective-permute-start.3 = (f32[1536,16]{0,1:T(8,128)S(1)}, f32[1536,16]{0,1:T(8,128)S(1)}, u32[]{:S(2)}, u32[]{:S(2)}) collective-permute-start(f32[1536,16]{0,1:T(8,128)S(1)} %add_add_fusion.8), channel_id=1, source_target_pairs={{0,32},{4,36},{8,40},{12,44},{16,48},{20,52},{24,56},{28,60},{32,0... | collective-permute-start | bytes 294920 | tf_op jit(solution)/shard_map/while/body/eval_jaxpr/ppermute | solution.py:19
  62.5 5.8 %collective-permute-start.4 = (f32[1536,16]{0,1:T(8,128)S(1)}, f32[1536,16]{0,1:T(8,128)S(1)}, u32[]{:S(2)}, u32[]{:S(2)}) collective-permute-start(f32[1536,16]{0,1:T(8,128)S(1)} %add_add_fusion.8), channel_id=1, source_target_pairs={{0,48},{4,52},{8,56},{12,60},{16,32},{20,36},{24,40},{28,44},{32,1... | collective-permute-start | bytes 294920 | tf_op jit(solution)/shard_map/while/body/eval_jaxpr/ppermute | solution.py:19
  63.6 4.7 %collective-permute-start.5 = (f32[1536,16]{0,1:T(8,128)S(1)}, f32[1536,16]{0,1:T(8,128)S(1)}, u32[]{:S(2)}, u32[]{:S(2)}) collective-permute-start(f32[1536,16]{0,1:T(8,128)S(1)} %add_add_fusion.8), channel_id=1, source_target_pairs={{0,16},{4,20},{8,24},{12,28},{16,0},{20,4},{24,8},{28,12},{32,48},... | collective-permute-start | bytes 294920 | tf_op jit(solution)/shard_map/while/body/eval_jaxpr/ppermute | solution.py:19
  68.3 6.2 %collective-permute-start.6 = (f32[1536,16]{0,1:T(8,128)S(1)}, f32[1536,16]{0,1:T(8,128)S(1)}, u32[]{:S(2)}, u32[]{:S(2)}) collective-permute-start(f32[1536,16]{0,1:T(8,128)S(1)} %add_add_fusion.9), channel_id=1, source_target_pairs={{0,64},{4,68},{8,72},{12,76},{16,80},{20,84},{24,88},{28,92},{32,9... | collective-permute-start | bytes 294920 | tf_op jit(solution)/shard_map/while/body/eval_jaxpr/ppermute | solution.py:19
  84.3 6.2 %collective-permute-start = (f32[1536,16]{0,1:T(8,128)S(1)}, f32[1536,16]{0,1:T(8,128)S(1)}, u32[]{:S(2)}, u32[]{:S(2)}) collective-permute-start(f32[1536,16]{0,1:T(8,128)S(1)} %slice_add_fusion.9), channel_id=1, source_target_pairs={{0,8},{4,12},{8,0},{12,4},{16,24},{20,28},{24,16},{28,20},{32,40},... | collective-permute-start | bytes 294920 | tf_op jit(solution)/shard_map/while/body/eval_jaxpr/ppermute | solution.py:19
  85.9 5.8 %collective-permute-start.1 = (f32[1536,16]{0,1:T(8,128)S(1)}, f32[1536,16]{0,1:T(8,128)S(1)}, u32[]{:S(2)}, u32[]{:S(2)}) collective-permute-start(f32[1536,16]{0,1:T(8,128)S(1)} %slice_add_fusion.9), channel_id=1, source_target_pairs={{0,12},{4,8},{8,4},{12,0},{16,28},{20,24},{24,20},{28,16},{32,44},... | collective-permute-start | bytes 294920 | tf_op jit(solution)/shard_map/while/body/eval_jaxpr/ppermute | solution.py:19
  87.9 4.6 %collective-permute-start.2 = (f32[1536,16]{0,1:T(8,128)S(1)}, f32[1536,16]{0,1:T(8,128)S(1)}, u32[]{:S(2)}, u32[]{:S(2)}) collective-permute-start(f32[1536,16]{0,1:T(8,128)S(1)} %slice_add_fusion.9), channel_id=1, source_target_pairs={{0,4},{4,0},{8,12},{12,8},{16,20},{20,16},{24,28},{28,24},{32,36},... | collective-permute-start | bytes 294920 | tf_op jit(solution)/shard_map/while/body/eval_jaxpr/ppermute | solution.py:19
  92.6 6.2 %collective-permute-start.3 = (f32[1536,16]{0,1:T(8,128)S(1)}, f32[1536,16]{0,1:T(8,128)S(1)}, u32[]{:S(2)}, u32[]{:S(2)}) collective-permute-start(f32[1536,16]{0,1:T(8,128)S(1)} %add_add_fusion.8), channel_id=1, source_target_pairs={{0,32},{4,36},{8,40},{12,44},{16,48},{20,52},{24,56},{28,60},{32,0... | collective-permute-start | bytes 294920 | tf_op jit(solution)/shard_map/while/body/eval_jaxpr/ppermute | solution.py:19
  94.1 5.8 %collective-permute-start.4 = (f32[1536,16]{0,1:T(8,128)S(1)}, f32[1536,16]{0,1:T(8,128)S(1)}, u32[]{:S(2)}, u32[]{:S(2)}) collective-permute-start(f32[1536,16]{0,1:T(8,128)S(1)} %add_add_fusion.8), channel_id=1, source_target_pairs={{0,48},{4,52},{8,56},{12,60},{16,32},{20,36},{24,40},{28,44},{32,1... | collective-permute-start | bytes 294920 | tf_op jit(solution)/shard_map/while/body/eval_jaxpr/ppermute | solution.py:19
  100.9 6.2 %collective-permute-start.6 = (f32[1536,16]{0,1:T(8,128)S(1)}, f32[1536,16]{0,1:T(8,128)S(1)}, u32[]{:S(2)}, u32[]{:S(2)}) collective-permute-start(f32[1536,16]{0,1:T(8,128)S(1)} %add_add_fusion.9), channel_id=1, source_target_pairs={{0,64},{4,68},{8,72},{12,76},{16,80},{20,84},{24,88},{28,92},{32,9... | collective-permute-start | bytes 294920 | tf_op jit(solution)/shard_map/while/body/eval_jaxpr/ppermute | solution.py:19
  116.9 6.2 %collective-permute-start = (f32[1536,16]{0,1:T(8,128)S(1)}, f32[1536,16]{0,1:T(8,128)S(1)}, u32[]{:S(2)}, u32[]{:S(2)}) collective-permute-start(f32[1536,16]{0,1:T(8,128)S(1)} %slice_add_fusion.9), channel_id=1, source_target_pairs={{0,8},{4,12},{8,0},{12,4},{16,24},{20,28},{24,16},{28,20},{32,40},... | collective-permute-start | bytes 294920 | tf_op jit(solution)/shard_map/while/body/eval_jaxpr/ppermute | solution.py:19
  118.6 5.8 %collective-permute-start.1 = (f32[1536,16]{0,1:T(8,128)S(1)}, f32[1536,16]{0,1:T(8,128)S(1)}, u32[]{:S(2)}, u32[]{:S(2)}) collective-permute-start(f32[1536,16]{0,1:T(8,128)S(1)} %slice_add_fusion.9), channel_id=1, source_target_pairs={{0,12},{4,8},{8,4},{12,0},{16,28},{20,24},{24,20},{28,16},{32,44},... | collective-permute-start | bytes 294920 | tf_op jit(solution)/shard_map/while/body/eval_jaxpr/ppermute | solution.py:19
  124.5 6.2 %collective-permute-start.3 = (f32[1536,16]{0,1:T(8,128)S(1)}, f32[1536,16]{0,1:T(8,128)S(1)}, u32[]{:S(2)}, u32[]{:S(2)}) collective-permute-start(f32[1536,16]{0,1:T(8,128)S(1)} %add_add_fusion.8), channel_id=1, source_target_pairs={{0,32},{4,36},{8,40},{12,44},{16,48},{20,52},{24,56},{28,60},{32,0... | collective-permute-start | bytes 294920 | tf_op jit(solution)/shard_map/while/body/eval_jaxpr/ppermute | solution.py:19
  126.1 5.8 %collective-permute-start.4 = (f32[1536,16]{0,1:T(8,128)S(1)}, f32[1536,16]{0,1:T(8,128)S(1)}, u32[]{:S(2)}, u32[]{:S(2)}) collective-permute-start(f32[1536,16]{0,1:T(8,128)S(1)} %add_add_fusion.8), channel_id=1, source_target_pairs={{0,48},{4,52},{8,56},{12,60},{16,32},{20,36},{24,40},{28,44},{32,1... | collective-permute-start | bytes 294920 | tf_op jit(solution)/shard_map/while/body/eval_jaxpr/ppermute | solution.py:19
  132.0 6.2 %collective-permute-start.6 = (f32[1536,16]{0,1:T(8,128)S(1)}, f32[1536,16]{0,1:T(8,128)S(1)}, u32[]{:S(2)}, u32[]{:S(2)}) collective-permute-start(f32[1536,16]{0,1:T(8,128)S(1)} %add_add_fusion.9), channel_id=1, source_target_pairs={{0,64},{4,68},{8,72},{12,76},{16,80},{20,84},{24,88},{28,92},{32,9... | collective-permute-start | bytes 294920 | tf_op jit(solution)/shard_map/while/body/eval_jaxpr/ppermute | solution.py:19
  148.0 6.2 %collective-permute-start = (f32[1536,16]{0,1:T(8,128)S(1)}, f32[1536,16]{0,1:T(8,128)S(1)}, u32[]{:S(2)}, u32[]{:S(2)}) collective-permute-start(f32[1536,16]{0,1:T(8,128)S(1)} %slice_add_fusion.9), channel_id=1, source_target_pairs={{0,8},{4,12},{8,0},{12,4},{16,24},{20,28},{24,16},{28,20},{32,40},... | collective-permute-start | bytes 294920 | tf_op jit(solution)/shard_map/while/body/eval_jaxpr/ppermute | solution.py:19
  149.7 5.8 %collective-permute-start.1 = (f32[1536,16]{0,1:T(8,128)S(1)}, f32[1536,16]{0,1:T(8,128)S(1)}, u32[]{:S(2)}, u32[]{:S(2)}) collective-permute-start(f32[1536,16]{0,1:T(8,128)S(1)} %slice_add_fusion.9), channel_id=1, source_target_pairs={{0,12},{4,8},{8,4},{12,0},{16,28},{20,24},{24,20},{28,16},{32,44},... | collective-permute-start | bytes 294920 | tf_op jit(solution)/shard_map/while/body/eval_jaxpr/ppermute | solution.py:19
  156.0 6.2 %collective-permute-start.3 = (f32[1536,16]{0,1:T(8,128)S(1)}, f32[1536,16]{0,1:T(8,128)S(1)}, u32[]{:S(2)}, u32[]{:S(2)}) collective-permute-start(f32[1536,16]{0,1:T(8,128)S(1)} %add_add_fusion.8), channel_id=1, source_target_pairs={{0,32},{4,36},{8,40},{12,44},{16,48},{20,52},{24,56},{28,60},{32,0... | collective-permute-start | bytes 294920 | tf_op jit(solution)/shard_map/while/body/eval_jaxpr/ppermute | solution.py:19
  157.8 5.8 %collective-permute-start.4 = (f32[1536,16]{0,1:T(8,128)S(1)}, f32[1536,16]{0,1:T(8,128)S(1)}, u32[]{:S(2)}, u32[]{:S(2)}) collective-permute-start(f32[1536,16]{0,1:T(8,128)S(1)} %add_add_fusion.8), channel_id=1, source_target_pairs={{0,48},{4,52},{8,56},{12,60},{16,32},{20,36},{24,40},{28,44},{32,1... | collective-permute-start | bytes 294920 | tf_op jit(solution)/shard_map/while/body/eval_jaxpr/ppermute | solution.py:19
  159.4 4.6 %collective-permute-start.5 = (f32[1536,16]{0,1:T(8,128)S(1)}, f32[1536,16]{0,1:T(8,128)S(1)}, u32[]{:S(2)}, u32[]{:S(2)}) collective-permute-start(f32[1536,16]{0,1:T(8,128)S(1)} %add_add_fusion.8), channel_id=1, source_target_pairs={{0,16},{4,20},{8,24},{12,28},{16,0},{20,4},{24,8},{28,12},{32,48},... | collective-permute-start | bytes 294920 | tf_op jit(solution)/shard_map/while/body/eval_jaxpr/ppermute | solution.py:19
  164.0 6.2 %collective-permute-start.6 = (f32[1536,16]{0,1:T(8,128)S(1)}, f32[1536,16]{0,1:T(8,128)S(1)}, u32[]{:S(2)}, u32[]{:S(2)}) collective-permute-start(f32[1536,16]{0,1:T(8,128)S(1)} %add_add_fusion.9), channel_id=1, source_target_pairs={{0,64},{4,68},{8,72},{12,76},{16,80},{20,84},{24,88},{28,92},{32,9... | collective-permute-start | bytes 294920 | tf_op jit(solution)/shard_map/while/body/eval_jaxpr/ppermute | solution.py:19
  180.0 6.2 %collective-permute-start = (f32[1536,16]{0,1:T(8,128)S(1)}, f32[1536,16]{0,1:T(8,128)S(1)}, u32[]{:S(2)}, u32[]{:S(2)}) collective-permute-start(f32[1536,16]{0,1:T(8,128)S(1)} %slice_add_fusion.9), channel_id=1, source_target_pairs={{0,8},{4,12},{8,0},{12,4},{16,24},{20,28},{24,16},{28,20},{32,40},... | collective-permute-start | bytes 294920 | tf_op jit(solution)/shard_map/while/body/eval_jaxpr/ppermute | solution.py:19
  181.7 5.8 %collective-permute-start.1 = (f32[1536,16]{0,1:T(8,128)S(1)}, f32[1536,16]{0,1:T(8,128)S(1)}, u32[]{:S(2)}, u32[]{:S(2)}) collective-permute-start(f32[1536,16]{0,1:T(8,128)S(1)} %slice_add_fusion.9), channel_id=1, source_target_pairs={{0,12},{4,8},{8,4},{12,0},{16,28},{20,24},{24,20},{28,16},{32,44},... | collective-permute-start | bytes 294920 | tf_op jit(solution)/shard_map/while/body/eval_jaxpr/ppermute | solution.py:19
  187.7 6.2 %collective-permute-start.3 = (f32[1536,16]{0,1:T(8,128)S(1)}, f32[1536,16]{0,1:T(8,128)S(1)}, u32[]{:S(2)}, u32[]{:S(2)}) collective-permute-start(f32[1536,16]{0,1:T(8,128)S(1)} %add_add_fusion.8), channel_id=1, source_target_pairs={{0,32},{4,36},{8,40},{12,44},{16,48},{20,52},{24,56},{28,60},{32,0... | collective-permute-start | bytes 294920 | tf_op jit(solution)/shard_map/while/body/eval_jaxpr/ppermute | solution.py:19
  189.2 5.8 %collective-permute-start.4 = (f32[1536,16]{0,1:T(8,128)S(1)}, f32[1536,16]{0,1:T(8,128)S(1)}, u32[]{:S(2)}, u32[]{:S(2)}) collective-permute-start(f32[1536,16]{0,1:T(8,128)S(1)} %add_add_fusion.8), channel_id=1, source_target_pairs={{0,48},{4,52},{8,56},{12,60},{16,32},{20,36},{24,40},{28,44},{32,1... | collective-permute-start | bytes 294920 | tf_op jit(solution)/shard_map/while/body/eval_jaxpr/ppermute | solution.py:19
  195.2 6.2 %collective-permute-start.6 = (f32[1536,16]{0,1:T(8,128)S(1)}, f32[1536,16]{0,1:T(8,128)S(1)}, u32[]{:S(2)}, u32[]{:S(2)}) collective-permute-start(f32[1536,16]{0,1:T(8,128)S(1)} %add_add_fusion.9), channel_id=1, source_target_pairs={{0,64},{4,68},{8,72},{12,76},{16,80},{20,84},{24,88},{28,92},{32,9... | collective-permute-start | bytes 294920 | tf_op jit(solution)/shard_map/while/body/eval_jaxpr/ppermute | solution.py:19
  211.2 6.2 %collective-permute-start = (f32[1536,16]{0,1:T(8,128)S(1)}, f32[1536,16]{0,1:T(8,128)S(1)}, u32[]{:S(2)}, u32[]{:S(2)}) collective-permute-start(f32[1536,16]{0,1:T(8,128)S(1)} %slice_add_fusion.9), channel_id=1, source_target_pairs={{0,8},{4,12},{8,0},{12,4},{16,24},{20,28},{24,16},{28,20},{32,40},... | collective-permute-start | bytes 294920 | tf_op jit(solution)/shard_map/while/body/eval_jaxpr/ppermute | solution.py:19
  212.9 5.8 %collective-permute-start.1 = (f32[1536,16]{0,1:T(8,128)S(1)}, f32[1536,16]{0,1:T(8,128)S(1)}, u32[]{:S(2)}, u32[]{:S(2)}) collective-permute-start(f32[1536,16]{0,1:T(8,128)S(1)} %slice_add_fusion.9), channel_id=1, source_target_pairs={{0,12},{4,8},{8,4},{12,0},{16,28},{20,24},{24,20},{28,16},{32,44},... | collective-permute-start | bytes 294920 | tf_op jit(solution)/shard_map/while/body/eval_jaxpr/ppermute | solution.py:19
  219.1 6.2 %collective-permute-start.3 = (f32[1536,16]{0,1:T(8,128)S(1)}, f32[1536,16]{0,1:T(8,128)S(1)}, u32[]{:S(2)}, u32[]{:S(2)}) collective-permute-start(f32[1536,16]{0,1:T(8,128)S(1)} %add_add_fusion.8), channel_id=1, source_target_pairs={{0,32},{4,36},{8,40},{12,44},{16,48},{20,52},{24,56},{28,60},{32,0... | collective-permute-start | bytes 294920 | tf_op jit(solution)/shard_map/while/body/eval_jaxpr/ppermute | solution.py:19
  221.0 5.8 %collective-permute-start.4 = (f32[1536,16]{0,1:T(8,128)S(1)}, f32[1536,16]{0,1:T(8,128)S(1)}, u32[]{:S(2)}, u32[]{:S(2)}) collective-permute-start(f32[1536,16]{0,1:T(8,128)S(1)} %add_add_fusion.8), channel_id=1, source_target_pairs={{0,48},{4,52},{8,56},{12,60},{16,32},{20,36},{24,40},{28,44},{32,1... | collective-permute-start | bytes 294920 | tf_op jit(solution)/shard_map/while/body/eval_jaxpr/ppermute | solution.py:19
  227.2 6.2 %collective-permute-start.6 = (f32[1536,16]{0,1:T(8,128)S(1)}, f32[1536,16]{0,1:T(8,128)S(1)}, u32[]{:S(2)}, u32[]{:S(2)}) collective-permute-start(f32[1536,16]{0,1:T(8,128)S(1)} %add_add_fusion.9), channel_id=1, source_target_pairs={{0,64},{4,68},{8,72},{12,76},{16,80},{20,84},{24,88},{28,92},{32,9... | collective-permute-start | bytes 294920 | tf_op jit(solution)/shard_map/while/body/eval_jaxpr/ppermute | solution.py:19
  241.9 10.9 %collective-permute-start.16 = (f32[16]{0:T(128)S(1)}, f32[16]{0:T(128)S(1)}, u32[]{:S(2)}, u32[]{:S(2)}) collective-permute-start(f32[16]{0:T(128)S(1)} %get-tuple-element.35), channel_id=1, source_target_pairs={{0,4},{4,0},{8,12},{12,8},{16,20},{20,16},{24,28},{28,24},{32,36},... | collective-permute-start | bytes 200 | tf_op jit(solution)/shard_map/ppermute | solution.py:19
  242.3 10.5 %collective-permute-start.17 = (f32[16]{0:T(128)S(1)}, f32[16]{0:T(128)S(1)}, u32[]{:S(2)}, u32[]{:S(2)}) collective-permute-start(f32[16]{0:T(128)S(1)} %get-tuple-element.35), channel_id=1, source_target_pairs={{0,8},{4,12},{8,0},{12,4},{16,24},{20,28},{24,16},{28,20},{32,40},... | collective-permute-start | bytes 200 | tf_op jit(solution)/shard_map/ppermute | solution.py:19
  245.2 7.6 %collective-permute-start.18 = (f32[16]{0:T(128)S(1)}, f32[16]{0:T(128)S(1)}, u32[]{:S(2)}, u32[]{:S(2)}) collective-permute-start(f32[16]{0:T(128)S(1)} %get-tuple-element.35), channel_id=1, source_target_pairs={{0,12},{4,8},{8,4},{12,0},{16,28},{20,24},{24,20},{28,16},{32,44},... | collective-permute-start | bytes 200 | tf_op jit(solution)/shard_map/ppermute | solution.py:19
  252.8 4.8 %collective-permute-start.19 = (f32[16]{0:T(128)S(1)}, f32[16]{0:T(128)S(1)}, u32[]{:S(2)}, u32[]{:S(2)}) collective-permute-start(f32[16]{0:T(128)S(1)} %add_add_fusion.5), channel_id=1, source_target_pairs={{0,16},{4,20},{8,24},{12,28},{16,0},{20,4},{24,8},{28,12},{32,48},... | collective-permute-start | bytes 200 | tf_op jit(solution)/shard_map/ppermute | solution.py:19
  253.1 5.1 %collective-permute-start.20 = (f32[16]{0:T(128)S(1)}, f32[16]{0:T(128)S(1)}, u32[]{:S(2)}, u32[]{:S(2)}) collective-permute-start(f32[16]{0:T(128)S(1)} %add_add_fusion.5), channel_id=1, source_target_pairs={{0,32},{4,36},{8,40},{12,44},{16,48},{20,52},{24,56},{28,60},{32,0... | collective-permute-start | bytes 200 | tf_op jit(solution)/shard_map/ppermute | solution.py:19
  256.1 4.8 %collective-permute-start.21 = (f32[16]{0:T(128)S(1)}, f32[16]{0:T(128)S(1)}, u32[]{:S(2)}, u32[]{:S(2)}) collective-permute-start(f32[16]{0:T(128)S(1)} %add_add_fusion.5), channel_id=1, source_target_pairs={{0,48},{4,52},{8,56},{12,60},{16,32},{20,36},{24,40},{28,44},{32,1... | collective-permute-start | bytes 200 | tf_op jit(solution)/shard_map/ppermute | solution.py:19
  260.8 5.1 %collective-permute-start.22 = (f32[16]{0:T(128)S(1)}, f32[16]{0:T(128)S(1)}, u32[]{:S(2)}, u32[]{:S(2)}) collective-permute-start(f32[16]{0:T(128)S(1)} %add_add_fusion.4), channel_id=1, source_target_pairs={{0,64},{4,68},{8,72},{12,76},{16,80},{20,84},{24,88},{28,92},{32,9... | collective-permute-start | bytes 200 | tf_op jit(solution)/shard_map/ppermute | solution.py:19
  (23 other events, 139.4 us)
